TPU v7x, 32 devices: a whole 2x2x4 slice. The times are simulated.
32 devices in a mesh: leaf: 8 (over z, y), case: 4 (over x, core).
Axes of the slice: x: 2, y: 2, z: 4, core: 2. Of those that a mesh axis runs over, the one named last changes fastest.
Arguments:
- features: bfloat16 [8, 16384, 128], P('case', 'leaf'), may hold values from -6 to 6
- cotangent: bfloat16 [8, 16384, 128], P('case', 'leaf'), may hold values from -6 to 6
- kernel_blocks: bfloat16 [128, 12, 128, 128], P('leaf'), may hold values from -0.15625 to 0.15625
- near_pairs: int32 [128, 12], P('leaf'), may hold values from 0 to 127, as said below
- leaf_basis: bfloat16 [64, 16384], P(None, 'leaf'), may hold values from -0.125 to 0.125
- w_near: bfloat16 [128, 128], replicated, may hold values from -0.5 to 0.5
- w_far: bfloat16 [128, 128], replicated, may hold values from -0.5 to 0.5
- translations: float32 [3, 64, 64], replicated, may hold values from -0.75 to 0.75
Outputs:
- output: bfloat16 [8, 16384, 128], P('case', 'leaf')
- grad_features: bfloat16 [8, 16384, 128], P('case', 'leaf')
- grad_near: float32 [128, 128], replicated
- grad_far: float32 [128, 128], replicated
Inputs may be any that keep to these rules, and one draw needn't show every extreme that they name: `near_pairs`: A target block held by one index of leaf names blocks of that index, or blocks at most 8 places beyond its first or last block; on every index both of these farthest blocks occur where they exist; 0 and 127 both occur.
All inputs are finite; a program needn't handle non-finite values.
Results may differ from a plain program's by a relative error of at most 0.0085.
Values may be sent and summed in bfloat16 or wider, within the bound.
No kernel may reach another device: no remote copies, remote signals or barrier semaphores. Data moves between devices by JAX's collectives and lax.ppermute only.
A program may use at most 128 MiB of HBM per device.

v0:
```python
import math

import jax
import jax.numpy as jnp
from jax import lax
from jax.sharding import PartitionSpec as P


def partner(shard, axis, apart):
    return lax.ppermute(shard, axis, [(i, i ^ 1 << apart) for i in range(lax.axis_size(axis))])


def with_halo(cells, sides, width):
    for axis, dim in sides:
        count = lax.axis_size(axis)
        ends = count - 1
        head = lax.slice_in_dim(cells, 0, width, axis=dim)
        tail = lax.slice_in_dim(cells, cells.shape[dim] - width, cells.shape[dim], axis=dim)
        cells = jnp.concatenate(
            [
                lax.ppermute(tail, axis, [(i, (i + 1) % count) for i in range(ends)]),
                cells,
                lax.ppermute(head, axis, [((i + 1) % count, i) for i in range(ends)]),
            ],
            axis=dim,
        )
    return cells


def shifted(value, axis, steps):
    count = lax.axis_size(axis)
    leading, last = (max(0, -steps), min(count, count - steps))
    return lax.ppermute(value, axis, [(source, source + steps) for source in range(leading, last)])


def apply_level(matrix, sibling, flipped):
    if flipped:
        return jnp.einsum("sr,asc->arc", matrix, sibling, precision=lax.Precision.HIGHEST)
    return jnp.einsum("rs,asc->arc", matrix, sibling, precision=lax.Precision.HIGHEST)


def expand(own_value, translations, flipped):
    depth_count = lax.axis_size("leaf").bit_length() - 1
    summed = jnp.zeros(own_value.shape, jnp.float32)
    node_value = own_value
    for height in range(depth_count):
        sibling = partner(node_value, "leaf", height)
        summed = summed + apply_level(translations[height], sibling, flipped)
        node_value = node_value + sibling
    return summed


def on_device(
    features, cotangent, kernel_blocks, near_pairs, leaf_basis, w_near, w_far, translations
):
    cases_here, points_here, width = features.shape
    blocks_here, pair_count, block_rows = (
        kernel_blocks.shape[0],
        kernel_blocks.shape[1],
        kernel_blocks.shape[2],
    )
    position = lax.axis_index("leaf")
    extended = with_halo(features, (("leaf", 1),), points_here)
    span_blocks = blocks_here + 2 * blocks_here
    ext_blocks = extended.reshape(cases_here, span_blocks, block_rows, width)
    local_ids = (near_pairs - (position * blocks_here - blocks_here)).reshape(-1)
    picked = jnp.take(ext_blocks, local_ids, axis=1).reshape(
        cases_here, blocks_here, pair_count, block_rows, width
    )
    near_sum = jnp.einsum(
        "bkij,abkjc->abic", kernel_blocks, picked, preferred_element_type=jnp.float32
    )
    near_bf = near_sum.reshape(cases_here, points_here, width).astype(jnp.bfloat16)
    summary = jnp.einsum("rp,apc->arc", leaf_basis, features, preferred_element_type=jnp.float32)
    expansion = expand(summary, translations, False)
    exp_bf = expansion.astype(jnp.bfloat16)
    far_coeff = jnp.einsum("arc,cd->ard", exp_bf, w_far, preferred_element_type=jnp.float32).astype(
        jnp.bfloat16
    )
    far_field = jnp.einsum("rp,ard->apd", leaf_basis, far_coeff, preferred_element_type=jnp.float32)
    mixed = (
        jnp.einsum("apc,cd->apd", near_bf, w_near, preferred_element_type=jnp.float32) + far_field
    )
    output = jax.nn.gelu(mixed).astype(jnp.bfloat16)
    _, pullback = jax.vjp(jax.nn.gelu, mixed)
    slope = pullback(cotangent.astype(jnp.float32))[0].astype(jnp.bfloat16)
    projected = jnp.einsum(
        "rp,apc->arc", leaf_basis, slope, preferred_element_type=jnp.float32
    ).astype(jnp.bfloat16)
    back_coeff = jnp.einsum("arc,dc->ard", projected, w_far, preferred_element_type=jnp.float32)
    back_exp = expand(back_coeff, translations, True)
    back_far = jnp.einsum(
        "rp,arc->apc", leaf_basis, back_exp.astype(jnp.bfloat16), preferred_element_type=jnp.float32
    )
    back_near = jnp.einsum("apc,dc->apd", slope, w_near, preferred_element_type=jnp.float32).astype(
        jnp.bfloat16
    )
    back_blocks = back_near.reshape(cases_here, blocks_here, block_rows, width)
    contrib = jnp.einsum(
        "bkij,abic->bkajc", kernel_blocks, back_blocks, preferred_element_type=jnp.float32
    )
    contrib = contrib.reshape(blocks_here * pair_count, cases_here, block_rows, width)
    landed = jax.ops.segment_sum(contrib, local_ids, num_segments=span_blocks)
    left_part = landed[:blocks_here]
    middle_part = landed[blocks_here : blocks_here + blocks_here]
    right_part = landed[blocks_here + blocks_here :]
    from_next = shifted(left_part.astype(jnp.bfloat16), "leaf", -1).astype(left_part.dtype)
    from_prev = shifted(right_part.astype(jnp.bfloat16), "leaf", 1).astype(right_part.dtype)
    gathered_near = middle_part + from_next + from_prev
    back_near_sum = gathered_near.transpose(1, 0, 2, 3).reshape(cases_here, points_here, width)
    grad_features = (back_near_sum + back_far).astype(jnp.bfloat16)
    scale = 1.0 / math.sqrt(
        cases_here * lax.axis_size("case") * points_here * lax.axis_size("leaf")
    )
    near_term = (
        jnp.einsum("apc,apd->cd", near_bf, slope, preferred_element_type=jnp.float32) * scale
    )
    far_term = (
        jnp.einsum("arc,ard->cd", exp_bf, projected, preferred_element_type=jnp.float32) * scale
    )
    grad_near, grad_far = lax.psum((near_term, far_term), ("leaf", "case"))
    return (output, grad_features, grad_near, grad_far)


def solution(mesh):
    return jax.shard_map(
        on_device,
        mesh=mesh,
        in_specs=(
            P("case", "leaf", None),
            P("case", "leaf", None),
            P("leaf", None, None, None),
            P("leaf", None),
            P(None, "leaf"),
            P(),
            P(),
            P(),
        ),
        out_specs=(P("case", "leaf", None), P("case", "leaf", None), P(), P()),
        check_vma=False,
    )
```

profile of v0, /device:TPU:16, one launch (start us, length us, event | category | flops | bytes accessed | tf_op | source)
XLA Modules:
  0.0 356.6 jit_solution(16556230183017255712)
XLA Ops:
  7.2 3.6 collective-permute-start
  10.8 3.3 collective-permute-start.1
  14.1 1.6 convolution_bitcast_fusion.3
  17.3 41.9 %collective-permute-done.2 = f32[2,64,128]{2,1,0:T(8,128)S(1)} collective-permute-done((f32[2,64,128]{2,1,0:T(8,128)S(1)}, f32[2,64,128]{2,1,0:T(8,128)S(1)}, u32[]{:S(2)}, u32[]{:S(2)}) %collective-permute-start.2) | collective-permute-done | bytes 65568 | tf_op jit(solution)/shard_map/ppermute | solution.py:10
  59.2 1.6 collective-permute-start.3
  60.8 2.7 collective-permute-done.3
  64.6 4.2 %collective-permute-done.4 = f32[2,64,128]{2,1,0:T(8,128)S(1)} collective-permute-done((f32[2,64,128]{2,1,0:T(8,128)S(1)}, f32[2,64,128]{2,1,0:T(8,128)S(1)}, u32[]{:S(2)}, u32[]{:S(2)}) %collective-permute-start.4) | collective-permute-done | bytes 65568 | tf_op jit(solution)/shard_map/ppermute | solution.py:10
  71.0 2.0 pad_maximum_fusion
  72.9 8.2 %gather_fusion = bf16[192,2,128,128]{3,2,1,0:T(8,128)(2,1)} fusion(bf16[2,48,128,128]{3,2,1,0:T(8,128)(2,1)S(1)} %bitcast.123, s32[1024]{0:T(1024)S(1)} %pad_clamp_fusion), kind=kCustom, calls=%fused_computation | custom fusion | bytes 25166592 | tf_op jit(solution)/shard_map/jit(_take)/gather | solution.py:67
  81.1 6.5 %copy.24 = bf16[2,192,128,128]{3,2,1,0:T(8,128)(2,1)S(1)} copy(bf16[2,192,128,128]{3,2,0,1:T(8,128)(2,1)} %bitcast.124) | data formatting | bytes 25165824 | tf_op jit(solution)/shard_map/jit(_take)/gather | solution.py:67
  87.7 5.5 %fusion.21 = bf16[2,16,128,128]{3,2,0,1:T(8,128)(2,1)} fusion(bf16[16,12,128,128]{3,2,1,0:T(8,128)(2,1)} %param.10, bf16[2,16,12,128,128]{4,3,2,1,0:T(8,128)(2,1)S(1)} %bitcast.125, pred[16,12]{1,0:T(8,128)(4,1)S(1)} %get-tuple-element.18), kind=kOutput, calls=%fused_computation.33 | convolution fusion | flops 1617428480 | bytes 19923136 | tf_op jit(solution)/shard_map/bkij,abkjc->abic/dot_general | solution.py:70
  94.5 1.8 fusion.55
  96.3 5.0 %fusion.7 = (bf16[2,2048,128]{2,1,0:T(8,128)(2,1)S(1)}, bf16[2,2048,128]{2,1,0:T(8,128)(2,1)}) fusion(bf16[2,2048,128]{2,1,0:T(8,128)(2,1)} %param.9, f32[2,2048,128]{2,1,0:T(8,128)} %fusion.55, bf16[64,2048]{1,0:T(8,128)(2,1)S(1)} %copy-done, bf16[2,64,128]{2,1,0:T(8,128)(2,1)S(1)} %fusion.34, bf16[128,128]{1,0:T(8,128)(2,1)S(1)} %copy-done.8), kind=kOutput, calls=%fused_computation.19 | convolution fusion | flops 83902464 | bytes 5570560 | tf_op jit(solution)/shard_map/rp,ard->apd/dot_general | solution.py:80
  103.3 12.9 %convolution_bitcast_fusion = f32[16,12,2,128,128]{3,4,1,2,0:T(8,128)} fusion(bf16[16,12,128,128]{3,2,1,0:T(8,128)(2,1)} %param.10, bf16[2,16,128,128,1]{3,2,1,0,4:T(8,128)(2,1)S(1)} %bitcast.128), kind=kOutput, calls=%fused_computation.5 | convolution fusion | flops 1610612736 | bytes 32505856 | tf_op jit(solution)/shard_map/bkij,abic->bkajc/dot_general | solution.py:99
  116.3 24.7 %copy.29 = f32[16,12,2,128,128]{4,3,2,1,0:T(8,128)} copy(f32[16,12,2,128,128]{3,4,1,2,0:T(8,128)} %convolution_bitcast_fusion) | data formatting | bytes 50331648 | tf_op jit(solution)/shard_map/bkij,abic->bkajc/transpose | solution.py:99
  141.0 3.5 broadcast_in_dim.15
  144.5 56.8 %scatter_fusion = f32[48,2,128,128]{3,2,1,0:T(8,128)} fusion(f32[48,2,128,128]{3,2,1,0:T(8,128)} %broadcast_in_dim.15, s32[192]{0:T(256)S(1)} %reshape.77, f32[192,2,128,128]{3,2,1,0:T(8,128)} %bitcast.122), kind=kCustom, calls=%fused_computation.1 | custom fusion | flops 6291456 | bytes 75498240 | tf_op jit(solution)/shard_map/scatter-add | solution.py:103
  201.3 3.5 convert.4
  207.0 3.0 collective-permute-start.5
  210.0 3.0 collective-permute-start.6
  213.9 1.5 collective-permute-start.8
  216.3 18.1 %collective-permute-done.8 = f32[2,64,128]{2,1,0:T(8,128)S(1)} collective-permute-done((f32[2,64,128]{2,1,0:T(8,128)S(1)}, f32[2,64,128]{2,1,0:T(8,128)S(1)}, u32[]{:S(2)}, u32[]{:S(2)}) %collective-permute-start.8) | collective-permute-done | bytes 65568 | tf_op jit(solution)/shard_map/ppermute | solution.py:10
  234.8 4.9 %collective-permute-done.9 = f32[2,64,128]{2,1,0:T(8,128)S(1)} collective-permute-done((f32[2,64,128]{2,1,0:T(8,128)S(1)}, f32[2,64,128]{2,1,0:T(8,128)S(1)}, u32[]{:S(2)}, u32[]{:S(2)}) %collective-permute-start.9) | collective-permute-done | bytes 65568 | tf_op jit(solution)/shard_map/ppermute | solution.py:10
  241.1 1.8 convolution_bitcast_fusion.1
  242.8 11.3 %collective-permute-done.5 = bf16[16,2,128,128]{3,2,1,0:T(8,128)(2,1)S(1)} collective-permute-done((bf16[16,2,128,128]{3,2,1,0:T(8,128)(2,1)}, bf16[16,2,128,128]{3,2,1,0:T(8,128)(2,1)S(1)}, u32[]{:S(2)}, u32[]{:S(2)}) %collective-permute-start.5) | collective-permute-done | bytes 1048608 | tf_op jit(solution)/shard_map/ppermute | solution.py:33
  255.1 2.6 fusion.16
  257.7 2.0 copy.30
  259.6 2.8 reshape.66
  262.5 1.8 add_convert_fusion
  265.6 81.2 %all-reduce.3.cloned.1.call-done = (f32[128,128]{1,0:T(8,128)}, f32[128,128]{1,0:T(8,128)}) async-done(((f32[128,128]{1,0:T(8,128)}, f32[128,128]{1,0:T(8,128)}), (f32[128,128]{1,0:T(8,128)}, f32[128,128]{1,0:T(8,128)})) %all-reduce.3.cloned.1.call-update) | async-done | bytes 131088 | tf_op jit(solution)/shard_map/psum | solution.py:121
  346.8 1.5 copy.60
  348.3 1.5 copy.61
  (51 shorter events, 16.1 us)
Async XLA Ops:
  7.2 7.0 %copy-start = (bf16[64,2048]{1,0:T(8,128)(2,1)S(1)}, bf16[64,2048]{1,0:T(8,128)(2,1)}, u32[]{:S(2)}) copy-start(bf16[64,2048]{1,0:T(8,128)(2,1)} %param.12) | copy-start | bytes 786436
  7.2 62.6 %copy-start.4 = (f32[3,64,64]{2,1,0:T(8,128)S(1)}, f32[3,64,64]{2,1,0:T(8,128)}, u32[]{:S(2)}) copy-start(f32[3,64,64]{2,1,0:T(8,128)} %param.15) | copy-start | bytes 147460
  7.2 339.6 %all-reduce.3.cloned.1.call-start = ((), (), s32[]{:S(2)}) async-start(), calls=%async_computation | async-start | bytes 262144 | tf_op jit(solution)/shard_map/psum | solution.py:121
  7.2 62.8 %collective-permute-start = (bf16[2,2048,128]{2,1,0:T(8,128)(2,1)}, bf16[2,2048,128]{2,1,0:T(8,128)(2,1)S(1)}, u32[]{:S(2)}, u32[]{:S(2)}) collective-permute-start(bf16[2,2048,128]{2,1,0:T(8,128)(2,1)} %param.8), channel_id=1, source_target_pairs={{0,4},{4,8},{8,12},{12,16},{16,20},{20,24},{24,28},{1,5},{5,9},{9,... | collective-permute-start | bytes 3145736 | tf_op jit(solution)/shard_map/ppermute | solution.py:21
  10.8 60.2 %collective-permute-start.1 = (bf16[2,2048,128]{2,1,0:T(8,128)(2,1)}, bf16[2,2048,128]{2,1,0:T(8,128)(2,1)}, u32[]{:S(2)}, u32[]{:S(2)}) collective-permute-start(bf16[2,2048,128]{2,1,0:T(8,128)(2,1)} %param.8), channel_id=1, source_target_pairs={{4,0},{8,4},{12,8},{16,12},{20,16},{24,20},{28,24},{5,1},{9,5},{13... | collective-permute-start | bytes 3145736 | tf_op jit(solution)/shard_map/ppermute | solution.py:23
  15.7 43.4 %collective-permute-start.2 = (f32[2,64,128]{2,1,0:T(8,128)S(1)}, f32[2,64,128]{2,1,0:T(8,128)S(1)}, u32[]{:S(2)}, u32[]{:S(2)}) collective-permute-start(f32[2,64,128]{2,1,0:T(8,128)S(1)} %convolution_bitcast_fusion.3), channel_id=1, source_target_pairs={{0,4},{4,0},{8,12},{12,8},{16,20},{20,16},{24,28},{28,24},{1,5},{5... | collective-permute-start | bytes 196616 | tf_op jit(solution)/shard_map/ppermute | solution.py:10
  59.2 4.3 %collective-permute-start.3 = (f32[2,64,128]{2,1,0:T(8,128)S(1)}, f32[2,64,128]{2,1,0:T(8,128)S(1)}, u32[]{:S(2)}, u32[]{:S(2)}) collective-permute-start(f32[2,64,128]{2,1,0:T(8,128)S(1)} %add.82), channel_id=1, source_target_pairs={{0,8},{4,12},{8,0},{12,4},{16,24},{20,28},{24,16},{28,20},{1,9},{5... | collective-permute-start | bytes 196616 | tf_op jit(solution)/shard_map/ppermute | solution.py:10
  63.5 5.3 %collective-permute-start.4 = (f32[2,64,128]{2,1,0:T(8,128)S(1)}, f32[2,64,128]{2,1,0:T(8,128)S(1)}, u32[]{:S(2)}, u32[]{:S(2)}) collective-permute-start(f32[2,64,128]{2,1,0:T(8,128)S(1)} %add.84), channel_id=1, source_target_pairs={{0,16},{4,20},{8,24},{12,28},{16,0},{20,4},{24,8},{28,12},{1,17},{... | collective-permute-start | bytes 196616 | tf_op jit(solution)/shard_map/ppermute | solution.py:10
  70.0 26.3 %copy-start.6 = (bf16[2,64,128]{2,1,0:T(8,128)(2,1)}, bf16[2,64,128]{2,1,0:T(8,128)(2,1)S(1)}, u32[]{:S(2)}) copy-start(bf16[2,64,128]{2,1,0:T(8,128)(2,1)S(1)} %fusion.34) | copy-start | bytes 98308
  70.0 1.0 copy-start.2
  93.2 1.3 copy-start.5
  94.5 1.8 copy-start.8
  102.8 110.2 %collective-permute-start.7 = (f32[2,64,128]{2,1,0:T(8,128)}, f32[2,64,128]{2,1,0:T(8,128)}, u32[]{:S(2)}, u32[]{:S(2)}) collective-permute-start(f32[2,64,128]{2,1,0:T(8,128)} %fusion.40), channel_id=1, source_target_pairs={{0,4},{4,0},{8,12},{12,8},{16,20},{20,16},{24,28},{28,24},{1,5},{5... | collective-permute-start | bytes 196616 | tf_op jit(solution)/shard_map/ppermute | solution.py:10
  205.9 9.6 %copy-start.7 = (bf16[2,64,128]{2,1,0:T(8,128)(2,1)S(1)}, bf16[2,64,128]{2,1,0:T(8,128)(2,1)}, u32[]{:S(2)}) copy-start(bf16[2,64,128]{2,1,0:T(8,128)(2,1)} %copy-done.6) | copy-start | bytes 98308
  207.0 47.1 %collective-permute-start.5 = (bf16[16,2,128,128]{3,2,1,0:T(8,128)(2,1)}, bf16[16,2,128,128]{3,2,1,0:T(8,128)(2,1)S(1)}, u32[]{:S(2)}, u32[]{:S(2)}) collective-permute-start(bf16[16,2,128,128]{3,2,1,0:T(8,128)(2,1)} %get-tuple-element.20), channel_id=1, source_target_pairs={{4,0},{8,4},{12,8},{16,12},{20,16},{24,20},{28,24},{5,1},{9,5},{13... | collective-permute-start | bytes 3145736 | tf_op jit(solution)/shard_map/ppermute | solution.py:33
  210.0 45.1 %collective-permute-start.6 = (bf16[16,2,128,128]{3,2,1,0:T(8,128)(2,1)S(1)}, bf16[16,2,128,128]{3,2,1,0:T(8,128)(2,1)}, u32[]{:S(2)}, u32[]{:S(2)}) collective-permute-start(bf16[16,2,128,128]{3,2,1,0:T(8,128)(2,1)S(1)} %get-tuple-element.21), channel_id=1, source_target_pairs={{0,4},{4,8},{8,12},{12,16},{16,20},{20,24},{24,28},{1,5},{5,9},{9,... | collective-permute-start | bytes 3145736 | tf_op jit(solution)/shard_map/ppermute | solution.py:33
  213.9 20.5 %collective-permute-start.8 = (f32[2,64,128]{2,1,0:T(8,128)S(1)}, f32[2,64,128]{2,1,0:T(8,128)S(1)}, u32[]{:S(2)}, u32[]{:S(2)}) collective-permute-start(f32[2,64,128]{2,1,0:T(8,128)S(1)} %add.91), channel_id=1, source_target_pairs={{0,8},{4,12},{8,0},{12,4},{16,24},{20,28},{24,16},{28,20},{1,9},{5... | collective-permute-start | bytes 196616 | tf_op jit(solution)/shard_map/ppermute | solution.py:10
  234.4 5.2 %collective-permute-start.9 = (f32[2,64,128]{2,1,0:T(8,128)S(1)}, f32[2,64,128]{2,1,0:T(8,128)S(1)}, u32[]{:S(2)}, u32[]{:S(2)}) collective-permute-start(f32[2,64,128]{2,1,0:T(8,128)S(1)} %add.93), channel_id=1, source_target_pairs={{0,16},{4,20},{8,24},{12,28},{16,0},{20,4},{24,8},{28,12},{1,17},{... | collective-permute-start | bytes 196616 | tf_op jit(solution)/shard_map/ppermute | solution.py:10
  254.1 1.0 copy-start.3
  259.6 2.9 copy-start.1
Sparse Core Ops, SparseCore 0:
  216.4 130.3 all-reduce.2
where the time goes:
time: 361 us; the launch traced here: 357 us
  waiting for transfers between devices  164 us (45%)
  other arithmetic  68.3 us (19%)
  local copies, waits for them, and re-layouts  56.6 us (16%)
  matrix products  35.7 us (10%)
  starting transfers between devices  17.5 us (5%)
  between operations  14.3 us (4%)
    psum x1, waiting for transfers between devices, on_device(): grad_near, grad_far = lax.psum((near_term, far_term), ('leaf', 'case'))  81.2 us
    ppermute x6, waiting for transfers between devices, partner(): lax.ppermute(shard, axis, [(i, i ^ 1 << apart) for i in range(lax.axis_si...  71.8 us
    scatter-add x1, other arithmetic, on_device(): landed = jax.ops.segment_sum(contrib, local_ids, num_segments=span_blocks)  56.8 us
    transpose x1, local copies, waits for them, and re-layouts, on_device(): jnp.einsum('bkij,abic->bkajc', kernel_blocks, back_blocks, preferred_elem...  24.7 us
    gather x2, local copies, waits for them, and re-layouts, on_device(): jnp.take(ext_blocks, local_ids, axis=1)  14.7 us
    dot_general x1, matrix products, on_device(): jnp.einsum('bkij,abic->bkajc', kernel_blocks, back_blocks, preferred_elem...  12.9 us
    ppermute x2, waiting for transfers between devices, shifted(): lax.ppermute(value, axis, [(source, source + steps) for source in range(l...  11.3 us
  transfers between devices with their start and end apart: 11, of which 7 were waited for; matrix products, arithmetic and copies ran while one was open for 35% of the time, Pallas kernels for 0%

commit v1 on v0

v1 whole, which is shorter than its diff:
```python
import functools
import math

import jax
import jax.numpy as jnp
from jax import lax
from jax.experimental import pallas as pl
from jax.experimental.pallas import tpu as pltpu
from jax.sharding import PartitionSpec as P

HALO = 8
TB = 4


def partner(shard, axis, apart):
    return lax.ppermute(shard, axis, [(i, i ^ 1 << apart) for i in range(lax.axis_size(axis))])


def shifted(value, axis, steps):
    count = lax.axis_size(axis)
    leading, last = (max(0, -steps), min(count, count - steps))
    return lax.ppermute(value, axis, [(source, source + steps) for source in range(leading, last)])


def apply_level(matrix, sibling, flipped):
    if flipped:
        return jnp.einsum("sr,asc->arc", matrix, sibling, precision=lax.Precision.HIGHEST)
    return jnp.einsum("rs,asc->arc", matrix, sibling, precision=lax.Precision.HIGHEST)


def expand(own_value, translations, flipped, rider=None):
    depth_count = lax.axis_size("leaf").bit_length() - 1
    summed = jnp.zeros(own_value.shape, jnp.float32)
    node_value = own_value
    rows = own_value.shape[0] * own_value.shape[1]
    for height in range(depth_count):
        if rider is None:
            sibling = partner(node_value, "leaf", height)
        else:
            packed = jnp.concatenate(
                [node_value.reshape(rows, own_value.shape[2]), rider], axis=0
            )
            got = partner(packed, "leaf", height)
            sibling = got[:rows].reshape(own_value.shape)
            rider = rider + got[rows:]
        summed = summed + apply_level(translations[height], sibling, flipped)
        node_value = node_value + sibling
    return summed, rider


def near_fwd_kernel(cases, pairs, rows, ids_ref, kb_ref, ext_ref, out_ref):
    g = pl.program_id(0)
    for tb in range(TB):
        t = g * TB + tb
        lhs = jnp.concatenate([kb_ref[tb, k] for k in range(pairs)], axis=1)
        parts = []
        for k in range(pairs):
            start = pl.multiple_of(ids_ref[t * pairs + k] * rows, rows)
            parts.append(
                jnp.concatenate([ext_ref[c, pl.ds(start, rows), :] for c in range(cases)], axis=1)
            )
        rhs = jnp.concatenate(parts, axis=0)
        acc = jnp.dot(lhs, rhs, preferred_element_type=jnp.float32)
        width = acc.shape[1] // cases
        for c in range(cases):
            out_ref[c, pl.ds(tb * rows, rows), :] = acc[:, c * width : (c + 1) * width].astype(
                out_ref.dtype
            )


def near_forward(ids, kernel_blocks, extended):
    cases, span_points, width = extended.shape
    blocks_here, pairs, rows, _ = kernel_blocks.shape
    steps = blocks_here // TB
    flops = 2 * blocks_here * pairs * rows * rows * cases * width
    return pl.pallas_call(
        functools.partial(near_fwd_kernel, cases, pairs, rows),
        out_shape=jax.ShapeDtypeStruct((cases, blocks_here * rows, width), jnp.bfloat16),
        grid_spec=pltpu.PrefetchScalarGridSpec(
            num_scalar_prefetch=1,
            grid=(steps,),
            in_specs=[
                pl.BlockSpec((TB, pairs, rows, rows), lambda g, ids: (g, 0, 0, 0)),
                pl.BlockSpec((cases, span_points, width), lambda g, ids: (0, 0, 0)),
            ],
            out_specs=pl.BlockSpec((cases, TB * rows, width), lambda g, ids: (0, g, 0)),
        ),
        compiler_params=pltpu.CompilerParams(dimension_semantics=("arbitrary",)),
        cost_estimate=pl.CostEstimate(
            flops=flops,
            transcendentals=0,
            bytes_accessed=kernel_blocks.size * 2 + extended.size * 2 + cases * blocks_here * rows * width * 2,
        ),
    )(ids, kernel_blocks, extended)


def near_bwd_kernel(cases, pairs, rows, steps, ids_ref, kb_ref, back_ref, mid_ref, lo_ref, hi_ref, acc_ref):
    g = pl.program_id(0)

    @pl.when(g == 0)
    def _():
        acc_ref[...] = jnp.zeros(acc_ref.shape, acc_ref.dtype)

    width = back_ref.shape[2]
    for tb in range(TB):
        t = g * TB + tb
        lhs = jnp.concatenate([kb_ref[tb, k] for k in range(pairs)], axis=1)
        rhs = jnp.concatenate(
            [back_ref[c, pl.ds(tb * rows, rows), :] for c in range(cases)], axis=1
        )
        res = lax.dot_general(
            lhs, rhs, (((0,), (0,)), ((), ())), preferred_element_type=jnp.float32
        )
        for k in range(pairs):
            start = pl.multiple_of(ids_ref[t * pairs + k] * rows, rows)
            piece = res[k * rows : (k + 1) * rows]
            for c in range(cases):
                acc_ref[c, pl.ds(start, rows), :] += piece[:, c * width : (c + 1) * width]

    @pl.when(g == steps - 1)
    def _():
        halo_points = lo_ref.shape[1]
        mid_points = mid_ref.shape[1]
        lo_ref[...] = acc_ref[:, :halo_points, :].astype(lo_ref.dtype)
        mid_ref[...] = acc_ref[:, halo_points : halo_points + mid_points, :]
        hi_ref[...] = acc_ref[:, halo_points + mid_points :, :].astype(hi_ref.dtype)


def near_backward(ids, kernel_blocks, back_near, halo_points):
    cases, points_here, width = back_near.shape
    blocks_here, pairs, rows, _ = kernel_blocks.shape
    steps = blocks_here // TB
    span_points = points_here + 2 * halo_points
    flops = 2 * blocks_here * pairs * rows * rows * cases * width
    return pl.pallas_call(
        functools.partial(near_bwd_kernel, cases, pairs, rows, steps),
        out_shape=(
            jax.ShapeDtypeStruct((cases, points_here, width), jnp.float32),
            jax.ShapeDtypeStruct((cases, halo_points, width), jnp.bfloat16),
            jax.ShapeDtypeStruct((cases, halo_points, width), jnp.bfloat16),
        ),
        grid_spec=pltpu.PrefetchScalarGridSpec(
            num_scalar_prefetch=1,
            grid=(steps,),
            in_specs=[
                pl.BlockSpec((TB, pairs, rows, rows), lambda g, ids: (g, 0, 0, 0)),
                pl.BlockSpec((cases, TB * rows, width), lambda g, ids: (0, g, 0)),
            ],
            out_specs=[
                pl.BlockSpec((cases, points_here, width), lambda g, ids: (0, 0, 0)),
                pl.BlockSpec((cases, halo_points, width), lambda g, ids: (0, 0, 0)),
                pl.BlockSpec((cases, halo_points, width), lambda g, ids: (0, 0, 0)),
            ],
            scratch_shapes=[pltpu.VMEM((cases, span_points, width), jnp.float32)],
        ),
        compiler_params=pltpu.CompilerParams(
            dimension_semantics=("arbitrary",), vmem_limit_bytes=60 * 1024 * 1024
        ),
        cost_estimate=pl.CostEstimate(
            flops=flops,
            transcendentals=0,
            bytes_accessed=kernel_blocks.size * 2 + back_near.size * 2 + cases * span_points * width * 4,
        ),
    )(ids, kernel_blocks, back_near)


def on_device(
    features, cotangent, kernel_blocks, near_pairs, leaf_basis, w_near, w_far, translations
):
    cases_here, points_here, width = features.shape
    blocks_here, pair_count, block_rows = (
        kernel_blocks.shape[0],
        kernel_blocks.shape[1],
        kernel_blocks.shape[2],
    )
    halo_points = HALO * block_rows
    span_blocks = blocks_here + 2 * HALO
    position = lax.axis_index("leaf")

    head = features[:, :halo_points]
    tail = features[:, points_here - halo_points :]
    from_prev = shifted(tail, "leaf", 1)
    from_next = shifted(head, "leaf", -1)
    extended = jnp.concatenate([from_prev, features, from_next], axis=1)
    local_ids = jnp.clip(
        near_pairs - (position * blocks_here - HALO), 0, span_blocks - 1
    ).reshape(-1).astype(jnp.int32)

    near_bf = near_forward(local_ids, kernel_blocks, extended)

    summary = jnp.einsum("rp,apc->arc", leaf_basis, features, preferred_element_type=jnp.float32)
    expansion, _ = expand(summary, translations, False)
    exp_bf = expansion.astype(jnp.bfloat16)
    far_coeff = jnp.einsum("arc,cd->ard", exp_bf, w_far, preferred_element_type=jnp.float32).astype(
        jnp.bfloat16
    )
    far_field = jnp.einsum("rp,ard->apd", leaf_basis, far_coeff, preferred_element_type=jnp.float32)
    mixed = (
        jnp.einsum("apc,cd->apd", near_bf, w_near, preferred_element_type=jnp.float32) + far_field
    )
    output = jax.nn.gelu(mixed).astype(jnp.bfloat16)
    _, pullback = jax.vjp(jax.nn.gelu, mixed)
    slope = pullback(cotangent.astype(jnp.float32))[0].astype(jnp.bfloat16)
    projected = jnp.einsum(
        "rp,apc->arc", leaf_basis, slope, preferred_element_type=jnp.float32
    ).astype(jnp.bfloat16)
    back_near = jnp.einsum("apc,dc->apd", slope, w_near, preferred_element_type=jnp.float32).astype(
        jnp.bfloat16
    )

    mid, lo, hi = near_backward(local_ids, kernel_blocks, back_near, halo_points)

    scale = 1.0 / math.sqrt(
        cases_here * lax.axis_size("case") * points_here * lax.axis_size("leaf")
    )
    near_term = (
        jnp.einsum("apc,apd->cd", near_bf, slope, preferred_element_type=jnp.float32) * scale
    )
    far_term = (
        jnp.einsum("arc,ard->cd", exp_bf, projected, preferred_element_type=jnp.float32) * scale
    )
    grads = jnp.concatenate([near_term, far_term], axis=0)

    back_coeff = jnp.einsum("arc,dc->ard", projected, w_far, preferred_element_type=jnp.float32)
    back_exp, grads = expand(back_coeff, translations, True, rider=grads)
    back_far = jnp.einsum(
        "rp,arc->apc", leaf_basis, back_exp.astype(jnp.bfloat16), preferred_element_type=jnp.float32
    )

    case_depth = lax.axis_size("case").bit_length() - 1
    for height in range(case_depth):
        grads = grads + partner(grads, "case", height)

    got_prev = shifted(hi, "leaf", 1).astype(jnp.float32)
    got_next = shifted(lo, "leaf", -1).astype(jnp.float32)
    near_back = jnp.concatenate(
        [
            mid[:, :halo_points] + got_prev,
            mid[:, halo_points : points_here - halo_points],
            mid[:, points_here - halo_points :] + got_next,
        ],
        axis=1,
    )
    grad_features = (near_back + back_far).astype(jnp.bfloat16)
    grad_near = grads[:width]
    grad_far = grads[width:]
    return (output, grad_features, grad_near, grad_far)


def solution(mesh):
    return jax.shard_map(
        on_device,
        mesh=mesh,
        in_specs=(
            P("case", "leaf", None),
            P("case", "leaf", None),
            P("leaf", None, None, None),
            P("leaf", None),
            P(None, "leaf"),
            P(),
            P(),
            P(),
        ),
        out_specs=(P("case", "leaf", None), P("case", "leaf", None), P(), P()),
        check_vma=False,
    )
```

time: 361 us -> 107 us (0.30)
  waiting for transfers between devices: 164 us -> 46.9 us
  other arithmetic: 68.3 us -> 4.66 us
  local copies, waits for them, and re-layouts: 56.6 us -> 3.32 us
  matrix products: 35.7 us -> 12.7 us
  Pallas kernels: 0 us -> 16.8 us
  between operations: 14.3 us -> 0.96 us
    psum x1 -> x0, waiting for transfers between devices: 81.2 us -> none  [on_device(): grad_near, grad_far = lax.psum((near_term, far_term), ('leaf', 'case'))]
    scatter-add x1 -> x0, other arithmetic: 56.8 us -> none  [on_device(): landed = jax.ops.segment_sum(contrib, local_ids, num_segments=span_blocks)]
    ppermute x6 -> x8, waiting for transfers between devices: 71.8 us -> 27.1 us  [partner(): lax.ppermute(shard, axis, [(i, i ^ 1 << apart) for i in range(lax.axis_si...]
    transpose x2 -> x0, local copies, waits for them, and re-layouts: 26.7 us -> none  [the longest x1 24.7 us: on_device(): jnp.einsum('bkij,abic->bkajc', kernel_blocks, back_blocks, preferred_elem...]
    dot_general x2 -> x0, matrix products: 18.5 us -> none  [the longest x1 12.9 us: on_device(): jnp.einsum('bkij,abic->bkajc', kernel_blocks, back_blocks, preferred_elem...]
    pallas_call x0 -> x2, Pallas kernels: none -> 16.8 us  [the longest x1 9.62 us: near_backward(): pl.pallas_call(functools.partial(near_bwd_kernel, cases, pairs, rows, ste...]
    gather x2 -> x0, local copies, waits for them, and re-layouts: 14.7 us -> none  [on_device(): jnp.take(ext_blocks, local_ids, axis=1)]
    ppermute x2 -> x4, waiting for transfers between devices: 11.3 us -> 19.8 us  [shifted(): lax.ppermute(value, axis, [(source, source + steps) for source in range(l...]
  transfers between devices with their start and end apart: 11 -> 12, of which waited for: 7 -> 7; matrix products, arithmetic and copies ran while one was open for 35% -> 8% of each run, Pallas kernels for 0% -> 9%
where the time goes in v1:
time: 107 us; the launch traced here: 105 us
  waiting for transfers between devices  46.9 us (44%)
  starting transfers between devices  20.2 us (19%)
  Pallas kernels  16.8 us (16%)
  matrix products  12.7 us (12%)
  other arithmetic  4.66 us (4%)
  local copies, waits for them, and re-layouts  3.32 us (3%)
    ppermute x8, waiting for transfers between devices, partner(): lax.ppermute(shard, axis, [(i, i ^ 1 << apart) for i in range(lax.axis_si...  27.1 us
    ppermute x4, waiting for transfers between devices, shifted(): lax.ppermute(value, axis, [(source, source + steps) for source in range(l...  19.8 us
    ppermute x4, starting transfers between devices, shifted(): lax.ppermute(value, axis, [(source, source + steps) for source in range(l...  13.5 us
    pallas_call x1, Pallas kernels, near_backward(): pl.pallas_call(functools.partial(near_bwd_kernel, cases, pairs, rows, ste...  9.62 us
    pallas_call x1, Pallas kernels, near_forward(): pl.pallas_call(functools.partial(near_fwd_kernel, cases, pairs, rows), ou...  7.18 us
    ppermute x8, starting transfers between devices, partner(): lax.ppermute(shard, axis, [(i, i ^ 1 << apart) for i in range(lax.axis_si...  6.7 us
    dot_general x1, matrix products, on_device(): jnp.einsum('apc,cd->apd', near_bf, w_near, preferred_element_type=jnp.flo...  4.54 us
    concatenate x1, other arithmetic, on_device(): extended = jnp.concatenate([from_prev, features, from_next], axis=1)  2.67 us
  transfers between devices with their start and end apart: 12, of which 7 were waited for; matrix products, arithmetic and copies ran while one was open for 8% of the time, Pallas kernels for 9%

profile of v1, /device:TPU:16, one launch (start us, length us, event | category | flops | bytes accessed | tf_op | source)
XLA Modules:
  0.0 105.5 jit_solution(7341077265479465598)
XLA Ops:
  0.7 0.9 copy-done
  1.6 1.5 %convolution_bitcast_fusion.2 = f32[2,64,128]{2,1,0:T(8,128)S(1)} fusion(bf16[2,2048,128]{2,1,0:T(8,128)(2,1)} %param.8, bf16[64,2048]{1,0:T(8,128)(2,1)S(1)} %copy-done), kind=kOutput, calls=%fused_computation.22 | convolution fusion | flops 67108864 | bytes 1376256 | tf_op jit(solution)/shard_map/rp,apc->arc/dot_general | solution.py:191
  3.1 1.6 %collective-permute-start.2 = (f32[2,64,128]{2,1,0:T(8,128)S(1)}, f32[2,64,128]{2,1,0:T(8,128)S(1)}, u32[]{:S(2)}, u32[]{:S(2)}) collective-permute-start(f32[2,64,128]{2,1,0:T(8,128)S(1)} %convolution_bitcast_fusion.2), channel_id=1, source_target_pairs={{0,4},{4,0},{8,12},{12,8},{16,20},{20,16},{24,28},{28,24},{1,5},{5... | collective-permute-start | bytes 196616 | tf_op jit(solution)/shard_map/ppermute | solution.py:16
  4.7 1.0 fusion.48
  5.7 2.4 %collective-permute-start = (bf16[2,1024,128]{2,1,0:T(8,128)(2,1)}, bf16[2,1024,128]{2,1,0:T(8,128)(2,1)}, u32[]{:S(2)}, u32[]{:S(2)}) collective-permute-start(bf16[2,1024,128]{2,1,0:T(8,128)(2,1)} %get-tuple-element.14), channel_id=1, source_target_pairs={{0,4},{4,8},{8,12},{12,16},{16,20},{20,24},{24,28},{1,5},{5,9},{9,... | collective-permute-start | bytes 1572872 | tf_op jit(solution)/shard_map/ppermute | solution.py:22
  8.2 4.3 %collective-permute-start.1 = (bf16[2,1024,128]{2,1,0:T(8,128)(2,1)}, bf16[2,1024,128]{2,1,0:T(8,128)(2,1)}, u32[]{:S(2)}, u32[]{:S(2)}) collective-permute-start(bf16[2,1024,128]{2,1,0:T(8,128)(2,1)} %get-tuple-element.15), channel_id=1, source_target_pairs={{4,0},{8,4},{12,8},{16,12},{20,16},{24,20},{28,24},{5,1},{9,5},{13... | collective-permute-start | bytes 1572872 | tf_op jit(solution)/shard_map/ppermute | solution.py:22
  12.5 1.6 %collective-permute-start.3 = (f32[2,64,128]{2,1,0:T(8,128)S(1)}, f32[2,64,128]{2,1,0:T(8,128)S(1)}, u32[]{:S(2)}, u32[]{:S(2)}) collective-permute-start(f32[2,64,128]{2,1,0:T(8,128)S(1)} %add.65), channel_id=1, source_target_pairs={{0,8},{4,12},{8,0},{12,4},{16,24},{20,28},{24,16},{28,20},{1,9},{5... | collective-permute-start | bytes 196616 | tf_op jit(solution)/shard_map/ppermute | solution.py:16
  14.2 0.7 reshape.29.ids_ref
  14.8 12.7 %collective-permute-done.3 = f32[2,64,128]{2,1,0:T(8,128)S(1)} collective-permute-done((f32[2,64,128]{2,1,0:T(8,128)S(1)}, f32[2,64,128]{2,1,0:T(8,128)S(1)}, u32[]{:S(2)}, u32[]{:S(2)}) %collective-permute-start.3) | collective-permute-done | bytes 65568 | tf_op jit(solution)/shard_map/ppermute | solution.py:16
  27.8 4.9 %collective-permute-done.4 = f32[2,64,128]{2,1,0:T(8,128)S(1)} collective-permute-done((f32[2,64,128]{2,1,0:T(8,128)S(1)}, f32[2,64,128]{2,1,0:T(8,128)S(1)}, u32[]{:S(2)}, u32[]{:S(2)}) %collective-permute-start.4) | collective-permute-done | bytes 65568 | tf_op jit(solution)/shard_map/ppermute | solution.py:16
  33.1 1.3 %convolution_bitcast_fusion.1 = f32[2,2048,128]{2,1,0:T(8,128)S(1)} fusion(bf16[2,64,128]{2,1,0:T(8,128)(2,1)S(1)} %fusion.19, bf16[64,2048]{1,0:T(8,128)(2,1)S(1)} %copy-done, bf16[128,128]{1,0:T(8,128)(2,1)} %param.14), kind=kOutput, calls=%fused_computation.3 | convolution fusion | flops 71319552 | bytes 2424832 | tf_op jit(solution)/shard_map/rp,ard->apd/dot_general | solution.py:197
  34.5 2.7 %pad_maximum_fusion.ext_ref = bf16[2,4096,128]{2,1,0:T(8,128)(2,1)} fusion(bf16[2,1024,128]{2,1,0:T(8,128)(2,1)} %collective-permute-done.1, bf16[2,2048,128]{2,1,0:T(8,128)(2,1)S(1)} %copy-done.1, bf16[2,1024,128]{2,1,0:T(8,128)(2,1)} %collective-permute-done), kind=kLoop, calls=%fused_computation.18 | loop fusion | flops 6291456 | bytes 4194304 | tf_op jit(solution)/shard_map/concatenate | solution.py:184
  37.2 7.2 %shard_map.111 = bf16[2,2048,128]{2,1,0:T(8,128)(2,1)} custom-call(s32[192]{0:T(256)} %reshape.29.ids_ref, bf16[16,12,128,128]{3,2,1,0:T(8,128)(2,1)} %kb_ref.3, bf16[2,4096,128]{2,1,0:T(8,128)(2,1)} %pad_maximum_fusion.ext_ref), custom_call_target="tpu_custom_call" | custom-call | flops 1610612736 | bytes 9437184 | tf_op jit(solution)/shard_map/pallas_call | solution.py:76
  44.4 4.5 %fusion.2 = (bf16[2,2048,128]{2,1,0:T(8,128)(2,1)S(1)}, bf16[2,2048,128]{2,1,0:T(8,128)(2,1)}) fusion(bf16[2,2048,128]{2,1,0:T(8,128)(2,1)} %param.9, f32[2,2048,128]{2,1,0:T(8,128)S(1)} %convolution_bitcast_fusion.1, bf16[2,2048,128]{2,1,0:T(8,128)(2,1)} %shard_map.111, bf16[128,128]{1,0:T(8,128)(2,1)S(1)} %copy-done.5), kind=kOutput, calls=%fused_computation.10 | convolution fusion | flops 146800640 | bytes 6324224 | tf_op jit(solution)/shard_map/apc,cd->apd/dot_general | solution.py:199
  48.9 0.5 fusion.13
  49.4 0.3 fusion.17
  50.1 5.8 %collective-permute-done.7 = f32[384,128]{1,0:T(8,128)S(1)} collective-permute-done((f32[384,128]{1,0:T(8,128)S(1)}, f32[384,128]{1,0:T(8,128)S(1)}, u32[]{:S(2)}, u32[]{:S(2)}) %collective-permute-start.7) | collective-permute-done | bytes 196640 | tf_op jit(solution)/shard_map/ppermute | solution.py:16
  56.0 1.6 %collective-permute-start.8 = (f32[384,128]{1,0:T(8,128)S(1)}, f32[384,128]{1,0:T(8,128)S(1)}, u32[]{:S(2)}, u32[]{:S(2)}) collective-permute-start(f32[384,128]{1,0:T(8,128)S(1)} %pad_maximum_fusion.2), channel_id=1, source_target_pairs={{0,8},{4,12},{8,0},{12,4},{16,24},{20,28},{24,16},{28,20},{1,9},{5... | collective-permute-start | bytes 589832 | tf_op jit(solution)/shard_map/ppermute | solution.py:16
  57.6 1.4 %convolution_convert_fusion.back_ref = bf16[2,2048,128]{2,1,0:T(8,128)(2,1)} fusion(bf16[2,2048,128]{2,1,0:T(8,128)(2,1)S(1)} %get-tuple-element.12, bf16[128,128]{1,0:T(8,128)(2,1)S(1)} %copy-done.5), kind=kOutput, calls=%fused_computation.7 | convolution fusion | flops 134742016 | bytes 2129920 | tf_op jit(solution)/shard_map/apc,dc->apd/dot_general | solution.py:207
  59.0 9.6 %shard_map.112 = (f32[2,2048,128]{2,1,0:T(8,128)}, bf16[2,1024,128]{2,1,0:T(8,128)(2,1)}, bf16[2,1024,128]{2,1,0:T(8,128)(2,1)}) custom-call(s32[192]{0:T(256)} %reshape.29.ids_ref, bf16[16,12,128,128]{3,2,1,0:T(8,128)(2,1)} %kb_ref.3, bf16[2,2048,128]{2,1,0:T(8,128)(2,1)} %convolution_convert_fusion.back_ref), custom_call_target="tpu_custom_call" | custom-call | flops 1610612736 | bytes 11534336 | tf_op jit(solution)/shard_map/pallas_call | solution.py:135
  68.6 2.2 %collective-permute-start.5 = (bf16[2,1024,128]{2,1,0:T(8,128)(2,1)}, bf16[2,1024,128]{2,1,0:T(8,128)(2,1)S(1)}, u32[]{:S(2)}, u32[]{:S(2)}) collective-permute-start(bf16[2,1024,128]{2,1,0:T(8,128)(2,1)} %get-tuple-element.8), channel_id=1, source_target_pairs={{0,4},{4,8},{8,12},{12,16},{16,20},{20,24},{24,28},{1,5},{5,9},{9,... | collective-permute-start | bytes 1572872 | tf_op jit(solution)/shard_map/ppermute | solution.py:22
  70.8 4.6 %collective-permute-start.6 = (bf16[2,1024,128]{2,1,0:T(8,128)(2,1)}, bf16[2,1024,128]{2,1,0:T(8,128)(2,1)S(1)}, u32[]{:S(2)}, u32[]{:S(2)}) collective-permute-start(bf16[2,1024,128]{2,1,0:T(8,128)(2,1)} %get-tuple-element.9), channel_id=1, source_target_pairs={{4,0},{8,4},{12,8},{16,12},{20,16},{24,20},{28,24},{5,1},{9,5},{13... | collective-permute-start | bytes 1572872 | tf_op jit(solution)/shard_map/ppermute | solution.py:22
  75.6 0.3 fusion.34
  75.8 17.1 %collective-permute-done.5 = bf16[2,1024,128]{2,1,0:T(8,128)(2,1)S(1)} collective-permute-done((bf16[2,1024,128]{2,1,0:T(8,128)(2,1)}, bf16[2,1024,128]{2,1,0:T(8,128)(2,1)S(1)}, u32[]{:S(2)}, u32[]{:S(2)}) %collective-permute-start.5) | collective-permute-done | bytes 524320 | tf_op jit(solution)/shard_map/ppermute | solution.py:22
  93.0 2.7 %collective-permute-done.6 = bf16[2,1024,128]{2,1,0:T(8,128)(2,1)S(1)} collective-permute-done((bf16[2,1024,128]{2,1,0:T(8,128)(2,1)}, bf16[2,1024,128]{2,1,0:T(8,128)(2,1)S(1)}, u32[]{:S(2)}, u32[]{:S(2)}) %collective-permute-start.6) | collective-permute-done | bytes 524320 | tf_op jit(solution)/shard_map/ppermute | solution.py:22
  95.6 1.8 %convert_add_fusion.1 = (f32[2,1024,128]{2,1,0:T(8,128)S(1)}, f32[2,1024,128]{2,1,0:T(8,128)S(1)}) fusion(bf16[2,1024,128]{2,1,0:T(8,128)(2,1)S(1)} %collective-permute-done.5, f32[2,2048,128]{2,1,0:T(8,128)} %get-tuple-element.7, bf16[2,1024,128]{2,1,0:T(8,128)(2,1)S(1)} %collective-permute-done.6), kind=kLoop, calls=%fused_computation.39 | loop fusion | flops 1048576 | bytes 5242880 | tf_op jit(solution)/shard_map/add | solution.py:238
  97.8 0.3 fusion.18
  98.1 1.1 %collective-permute-done.10 = f32[256,128]{1,0:T(8,128)S(1)} collective-permute-done((f32[256,128]{1,0:T(8,128)S(1)}, f32[256,128]{1,0:T(8,128)S(1)}, u32[]{:S(2)}, u32[]{:S(2)}) %collective-permute-start.10) | collective-permute-done | bytes 131104 | tf_op jit(solution)/shard_map/ppermute | solution.py:16
  99.2 1.5 %collective-permute-start.11 = (f32[256,128]{1,0:T(8,128)S(1)}, f32[256,128]{1,0:T(8,128)S(1)}, u32[]{:S(2)}, u32[]{:S(2)}) collective-permute-start(f32[256,128]{1,0:T(8,128)S(1)} %add.82), channel_id=1, source_target_pairs={{0,2},{1,3},{2,0},{3,1},{4,6},{5,7},{6,4},{7,5},{8,10},{9,11},{10,... | collective-permute-start | bytes 393224 | tf_op jit(solution)/shard_map/ppermute | solution.py:16
  100.7 1.5 %fusion.10 = bf16[2,2048,128]{2,1,0:T(8,128)(2,1)} fusion(f32[2,1024,128]{2,1,0:T(8,128)S(1)} %get-tuple-element.11, f32[2,1024,128]{2,1,0:T(8,128)S(1)} %get-tuple-element.10, bf16[2,64,128]{2,1,0:T(8,128)(2,1)S(1)} %fusion.18, bf16[64,2048]{1,0:T(8,128)(2,1)S(1)} %copy-done), kind=kOutput, calls=%fused_computation.20 | convolution fusion | flops 68681728 | bytes 3440640 | tf_op jit(solution)/shard_map/rp,arc->apc/dot_general | solution.py:226
  102.2 2.6 %collective-permute-done.11 = f32[256,128]{1,0:T(8,128)S(1)} collective-permute-done((f32[256,128]{1,0:T(8,128)S(1)}, f32[256,128]{1,0:T(8,128)S(1)}, u32[]{:S(2)}, u32[]{:S(2)}) %collective-permute-start.11) | collective-permute-done | bytes 131104 | tf_op jit(solution)/shard_map/ppermute | solution.py:16
  104.8 0.7 fusion.49
  (44 shorter events, 1.7 us)
Async XLA Ops:
  0.6 1.0 copy-start
  0.6 4.1 %copy-start.1 = (bf16[2,2048,128]{2,1,0:T(8,128)(2,1)S(1)}, bf16[2,2048,128]{2,1,0:T(8,128)(2,1)}, u32[]{:S(2)}) copy-start(bf16[2,2048,128]{2,1,0:T(8,128)(2,1)} %param.8) | copy-start | bytes 3145732
  0.7 13.5 %copy-start.6 = (s32[16,12]{1,0:T(8,128)S(1)}, s32[16,12]{1,0:T(8,128)}, u32[]{:S(2)}) copy-start(s32[16,12]{1,0:T(8,128)} %param.11) | copy-start | bytes 2308
  0.7 26.9 %copy-start.3 = (f32[3,64,64]{2,1,0:T(8,128)S(1)}, f32[3,64,64]{2,1,0:T(8,128)}, u32[]{:S(2)}) copy-start(f32[3,64,64]{2,1,0:T(8,128)} %param.15) | copy-start | bytes 147460
  3.1 9.4 %collective-permute-start.2 = (f32[2,64,128]{2,1,0:T(8,128)S(1)}, f32[2,64,128]{2,1,0:T(8,128)S(1)}, u32[]{:S(2)}, u32[]{:S(2)}) collective-permute-start(f32[2,64,128]{2,1,0:T(8,128)S(1)} %convolution_bitcast_fusion.2), channel_id=1, source_target_pairs={{0,4},{4,0},{8,12},{12,8},{16,20},{20,16},{24,28},{28,24},{1,5},{5... | collective-permute-start | bytes 196616 | tf_op jit(solution)/shard_map/ppermute | solution.py:16
  5.7 28.7 %collective-permute-start = (bf16[2,1024,128]{2,1,0:T(8,128)(2,1)}, bf16[2,1024,128]{2,1,0:T(8,128)(2,1)}, u32[]{:S(2)}, u32[]{:S(2)}) collective-permute-start(bf16[2,1024,128]{2,1,0:T(8,128)(2,1)} %get-tuple-element.14), channel_id=1, source_target_pairs={{0,4},{4,8},{8,12},{12,16},{16,20},{20,24},{24,28},{1,5},{5,9},{9,... | collective-permute-start | bytes 1572872 | tf_op jit(solution)/shard_map/ppermute | solution.py:22
  8.2 26.3 %collective-permute-start.1 = (bf16[2,1024,128]{2,1,0:T(8,128)(2,1)}, bf16[2,1024,128]{2,1,0:T(8,128)(2,1)}, u32[]{:S(2)}, u32[]{:S(2)}) collective-permute-start(bf16[2,1024,128]{2,1,0:T(8,128)(2,1)} %get-tuple-element.15), channel_id=1, source_target_pairs={{4,0},{8,4},{12,8},{16,12},{20,16},{24,20},{28,24},{5,1},{9,5},{13... | collective-permute-start | bytes 1572872 | tf_op jit(solution)/shard_map/ppermute | solution.py:22
  12.5 15.0 %collective-permute-start.3 = (f32[2,64,128]{2,1,0:T(8,128)S(1)}, f32[2,64,128]{2,1,0:T(8,128)S(1)}, u32[]{:S(2)}, u32[]{:S(2)}) collective-permute-start(f32[2,64,128]{2,1,0:T(8,128)S(1)} %add.65), channel_id=1, source_target_pairs={{0,8},{4,12},{8,0},{12,4},{16,24},{20,28},{24,16},{28,20},{1,9},{5... | collective-permute-start | bytes 196616 | tf_op jit(solution)/shard_map/ppermute | solution.py:16
  27.5 5.2 %collective-permute-start.4 = (f32[2,64,128]{2,1,0:T(8,128)S(1)}, f32[2,64,128]{2,1,0:T(8,128)S(1)}, u32[]{:S(2)}, u32[]{:S(2)}) collective-permute-start(f32[2,64,128]{2,1,0:T(8,128)S(1)} %add.67), channel_id=1, source_target_pairs={{0,16},{4,20},{8,24},{12,28},{16,0},{20,4},{24,8},{28,12},{1,17},{... | collective-permute-start | bytes 196616 | tf_op jit(solution)/shard_map/ppermute | solution.py:16
  37.2 7.2 %copy-start.5 = (bf16[128,128]{1,0:T(8,128)(2,1)S(1)}, bf16[128,128]{1,0:T(8,128)(2,1)}, u32[]{:S(2)}) copy-start(bf16[128,128]{1,0:T(8,128)(2,1)} %param.13) | copy-start | bytes 98308
  44.4 4.5 %copy-start.2 = (bf16[2,2048,128]{2,1,0:T(8,128)(2,1)S(1)}, bf16[2,2048,128]{2,1,0:T(8,128)(2,1)}, u32[]{:S(2)}) copy-start(bf16[2,2048,128]{2,1,0:T(8,128)(2,1)} %shard_map.111) | copy-start | bytes 3145732
  48.9 1.0 copy-start.4
  50.1 5.8 %collective-permute-start.7 = (f32[384,128]{1,0:T(8,128)S(1)}, f32[384,128]{1,0:T(8,128)S(1)}, u32[]{:S(2)}, u32[]{:S(2)}) collective-permute-start(f32[384,128]{1,0:T(8,128)S(1)} %pad_maximum_fusion.1), channel_id=1, source_target_pairs={{0,4},{4,0},{8,12},{12,8},{16,20},{20,16},{24,28},{28,24},{1,5},{5... | collective-permute-start | bytes 589832 | tf_op jit(solution)/shard_map/ppermute | solution.py:16
  56.0 19.4 %collective-permute-start.8 = (f32[384,128]{1,0:T(8,128)S(1)}, f32[384,128]{1,0:T(8,128)S(1)}, u32[]{:S(2)}, u32[]{:S(2)}) collective-permute-start(f32[384,128]{1,0:T(8,128)S(1)} %pad_maximum_fusion.2), channel_id=1, source_target_pairs={{0,8},{4,12},{8,0},{12,4},{16,24},{20,28},{24,16},{28,20},{1,9},{5... | collective-permute-start | bytes 589832 | tf_op jit(solution)/shard_map/ppermute | solution.py:16
  68.6 24.3 %collective-permute-start.5 = (bf16[2,1024,128]{2,1,0:T(8,128)(2,1)}, bf16[2,1024,128]{2,1,0:T(8,128)(2,1)S(1)}, u32[]{:S(2)}, u32[]{:S(2)}) collective-permute-start(bf16[2,1024,128]{2,1,0:T(8,128)(2,1)} %get-tuple-element.8), channel_id=1, source_target_pairs={{0,4},{4,8},{8,12},{12,16},{16,20},{20,24},{24,28},{1,5},{5,9},{9,... | collective-permute-start | bytes 1572872 | tf_op jit(solution)/shard_map/ppermute | solution.py:22
  70.8 24.8 %collective-permute-start.6 = (bf16[2,1024,128]{2,1,0:T(8,128)(2,1)}, bf16[2,1024,128]{2,1,0:T(8,128)(2,1)S(1)}, u32[]{:S(2)}, u32[]{:S(2)}) collective-permute-start(bf16[2,1024,128]{2,1,0:T(8,128)(2,1)} %get-tuple-element.9), channel_id=1, source_target_pairs={{4,0},{8,4},{12,8},{16,12},{20,16},{24,20},{28,24},{5,1},{9,5},{13... | collective-permute-start | bytes 1572872 | tf_op jit(solution)/shard_map/ppermute | solution.py:22
  75.5 21.9 %collective-permute-start.9 = (f32[384,128]{1,0:T(8,128)S(1)}, f32[384,128]{1,0:T(8,128)S(1)}, u32[]{:S(2)}, u32[]{:S(2)}) collective-permute-start(f32[384,128]{1,0:T(8,128)S(1)} %pad_maximum_fusion.3), channel_id=1, source_target_pairs={{0,16},{4,20},{8,24},{12,28},{16,0},{20,4},{24,8},{28,12},{1,17},{... | collective-permute-start | bytes 589832 | tf_op jit(solution)/shard_map/ppermute | solution.py:16
  97.7 1.4 %collective-permute-start.10 = (f32[256,128]{1,0:T(8,128)S(1)}, f32[256,128]{1,0:T(8,128)S(1)}, u32[]{:S(2)}, u32[]{:S(2)}) collective-permute-start(f32[256,128]{1,0:T(8,128)S(1)} %slice_add_fusion), channel_id=1, source_target_pairs={{0,1},{1,0},{2,3},{3,2},{4,5},{5,4},{6,7},{7,6},{8,9},{9,8},{10,11... | collective-permute-start | bytes 393224 | tf_op jit(solution)/shard_map/ppermute | solution.py:16
  99.2 5.6 %collective-permute-start.11 = (f32[256,128]{1,0:T(8,128)S(1)}, f32[256,128]{1,0:T(8,128)S(1)}, u32[]{:S(2)}, u32[]{:S(2)}) collective-permute-start(f32[256,128]{1,0:T(8,128)S(1)} %add.82), channel_id=1, source_target_pairs={{0,2},{1,3},{2,0},{3,1},{4,6},{5,7},{6,4},{7,5},{8,10},{9,11},{10,... | collective-permute-start | bytes 393224 | tf_op jit(solution)/shard_map/ppermute | solution.py:16

commit v2 on v1

--- a/solution.py
+++ b/solution.py
@@ -221,15 +221,18 @@
     )
     grads = jnp.concatenate([near_term, far_term], axis=0)
 
-    back_coeff = jnp.einsum("arc,dc->ard", projected, w_far, preferred_element_type=jnp.float32)
-    back_exp, grads = expand(back_coeff, translations, True, rider=grads)
-    back_far = jnp.einsum(
-        "rp,arc->apc", leaf_basis, back_exp.astype(jnp.bfloat16), preferred_element_type=jnp.float32
-    )
-
     case_depth = lax.axis_size("case").bit_length() - 1
     for height in range(case_depth):
         grads = grads + partner(grads, "case", height)
+    leaf_depth = lax.axis_size("leaf").bit_length() - 1
+    for height in range(leaf_depth):
+        grads = grads + partner(grads, "leaf", height)
+
+    back_coeff = jnp.einsum("arc,dc->ard", projected, w_far, preferred_element_type=jnp.float32)
+    back_exp, _ = expand(back_coeff, translations, True)
+    back_far = jnp.einsum(
+        "rp,arc->apc", leaf_basis, back_exp.astype(jnp.bfloat16), preferred_element_type=jnp.float32
+    )
 
     got_prev = shifted(hi, "leaf", 1).astype(jnp.float32)
     got_next = shifted(lo, "leaf", -1).astype(jnp.float32)

time: 107 us -> 112 us (1.047)
  the two profiles are of different devices: /device:TPU:16 before, /device:TPU:0 now
where the time goes in v2:
time: 112 us; the launch traced here: 111 us
  waiting for transfers between devices  40.6 us (36%)
  starting transfers between devices  34.1 us (30%)
  Pallas kernels  16.8 us (15%)
  matrix products  12.7 us (11%)
  local copies, waits for them, and re-layouts  3.31 us (3%)
  other arithmetic  3 us (3%)
    ppermute x11, waiting for transfers between devices, partner(): lax.ppermute(shard, axis, [(i, i ^ 1 << apart) for i in range(lax.axis_si...  40.6 us
    ppermute x11, starting transfers between devices, partner(): lax.ppermute(shard, axis, [(i, i ^ 1 << apart) for i in range(lax.axis_si...  26.7 us
    pallas_call x1, Pallas kernels, near_backward(): pl.pallas_call(functools.partial(near_bwd_kernel, cases, pairs, rows, ste...  9.63 us
    ppermute x4, starting transfers between devices, shifted(): lax.ppermute(value, axis, [(source, source + steps) for source in range(l...  7.39 us
    pallas_call x1, Pallas kernels, near_forward(): pl.pallas_call(functools.partial(near_fwd_kernel, cases, pairs, rows), ou...  7.2 us
    dot_general x1, matrix products, on_device(): jnp.einsum('apc,cd->apd', near_bf, w_near, preferred_element_type=jnp.flo...  4.54 us
    concatenate x1, other arithmetic, on_device(): extended = jnp.concatenate([from_prev, features, from_next], axis=1)  2.67 us
  transfers between devices with their start and end apart: 15, of which 8 were waited for; matrix products, arithmetic and copies ran while one was open for 6% of the time, Pallas kernels for 9%

profile of v2, /device:TPU:0, one launch (start us, length us, event | category | flops | bytes accessed | tf_op | source)
XLA Modules:
  0.0 111.4 jit_solution(12844725082305002017)
XLA Ops:
  0.7 0.9 copy-done
  1.6 1.5 %convolution_bitcast_fusion.2 = f32[2,64,128]{2,1,0:T(8,128)S(1)} fusion(bf16[2,2048,128]{2,1,0:T(8,128)(2,1)} %param.8, bf16[64,2048]{1,0:T(8,128)(2,1)S(1)} %copy-done), kind=kOutput, calls=%fused_computation.22 | convolution fusion | flops 67108864 | bytes 1376256 | tf_op jit(solution)/shard_map/rp,apc->arc/dot_general | solution.py:191
  3.1 3.0 %collective-permute-start.2 = (f32[2,64,128]{2,1,0:T(8,128)S(1)}, f32[2,64,128]{2,1,0:T(8,128)S(1)}, u32[]{:S(2)}, u32[]{:S(2)}) collective-permute-start(f32[2,64,128]{2,1,0:T(8,128)S(1)} %convolution_bitcast_fusion.2), channel_id=1, source_target_pairs={{0,4},{4,0},{8,12},{12,8},{16,20},{20,16},{24,28},{28,24},{1,5},{5... | collective-permute-start | bytes 196616 | tf_op jit(solution)/shard_map/ppermute | solution.py:16
  6.1 1.0 fusion.49
  7.2 2.7 %collective-permute-start = (bf16[2,1024,128]{2,1,0:T(8,128)(2,1)}, bf16[2,1024,128]{2,1,0:T(8,128)(2,1)}, u32[]{:S(2)}, u32[]{:S(2)}) collective-permute-start(bf16[2,1024,128]{2,1,0:T(8,128)(2,1)} %get-tuple-element.14), channel_id=1, source_target_pairs={{0,4},{4,8},{8,12},{12,16},{16,20},{20,24},{24,28},{1,5},{5,9},{9,... | collective-permute-start | bytes 1572872 | tf_op jit(solution)/shard_map/ppermute | solution.py:22
  9.9 1.3 %collective-permute-start.1 = (bf16[2,1024,128]{2,1,0:T(8,128)(2,1)}, bf16[2,1024,128]{2,1,0:T(8,128)(2,1)}, u32[]{:S(2)}, u32[]{:S(2)}) collective-permute-start(bf16[2,1024,128]{2,1,0:T(8,128)(2,1)} %get-tuple-element.15), channel_id=1, source_target_pairs={{4,0},{8,4},{12,8},{16,12},{20,16},{24,20},{28,24},{5,1},{9,5},{13... | collective-permute-start | bytes 1572872 | tf_op jit(solution)/shard_map/ppermute | solution.py:22
  11.2 4.4 %collective-permute-start.3 = (f32[2,64,128]{2,1,0:T(8,128)S(1)}, f32[2,64,128]{2,1,0:T(8,128)S(1)}, u32[]{:S(2)}, u32[]{:S(2)}) collective-permute-start(f32[2,64,128]{2,1,0:T(8,128)S(1)} %add.65), channel_id=1, source_target_pairs={{0,8},{4,12},{8,0},{12,4},{16,24},{20,28},{24,16},{28,20},{1,9},{5... | collective-permute-start | bytes 196616 | tf_op jit(solution)/shard_map/ppermute | solution.py:16
  15.6 0.7 reshape.11.ids_ref
  16.3 12.0 %collective-permute-done.3 = f32[2,64,128]{2,1,0:T(8,128)S(1)} collective-permute-done((f32[2,64,128]{2,1,0:T(8,128)S(1)}, f32[2,64,128]{2,1,0:T(8,128)S(1)}, u32[]{:S(2)}, u32[]{:S(2)}) %collective-permute-start.3) | collective-permute-done | bytes 65568 | tf_op jit(solution)/shard_map/ppermute | solution.py:16
  28.2 3.4 %collective-permute-start.4 = (f32[2,64,128]{2,1,0:T(8,128)S(1)}, f32[2,64,128]{2,1,0:T(8,128)S(1)}, u32[]{:S(2)}, u32[]{:S(2)}) collective-permute-start(f32[2,64,128]{2,1,0:T(8,128)S(1)} %add.67), channel_id=1, source_target_pairs={{0,16},{4,20},{8,24},{12,28},{16,0},{20,4},{24,8},{28,12},{1,17},{... | collective-permute-start | bytes 196616 | tf_op jit(solution)/shard_map/ppermute | solution.py:16
  31.8 2.0 %collective-permute-done.4 = f32[2,64,128]{2,1,0:T(8,128)S(1)} collective-permute-done((f32[2,64,128]{2,1,0:T(8,128)S(1)}, f32[2,64,128]{2,1,0:T(8,128)S(1)}, u32[]{:S(2)}, u32[]{:S(2)}) %collective-permute-start.4) | collective-permute-done | bytes 65568 | tf_op jit(solution)/shard_map/ppermute | solution.py:16
  34.3 1.3 %convolution_bitcast_fusion.1 = f32[2,2048,128]{2,1,0:T(8,128)S(1)} fusion(bf16[2,64,128]{2,1,0:T(8,128)(2,1)S(1)} %fusion.19, bf16[64,2048]{1,0:T(8,128)(2,1)S(1)} %copy-done, bf16[128,128]{1,0:T(8,128)(2,1)} %param.14), kind=kOutput, calls=%fused_computation.3 | convolution fusion | flops 71319552 | bytes 2424832 | tf_op jit(solution)/shard_map/rp,ard->apd/dot_general | solution.py:197
  35.6 2.7 %pad_maximum_fusion.ext_ref = bf16[2,4096,128]{2,1,0:T(8,128)(2,1)} fusion(bf16[2,1024,128]{2,1,0:T(8,128)(2,1)} %collective-permute-done.1, bf16[2,2048,128]{2,1,0:T(8,128)(2,1)S(1)} %copy-done.1, bf16[2,1024,128]{2,1,0:T(8,128)(2,1)} %collective-permute-done), kind=kLoop, calls=%fused_computation.18 | loop fusion | flops 6291456 | bytes 4194304 | tf_op jit(solution)/shard_map/concatenate | solution.py:184
  38.3 7.2 %shard_map.111 = bf16[2,2048,128]{2,1,0:T(8,128)(2,1)} custom-call(s32[192]{0:T(256)} %reshape.11.ids_ref, bf16[16,12,128,128]{3,2,1,0:T(8,128)(2,1)} %kb_ref.3, bf16[2,4096,128]{2,1,0:T(8,128)(2,1)} %pad_maximum_fusion.ext_ref), custom_call_target="tpu_custom_call" | custom-call | flops 1610612736 | bytes 9437184 | tf_op jit(solution)/shard_map/pallas_call | solution.py:76
  45.5 4.5 %fusion.2 = (bf16[2,2048,128]{2,1,0:T(8,128)(2,1)S(1)}, bf16[2,2048,128]{2,1,0:T(8,128)(2,1)}) fusion(bf16[2,2048,128]{2,1,0:T(8,128)(2,1)} %param.9, f32[2,2048,128]{2,1,0:T(8,128)S(1)} %convolution_bitcast_fusion.1, bf16[2,2048,128]{2,1,0:T(8,128)(2,1)} %shard_map.111, bf16[128,128]{1,0:T(8,128)(2,1)S(1)} %copy-done.6), kind=kOutput, calls=%fused_computation.10 | convolution fusion | flops 146800640 | bytes 6324224 | tf_op jit(solution)/shard_map/apc,cd->apd/dot_general | solution.py:199
  50.8 1.4 %convolution_convert_fusion.back_ref = bf16[2,2048,128]{2,1,0:T(8,128)(2,1)} fusion(bf16[2,2048,128]{2,1,0:T(8,128)(2,1)S(1)} %get-tuple-element.12, bf16[128,128]{1,0:T(8,128)(2,1)S(1)} %copy-done.6), kind=kOutput, calls=%fused_computation.7 | convolution fusion | flops 134742016 | bytes 2129920 | tf_op jit(solution)/shard_map/apc,dc->apd/dot_general | solution.py:207
  52.7 4.2 %collective-permute-done.7 = f32[2,64,128]{2,1,0:T(8,128)S(1)} collective-permute-done((f32[2,64,128]{2,1,0:T(8,128)S(1)}, f32[2,64,128]{2,1,0:T(8,128)S(1)}, u32[]{:S(2)}, u32[]{:S(2)}) %collective-permute-start.7) | collective-permute-done | bytes 65568 | tf_op jit(solution)/shard_map/ppermute | solution.py:16
  56.9 0.9 collective-permute-start.8
  57.8 9.6 %shard_map.112 = (f32[2,2048,128]{2,1,0:T(8,128)}, bf16[2,1024,128]{2,1,0:T(8,128)(2,1)}, bf16[2,1024,128]{2,1,0:T(8,128)(2,1)}) custom-call(s32[192]{0:T(256)} %reshape.11.ids_ref, bf16[16,12,128,128]{3,2,1,0:T(8,128)(2,1)} %kb_ref.3, bf16[2,2048,128]{2,1,0:T(8,128)(2,1)} %convolution_convert_fusion.back_ref), custom_call_target="tpu_custom_call" | custom-call | flops 1610612736 | bytes 11534336 | tf_op jit(solution)/shard_map/pallas_call | solution.py:135
  67.4 2.1 %collective-permute-start.5 = (bf16[2,1024,128]{2,1,0:T(8,128)(2,1)}, bf16[2,1024,128]{2,1,0:T(8,128)(2,1)S(1)}, u32[]{:S(2)}, u32[]{:S(2)}) collective-permute-start(bf16[2,1024,128]{2,1,0:T(8,128)(2,1)} %get-tuple-element.8), channel_id=1, source_target_pairs={{0,4},{4,8},{8,12},{12,16},{16,20},{20,24},{24,28},{1,5},{5,9},{9,... | collective-permute-start | bytes 1572872 | tf_op jit(solution)/shard_map/ppermute | solution.py:22
  69.5 1.3 %collective-permute-start.6 = (bf16[2,1024,128]{2,1,0:T(8,128)(2,1)}, bf16[2,1024,128]{2,1,0:T(8,128)(2,1)S(1)}, u32[]{:S(2)}, u32[]{:S(2)}) collective-permute-start(bf16[2,1024,128]{2,1,0:T(8,128)(2,1)} %get-tuple-element.9), channel_id=1, source_target_pairs={{4,0},{8,4},{12,8},{16,12},{20,16},{24,20},{28,24},{5,1},{9,5},{13... | collective-permute-start | bytes 1572872 | tf_op jit(solution)/shard_map/ppermute | solution.py:22
  70.8 6.1 %collective-permute-start.9 = (f32[2,64,128]{2,1,0:T(8,128)S(1)}, f32[2,64,128]{2,1,0:T(8,128)S(1)}, u32[]{:S(2)}, u32[]{:S(2)}) collective-permute-start(f32[2,64,128]{2,1,0:T(8,128)S(1)} %add.76), channel_id=1, source_target_pairs={{0,16},{4,20},{8,24},{12,28},{16,0},{20,4},{24,8},{28,12},{1,17},{... | collective-permute-start | bytes 196616 | tf_op jit(solution)/shard_map/ppermute | solution.py:16
  77.0 1.5 %collective-permute-start.11 = (f32[256,128]{1,0:T(8,128)S(1)}, f32[256,128]{1,0:T(8,128)S(1)}, u32[]{:S(2)}, u32[]{:S(2)}) collective-permute-start(f32[256,128]{1,0:T(8,128)S(1)} %fusion.48), channel_id=1, source_target_pairs={{0,2},{1,3},{2,0},{3,1},{4,6},{5,7},{6,4},{7,5},{8,10},{9,11},{10,... | collective-permute-start | bytes 393224 | tf_op jit(solution)/shard_map/ppermute | solution.py:16
  78.8 3.2 %collective-permute-done.11 = f32[256,128]{1,0:T(8,128)S(1)} collective-permute-done((f32[256,128]{1,0:T(8,128)S(1)}, f32[256,128]{1,0:T(8,128)S(1)}, u32[]{:S(2)}, u32[]{:S(2)}) %collective-permute-start.11) | collective-permute-done | bytes 131104 | tf_op jit(solution)/shard_map/ppermute | solution.py:16
  82.2 7.9 %collective-permute-done.9 = f32[2,64,128]{2,1,0:T(8,128)S(1)} collective-permute-done((f32[2,64,128]{2,1,0:T(8,128)S(1)}, f32[2,64,128]{2,1,0:T(8,128)S(1)}, u32[]{:S(2)}, u32[]{:S(2)}) %collective-permute-start.9) | collective-permute-done | bytes 65568 | tf_op jit(solution)/shard_map/ppermute | solution.py:16
  90.3 4.0 %collective-permute-done.12 = f32[256,128]{1,0:T(8,128)S(1)} collective-permute-done((f32[256,128]{1,0:T(8,128)S(1)}, f32[256,128]{1,0:T(8,128)S(1)}, u32[]{:S(2)}, u32[]{:S(2)}) %collective-permute-start.12) | collective-permute-done | bytes 131104 | tf_op jit(solution)/shard_map/ppermute | solution.py:16
  94.3 3.1 %collective-permute-start.13 = (f32[256,128]{1,0:T(8,128)S(1)}, f32[256,128]{1,0:T(8,128)S(1)}, u32[]{:S(2)}, u32[]{:S(2)}) collective-permute-start(f32[256,128]{1,0:T(8,128)S(1)} %add.81), channel_id=1, source_target_pairs={{0,8},{4,12},{8,0},{12,4},{16,24},{20,28},{24,16},{28,20},{1,9},{5... | collective-permute-start | bytes 393224 | tf_op jit(solution)/shard_map/ppermute | solution.py:16
  97.7 3.4 %collective-permute-done.13 = f32[256,128]{1,0:T(8,128)S(1)} collective-permute-done((f32[256,128]{1,0:T(8,128)S(1)}, f32[256,128]{1,0:T(8,128)S(1)}, u32[]{:S(2)}, u32[]{:S(2)}) %collective-permute-start.13) | collective-permute-done | bytes 131104 | tf_op jit(solution)/shard_map/ppermute | solution.py:16
  101.1 4.1 %collective-permute-start.14 = (f32[256,128]{1,0:T(8,128)S(1)}, f32[256,128]{1,0:T(8,128)S(1)}, u32[]{:S(2)}, u32[]{:S(2)}) collective-permute-start(f32[256,128]{1,0:T(8,128)S(1)} %add.82), channel_id=1, source_target_pairs={{0,16},{4,20},{8,24},{12,28},{16,0},{20,4},{24,8},{28,12},{1,17},{... | collective-permute-start | bytes 393224 | tf_op jit(solution)/shard_map/ppermute | solution.py:16
  105.4 1.5 %fusion.10 = bf16[2,2048,128]{2,1,0:T(8,128)(2,1)} fusion(f32[2,1024,128]{2,1,0:T(8,128)S(1)} %get-tuple-element.11, f32[2,1024,128]{2,1,0:T(8,128)S(1)} %get-tuple-element.10, bf16[2,64,128]{2,1,0:T(8,128)(2,1)S(1)} %fusion.18, bf16[64,2048]{1,0:T(8,128)(2,1)S(1)} %copy-done), kind=kOutput, calls=%fused_computation.20 | convolution fusion | flops 68681728 | bytes 3440640 | tf_op jit(solution)/shard_map/rp,arc->apc/dot_general | solution.py:233
  106.8 3.9 %collective-permute-done.14 = f32[256,128]{1,0:T(8,128)S(1)} collective-permute-done((f32[256,128]{1,0:T(8,128)S(1)}, f32[256,128]{1,0:T(8,128)S(1)}, u32[]{:S(2)}, u32[]{:S(2)}) %collective-permute-start.14) | collective-permute-done | bytes 131104 | tf_op jit(solution)/shard_map/ppermute | solution.py:16
  110.7 0.7 fusion.50
  (47 shorter events, 3.0 us)
Async XLA Ops:
  0.6 1.0 copy-start
  0.6 5.5 %copy-start.1 = (bf16[2,2048,128]{2,1,0:T(8,128)(2,1)S(1)}, bf16[2,2048,128]{2,1,0:T(8,128)(2,1)}, u32[]{:S(2)}) copy-start(bf16[2,2048,128]{2,1,0:T(8,128)(2,1)} %param.8) | copy-start | bytes 3145732
  0.7 15.0 %copy-start.7 = (s32[16,12]{1,0:T(8,128)S(1)}, s32[16,12]{1,0:T(8,128)}, u32[]{:S(2)}) copy-start(s32[16,12]{1,0:T(8,128)} %param.11) | copy-start | bytes 2308
  0.7 30.9 %copy-start.4 = (f32[3,64,64]{2,1,0:T(8,128)S(1)}, f32[3,64,64]{2,1,0:T(8,128)}, u32[]{:S(2)}) copy-start(f32[3,64,64]{2,1,0:T(8,128)} %param.15) | copy-start | bytes 147460
  3.1 8.1 %collective-permute-start.2 = (f32[2,64,128]{2,1,0:T(8,128)S(1)}, f32[2,64,128]{2,1,0:T(8,128)S(1)}, u32[]{:S(2)}, u32[]{:S(2)}) collective-permute-start(f32[2,64,128]{2,1,0:T(8,128)S(1)} %convolution_bitcast_fusion.2), channel_id=1, source_target_pairs={{0,4},{4,0},{8,12},{12,8},{16,20},{20,16},{24,28},{28,24},{1,5},{5... | collective-permute-start | bytes 196616 | tf_op jit(solution)/shard_map/ppermute | solution.py:16
  7.2 28.4 %collective-permute-start = (bf16[2,1024,128]{2,1,0:T(8,128)(2,1)}, bf16[2,1024,128]{2,1,0:T(8,128)(2,1)}, u32[]{:S(2)}, u32[]{:S(2)}) collective-permute-start(bf16[2,1024,128]{2,1,0:T(8,128)(2,1)} %get-tuple-element.14), channel_id=1, source_target_pairs={{0,4},{4,8},{8,12},{12,16},{16,20},{20,24},{24,28},{1,5},{5,9},{9,... | collective-permute-start | bytes 1572872 | tf_op jit(solution)/shard_map/ppermute | solution.py:22
  9.9 25.7 %collective-permute-start.1 = (bf16[2,1024,128]{2,1,0:T(8,128)(2,1)}, bf16[2,1024,128]{2,1,0:T(8,128)(2,1)}, u32[]{:S(2)}, u32[]{:S(2)}) collective-permute-start(bf16[2,1024,128]{2,1,0:T(8,128)(2,1)} %get-tuple-element.15), channel_id=1, source_target_pairs={{4,0},{8,4},{12,8},{16,12},{20,16},{24,20},{28,24},{5,1},{9,5},{13... | collective-permute-start | bytes 1572872 | tf_op jit(solution)/shard_map/ppermute | solution.py:22
  11.2 17.0 %collective-permute-start.3 = (f32[2,64,128]{2,1,0:T(8,128)S(1)}, f32[2,64,128]{2,1,0:T(8,128)S(1)}, u32[]{:S(2)}, u32[]{:S(2)}) collective-permute-start(f32[2,64,128]{2,1,0:T(8,128)S(1)} %add.65), channel_id=1, source_target_pairs={{0,8},{4,12},{8,0},{12,4},{16,24},{20,28},{24,16},{28,20},{1,9},{5... | collective-permute-start | bytes 196616 | tf_op jit(solution)/shard_map/ppermute | solution.py:16
  28.2 5.6 %collective-permute-start.4 = (f32[2,64,128]{2,1,0:T(8,128)S(1)}, f32[2,64,128]{2,1,0:T(8,128)S(1)}, u32[]{:S(2)}, u32[]{:S(2)}) collective-permute-start(f32[2,64,128]{2,1,0:T(8,128)S(1)} %add.67), channel_id=1, source_target_pairs={{0,16},{4,20},{8,24},{12,28},{16,0},{20,4},{24,8},{28,12},{1,17},{... | collective-permute-start | bytes 196616 | tf_op jit(solution)/shard_map/ppermute | solution.py:16
  38.3 7.2 %copy-start.6 = (bf16[128,128]{1,0:T(8,128)(2,1)S(1)}, bf16[128,128]{1,0:T(8,128)(2,1)}, u32[]{:S(2)}) copy-start(bf16[128,128]{1,0:T(8,128)(2,1)} %param.13) | copy-start | bytes 98308
  45.5 4.5 %copy-start.2 = (bf16[2,2048,128]{2,1,0:T(8,128)(2,1)S(1)}, bf16[2,2048,128]{2,1,0:T(8,128)(2,1)}, u32[]{:S(2)}) copy-start(bf16[2,2048,128]{2,1,0:T(8,128)(2,1)} %shard_map.111) | copy-start | bytes 3145732
  50.5 1.9 %copy-start.5 = (bf16[128,128]{1,0:T(8,128)(2,1)S(1)}, bf16[128,128]{1,0:T(8,128)(2,1)}, u32[]{:S(2)}) copy-start(bf16[128,128]{1,0:T(8,128)(2,1)} %param.14) | copy-start | bytes 98308
  52.6 4.3 %collective-permute-start.7 = (f32[2,64,128]{2,1,0:T(8,128)S(1)}, f32[2,64,128]{2,1,0:T(8,128)S(1)}, u32[]{:S(2)}, u32[]{:S(2)}) collective-permute-start(f32[2,64,128]{2,1,0:T(8,128)S(1)} %fusion.26), channel_id=1, source_target_pairs={{0,4},{4,0},{8,12},{12,8},{16,20},{20,16},{24,28},{28,24},{1,5},{5... | collective-permute-start | bytes 196616 | tf_op jit(solution)/shard_map/ppermute | solution.py:16
  52.6 24.4 %collective-permute-start.10 = (f32[256,128]{1,0:T(8,128)S(1)}, f32[256,128]{1,0:T(8,128)S(1)}, u32[]{:S(2)}, u32[]{:S(2)}) collective-permute-start(f32[256,128]{1,0:T(8,128)S(1)} %pad_maximum_fusion.1), channel_id=1, source_target_pairs={{0,1},{1,0},{2,3},{3,2},{4,5},{5,4},{6,7},{7,6},{8,9},{9,8},{10,11... | collective-permute-start | bytes 393224 | tf_op jit(solution)/shard_map/ppermute | solution.py:16
  56.9 14.0 %collective-permute-start.8 = (f32[2,64,128]{2,1,0:T(8,128)S(1)}, f32[2,64,128]{2,1,0:T(8,128)S(1)}, u32[]{:S(2)}, u32[]{:S(2)}) collective-permute-start(f32[2,64,128]{2,1,0:T(8,128)S(1)} %add.74), channel_id=1, source_target_pairs={{0,8},{4,12},{8,0},{12,4},{16,24},{20,28},{24,16},{28,20},{1,9},{5... | collective-permute-start | bytes 196616 | tf_op jit(solution)/shard_map/ppermute | solution.py:16
  67.4 37.8 %copy-start.3 = (f32[2,2048,128]{2,1,0:T(8,128)S(1)}, f32[2,2048,128]{2,1,0:T(8,128)}, u32[]{:S(2)}) copy-start(f32[2,2048,128]{2,1,0:T(8,128)} %get-tuple-element.7) | copy-start | bytes 6291460
  67.4 37.8 %collective-permute-start.5 = (bf16[2,1024,128]{2,1,0:T(8,128)(2,1)}, bf16[2,1024,128]{2,1,0:T(8,128)(2,1)S(1)}, u32[]{:S(2)}, u32[]{:S(2)}) collective-permute-start(bf16[2,1024,128]{2,1,0:T(8,128)(2,1)} %get-tuple-element.8), channel_id=1, source_target_pairs={{0,4},{4,8},{8,12},{12,16},{16,20},{20,24},{24,28},{1,5},{5,9},{9,... | collective-permute-start | bytes 1572872 | tf_op jit(solution)/shard_map/ppermute | solution.py:22
  69.5 35.7 %collective-permute-start.6 = (bf16[2,1024,128]{2,1,0:T(8,128)(2,1)}, bf16[2,1024,128]{2,1,0:T(8,128)(2,1)S(1)}, u32[]{:S(2)}, u32[]{:S(2)}) collective-permute-start(bf16[2,1024,128]{2,1,0:T(8,128)(2,1)} %get-tuple-element.9), channel_id=1, source_target_pairs={{4,0},{8,4},{12,8},{16,12},{20,16},{24,20},{28,24},{5,1},{9,5},{13... | collective-permute-start | bytes 1572872 | tf_op jit(solution)/shard_map/ppermute | solution.py:22
  70.8 19.2 %collective-permute-start.9 = (f32[2,64,128]{2,1,0:T(8,128)S(1)}, f32[2,64,128]{2,1,0:T(8,128)S(1)}, u32[]{:S(2)}, u32[]{:S(2)}) collective-permute-start(f32[2,64,128]{2,1,0:T(8,128)S(1)} %add.76), channel_id=1, source_target_pairs={{0,16},{4,20},{8,24},{12,28},{16,0},{20,4},{24,8},{28,12},{1,17},{... | collective-permute-start | bytes 196616 | tf_op jit(solution)/shard_map/ppermute | solution.py:16
  77.0 5.0 %collective-permute-start.11 = (f32[256,128]{1,0:T(8,128)S(1)}, f32[256,128]{1,0:T(8,128)S(1)}, u32[]{:S(2)}, u32[]{:S(2)}) collective-permute-start(f32[256,128]{1,0:T(8,128)S(1)} %fusion.48), channel_id=1, source_target_pairs={{0,2},{1,3},{2,0},{3,1},{4,6},{5,7},{6,4},{7,5},{8,10},{9,11},{10,... | collective-permute-start | bytes 393224 | tf_op jit(solution)/shard_map/ppermute | solution.py:16
  82.1 12.2 %collective-permute-start.12 = (f32[256,128]{1,0:T(8,128)S(1)}, f32[256,128]{1,0:T(8,128)S(1)}, u32[]{:S(2)}, u32[]{:S(2)}) collective-permute-start(f32[256,128]{1,0:T(8,128)S(1)} %add.80), channel_id=1, source_target_pairs={{0,4},{4,0},{8,12},{12,8},{16,20},{20,16},{24,28},{28,24},{1,5},{5... | collective-permute-start | bytes 393224 | tf_op jit(solution)/shard_map/ppermute | solution.py:16
  94.3 6.8 %collective-permute-start.13 = (f32[256,128]{1,0:T(8,128)S(1)}, f32[256,128]{1,0:T(8,128)S(1)}, u32[]{:S(2)}, u32[]{:S(2)}) collective-permute-start(f32[256,128]{1,0:T(8,128)S(1)} %add.81), channel_id=1, source_target_pairs={{0,8},{4,12},{8,0},{12,4},{16,24},{20,28},{24,16},{28,20},{1,9},{5... | collective-permute-start | bytes 393224 | tf_op jit(solution)/shard_map/ppermute | solution.py:16
  101.1 9.6 %collective-permute-start.14 = (f32[256,128]{1,0:T(8,128)S(1)}, f32[256,128]{1,0:T(8,128)S(1)}, u32[]{:S(2)}, u32[]{:S(2)}) collective-permute-start(f32[256,128]{1,0:T(8,128)S(1)} %add.82), channel_id=1, source_target_pairs={{0,16},{4,20},{8,24},{12,28},{16,0},{20,4},{24,8},{28,12},{1,17},{... | collective-permute-start | bytes 393224 | tf_op jit(solution)/shard_map/ppermute | solution.py:16

commit v3 on v2

--- a/solution.py
+++ b/solution.py
@@ -22,18 +22,45 @@
     return lax.ppermute(value, axis, [(source, source + steps) for source in range(leading, last)])
 
 
+def split3(x):
+    hi = lax.reduce_precision(x, exponent_bits=8, mantissa_bits=7)
+    rest = x - hi
+    mid = lax.reduce_precision(rest, exponent_bits=8, mantissa_bits=7)
+    lo = rest - mid
+    return jnp.concatenate(
+        [hi.astype(jnp.bfloat16), mid.astype(jnp.bfloat16), lo.astype(jnp.bfloat16)], axis=0
+    )
+
+
+def join3(parts):
+    n = parts.shape[0] // 3
+    return (parts[:n].astype(jnp.float32) + parts[n : 2 * n].astype(jnp.float32)) + parts[
+        2 * n :
+    ].astype(jnp.float32)
+
+
+def neighbour_exchange(down_payload, up_payload, rider):
+    parts = split3(rider)
+    n = down_payload.shape[0]
+    got_next = shifted(jnp.concatenate([down_payload, parts], axis=0), "leaf", -1)
+    got_prev = shifted(jnp.concatenate([up_payload, parts], axis=0), "leaf", 1)
+    even = lax.axis_index("leaf") % 2 == 0
+    sib = join3(jnp.where(even, got_next[n:], got_prev[n:]))
+    return got_next[:n], got_prev[:n], sib, join3(parts)
+
+
 def apply_level(matrix, sibling, flipped):
     if flipped:
         return jnp.einsum("sr,asc->arc", matrix, sibling, precision=lax.Precision.HIGHEST)
     return jnp.einsum("rs,asc->arc", matrix, sibling, precision=lax.Precision.HIGHEST)
 
 
-def expand(own_value, translations, flipped, rider=None):
+def expand(own_value, translations, flipped, sibling0, rider=None):
     depth_count = lax.axis_size("leaf").bit_length() - 1
-    summed = jnp.zeros(own_value.shape, jnp.float32)
-    node_value = own_value
+    summed = apply_level(translations[0], sibling0, flipped)
+    node_value = own_value + sibling0
     rows = own_value.shape[0] * own_value.shape[1]
-    for height in range(depth_count):
+    for height in range(1, depth_count):
         if rider is None:
             sibling = partner(node_value, "leaf", height)
         else:
@@ -177,10 +204,13 @@
     span_blocks = blocks_here + 2 * HALO
     position = lax.axis_index("leaf")
 
-    head = features[:, :halo_points]
-    tail = features[:, points_here - halo_points :]
-    from_prev = shifted(tail, "leaf", 1)
-    from_next = shifted(head, "leaf", -1)
+    summary = jnp.einsum("rp,apc->arc", leaf_basis, features, preferred_element_type=jnp.float32)
+    summary_rows = summary.reshape(cases_here * summary.shape[1], width)
+    head = features[:, :halo_points].reshape(cases_here * halo_points, width)
+    tail = features[:, points_here - halo_points :].reshape(cases_here * halo_points, width)
+    from_next, from_prev, sib_rows, _ = neighbour_exchange(head, tail, summary_rows)
+    from_prev = from_prev.reshape(cases_here, halo_points, width)
+    from_next = from_next.reshape(cases_here, halo_points, width)
     extended = jnp.concatenate([from_prev, features, from_next], axis=1)
     local_ids = jnp.clip(
         near_pairs - (position * blocks_here - HALO), 0, span_blocks - 1
@@ -188,8 +218,7 @@
 
     near_bf = near_forward(local_ids, kernel_blocks, extended)
 
-    summary = jnp.einsum("rp,apc->arc", leaf_basis, features, preferred_element_type=jnp.float32)
-    expansion, _ = expand(summary, translations, False)
+    expansion, _ = expand(summary, translations, False, sib_rows.reshape(summary.shape))
     exp_bf = expansion.astype(jnp.bfloat16)
     far_coeff = jnp.einsum("arc,cd->ard", exp_bf, w_far, preferred_element_type=jnp.float32).astype(
         jnp.bfloat16
@@ -220,22 +249,29 @@
         jnp.einsum("arc,ard->cd", exp_bf, projected, preferred_element_type=jnp.float32) * scale
     )
     grads = jnp.concatenate([near_term, far_term], axis=0)
-
     case_depth = lax.axis_size("case").bit_length() - 1
     for height in range(case_depth):
         grads = grads + partner(grads, "case", height)
-    leaf_depth = lax.axis_size("leaf").bit_length() - 1
-    for height in range(leaf_depth):
-        grads = grads + partner(grads, "leaf", height)
 
     back_coeff = jnp.einsum("arc,dc->ard", projected, w_far, preferred_element_type=jnp.float32)
-    back_exp, _ = expand(back_coeff, translations, True)
+    coeff_rows = back_coeff.reshape(cases_here * back_coeff.shape[1], width)
+    rider = jnp.concatenate([coeff_rows, grads], axis=0)
+    got_next, got_prev, sib, own = neighbour_exchange(
+        lo.reshape(cases_here * halo_points, width),
+        hi.reshape(cases_here * halo_points, width),
+        rider,
+    )
+    coeff_count = coeff_rows.shape[0]
+    grads = own[coeff_count:] + sib[coeff_count:]
+    back_exp, grads = expand(
+        back_coeff, translations, True, sib[:coeff_count].reshape(back_coeff.shape), rider=grads
+    )
     back_far = jnp.einsum(
         "rp,arc->apc", leaf_basis, back_exp.astype(jnp.bfloat16), preferred_element_type=jnp.float32
     )
 
-    got_prev = shifted(hi, "leaf", 1).astype(jnp.float32)
-    got_next = shifted(lo, "leaf", -1).astype(jnp.float32)
+    got_prev = got_prev.reshape(cases_here, halo_points, width).astype(jnp.float32)
+    got_next = got_next.reshape(cases_here, halo_points, width).astype(jnp.float32)
     near_back = jnp.concatenate(
         [
             mid[:, :halo_points] + got_prev,

time: 112 us -> 139 us (1.24)
  waiting for transfers between devices: 40.6 us -> 74.9 us
  starting transfers between devices: 34.1 us -> 23.2 us
    ppermute x4, waiting for transfers between devices: 0.01 us -> 57 us  [shifted(): lax.ppermute(value, axis, [(source, source + steps) for source in range(l...]
    ppermute x11 -> x6, waiting for transfers between devices: 40.6 us -> 18 us  [partner(): lax.ppermute(shard, axis, [(i, i ^ 1 << apart) for i in range(lax.axis_si...]
    ppermute x11 -> x6, starting transfers between devices: 26.7 us -> 11.1 us  [partner(): lax.ppermute(shard, axis, [(i, i ^ 1 << apart) for i in range(lax.axis_si...]
    ppermute x4, starting transfers between devices: 7.39 us -> 12.1 us  [shifted(): lax.ppermute(value, axis, [(source, source + steps) for source in range(l...]
    dot_general x1, matrix products: 1.33 us -> 5.06 us  [on_device(): jnp.einsum('rp,ard->apd', leaf_basis, far_coeff, preferred_element_type=j...]
    dot_general x1, matrix products: 4.54 us -> 3 us  [on_device(): jnp.einsum('apc,cd->apd', near_bf, w_near, preferred_element_type=jnp.flo...]
    slice x1 -> x8, local copies, waits for them, and re-layouts: 1.04 us -> 2.57 us  [the longest x1 1.37 us: on_device(): features[:, points_here - halo_points:]]
    concatenate x0 -> x4, other arithmetic: none -> 1.42 us  [the longest x1 1.31 us: neighbour_exchange(): jnp.concatenate([down_payload, parts], axis=0)]
  transfers between devices with their start and end apart: 15 -> 10, of which waited for: 8 -> 7; matrix products, arithmetic and copies ran while one was open for 6% -> 5% of each run, Pallas kernels for 9% -> 12%
where the time goes in v3:
time: 139 us; the launch traced here: 138 us
  waiting for transfers between devices  74.9 us (54%)
  starting transfers between devices  23.2 us (17%)
  Pallas kernels  16.8 us (12%)
  matrix products  13.7 us (10%)
  local copies, waits for them, and re-layouts  4.46 us (3%)
  other arithmetic  4.29 us (3%)
    ppermute x4, waiting for transfers between devices, shifted(): lax.ppermute(value, axis, [(source, source + steps) for source in range(l...  57 us
    ppermute x6, waiting for transfers between devices, partner(): lax.ppermute(shard, axis, [(i, i ^ 1 << apart) for i in range(lax.axis_si...  18 us
    ppermute x4, starting transfers between devices, shifted(): lax.ppermute(value, axis, [(source, source + steps) for source in range(l...  12.1 us
    ppermute x6, starting transfers between devices, partner(): lax.ppermute(shard, axis, [(i, i ^ 1 << apart) for i in range(lax.axis_si...  11.1 us
    pallas_call x1, Pallas kernels, near_backward(): pl.pallas_call(functools.partial(near_bwd_kernel, cases, pairs, rows, ste...  9.6 us
    pallas_call x1, Pallas kernels, near_forward(): pl.pallas_call(functools.partial(near_fwd_kernel, cases, pairs, rows), ou...  7.18 us
    dot_general x1, matrix products, on_device(): jnp.einsum('rp,ard->apd', leaf_basis, far_coeff, preferred_element_type=j...  5.06 us
    dot_general x1, matrix products, on_device(): jnp.einsum('apc,cd->apd', near_bf, w_near, preferred_element_type=jnp.flo...  3 us
  transfers between devices with their start and end apart: 10, of which 7 were waited for; matrix products, arithmetic and copies ran while one was open for 5% of the time, Pallas kernels for 12%

profile of v3, /device:TPU:0, one launch (start us, length us, event | category | flops | bytes accessed | tf_op | source)
XLA Modules:
  0.0 138.4 jit_solution(1082070470725430642)
XLA Ops:
  0.7 1.4 fusion.49
  2.7 4.9 %collective-permute-start = (bf16[2432,128]{1,0:T(8,128)(2,1)S(1)}, bf16[2432,128]{1,0:T(8,128)(2,1)S(1)}, u32[]{:S(2)}, u32[]{:S(2)}) collective-permute-start(bf16[2432,128]{1,0:T(8,128)(2,1)S(1)} %get-tuple-element.23), channel_id=1, source_target_pairs={{0,4},{4,8},{8,12},{12,16},{16,20},{20,24},{24,28},{1,5},{5,9},{9,... | collective-permute-start | bytes 1867784 | tf_op jit(solution)/shard_map/ppermute | solution.py:22
  7.6 1.3 collective-permute-start.1
  8.9 0.7 reshape.59.ids_ref
  9.6 24.6 %collective-permute-done = bf16[2432,128]{1,0:T(8,128)(2,1)S(1)} collective-permute-done((bf16[2432,128]{1,0:T(8,128)(2,1)S(1)}, bf16[2432,128]{1,0:T(8,128)(2,1)S(1)}, u32[]{:S(2)}, u32[]{:S(2)}) %collective-permute-start) | collective-permute-done | bytes 622624 | tf_op jit(solution)/shard_map/ppermute | solution.py:22
  34.2 0.9 slice_select_fusion.1
  35.1 3.6 %collective-permute-start.2 = (f32[2,64,128]{2,1,0:T(8,128)S(1)}, f32[2,64,128]{2,1,0:T(8,128)S(1)}, u32[]{:S(2)}, u32[]{:S(2)}) collective-permute-start(f32[2,64,128]{2,1,0:T(8,128)S(1)} %bitcast_add_fusion), channel_id=1, source_target_pairs={{0,8},{4,12},{8,0},{12,4},{16,24},{20,28},{24,16},{28,20},{1,9},{5... | collective-permute-start | bytes 196616 | tf_op jit(solution)/shard_map/ppermute | solution.py:16
  38.8 1.1 slice.124
  39.9 1.5 %pad_maximum_fusion.ext_ref = bf16[2,4096,128]{2,1,0:T(8,128)(2,1)} fusion(bf16[2,1024,128]{2,1,0:T(8,128)(2,1)S(1)} %bitcast.115, bf16[2,2048,128]{2,1,0:T(8,128)(2,1)S(1)} %copy-done.2, bf16[2,1024,128]{2,1,0:T(8,128)(2,1)S(1)} %bitcast.114), kind=kLoop, calls=%fused_computation.20 | loop fusion | flops 6291456 | bytes 4194304 | tf_op jit(solution)/shard_map/concatenate | solution.py:214
  41.3 7.2 %shard_map.111 = bf16[2,2048,128]{2,1,0:T(8,128)(2,1)} custom-call(s32[192]{0:T(256)} %reshape.59.ids_ref, bf16[16,12,128,128]{3,2,1,0:T(8,128)(2,1)} %kb_ref.3, bf16[2,4096,128]{2,1,0:T(8,128)(2,1)} %pad_maximum_fusion.ext_ref), custom_call_target="tpu_custom_call" | custom-call | flops 1610612736 | bytes 9437184 | tf_op jit(solution)/shard_map/pallas_call | solution.py:103
  48.5 3.0 %fusion.40 = f32[2,2048,128]{2,1,0:T(8,128)} fusion(bf16[2,2048,128]{2,1,0:T(8,128)(2,1)} %shard_map.111, bf16[128,128]{1,0:T(8,128)(2,1)S(1)} %copy-done.5), kind=kOutput, calls=%fused_computation.90 | convolution fusion | flops 134217728 | bytes 3178496 | tf_op jit(solution)/shard_map/apc,cd->apd/dot_general | solution.py:228
  51.8 2.7 %collective-permute-start.3 = (f32[2,64,128]{2,1,0:T(8,128)S(1)}, f32[2,64,128]{2,1,0:T(8,128)S(1)}, u32[]{:S(2)}, u32[]{:S(2)}) collective-permute-start(f32[2,64,128]{2,1,0:T(8,128)S(1)} %add.93), channel_id=1, source_target_pairs={{0,16},{4,20},{8,24},{12,28},{16,0},{20,4},{24,8},{28,12},{1,17},{... | collective-permute-start | bytes 196616 | tf_op jit(solution)/shard_map/ppermute | solution.py:16
  54.6 3.1 %collective-permute-done.3 = f32[2,64,128]{2,1,0:T(8,128)S(1)} collective-permute-done((f32[2,64,128]{2,1,0:T(8,128)S(1)}, f32[2,64,128]{2,1,0:T(8,128)S(1)}, u32[]{:S(2)}, u32[]{:S(2)}) %collective-permute-start.3) | collective-permute-done | bytes 65568 | tf_op jit(solution)/shard_map/ppermute | solution.py:16
  57.9 5.1 %fusion.5 = (bf16[2,2048,128]{2,1,0:T(8,128)(2,1)S(1)}, bf16[2,2048,128]{2,1,0:T(8,128)(2,1)}) fusion(bf16[2,2048,128]{2,1,0:T(8,128)(2,1)} %param.9, f32[2,2048,128]{2,1,0:T(8,128)} %fusion.40, bf16[64,2048]{1,0:T(8,128)(2,1)S(1)} %copy-done, bf16[2,64,128]{2,1,0:T(8,128)(2,1)S(1)} %fusion.19, bf16[128,128]{1,0:T(8,128)(2,1)S(1)} %copy-done.6), kind=kOutput, calls=%fused_computation.12 | convolution fusion | flops 83902464 | bytes 5570560 | tf_op jit(solution)/shard_map/rp,ard->apd/dot_general | solution.py:226
  63.0 0.5 fusion.14
  63.5 0.3 fusion.17
  63.8 1.4 %convolution_convert_fusion.back_ref = bf16[2,2048,128]{2,1,0:T(8,128)(2,1)} fusion(bf16[2,2048,128]{2,1,0:T(8,128)(2,1)S(1)} %get-tuple-element.12, bf16[128,128]{1,0:T(8,128)(2,1)S(1)} %copy-done.5), kind=kOutput, calls=%fused_computation.9 | convolution fusion | flops 134742016 | bytes 2129920 | tf_op jit(solution)/shard_map/apc,dc->apd/dot_general | solution.py:236
  65.6 1.2 collective-permute-done.4
  66.8 1.5 %collective-permute-start.5 = (f32[256,128]{1,0:T(8,128)S(1)}, f32[256,128]{1,0:T(8,128)S(1)}, u32[]{:S(2)}, u32[]{:S(2)}) collective-permute-start(f32[256,128]{1,0:T(8,128)S(1)} %fusion.48), channel_id=1, source_target_pairs={{0,2},{1,3},{2,0},{3,1},{4,6},{5,7},{6,4},{7,5},{8,10},{9,11},{10,... | collective-permute-start | bytes 393224 | tf_op jit(solution)/shard_map/ppermute | solution.py:16
  68.4 9.6 %shard_map.112 = (f32[2,2048,128]{2,1,0:T(8,128)}, bf16[2,1024,128]{2,1,0:T(8,128)(2,1)}, bf16[2,1024,128]{2,1,0:T(8,128)(2,1)}) custom-call(s32[192]{0:T(256)} %reshape.59.ids_ref, bf16[16,12,128,128]{3,2,1,0:T(8,128)(2,1)} %kb_ref.3, bf16[2,2048,128]{2,1,0:T(8,128)(2,1)} %convolution_convert_fusion.back_ref), custom_call_target="tpu_custom_call" | custom-call | flops 1610612736 | bytes 11534336 | tf_op jit(solution)/shard_map/pallas_call | solution.py:162
  78.0 1.3 pad_maximum_fusion.1
  79.4 1.3 collective-permute-start.7
  80.7 4.6 %collective-permute-start.6 = (bf16[3200,128]{1,0:T(8,128)(2,1)S(1)}, bf16[3200,128]{1,0:T(8,128)(2,1)S(1)}, u32[]{:S(2)}, u32[]{:S(2)}) collective-permute-start(bf16[3200,128]{1,0:T(8,128)(2,1)S(1)} %get-tuple-element.17), channel_id=1, source_target_pairs={{0,4},{4,8},{8,12},{12,16},{16,20},{20,24},{24,28},{1,5},{5,9},{9,... | collective-permute-start | bytes 2457608 | tf_op jit(solution)/shard_map/ppermute | solution.py:22
  85.3 16.0 %collective-permute-done.7 = bf16[3200,128]{1,0:T(8,128)(2,1)S(1)} collective-permute-done((bf16[3200,128]{1,0:T(8,128)(2,1)S(1)}, bf16[3200,128]{1,0:T(8,128)(2,1)S(1)}, u32[]{:S(2)}, u32[]{:S(2)}) %collective-permute-start.7) | collective-permute-done | bytes 819232 | tf_op jit(solution)/shard_map/ppermute | solution.py:22
  101.3 16.4 %collective-permute-done.6 = bf16[3200,128]{1,0:T(8,128)(2,1)S(1)} collective-permute-done((bf16[3200,128]{1,0:T(8,128)(2,1)S(1)}, bf16[3200,128]{1,0:T(8,128)(2,1)S(1)}, u32[]{:S(2)}, u32[]{:S(2)}) %collective-permute-start.6) | collective-permute-done | bytes 819232 | tf_op jit(solution)/shard_map/ppermute | solution.py:22
  117.8 1.0 collective-permute-start.8
  119.0 0.3 copy-done.3
  119.7 5.0 %collective-permute-done.8 = f32[384,128]{1,0:T(8,128)S(1)} collective-permute-done((f32[384,128]{1,0:T(8,128)S(1)}, f32[384,128]{1,0:T(8,128)S(1)}, u32[]{:S(2)}, u32[]{:S(2)}) %collective-permute-start.8) | collective-permute-done | bytes 196640 | tf_op jit(solution)/shard_map/ppermute | solution.py:16
  124.8 2.2 %collective-permute-start.9 = (f32[384,128]{1,0:T(8,128)S(1)}, f32[384,128]{1,0:T(8,128)S(1)}, u32[]{:S(2)}, u32[]{:S(2)}) collective-permute-start(f32[384,128]{1,0:T(8,128)S(1)} %pad_maximum_fusion.15), channel_id=1, source_target_pairs={{0,16},{4,20},{8,24},{12,28},{16,0},{20,4},{24,8},{28,12},{1,17},{... | collective-permute-start | bytes 589832 | tf_op jit(solution)/shard_map/ppermute | solution.py:16
  127.3 8.7 %collective-permute-done.9 = f32[384,128]{1,0:T(8,128)S(1)} collective-permute-done((f32[384,128]{1,0:T(8,128)S(1)}, f32[384,128]{1,0:T(8,128)S(1)}, u32[]{:S(2)}, u32[]{:S(2)}) %collective-permute-start.9) | collective-permute-done | bytes 196640 | tf_op jit(solution)/shard_map/ppermute | solution.py:16
  136.0 0.7 fusion.50
  136.9 1.5 %fusion.2 = bf16[2,2048,128]{2,1,0:T(8,128)(2,1)} fusion(bf16[2,64,128]{2,1,0:T(8,128)(2,1)S(1)} %fusion.18, f32[2,1024,128]{2,1,0:T(8,128)S(1)} %get-tuple-element.11, f32[2,1024,128]{2,1,0:T(8,128)S(1)} %get-tuple-element.10, bf16[64,2048]{1,0:T(8,128)(2,1)S(1)} %copy-done), kind=kOutput, calls=%fused_computation.8 | convolution fusion | flops 68681728 | bytes 3440640 | tf_op jit(solution)/shard_map/rp,arc->apc/dot_general | solution.py:269
  (54 shorter events, 3.0 us)
Async XLA Ops:
  0.6 1.4 %copy-start = (bf16[64,2048]{1,0:T(8,128)(2,1)S(1)}, bf16[64,2048]{1,0:T(8,128)(2,1)}, u32[]{:S(2)}) copy-start(bf16[64,2048]{1,0:T(8,128)(2,1)} %param.12) | copy-start | bytes 786436
  0.6 1.6 %copy-start.2 = (bf16[2,2048,128]{2,1,0:T(8,128)(2,1)S(1)}, bf16[2,2048,128]{2,1,0:T(8,128)(2,1)}, u32[]{:S(2)}) copy-start(bf16[2,2048,128]{2,1,0:T(8,128)(2,1)} %param.8) | copy-start | bytes 3145732
  2.3 6.7 %copy-start.7 = (s32[16,12]{1,0:T(8,128)S(1)}, s32[16,12]{1,0:T(8,128)}, u32[]{:S(2)}) copy-start(s32[16,12]{1,0:T(8,128)} %param.11) | copy-start | bytes 2308
  2.7 31.5 %collective-permute-start = (bf16[2432,128]{1,0:T(8,128)(2,1)S(1)}, bf16[2432,128]{1,0:T(8,128)(2,1)S(1)}, u32[]{:S(2)}, u32[]{:S(2)}) collective-permute-start(bf16[2432,128]{1,0:T(8,128)(2,1)S(1)} %get-tuple-element.23), channel_id=1, source_target_pairs={{0,4},{4,8},{8,12},{12,16},{16,20},{20,24},{24,28},{1,5},{5,9},{9,... | collective-permute-start | bytes 1867784 | tf_op jit(solution)/shard_map/ppermute | solution.py:22
  7.6 26.6 %collective-permute-start.1 = (bf16[2432,128]{1,0:T(8,128)(2,1)S(1)}, bf16[2432,128]{1,0:T(8,128)(2,1)}, u32[]{:S(2)}, u32[]{:S(2)}) collective-permute-start(bf16[2432,128]{1,0:T(8,128)(2,1)S(1)} %get-tuple-element.24), channel_id=1, source_target_pairs={{4,0},{8,4},{12,8},{16,12},{20,16},{24,20},{28,24},{5,1},{9,5},{13... | collective-permute-start | bytes 1867784 | tf_op jit(solution)/shard_map/ppermute | solution.py:22
  35.1 16.6 %collective-permute-start.2 = (f32[2,64,128]{2,1,0:T(8,128)S(1)}, f32[2,64,128]{2,1,0:T(8,128)S(1)}, u32[]{:S(2)}, u32[]{:S(2)}) collective-permute-start(f32[2,64,128]{2,1,0:T(8,128)S(1)} %bitcast_add_fusion), channel_id=1, source_target_pairs={{0,8},{4,12},{8,0},{12,4},{16,24},{20,28},{24,16},{28,20},{1,9},{5... | collective-permute-start | bytes 196616 | tf_op jit(solution)/shard_map/ppermute | solution.py:16
  41.3 7.2 %copy-start.5 = (bf16[128,128]{1,0:T(8,128)(2,1)S(1)}, bf16[128,128]{1,0:T(8,128)(2,1)}, u32[]{:S(2)}) copy-start(bf16[128,128]{1,0:T(8,128)(2,1)} %param.13) | copy-start | bytes 98308
  48.5 3.0 %copy-start.4 = (f32[3,64,64]{2,1,0:T(8,128)S(1)}, f32[3,64,64]{2,1,0:T(8,128)}, u32[]{:S(2)}) copy-start(f32[3,64,64]{2,1,0:T(8,128)} %param.15) | copy-start | bytes 147460
  48.5 9.4 %copy-start.6 = (bf16[128,128]{1,0:T(8,128)(2,1)S(1)}, bf16[128,128]{1,0:T(8,128)(2,1)}, u32[]{:S(2)}) copy-start(bf16[128,128]{1,0:T(8,128)(2,1)} %param.14) | copy-start | bytes 98308
  51.8 5.9 %collective-permute-start.3 = (f32[2,64,128]{2,1,0:T(8,128)S(1)}, f32[2,64,128]{2,1,0:T(8,128)S(1)}, u32[]{:S(2)}, u32[]{:S(2)}) collective-permute-start(f32[2,64,128]{2,1,0:T(8,128)S(1)} %add.93), channel_id=1, source_target_pairs={{0,16},{4,20},{8,24},{12,28},{16,0},{20,4},{24,8},{28,12},{1,17},{... | collective-permute-start | bytes 196616 | tf_op jit(solution)/shard_map/ppermute | solution.py:16
  57.9 5.1 %copy-start.1 = (bf16[2,2048,128]{2,1,0:T(8,128)(2,1)S(1)}, bf16[2,2048,128]{2,1,0:T(8,128)(2,1)}, u32[]{:S(2)}) copy-start(bf16[2,2048,128]{2,1,0:T(8,128)(2,1)} %shard_map.111) | copy-start | bytes 3145732
  65.4 1.4 %collective-permute-start.4 = (f32[256,128]{1,0:T(8,128)S(1)}, f32[256,128]{1,0:T(8,128)S(1)}, u32[]{:S(2)}, u32[]{:S(2)}) collective-permute-start(f32[256,128]{1,0:T(8,128)S(1)} %pad_maximum_fusion.16), channel_id=1, source_target_pairs={{0,1},{1,0},{2,3},{3,2},{4,5},{5,4},{6,7},{7,6},{8,9},{9,8},{10,11... | collective-permute-start | bytes 393224 | tf_op jit(solution)/shard_map/ppermute | solution.py:16
  66.8 11.1 %collective-permute-start.5 = (f32[256,128]{1,0:T(8,128)S(1)}, f32[256,128]{1,0:T(8,128)S(1)}, u32[]{:S(2)}, u32[]{:S(2)}) collective-permute-start(f32[256,128]{1,0:T(8,128)S(1)} %fusion.48), channel_id=1, source_target_pairs={{0,2},{1,3},{2,0},{3,1},{4,6},{5,7},{6,4},{7,5},{8,10},{9,11},{10,... | collective-permute-start | bytes 393224 | tf_op jit(solution)/shard_map/ppermute | solution.py:16
  79.4 21.9 %collective-permute-start.7 = (bf16[3200,128]{1,0:T(8,128)(2,1)S(1)}, bf16[3200,128]{1,0:T(8,128)(2,1)S(1)}, u32[]{:S(2)}, u32[]{:S(2)}) collective-permute-start(bf16[3200,128]{1,0:T(8,128)(2,1)S(1)} %get-tuple-element.16), channel_id=1, source_target_pairs={{4,0},{8,4},{12,8},{16,12},{20,16},{24,20},{28,24},{5,1},{9,5},{13... | collective-permute-start | bytes 2457608 | tf_op jit(solution)/shard_map/ppermute | solution.py:22
  80.7 37.0 %collective-permute-start.6 = (bf16[3200,128]{1,0:T(8,128)(2,1)S(1)}, bf16[3200,128]{1,0:T(8,128)(2,1)S(1)}, u32[]{:S(2)}, u32[]{:S(2)}) collective-permute-start(bf16[3200,128]{1,0:T(8,128)(2,1)S(1)} %get-tuple-element.17), channel_id=1, source_target_pairs={{0,4},{4,8},{8,12},{12,16},{16,20},{20,24},{24,28},{1,5},{5,9},{9,... | collective-permute-start | bytes 2457608 | tf_op jit(solution)/shard_map/ppermute | solution.py:22
  117.7 1.6 %copy-start.3 = (f32[2,2048,128]{2,1,0:T(8,128)S(1)}, f32[2,2048,128]{2,1,0:T(8,128)}, u32[]{:S(2)}) copy-start(f32[2,2048,128]{2,1,0:T(8,128)} %get-tuple-element.7) | copy-start | bytes 6291460
  117.8 6.9 %collective-permute-start.8 = (f32[384,128]{1,0:T(8,128)S(1)}, f32[384,128]{1,0:T(8,128)S(1)}, u32[]{:S(2)}, u32[]{:S(2)}) collective-permute-start(f32[384,128]{1,0:T(8,128)S(1)} %pad_maximum_fusion.14), channel_id=1, source_target_pairs={{0,8},{4,12},{8,0},{12,4},{16,24},{20,28},{24,16},{28,20},{1,9},{5... | collective-permute-start | bytes 589832 | tf_op jit(solution)/shard_map/ppermute | solution.py:16
  124.8 11.2 %collective-permute-start.9 = (f32[384,128]{1,0:T(8,128)S(1)}, f32[384,128]{1,0:T(8,128)S(1)}, u32[]{:S(2)}, u32[]{:S(2)}) collective-permute-start(f32[384,128]{1,0:T(8,128)S(1)} %pad_maximum_fusion.15), channel_id=1, source_target_pairs={{0,16},{4,20},{8,24},{12,28},{16,0},{20,4},{24,8},{28,12},{1,17},{... | collective-permute-start | bytes 589832 | tf_op jit(solution)/shard_map/ppermute | solution.py:16

commit v4 on v1

--- a/solution.py
+++ b/solution.py
@@ -28,7 +28,7 @@
     return jnp.einsum("rs,asc->arc", matrix, sibling, precision=lax.Precision.HIGHEST)
 
 
-def expand(own_value, translations, flipped, rider=None):
+def expand(own_value, translations, flipped, rider=None, cover=None):
     depth_count = lax.axis_size("leaf").bit_length() - 1
     summed = jnp.zeros(own_value.shape, jnp.float32)
     node_value = own_value
@@ -41,11 +41,15 @@
                 [node_value.reshape(rows, own_value.shape[2]), rider], axis=0
             )
             got = partner(packed, "leaf", height)
+            if cover is not None and height < 2:
+                got, cover = lax.optimization_barrier((got, cover))
             sibling = got[:rows].reshape(own_value.shape)
             rider = rider + got[rows:]
         summed = summed + apply_level(translations[height], sibling, flipped)
         node_value = node_value + sibling
-    return summed, rider
+    if cover is None:
+        return summed, rider
+    return summed, rider, cover
 
 
 def near_fwd_kernel(cases, pairs, rows, ids_ref, kb_ref, ext_ref, out_ref):
@@ -222,7 +226,9 @@
     grads = jnp.concatenate([near_term, far_term], axis=0)
 
     back_coeff = jnp.einsum("arc,dc->ard", projected, w_far, preferred_element_type=jnp.float32)
-    back_exp, grads = expand(back_coeff, translations, True, rider=grads)
+    back_exp, grads, (mid, lo, hi) = expand(
+        back_coeff, translations, True, rider=grads, cover=(mid, lo, hi)
+    )
     back_far = jnp.einsum(
         "rp,arc->apc", leaf_basis, back_exp.astype(jnp.bfloat16), preferred_element_type=jnp.float32
     )

time: 107 us -> 100 us (0.935)
  waiting for transfers between devices: 46.9 us -> 41 us
  other arithmetic: 4.66 us -> 3.04 us
    ppermute x4, waiting for transfers between devices: 19.8 us -> 13.3 us  [shifted(): lax.ppermute(value, axis, [(source, source + steps) for source in range(l...]
    add x1, other arithmetic: 1.79 us -> 0.18 us  [on_device(): mid[:, :halo_points] + got_prev]
    ppermute x4, starting transfers between devices: 13.5 us -> 14.6 us  [shifted(): lax.ppermute(value, axis, [(source, source + steps) for source in range(l...]
  transfers between devices with their start and end apart: 12 -> 12, of which waited for: 7 -> 7; matrix products, arithmetic and copies ran while one was open for 8% -> 7% of each run, Pallas kernels for 9% -> 10%
where the time goes in v4:
time: 100 us; the launch traced here: 98.3 us
  waiting for transfers between devices  41 us (41%)
  starting transfers between devices  20.4 us (20%)
  Pallas kernels  16.8 us (17%)
  matrix products  12.7 us (13%)
  local copies, waits for them, and re-layouts  3.33 us (3%)
  other arithmetic  3.04 us (3%)
    ppermute x8, waiting for transfers between devices, partner(): lax.ppermute(shard, axis, [(i, i ^ 1 << apart) for i in range(lax.axis_si...  27.7 us
    ppermute x4, starting transfers between devices, shifted(): lax.ppermute(value, axis, [(source, source + steps) for source in range(l...  14.6 us
    ppermute x4, waiting for transfers between devices, shifted(): lax.ppermute(value, axis, [(source, source + steps) for source in range(l...  13.3 us
    pallas_call x1, Pallas kernels, near_backward(): pl.pallas_call(functools.partial(near_bwd_kernel, cases, pairs, rows, ste...  9.6 us
    pallas_call x1, Pallas kernels, near_forward(): pl.pallas_call(functools.partial(near_fwd_kernel, cases, pairs, rows), ou...  7.2 us
    ppermute x8, starting transfers between devices, partner(): lax.ppermute(shard, axis, [(i, i ^ 1 << apart) for i in range(lax.axis_si...  5.86 us
    dot_general x1, matrix products, on_device(): jnp.einsum('apc,cd->apd', near_bf, w_near, preferred_element_type=jnp.flo...  4.54 us
    concatenate x1, other arithmetic, on_device(): extended = jnp.concatenate([from_prev, features, from_next], axis=1)  2.67 us
  transfers between devices with their start and end apart: 12, of which 7 were waited for; matrix products, arithmetic and copies ran while one was open for 7% of the time, Pallas kernels for 10%

profile of v4, /device:TPU:16, one launch (start us, length us, event | category | flops | bytes accessed | tf_op | source)
XLA Modules:
  0.0 98.3 jit_solution(5427012800007069450)
XLA Ops:
  0.7 0.9 copy-done
  1.6 1.5 %convolution_bitcast_fusion.2 = f32[2,64,128]{2,1,0:T(8,128)S(1)} fusion(bf16[2,2048,128]{2,1,0:T(8,128)(2,1)} %param.8, bf16[64,2048]{1,0:T(8,128)(2,1)S(1)} %copy-done), kind=kOutput, calls=%fused_computation.22 | convolution fusion | flops 67108864 | bytes 1376256 | tf_op jit(solution)/shard_map/rp,apc->arc/dot_general | solution.py:195
  3.1 1.6 %collective-permute-start.2 = (f32[2,64,128]{2,1,0:T(8,128)S(1)}, f32[2,64,128]{2,1,0:T(8,128)S(1)}, u32[]{:S(2)}, u32[]{:S(2)}) collective-permute-start(f32[2,64,128]{2,1,0:T(8,128)S(1)} %convolution_bitcast_fusion.2), channel_id=1, source_target_pairs={{0,4},{4,0},{8,12},{12,8},{16,20},{20,16},{24,28},{28,24},{1,5},{5... | collective-permute-start | bytes 196616 | tf_op jit(solution)/shard_map/ppermute | solution.py:16
  4.7 1.0 %fusion.46 = (bf16[2,1024,128]{2,1,0:T(8,128)(2,1)}, bf16[2,1024,128]{2,1,0:T(8,128)(2,1)}) fusion(bf16[2,2048,128]{2,1,0:T(8,128)(2,1)S(1)} %copy-done.1), kind=kLoop, calls=%fused_computation.71 | loop fusion | bytes 2097152 | tf_op jit(solution)/shard_map/slice | solution.py:185
  5.7 2.4 %collective-permute-start = (bf16[2,1024,128]{2,1,0:T(8,128)(2,1)}, bf16[2,1024,128]{2,1,0:T(8,128)(2,1)}, u32[]{:S(2)}, u32[]{:S(2)}) collective-permute-start(bf16[2,1024,128]{2,1,0:T(8,128)(2,1)} %get-tuple-element.30), channel_id=1, source_target_pairs={{0,4},{4,8},{8,12},{12,16},{16,20},{20,24},{24,28},{1,5},{5,9},{9,... | collective-permute-start | bytes 1572872 | tf_op jit(solution)/shard_map/ppermute | solution.py:22
  8.2 4.3 %collective-permute-start.1 = (bf16[2,1024,128]{2,1,0:T(8,128)(2,1)}, bf16[2,1024,128]{2,1,0:T(8,128)(2,1)}, u32[]{:S(2)}, u32[]{:S(2)}) collective-permute-start(bf16[2,1024,128]{2,1,0:T(8,128)(2,1)} %get-tuple-element.31), channel_id=1, source_target_pairs={{4,0},{8,4},{12,8},{16,12},{20,16},{24,20},{28,24},{5,1},{9,5},{13... | collective-permute-start | bytes 1572872 | tf_op jit(solution)/shard_map/ppermute | solution.py:22
  12.5 1.6 %collective-permute-start.3 = (f32[2,64,128]{2,1,0:T(8,128)S(1)}, f32[2,64,128]{2,1,0:T(8,128)S(1)}, u32[]{:S(2)}, u32[]{:S(2)}) collective-permute-start(f32[2,64,128]{2,1,0:T(8,128)S(1)} %add.65), channel_id=1, source_target_pairs={{0,8},{4,12},{8,0},{12,4},{16,24},{20,28},{24,16},{28,20},{1,9},{5... | collective-permute-start | bytes 196616 | tf_op jit(solution)/shard_map/ppermute | solution.py:16
  14.2 0.7 reshape.29.ids_ref
  14.8 12.7 %collective-permute-done.3 = f32[2,64,128]{2,1,0:T(8,128)S(1)} collective-permute-done((f32[2,64,128]{2,1,0:T(8,128)S(1)}, f32[2,64,128]{2,1,0:T(8,128)S(1)}, u32[]{:S(2)}, u32[]{:S(2)}) %collective-permute-start.3) | collective-permute-done | bytes 65568 | tf_op jit(solution)/shard_map/ppermute | solution.py:16
  27.8 4.9 %collective-permute-done.4 = f32[2,64,128]{2,1,0:T(8,128)S(1)} collective-permute-done((f32[2,64,128]{2,1,0:T(8,128)S(1)}, f32[2,64,128]{2,1,0:T(8,128)S(1)}, u32[]{:S(2)}, u32[]{:S(2)}) %collective-permute-start.4) | collective-permute-done | bytes 65568 | tf_op jit(solution)/shard_map/ppermute | solution.py:16
  33.1 1.3 %convolution_bitcast_fusion.1 = f32[2,2048,128]{2,1,0:T(8,128)S(1)} fusion(bf16[2,64,128]{2,1,0:T(8,128)(2,1)S(1)} %fusion.18, bf16[64,2048]{1,0:T(8,128)(2,1)S(1)} %copy-done, bf16[128,128]{1,0:T(8,128)(2,1)} %param.14), kind=kOutput, calls=%fused_computation.3 | convolution fusion | flops 71319552 | bytes 2424832 | tf_op jit(solution)/shard_map/rp,ard->apd/dot_general | solution.py:201
  34.5 2.7 %pad_maximum_fusion.ext_ref = bf16[2,4096,128]{2,1,0:T(8,128)(2,1)} fusion(bf16[2,1024,128]{2,1,0:T(8,128)(2,1)} %collective-permute-done.1, bf16[2,2048,128]{2,1,0:T(8,128)(2,1)S(1)} %copy-done.1, bf16[2,1024,128]{2,1,0:T(8,128)(2,1)} %collective-permute-done), kind=kLoop, calls=%fused_computation.18 | loop fusion | flops 6291456 | bytes 4194304 | tf_op jit(solution)/shard_map/concatenate | solution.py:188
  37.2 7.2 %shard_map.111 = bf16[2,2048,128]{2,1,0:T(8,128)(2,1)} custom-call(s32[192]{0:T(256)} %reshape.29.ids_ref, bf16[16,12,128,128]{3,2,1,0:T(8,128)(2,1)} %kb_ref.3, bf16[2,4096,128]{2,1,0:T(8,128)(2,1)} %pad_maximum_fusion.ext_ref), custom_call_target="tpu_custom_call" | custom-call | flops 1610612736 | bytes 9437184 | tf_op jit(solution)/shard_map/pallas_call | solution.py:80
  44.4 4.5 %fusion.2 = (bf16[2,2048,128]{2,1,0:T(8,128)(2,1)S(1)}, bf16[2,2048,128]{2,1,0:T(8,128)(2,1)}) fusion(bf16[2,2048,128]{2,1,0:T(8,128)(2,1)} %param.9, f32[2,2048,128]{2,1,0:T(8,128)S(1)} %convolution_bitcast_fusion.1, bf16[2,2048,128]{2,1,0:T(8,128)(2,1)} %shard_map.111, bf16[128,128]{1,0:T(8,128)(2,1)S(1)} %copy-done.6), kind=kOutput, calls=%fused_computation.10 | convolution fusion | flops 146800640 | bytes 6324224 | tf_op jit(solution)/shard_map/apc,cd->apd/dot_general | solution.py:203
  48.9 0.5 fusion.12
  49.4 0.3 fusion.16
  50.2 1.4 %convolution_convert_fusion.back_ref = bf16[2,2048,128]{2,1,0:T(8,128)(2,1)} fusion(bf16[2,2048,128]{2,1,0:T(8,128)(2,1)S(1)} %get-tuple-element.28, bf16[128,128]{1,0:T(8,128)(2,1)S(1)} %copy-done.6), kind=kOutput, calls=%fused_computation.7 | convolution fusion | flops 134742016 | bytes 2129920 | tf_op jit(solution)/shard_map/apc,dc->apd/dot_general | solution.py:211
  51.6 9.6 %shard_map.112 = (f32[2,2048,128]{2,1,0:T(8,128)}, bf16[2,1024,128]{2,1,0:T(8,128)(2,1)}, bf16[2,1024,128]{2,1,0:T(8,128)(2,1)}) custom-call(s32[192]{0:T(256)} %reshape.29.ids_ref, bf16[16,12,128,128]{3,2,1,0:T(8,128)(2,1)} %kb_ref.3, bf16[2,2048,128]{2,1,0:T(8,128)(2,1)} %convolution_convert_fusion.back_ref), custom_call_target="tpu_custom_call" | custom-call | flops 1610612736 | bytes 11534336 | tf_op jit(solution)/shard_map/pallas_call | solution.py:139
  61.3 0.6 collective-permute-start.6
  61.9 5.2 %collective-permute-done.6 = f32[384,128]{1,0:T(8,128)S(1)} collective-permute-done((f32[384,128]{1,0:T(8,128)S(1)}, f32[384,128]{1,0:T(8,128)S(1)}, u32[]{:S(2)}, u32[]{:S(2)}) %collective-permute-start.6) | collective-permute-done | bytes 196640 | tf_op jit(solution)/shard_map/ppermute | solution.py:16
  67.2 0.3 collective-permute-start.9
  67.7 3.7 %collective-permute-start.7 = (bf16[2,1024,128]{2,1,0:T(8,128)(2,1)S(1)}, bf16[2,1024,128]{2,1,0:T(8,128)(2,1)S(1)}, u32[]{:S(2)}, u32[]{:S(2)}) collective-permute-start(bf16[2,1024,128]{2,1,0:T(8,128)(2,1)S(1)} %copy-done.9), channel_id=1, source_target_pairs={{0,4},{4,8},{8,12},{12,16},{16,20},{20,24},{24,28},{1,5},{5,9},{9,... | collective-permute-start | bytes 1572872 | tf_op jit(solution)/shard_map/ppermute | solution.py:22
  71.4 4.2 %collective-permute-start.8 = (bf16[2,1024,128]{2,1,0:T(8,128)(2,1)S(1)}, bf16[2,1024,128]{2,1,0:T(8,128)(2,1)S(1)}, u32[]{:S(2)}, u32[]{:S(2)}) collective-permute-start(bf16[2,1024,128]{2,1,0:T(8,128)(2,1)S(1)} %copy-done.8), channel_id=1, source_target_pairs={{4,0},{8,4},{12,8},{16,12},{20,16},{24,20},{28,24},{5,1},{9,5},{13... | collective-permute-start | bytes 1572872 | tf_op jit(solution)/shard_map/ppermute | solution.py:22
  75.7 0.3 convolution_add_fusion.2
  76.0 1.1 %collective-permute-done.10 = f32[256,128]{1,0:T(8,128)S(1)} collective-permute-done((f32[256,128]{1,0:T(8,128)S(1)}, f32[256,128]{1,0:T(8,128)S(1)}, u32[]{:S(2)}, u32[]{:S(2)}) %collective-permute-start.10) | collective-permute-done | bytes 131104 | tf_op jit(solution)/shard_map/ppermute | solution.py:16
  77.0 1.6 %collective-permute-start.11 = (f32[256,128]{1,0:T(8,128)S(1)}, f32[256,128]{1,0:T(8,128)S(1)}, u32[]{:S(2)}, u32[]{:S(2)}) collective-permute-start(f32[256,128]{1,0:T(8,128)S(1)} %add.82), channel_id=1, source_target_pairs={{0,2},{1,3},{2,0},{3,1},{4,6},{5,7},{6,4},{7,5},{8,10},{9,11},{10,... | collective-permute-start | bytes 393224 | tf_op jit(solution)/shard_map/ppermute | solution.py:16
  78.6 0.3 fusion.17
  78.9 3.8 %collective-permute-done.11 = f32[256,128]{1,0:T(8,128)S(1)} collective-permute-done((f32[256,128]{1,0:T(8,128)S(1)}, f32[256,128]{1,0:T(8,128)S(1)}, u32[]{:S(2)}, u32[]{:S(2)}) %collective-permute-start.11) | collective-permute-done | bytes 131104 | tf_op jit(solution)/shard_map/ppermute | solution.py:16
  82.7 0.7 fusion.47
  83.3 8.4 %collective-permute-done.7 = bf16[2,1024,128]{2,1,0:T(8,128)(2,1)S(1)} collective-permute-done((bf16[2,1024,128]{2,1,0:T(8,128)(2,1)S(1)}, bf16[2,1024,128]{2,1,0:T(8,128)(2,1)S(1)}, u32[]{:S(2)}, u32[]{:S(2)}) %collective-permute-start.7) | collective-permute-done | bytes 524320 | tf_op jit(solution)/shard_map/ppermute | solution.py:22
  91.7 4.9 %collective-permute-done.8 = bf16[2,1024,128]{2,1,0:T(8,128)(2,1)S(1)} collective-permute-done((bf16[2,1024,128]{2,1,0:T(8,128)(2,1)S(1)}, bf16[2,1024,128]{2,1,0:T(8,128)(2,1)S(1)}, u32[]{:S(2)}, u32[]{:S(2)}) %collective-permute-start.8) | collective-permute-done | bytes 524320 | tf_op jit(solution)/shard_map/ppermute | solution.py:22
  96.8 1.5 %fusion.10 = bf16[2,2048,128]{2,1,0:T(8,128)(2,1)} fusion(f32[2,1024,128]{2,1,0:T(8,128)S(1)} %get-tuple-element.27, f32[2,1024,128]{2,1,0:T(8,128)S(1)} %get-tuple-element.26, bf16[2,64,128]{2,1,0:T(8,128)(2,1)S(1)} %fusion.17, bf16[64,2048]{1,0:T(8,128)(2,1)S(1)} %copy-done), kind=kOutput, calls=%fused_computation.20 | convolution fusion | flops 68681728 | bytes 3440640 | tf_op jit(solution)/shard_map/rp,arc->apc/dot_general | solution.py:232
  (50 shorter events, 1.8 us)
Async XLA Ops:
  0.6 1.0 copy-start
  0.6 4.1 %copy-start.1 = (bf16[2,2048,128]{2,1,0:T(8,128)(2,1)S(1)}, bf16[2,2048,128]{2,1,0:T(8,128)(2,1)}, u32[]{:S(2)}) copy-start(bf16[2,2048,128]{2,1,0:T(8,128)(2,1)} %param.8) | copy-start | bytes 3145732
  0.7 13.5 %copy-start.7 = (s32[16,12]{1,0:T(8,128)S(1)}, s32[16,12]{1,0:T(8,128)}, u32[]{:S(2)}) copy-start(s32[16,12]{1,0:T(8,128)} %param.11) | copy-start | bytes 2308
  0.7 26.9 %copy-start.4 = (f32[3,64,64]{2,1,0:T(8,128)S(1)}, f32[3,64,64]{2,1,0:T(8,128)}, u32[]{:S(2)}) copy-start(f32[3,64,64]{2,1,0:T(8,128)} %param.15) | copy-start | bytes 147460
  3.1 9.4 %collective-permute-start.2 = (f32[2,64,128]{2,1,0:T(8,128)S(1)}, f32[2,64,128]{2,1,0:T(8,128)S(1)}, u32[]{:S(2)}, u32[]{:S(2)}) collective-permute-start(f32[2,64,128]{2,1,0:T(8,128)S(1)} %convolution_bitcast_fusion.2), channel_id=1, source_target_pairs={{0,4},{4,0},{8,12},{12,8},{16,20},{20,16},{24,28},{28,24},{1,5},{5... | collective-permute-start | bytes 196616 | tf_op jit(solution)/shard_map/ppermute | solution.py:16
  5.7 28.7 %collective-permute-start = (bf16[2,1024,128]{2,1,0:T(8,128)(2,1)}, bf16[2,1024,128]{2,1,0:T(8,128)(2,1)}, u32[]{:S(2)}, u32[]{:S(2)}) collective-permute-start(bf16[2,1024,128]{2,1,0:T(8,128)(2,1)} %get-tuple-element.30), channel_id=1, source_target_pairs={{0,4},{4,8},{8,12},{12,16},{16,20},{20,24},{24,28},{1,5},{5,9},{9,... | collective-permute-start | bytes 1572872 | tf_op jit(solution)/shard_map/ppermute | solution.py:22
  8.2 26.3 %collective-permute-start.1 = (bf16[2,1024,128]{2,1,0:T(8,128)(2,1)}, bf16[2,1024,128]{2,1,0:T(8,128)(2,1)}, u32[]{:S(2)}, u32[]{:S(2)}) collective-permute-start(bf16[2,1024,128]{2,1,0:T(8,128)(2,1)} %get-tuple-element.31), channel_id=1, source_target_pairs={{4,0},{8,4},{12,8},{16,12},{20,16},{24,20},{28,24},{5,1},{9,5},{13... | collective-permute-start | bytes 1572872 | tf_op jit(solution)/shard_map/ppermute | solution.py:22
  12.5 15.0 %collective-permute-start.3 = (f32[2,64,128]{2,1,0:T(8,128)S(1)}, f32[2,64,128]{2,1,0:T(8,128)S(1)}, u32[]{:S(2)}, u32[]{:S(2)}) collective-permute-start(f32[2,64,128]{2,1,0:T(8,128)S(1)} %add.65), channel_id=1, source_target_pairs={{0,8},{4,12},{8,0},{12,4},{16,24},{20,28},{24,16},{28,20},{1,9},{5... | collective-permute-start | bytes 196616 | tf_op jit(solution)/shard_map/ppermute | solution.py:16
  27.5 5.2 %collective-permute-start.4 = (f32[2,64,128]{2,1,0:T(8,128)S(1)}, f32[2,64,128]{2,1,0:T(8,128)S(1)}, u32[]{:S(2)}, u32[]{:S(2)}) collective-permute-start(f32[2,64,128]{2,1,0:T(8,128)S(1)} %add.67), channel_id=1, source_target_pairs={{0,16},{4,20},{8,24},{12,28},{16,0},{20,4},{24,8},{28,12},{1,17},{... | collective-permute-start | bytes 196616 | tf_op jit(solution)/shard_map/ppermute | solution.py:16
  37.2 7.2 %copy-start.6 = (bf16[128,128]{1,0:T(8,128)(2,1)S(1)}, bf16[128,128]{1,0:T(8,128)(2,1)}, u32[]{:S(2)}) copy-start(bf16[128,128]{1,0:T(8,128)(2,1)} %param.13) | copy-start | bytes 98308
  44.4 4.5 %copy-start.2 = (bf16[2,2048,128]{2,1,0:T(8,128)(2,1)S(1)}, bf16[2,2048,128]{2,1,0:T(8,128)(2,1)}, u32[]{:S(2)}) copy-start(bf16[2,2048,128]{2,1,0:T(8,128)(2,1)} %shard_map.111) | copy-start | bytes 3145732
  48.9 1.0 %copy-start.5 = (bf16[128,128]{1,0:T(8,128)(2,1)S(1)}, bf16[128,128]{1,0:T(8,128)(2,1)}, u32[]{:S(2)}) copy-start(bf16[128,128]{1,0:T(8,128)(2,1)} %param.14) | copy-start | bytes 98308
  50.1 11.1 %collective-permute-start.5 = (f32[384,128]{1,0:T(8,128)S(1)}, f32[384,128]{1,0:T(8,128)S(1)}, u32[]{:S(2)}, u32[]{:S(2)}) collective-permute-start(f32[384,128]{1,0:T(8,128)S(1)} %pad_maximum_fusion.1), channel_id=1, source_target_pairs={{0,4},{4,0},{8,12},{12,8},{16,20},{20,16},{24,28},{28,24},{1,5},{5... | collective-permute-start | bytes 589832 | tf_op jit(solution)/shard_map/ppermute | solution.py:16
  61.2 6.5 %copy-start.9 = (bf16[2,1024,128]{2,1,0:T(8,128)(2,1)S(1)}, bf16[2,1024,128]{2,1,0:T(8,128)(2,1)}, u32[]{:S(2)}) copy-start(bf16[2,1024,128]{2,1,0:T(8,128)(2,1)} %get-tuple-element.23) | copy-start | bytes 1572868
  61.2 10.2 %copy-start.8 = (bf16[2,1024,128]{2,1,0:T(8,128)(2,1)S(1)}, bf16[2,1024,128]{2,1,0:T(8,128)(2,1)}, u32[]{:S(2)}) copy-start(bf16[2,1024,128]{2,1,0:T(8,128)(2,1)} %get-tuple-element.24) | copy-start | bytes 1572868
  61.2 35.5 %copy-start.3 = (f32[2,2048,128]{2,1,0:T(8,128)S(1)}, f32[2,2048,128]{2,1,0:T(8,128)}, u32[]{:S(2)}) copy-start(f32[2,2048,128]{2,1,0:T(8,128)} %get-tuple-element.22) | copy-start | bytes 6291460
  61.3 5.8 %collective-permute-start.6 = (f32[384,128]{1,0:T(8,128)S(1)}, f32[384,128]{1,0:T(8,128)S(1)}, u32[]{:S(2)}, u32[]{:S(2)}) collective-permute-start(f32[384,128]{1,0:T(8,128)S(1)} %pad_maximum_fusion.2), channel_id=1, source_target_pairs={{0,8},{4,12},{8,0},{12,4},{16,24},{20,28},{24,16},{28,20},{1,9},{5... | collective-permute-start | bytes 589832 | tf_op jit(solution)/shard_map/ppermute | solution.py:16
  67.2 8.4 %collective-permute-start.9 = (f32[384,128]{1,0:T(8,128)S(1)}, f32[384,128]{1,0:T(8,128)S(1)}, u32[]{:S(2)}, u32[]{:S(2)}) collective-permute-start(f32[384,128]{1,0:T(8,128)S(1)} %pad_maximum_fusion.3), channel_id=1, source_target_pairs={{0,16},{4,20},{8,24},{12,28},{16,0},{20,4},{24,8},{28,12},{1,17},{... | collective-permute-start | bytes 589832 | tf_op jit(solution)/shard_map/ppermute | solution.py:16
  67.7 24.0 %collective-permute-start.7 = (bf16[2,1024,128]{2,1,0:T(8,128)(2,1)S(1)}, bf16[2,1024,128]{2,1,0:T(8,128)(2,1)S(1)}, u32[]{:S(2)}, u32[]{:S(2)}) collective-permute-start(bf16[2,1024,128]{2,1,0:T(8,128)(2,1)S(1)} %copy-done.9), channel_id=1, source_target_pairs={{0,4},{4,8},{8,12},{12,16},{16,20},{20,24},{24,28},{1,5},{5,9},{9,... | collective-permute-start | bytes 1572872 | tf_op jit(solution)/shard_map/ppermute | solution.py:22
  71.4 25.3 %collective-permute-start.8 = (bf16[2,1024,128]{2,1,0:T(8,128)(2,1)S(1)}, bf16[2,1024,128]{2,1,0:T(8,128)(2,1)S(1)}, u32[]{:S(2)}, u32[]{:S(2)}) collective-permute-start(bf16[2,1024,128]{2,1,0:T(8,128)(2,1)S(1)} %copy-done.8), channel_id=1, source_target_pairs={{4,0},{8,4},{12,8},{16,12},{20,16},{24,20},{28,24},{5,1},{9,5},{13... | collective-permute-start | bytes 1572872 | tf_op jit(solution)/shard_map/ppermute | solution.py:22
  75.6 1.4 %collective-permute-start.10 = (f32[256,128]{1,0:T(8,128)S(1)}, f32[256,128]{1,0:T(8,128)S(1)}, u32[]{:S(2)}, u32[]{:S(2)}) collective-permute-start(f32[256,128]{1,0:T(8,128)S(1)} %slice_add_fusion), channel_id=1, source_target_pairs={{0,1},{1,0},{2,3},{3,2},{4,5},{5,4},{6,7},{7,6},{8,9},{9,8},{10,11... | collective-permute-start | bytes 393224 | tf_op jit(solution)/shard_map/ppermute | solution.py:16
  77.0 5.6 %collective-permute-start.11 = (f32[256,128]{1,0:T(8,128)S(1)}, f32[256,128]{1,0:T(8,128)S(1)}, u32[]{:S(2)}, u32[]{:S(2)}) collective-permute-start(f32[256,128]{1,0:T(8,128)S(1)} %add.82), channel_id=1, source_target_pairs={{0,2},{1,3},{2,0},{3,1},{4,6},{5,7},{6,4},{7,5},{8,10},{9,11},{10,... | collective-permute-start | bytes 393224 | tf_op jit(solution)/shard_map/ppermute | solution.py:16

commit v5 on v4

--- a/solution.py
+++ b/solution.py
@@ -185,6 +185,8 @@
     tail = features[:, points_here - halo_points :]
     from_prev = shifted(tail, "leaf", 1)
     from_next = shifted(head, "leaf", -1)
+    summary = jnp.einsum("rp,apc->arc", leaf_basis, features, preferred_element_type=jnp.float32)
+    summary, from_prev, from_next = lax.optimization_barrier((summary, from_prev, from_next))
     extended = jnp.concatenate([from_prev, features, from_next], axis=1)
     local_ids = jnp.clip(
         near_pairs - (position * blocks_here - HALO), 0, span_blocks - 1
@@ -192,7 +194,6 @@
 
     near_bf = near_forward(local_ids, kernel_blocks, extended)
 
-    summary = jnp.einsum("rp,apc->arc", leaf_basis, features, preferred_element_type=jnp.float32)
     expansion, _ = expand(summary, translations, False)
     exp_bf = expansion.astype(jnp.bfloat16)
     far_coeff = jnp.einsum("arc,cd->ard", exp_bf, w_far, preferred_element_type=jnp.float32).astype(

time: 100 us -> 104 us (1.040); the launches traced: 98.3 us -> 103 us
  waiting for transfers between devices: 41 us -> 47.4 us
  other arithmetic: 3.04 us -> 1.84 us
    ppermute x4, waiting for transfers between devices: 13.3 us -> 32.3 us  [shifted(): lax.ppermute(value, axis, [(source, source + steps) for source in range(l...]
    ppermute x8, waiting for transfers between devices: 27.7 us -> 15.1 us  [partner(): lax.ppermute(shard, axis, [(i, i ^ 1 << apart) for i in range(lax.axis_si...]
    dot_general x1, matrix products: 1.33 us -> 5.05 us  [on_device(): jnp.einsum('rp,ard->apd', leaf_basis, far_coeff, preferred_element_type=j...]
    ppermute x4, starting transfers between devices: 14.6 us -> 12.6 us  [shifted(): lax.ppermute(value, axis, [(source, source + steps) for source in range(l...]
    ppermute x8, starting transfers between devices: 5.86 us -> 7.45 us  [partner(): lax.ppermute(shard, axis, [(i, i ^ 1 << apart) for i in range(lax.axis_si...]
    dot_general x1, matrix products: 4.54 us -> 2.97 us  [on_device(): jnp.einsum('apc,cd->apd', near_bf, w_near, preferred_element_type=jnp.flo...]
    dot_general x1, matrix products: 1.51 us -> 0.3 us  [on_device(): jnp.einsum('rp,apc->arc', leaf_basis, features, preferred_element_type=jn...]
    concatenate x1, other arithmetic: 2.67 us -> 1.46 us  [on_device(): extended = jnp.concatenate([from_prev, features, from_next], axis=1)]
  transfers between devices with their start and end apart: 12 -> 12, of which waited for: 7 -> 9; matrix products, arithmetic and copies ran while one was open for 7% -> 8% of each run, Pallas kernels for 10% -> 16%
where the time goes in v5:
time: 104 us; the launch traced here: 103 us
  waiting for transfers between devices  47.4 us (46%)
  starting transfers between devices  20 us (19%)
  Pallas kernels  16.8 us (16%)
  matrix products  13.6 us (13%)
  local copies, waits for them, and re-layouts  2.76 us (3%)
  other arithmetic  1.84 us (2%)
    ppermute x4, waiting for transfers between devices, shifted(): lax.ppermute(value, axis, [(source, source + steps) for source in range(l...  32.3 us
    ppermute x8, waiting for transfers between devices, partner(): lax.ppermute(shard, axis, [(i, i ^ 1 << apart) for i in range(lax.axis_si...  15.1 us
    ppermute x4, starting transfers between devices, shifted(): lax.ppermute(value, axis, [(source, source + steps) for source in range(l...  12.6 us
    pallas_call x1, Pallas kernels, near_backward(): pl.pallas_call(functools.partial(near_bwd_kernel, cases, pairs, rows, ste...  9.6 us
    ppermute x8, starting transfers between devices, partner(): lax.ppermute(shard, axis, [(i, i ^ 1 << apart) for i in range(lax.axis_si...  7.45 us
    pallas_call x1, Pallas kernels, near_forward(): pl.pallas_call(functools.partial(near_fwd_kernel, cases, pairs, rows), ou...  7.19 us
    dot_general x1, matrix products, on_device(): jnp.einsum('rp,ard->apd', leaf_basis, far_coeff, preferred_element_type=j...  5.05 us
    dot_general x1, matrix products, on_device(): jnp.einsum('apc,cd->apd', near_bf, w_near, preferred_element_type=jnp.flo...  2.97 us
  transfers between devices with their start and end apart: 12, of which 9 were waited for; matrix products, arithmetic and copies ran while one was open for 8% of the time, Pallas kernels for 16%

profile of v5, /device:TPU:16, one launch (start us, length us, event | category | flops | bytes accessed | tf_op | source)
XLA Modules:
  0.0 103.4 jit_solution(11280295358290575601)
XLA Ops:
  0.7 1.4 %fusion.48 = (bf16[2,1024,128]{2,1,0:T(8,128)(2,1)S(1)}, bf16[2,1024,128]{2,1,0:T(8,128)(2,1)S(1)}) fusion(bf16[2,2048,128]{2,1,0:T(8,128)(2,1)} %param.8), kind=kLoop, calls=%fused_computation.72 | loop fusion | bytes 2097152 | tf_op jit(solution)/shard_map/slice | solution.py:184
  2.1 3.3 %collective-permute-start.1 = (bf16[2,1024,128]{2,1,0:T(8,128)(2,1)S(1)}, bf16[2,1024,128]{2,1,0:T(8,128)(2,1)S(1)}, u32[]{:S(2)}, u32[]{:S(2)}) collective-permute-start(bf16[2,1024,128]{2,1,0:T(8,128)(2,1)S(1)} %get-tuple-element.36), channel_id=1, source_target_pairs={{4,0},{8,4},{12,8},{16,12},{20,16},{24,20},{28,24},{5,1},{9,5},{13... | collective-permute-start | bytes 1572872 | tf_op jit(solution)/shard_map/ppermute | solution.py:22
  5.4 2.5 %collective-permute-start = (bf16[2,1024,128]{2,1,0:T(8,128)(2,1)S(1)}, bf16[2,1024,128]{2,1,0:T(8,128)(2,1)S(1)}, u32[]{:S(2)}, u32[]{:S(2)}) collective-permute-start(bf16[2,1024,128]{2,1,0:T(8,128)(2,1)S(1)} %get-tuple-element.37), channel_id=1, source_target_pairs={{0,4},{4,8},{8,12},{12,16},{16,20},{20,24},{24,28},{1,5},{5,9},{9,... | collective-permute-start | bytes 1572872 | tf_op jit(solution)/shard_map/ppermute | solution.py:22
  7.9 0.7 reshape.29.ids_ref
  8.6 0.3 convolution_bitcast_fusion.2
  8.9 19.9 %collective-permute-done.1 = bf16[2,1024,128]{2,1,0:T(8,128)(2,1)S(1)} collective-permute-done((bf16[2,1024,128]{2,1,0:T(8,128)(2,1)S(1)}, bf16[2,1024,128]{2,1,0:T(8,128)(2,1)S(1)}, u32[]{:S(2)}, u32[]{:S(2)}) %collective-permute-start.1) | collective-permute-done | bytes 524320 | tf_op jit(solution)/shard_map/ppermute | solution.py:22
  28.9 2.4 %collective-permute-start.2 = (f32[2,64,128]{2,1,0:T(8,128)S(1)}, f32[2,64,128]{2,1,0:T(8,128)S(1)}, u32[]{:S(2)}, u32[]{:S(2)}) collective-permute-start(f32[2,64,128]{2,1,0:T(8,128)S(1)} %convolution_bitcast_fusion.2), channel_id=1, source_target_pairs={{0,4},{4,0},{8,12},{12,8},{16,20},{20,16},{24,28},{28,24},{1,5},{5... | collective-permute-start | bytes 196616 | tf_op jit(solution)/shard_map/ppermute | solution.py:16
  31.3 1.5 %pad_maximum_fusion.ext_ref = bf16[2,4096,128]{2,1,0:T(8,128)(2,1)} fusion(bf16[2,1024,128]{2,1,0:T(8,128)(2,1)S(1)} %collective-permute-done.1, bf16[2,2048,128]{2,1,0:T(8,128)(2,1)S(1)} %copy-done.2, bf16[2,1024,128]{2,1,0:T(8,128)(2,1)S(1)} %collective-permute-done), kind=kLoop, calls=%fused_computation.18 | loop fusion | flops 6291456 | bytes 4194304 | tf_op jit(solution)/shard_map/concatenate | solution.py:190
  32.7 7.2 %shard_map.111 = bf16[2,2048,128]{2,1,0:T(8,128)(2,1)} custom-call(s32[192]{0:T(256)} %reshape.29.ids_ref, bf16[16,12,128,128]{3,2,1,0:T(8,128)(2,1)} %kb_ref.3, bf16[2,4096,128]{2,1,0:T(8,128)(2,1)} %pad_maximum_fusion.ext_ref), custom_call_target="tpu_custom_call" | custom-call | flops 1610612736 | bytes 9437184 | tf_op jit(solution)/shard_map/pallas_call | solution.py:80
  40.0 3.0 %fusion.40 = f32[2,2048,128]{2,1,0:T(8,128)} fusion(bf16[2,2048,128]{2,1,0:T(8,128)(2,1)} %shard_map.111, bf16[128,128]{1,0:T(8,128)(2,1)S(1)} %copy-done.5), kind=kOutput, calls=%fused_computation.63 | convolution fusion | flops 134217728 | bytes 3178496 | tf_op jit(solution)/shard_map/apc,cd->apd/dot_general | solution.py:204
  43.0 1.3 %collective-permute-done.3 = f32[2,64,128]{2,1,0:T(8,128)S(1)} collective-permute-done((f32[2,64,128]{2,1,0:T(8,128)S(1)}, f32[2,64,128]{2,1,0:T(8,128)S(1)}, u32[]{:S(2)}, u32[]{:S(2)}) %collective-permute-start.3) | collective-permute-done | bytes 65568 | tf_op jit(solution)/shard_map/ppermute | solution.py:16
  44.3 0.7 collective-permute-start.4
  45.2 4.3 %collective-permute-done.4 = f32[2,64,128]{2,1,0:T(8,128)S(1)} collective-permute-done((f32[2,64,128]{2,1,0:T(8,128)S(1)}, f32[2,64,128]{2,1,0:T(8,128)S(1)}, u32[]{:S(2)}, u32[]{:S(2)}) %collective-permute-start.4) | collective-permute-done | bytes 65568 | tf_op jit(solution)/shard_map/ppermute | solution.py:16
  50.0 5.0 %fusion.3 = (bf16[2,2048,128]{2,1,0:T(8,128)(2,1)S(1)}, bf16[2,2048,128]{2,1,0:T(8,128)(2,1)}) fusion(bf16[2,2048,128]{2,1,0:T(8,128)(2,1)} %param.9, f32[2,2048,128]{2,1,0:T(8,128)} %fusion.40, bf16[64,2048]{1,0:T(8,128)(2,1)S(1)} %copy-done, bf16[2,64,128]{2,1,0:T(8,128)(2,1)S(1)} %fusion.19, bf16[128,128]{1,0:T(8,128)(2,1)S(1)} %copy-done.6), kind=kOutput, calls=%fused_computation.10 | convolution fusion | flops 83902464 | bytes 5570560 | tf_op jit(solution)/shard_map/rp,ard->apd/dot_general | solution.py:202
  55.0 0.5 fusion.13
  55.5 0.3 fusion.17
  56.3 1.4 %convolution_convert_fusion.back_ref = bf16[2,2048,128]{2,1,0:T(8,128)(2,1)} fusion(bf16[2,2048,128]{2,1,0:T(8,128)(2,1)S(1)} %get-tuple-element.34, bf16[128,128]{1,0:T(8,128)(2,1)S(1)} %copy-done.5), kind=kOutput, calls=%fused_computation.7 | convolution fusion | flops 134742016 | bytes 2129920 | tf_op jit(solution)/shard_map/apc,dc->apd/dot_general | solution.py:212
  57.7 9.6 %shard_map.112 = (f32[2,2048,128]{2,1,0:T(8,128)}, bf16[2,1024,128]{2,1,0:T(8,128)(2,1)}, bf16[2,1024,128]{2,1,0:T(8,128)(2,1)}) custom-call(s32[192]{0:T(256)} %reshape.29.ids_ref, bf16[16,12,128,128]{3,2,1,0:T(8,128)(2,1)} %kb_ref.3, bf16[2,2048,128]{2,1,0:T(8,128)(2,1)} %convolution_convert_fusion.back_ref), custom_call_target="tpu_custom_call" | custom-call | flops 1610612736 | bytes 11534336 | tf_op jit(solution)/shard_map/pallas_call | solution.py:139
  67.4 1.9 %collective-permute-start.6 = (f32[384,128]{1,0:T(8,128)S(1)}, f32[384,128]{1,0:T(8,128)S(1)}, u32[]{:S(2)}, u32[]{:S(2)}) collective-permute-start(f32[384,128]{1,0:T(8,128)S(1)} %pad_maximum_fusion.2), channel_id=1, source_target_pairs={{0,8},{4,12},{8,0},{12,4},{16,24},{20,28},{24,16},{28,20},{1,9},{5... | collective-permute-start | bytes 589832 | tf_op jit(solution)/shard_map/ppermute | solution.py:16
  69.3 4.2 %collective-permute-done.6 = f32[384,128]{1,0:T(8,128)S(1)} collective-permute-done((f32[384,128]{1,0:T(8,128)S(1)}, f32[384,128]{1,0:T(8,128)S(1)}, u32[]{:S(2)}, u32[]{:S(2)}) %collective-permute-start.6) | collective-permute-done | bytes 196640 | tf_op jit(solution)/shard_map/ppermute | solution.py:16
  73.6 0.6 collective-permute-start.9
  74.5 3.8 %collective-permute-start.7 = (bf16[2,1024,128]{2,1,0:T(8,128)(2,1)S(1)}, bf16[2,1024,128]{2,1,0:T(8,128)(2,1)S(1)}, u32[]{:S(2)}, u32[]{:S(2)}) collective-permute-start(bf16[2,1024,128]{2,1,0:T(8,128)(2,1)S(1)} %copy-done.9), channel_id=1, source_target_pairs={{0,4},{4,8},{8,12},{12,16},{16,20},{20,24},{24,28},{1,5},{5,9},{9,... | collective-permute-start | bytes 1572872 | tf_op jit(solution)/shard_map/ppermute | solution.py:22
  78.2 3.0 %collective-permute-start.8 = (bf16[2,1024,128]{2,1,0:T(8,128)(2,1)S(1)}, bf16[2,1024,128]{2,1,0:T(8,128)(2,1)S(1)}, u32[]{:S(2)}, u32[]{:S(2)}) collective-permute-start(bf16[2,1024,128]{2,1,0:T(8,128)(2,1)S(1)} %copy-done.8), channel_id=1, source_target_pairs={{4,0},{8,4},{12,8},{16,12},{20,16},{24,20},{28,24},{5,1},{9,5},{13... | collective-permute-start | bytes 1572872 | tf_op jit(solution)/shard_map/ppermute | solution.py:22
  81.2 0.4 collective-permute-done.9
  81.7 0.3 convolution_add_fusion.1
  82.0 1.1 %collective-permute-done.10 = f32[256,128]{1,0:T(8,128)S(1)} collective-permute-done((f32[256,128]{1,0:T(8,128)S(1)}, f32[256,128]{1,0:T(8,128)S(1)}, u32[]{:S(2)}, u32[]{:S(2)}) %collective-permute-start.10) | collective-permute-done | bytes 131104 | tf_op jit(solution)/shard_map/ppermute | solution.py:16
  83.1 1.6 %collective-permute-start.11 = (f32[256,128]{1,0:T(8,128)S(1)}, f32[256,128]{1,0:T(8,128)S(1)}, u32[]{:S(2)}, u32[]{:S(2)}) collective-permute-start(f32[256,128]{1,0:T(8,128)S(1)} %add.82), channel_id=1, source_target_pairs={{0,2},{1,3},{2,0},{3,1},{4,6},{5,7},{6,4},{7,5},{8,10},{9,11},{10,... | collective-permute-start | bytes 393224 | tf_op jit(solution)/shard_map/ppermute | solution.py:16
  84.9 3.8 %collective-permute-done.11 = f32[256,128]{1,0:T(8,128)S(1)} collective-permute-done((f32[256,128]{1,0:T(8,128)S(1)}, f32[256,128]{1,0:T(8,128)S(1)}, u32[]{:S(2)}, u32[]{:S(2)}) %collective-permute-start.11) | collective-permute-done | bytes 131104 | tf_op jit(solution)/shard_map/ppermute | solution.py:16
  88.7 0.7 fusion.49
  89.4 8.4 %collective-permute-done.7 = bf16[2,1024,128]{2,1,0:T(8,128)(2,1)S(1)} collective-permute-done((bf16[2,1024,128]{2,1,0:T(8,128)(2,1)S(1)}, bf16[2,1024,128]{2,1,0:T(8,128)(2,1)S(1)}, u32[]{:S(2)}, u32[]{:S(2)}) %collective-permute-start.7) | collective-permute-done | bytes 524320 | tf_op jit(solution)/shard_map/ppermute | solution.py:22
  97.8 4.0 %collective-permute-done.8 = bf16[2,1024,128]{2,1,0:T(8,128)(2,1)S(1)} collective-permute-done((bf16[2,1024,128]{2,1,0:T(8,128)(2,1)S(1)}, bf16[2,1024,128]{2,1,0:T(8,128)(2,1)S(1)}, u32[]{:S(2)}, u32[]{:S(2)}) %collective-permute-start.8) | collective-permute-done | bytes 524320 | tf_op jit(solution)/shard_map/ppermute | solution.py:22
  102.0 1.5 %fusion.11 = bf16[2,2048,128]{2,1,0:T(8,128)(2,1)} fusion(f32[2,1024,128]{2,1,0:T(8,128)S(1)} %get-tuple-element.33, f32[2,1024,128]{2,1,0:T(8,128)S(1)} %get-tuple-element.32, bf16[2,64,128]{2,1,0:T(8,128)(2,1)S(1)} %fusion.18, bf16[64,2048]{1,0:T(8,128)(2,1)S(1)} %copy-done), kind=kOutput, calls=%fused_computation.20 | convolution fusion | flops 68681728 | bytes 3440640 | tf_op jit(solution)/shard_map/rp,arc->apc/dot_general | solution.py:233
  (50 shorter events, 2.2 us)
Async XLA Ops:
  0.6 8.0 %copy-start = (bf16[64,2048]{1,0:T(8,128)(2,1)S(1)}, bf16[64,2048]{1,0:T(8,128)(2,1)}, u32[]{:S(2)}) copy-start(bf16[64,2048]{1,0:T(8,128)(2,1)} %param.12) | copy-start | bytes 786436
  0.6 8.0 %copy-start.2 = (bf16[2,2048,128]{2,1,0:T(8,128)(2,1)S(1)}, bf16[2,2048,128]{2,1,0:T(8,128)(2,1)}, u32[]{:S(2)}) copy-start(bf16[2,2048,128]{2,1,0:T(8,128)(2,1)} %param.8) | copy-start | bytes 3145732
  0.7 7.3 %copy-start.7 = (s32[16,12]{1,0:T(8,128)S(1)}, s32[16,12]{1,0:T(8,128)}, u32[]{:S(2)}) copy-start(s32[16,12]{1,0:T(8,128)} %param.11) | copy-start | bytes 2308
  2.1 26.8 %collective-permute-start.1 = (bf16[2,1024,128]{2,1,0:T(8,128)(2,1)S(1)}, bf16[2,1024,128]{2,1,0:T(8,128)(2,1)S(1)}, u32[]{:S(2)}, u32[]{:S(2)}) collective-permute-start(bf16[2,1024,128]{2,1,0:T(8,128)(2,1)S(1)} %get-tuple-element.36), channel_id=1, source_target_pairs={{4,0},{8,4},{12,8},{16,12},{20,16},{24,20},{28,24},{5,1},{9,5},{13... | collective-permute-start | bytes 1572872 | tf_op jit(solution)/shard_map/ppermute | solution.py:22
  5.4 23.5 %collective-permute-start = (bf16[2,1024,128]{2,1,0:T(8,128)(2,1)S(1)}, bf16[2,1024,128]{2,1,0:T(8,128)(2,1)S(1)}, u32[]{:S(2)}, u32[]{:S(2)}) collective-permute-start(bf16[2,1024,128]{2,1,0:T(8,128)(2,1)S(1)} %get-tuple-element.37), channel_id=1, source_target_pairs={{0,4},{4,8},{8,12},{12,16},{16,20},{20,24},{24,28},{1,5},{5,9},{9,... | collective-permute-start | bytes 1572872 | tf_op jit(solution)/shard_map/ppermute | solution.py:22
  28.9 11.1 %collective-permute-start.2 = (f32[2,64,128]{2,1,0:T(8,128)S(1)}, f32[2,64,128]{2,1,0:T(8,128)S(1)}, u32[]{:S(2)}, u32[]{:S(2)}) collective-permute-start(f32[2,64,128]{2,1,0:T(8,128)S(1)} %convolution_bitcast_fusion.2), channel_id=1, source_target_pairs={{0,4},{4,0},{8,12},{12,8},{16,20},{20,16},{24,28},{28,24},{1,5},{5... | collective-permute-start | bytes 196616 | tf_op jit(solution)/shard_map/ppermute | solution.py:16
  32.7 7.3 %copy-start.5 = (bf16[128,128]{1,0:T(8,128)(2,1)S(1)}, bf16[128,128]{1,0:T(8,128)(2,1)}, u32[]{:S(2)}) copy-start(bf16[128,128]{1,0:T(8,128)(2,1)} %param.13) | copy-start | bytes 98308
  39.9 5.1 %copy-start.4 = (f32[3,64,64]{2,1,0:T(8,128)S(1)}, f32[3,64,64]{2,1,0:T(8,128)}, u32[]{:S(2)}) copy-start(f32[3,64,64]{2,1,0:T(8,128)} %param.15) | copy-start | bytes 147460
  39.9 10.0 %copy-start.6 = (bf16[128,128]{1,0:T(8,128)(2,1)S(1)}, bf16[128,128]{1,0:T(8,128)(2,1)}, u32[]{:S(2)}) copy-start(bf16[128,128]{1,0:T(8,128)(2,1)} %param.14) | copy-start | bytes 98308
  40.0 4.3 %collective-permute-start.3 = (f32[2,64,128]{2,1,0:T(8,128)S(1)}, f32[2,64,128]{2,1,0:T(8,128)S(1)}, u32[]{:S(2)}, u32[]{:S(2)}) collective-permute-start(f32[2,64,128]{2,1,0:T(8,128)S(1)} %add.65), channel_id=1, source_target_pairs={{0,8},{4,12},{8,0},{12,4},{16,24},{20,28},{24,16},{28,20},{1,9},{5... | collective-permute-start | bytes 196616 | tf_op jit(solution)/shard_map/ppermute | solution.py:16
  44.3 5.2 %collective-permute-start.4 = (f32[2,64,128]{2,1,0:T(8,128)S(1)}, f32[2,64,128]{2,1,0:T(8,128)S(1)}, u32[]{:S(2)}, u32[]{:S(2)}) collective-permute-start(f32[2,64,128]{2,1,0:T(8,128)S(1)} %add.67), channel_id=1, source_target_pairs={{0,16},{4,20},{8,24},{12,28},{16,0},{20,4},{24,8},{28,12},{1,17},{... | collective-permute-start | bytes 196616 | tf_op jit(solution)/shard_map/ppermute | solution.py:16
  49.9 5.1 %copy-start.1 = (bf16[2,2048,128]{2,1,0:T(8,128)(2,1)S(1)}, bf16[2,2048,128]{2,1,0:T(8,128)(2,1)}, u32[]{:S(2)}) copy-start(bf16[2,2048,128]{2,1,0:T(8,128)(2,1)} %shard_map.111) | copy-start | bytes 3145732
  56.2 11.2 %collective-permute-start.5 = (f32[384,128]{1,0:T(8,128)S(1)}, f32[384,128]{1,0:T(8,128)S(1)}, u32[]{:S(2)}, u32[]{:S(2)}) collective-permute-start(f32[384,128]{1,0:T(8,128)S(1)} %pad_maximum_fusion.1), channel_id=1, source_target_pairs={{0,4},{4,0},{8,12},{12,8},{16,20},{20,16},{24,28},{28,24},{1,5},{5... | collective-permute-start | bytes 589832 | tf_op jit(solution)/shard_map/ppermute | solution.py:16
  67.3 7.1 %copy-start.9 = (bf16[2,1024,128]{2,1,0:T(8,128)(2,1)S(1)}, bf16[2,1024,128]{2,1,0:T(8,128)(2,1)}, u32[]{:S(2)}) copy-start(bf16[2,1024,128]{2,1,0:T(8,128)(2,1)} %get-tuple-element.29) | copy-start | bytes 1572868
  67.3 10.9 %copy-start.8 = (bf16[2,1024,128]{2,1,0:T(8,128)(2,1)S(1)}, bf16[2,1024,128]{2,1,0:T(8,128)(2,1)}, u32[]{:S(2)}) copy-start(bf16[2,1024,128]{2,1,0:T(8,128)(2,1)} %get-tuple-element.30) | copy-start | bytes 1572868
  67.4 34.4 %copy-start.3 = (f32[2,2048,128]{2,1,0:T(8,128)S(1)}, f32[2,2048,128]{2,1,0:T(8,128)}, u32[]{:S(2)}) copy-start(f32[2,2048,128]{2,1,0:T(8,128)} %get-tuple-element.28) | copy-start | bytes 6291460
  67.4 6.1 %collective-permute-start.6 = (f32[384,128]{1,0:T(8,128)S(1)}, f32[384,128]{1,0:T(8,128)S(1)}, u32[]{:S(2)}, u32[]{:S(2)}) collective-permute-start(f32[384,128]{1,0:T(8,128)S(1)} %pad_maximum_fusion.2), channel_id=1, source_target_pairs={{0,8},{4,12},{8,0},{12,4},{16,24},{20,28},{24,16},{28,20},{1,9},{5... | collective-permute-start | bytes 589832 | tf_op jit(solution)/shard_map/ppermute | solution.py:16
  73.6 8.1 %collective-permute-start.9 = (f32[384,128]{1,0:T(8,128)S(1)}, f32[384,128]{1,0:T(8,128)S(1)}, u32[]{:S(2)}, u32[]{:S(2)}) collective-permute-start(f32[384,128]{1,0:T(8,128)S(1)} %pad_maximum_fusion.3), channel_id=1, source_target_pairs={{0,16},{4,20},{8,24},{12,28},{16,0},{20,4},{24,8},{28,12},{1,17},{... | collective-permute-start | bytes 589832 | tf_op jit(solution)/shard_map/ppermute | solution.py:16
  74.5 23.3 %collective-permute-start.7 = (bf16[2,1024,128]{2,1,0:T(8,128)(2,1)S(1)}, bf16[2,1024,128]{2,1,0:T(8,128)(2,1)S(1)}, u32[]{:S(2)}, u32[]{:S(2)}) collective-permute-start(bf16[2,1024,128]{2,1,0:T(8,128)(2,1)S(1)} %copy-done.9), channel_id=1, source_target_pairs={{0,4},{4,8},{8,12},{12,16},{16,20},{20,24},{24,28},{1,5},{5,9},{9,... | collective-permute-start | bytes 1572872 | tf_op jit(solution)/shard_map/ppermute | solution.py:22
  78.2 23.6 %collective-permute-start.8 = (bf16[2,1024,128]{2,1,0:T(8,128)(2,1)S(1)}, bf16[2,1024,128]{2,1,0:T(8,128)(2,1)S(1)}, u32[]{:S(2)}, u32[]{:S(2)}) collective-permute-start(bf16[2,1024,128]{2,1,0:T(8,128)(2,1)S(1)} %copy-done.8), channel_id=1, source_target_pairs={{4,0},{8,4},{12,8},{16,12},{20,16},{24,20},{28,24},{5,1},{9,5},{13... | collective-permute-start | bytes 1572872 | tf_op jit(solution)/shard_map/ppermute | solution.py:22
  81.7 1.4 %collective-permute-start.10 = (f32[256,128]{1,0:T(8,128)S(1)}, f32[256,128]{1,0:T(8,128)S(1)}, u32[]{:S(2)}, u32[]{:S(2)}) collective-permute-start(f32[256,128]{1,0:T(8,128)S(1)} %slice_add_fusion), channel_id=1, source_target_pairs={{0,1},{1,0},{2,3},{3,2},{4,5},{5,4},{6,7},{7,6},{8,9},{9,8},{10,11... | collective-permute-start | bytes 393224 | tf_op jit(solution)/shard_map/ppermute | solution.py:16
  83.1 5.6 %collective-permute-start.11 = (f32[256,128]{1,0:T(8,128)S(1)}, f32[256,128]{1,0:T(8,128)S(1)}, u32[]{:S(2)}, u32[]{:S(2)}) collective-permute-start(f32[256,128]{1,0:T(8,128)S(1)} %add.82), channel_id=1, source_target_pairs={{0,2},{1,3},{2,0},{3,1},{4,6},{5,7},{6,4},{7,5},{8,10},{9,11},{10,... | collective-permute-start | bytes 393224 | tf_op jit(solution)/shard_map/ppermute | solution.py:16

commit v6 on v4

--- a/solution.py
+++ b/solution.py
@@ -41,7 +41,7 @@
                 [node_value.reshape(rows, own_value.shape[2]), rider], axis=0
             )
             got = partner(packed, "leaf", height)
-            if cover is not None and height < 2:
+            if cover is not None and height < 1:
                 got, cover = lax.optimization_barrier((got, cover))
             sibling = got[:rows].reshape(own_value.shape)
             rider = rider + got[rows:]

time: 100 us -> 101 us (1.010)
  the two profiles are of different devices: /device:TPU:16 before, /device:TPU:0 now
where the time goes in v6:
time: 101 us; the launch traced here: 100 us
  waiting for transfers between devices  36.7 us (36%)
  starting transfers between devices  26.8 us (27%)
  Pallas kernels  16.8 us (17%)
  matrix products  12.7 us (13%)
  local copies, waits for them, and re-layouts  3.32 us (3%)
  other arithmetic  3.05 us (3%)
    ppermute x8, waiting for transfers between devices, partner(): lax.ppermute(shard, axis, [(i, i ^ 1 << apart) for i in range(lax.axis_si...  36.6 us
    ppermute x8, starting transfers between devices, partner(): lax.ppermute(shard, axis, [(i, i ^ 1 << apart) for i in range(lax.axis_si...  17.6 us
    pallas_call x1, Pallas kernels, near_backward(): pl.pallas_call(functools.partial(near_bwd_kernel, cases, pairs, rows, ste...  9.61 us
    ppermute x4, starting transfers between devices, shifted(): lax.ppermute(value, axis, [(source, source + steps) for source in range(l...  9.23 us
    pallas_call x1, Pallas kernels, near_forward(): pl.pallas_call(functools.partial(near_fwd_kernel, cases, pairs, rows), ou...  7.2 us
    dot_general x1, matrix products, on_device(): jnp.einsum('apc,cd->apd', near_bf, w_near, preferred_element_type=jnp.flo...  4.54 us
    concatenate x1, other arithmetic, on_device(): extended = jnp.concatenate([from_prev, features, from_next], axis=1)  2.68 us
  transfers between devices with their start and end apart: 12, of which 5 were waited for; matrix products, arithmetic and copies ran while one was open for 8% of the time, Pallas kernels for 10%

profile of v6, /device:TPU:0, one launch (start us, length us, event | category | flops | bytes accessed | tf_op | source)
XLA Modules:
  0.0 100.3 jit_solution(13924162528053189543)
XLA Ops:
  0.7 0.9 copy-done
  1.6 1.5 %convolution_bitcast_fusion.2 = f32[2,64,128]{2,1,0:T(8,128)S(1)} fusion(bf16[2,2048,128]{2,1,0:T(8,128)(2,1)} %param.8, bf16[64,2048]{1,0:T(8,128)(2,1)S(1)} %copy-done), kind=kOutput, calls=%fused_computation.22 | convolution fusion | flops 67108864 | bytes 1376256 | tf_op jit(solution)/shard_map/rp,apc->arc/dot_general | solution.py:195
  3.1 3.0 %collective-permute-start.2 = (f32[2,64,128]{2,1,0:T(8,128)S(1)}, f32[2,64,128]{2,1,0:T(8,128)S(1)}, u32[]{:S(2)}, u32[]{:S(2)}) collective-permute-start(f32[2,64,128]{2,1,0:T(8,128)S(1)} %convolution_bitcast_fusion.2), channel_id=1, source_target_pairs={{0,4},{4,0},{8,12},{12,8},{16,20},{20,16},{24,28},{28,24},{1,5},{5... | collective-permute-start | bytes 196616 | tf_op jit(solution)/shard_map/ppermute | solution.py:16
  6.1 1.0 %fusion.46 = (bf16[2,1024,128]{2,1,0:T(8,128)(2,1)}, bf16[2,1024,128]{2,1,0:T(8,128)(2,1)}) fusion(bf16[2,2048,128]{2,1,0:T(8,128)(2,1)S(1)} %copy-done.1), kind=kLoop, calls=%fused_computation.71 | loop fusion | bytes 2097152 | tf_op jit(solution)/shard_map/slice | solution.py:185
  7.2 2.7 %collective-permute-start = (bf16[2,1024,128]{2,1,0:T(8,128)(2,1)}, bf16[2,1024,128]{2,1,0:T(8,128)(2,1)}, u32[]{:S(2)}, u32[]{:S(2)}) collective-permute-start(bf16[2,1024,128]{2,1,0:T(8,128)(2,1)} %get-tuple-element.22), channel_id=1, source_target_pairs={{0,4},{4,8},{8,12},{12,16},{16,20},{20,24},{24,28},{1,5},{5,9},{9,... | collective-permute-start | bytes 1572872 | tf_op jit(solution)/shard_map/ppermute | solution.py:22
  9.9 1.3 %collective-permute-start.1 = (bf16[2,1024,128]{2,1,0:T(8,128)(2,1)}, bf16[2,1024,128]{2,1,0:T(8,128)(2,1)}, u32[]{:S(2)}, u32[]{:S(2)}) collective-permute-start(bf16[2,1024,128]{2,1,0:T(8,128)(2,1)} %get-tuple-element.23), channel_id=1, source_target_pairs={{4,0},{8,4},{12,8},{16,12},{20,16},{24,20},{28,24},{5,1},{9,5},{13... | collective-permute-start | bytes 1572872 | tf_op jit(solution)/shard_map/ppermute | solution.py:22
  11.2 4.4 %collective-permute-start.3 = (f32[2,64,128]{2,1,0:T(8,128)S(1)}, f32[2,64,128]{2,1,0:T(8,128)S(1)}, u32[]{:S(2)}, u32[]{:S(2)}) collective-permute-start(f32[2,64,128]{2,1,0:T(8,128)S(1)} %add.65), channel_id=1, source_target_pairs={{0,8},{4,12},{8,0},{12,4},{16,24},{20,28},{24,16},{28,20},{1,9},{5... | collective-permute-start | bytes 196616 | tf_op jit(solution)/shard_map/ppermute | solution.py:16
  15.6 0.7 reshape.29.ids_ref
  16.3 12.0 %collective-permute-done.3 = f32[2,64,128]{2,1,0:T(8,128)S(1)} collective-permute-done((f32[2,64,128]{2,1,0:T(8,128)S(1)}, f32[2,64,128]{2,1,0:T(8,128)S(1)}, u32[]{:S(2)}, u32[]{:S(2)}) %collective-permute-start.3) | collective-permute-done | bytes 65568 | tf_op jit(solution)/shard_map/ppermute | solution.py:16
  28.2 3.4 %collective-permute-start.4 = (f32[2,64,128]{2,1,0:T(8,128)S(1)}, f32[2,64,128]{2,1,0:T(8,128)S(1)}, u32[]{:S(2)}, u32[]{:S(2)}) collective-permute-start(f32[2,64,128]{2,1,0:T(8,128)S(1)} %add.67), channel_id=1, source_target_pairs={{0,16},{4,20},{8,24},{12,28},{16,0},{20,4},{24,8},{28,12},{1,17},{... | collective-permute-start | bytes 196616 | tf_op jit(solution)/shard_map/ppermute | solution.py:16
  31.8 2.0 %collective-permute-done.4 = f32[2,64,128]{2,1,0:T(8,128)S(1)} collective-permute-done((f32[2,64,128]{2,1,0:T(8,128)S(1)}, f32[2,64,128]{2,1,0:T(8,128)S(1)}, u32[]{:S(2)}, u32[]{:S(2)}) %collective-permute-start.4) | collective-permute-done | bytes 65568 | tf_op jit(solution)/shard_map/ppermute | solution.py:16
  34.3 1.3 %convolution_bitcast_fusion.1 = f32[2,2048,128]{2,1,0:T(8,128)S(1)} fusion(bf16[2,64,128]{2,1,0:T(8,128)(2,1)S(1)} %fusion.18, bf16[64,2048]{1,0:T(8,128)(2,1)S(1)} %copy-done, bf16[128,128]{1,0:T(8,128)(2,1)} %param.14), kind=kOutput, calls=%fused_computation.3 | convolution fusion | flops 71319552 | bytes 2424832 | tf_op jit(solution)/shard_map/rp,ard->apd/dot_general | solution.py:201
  35.6 2.7 %pad_maximum_fusion.ext_ref = bf16[2,4096,128]{2,1,0:T(8,128)(2,1)} fusion(bf16[2,1024,128]{2,1,0:T(8,128)(2,1)} %collective-permute-done.1, bf16[2,2048,128]{2,1,0:T(8,128)(2,1)S(1)} %copy-done.1, bf16[2,1024,128]{2,1,0:T(8,128)(2,1)} %collective-permute-done), kind=kLoop, calls=%fused_computation.18 | loop fusion | flops 6291456 | bytes 4194304 | tf_op jit(solution)/shard_map/concatenate | solution.py:188
  38.3 7.2 %shard_map.111 = bf16[2,2048,128]{2,1,0:T(8,128)(2,1)} custom-call(s32[192]{0:T(256)} %reshape.29.ids_ref, bf16[16,12,128,128]{3,2,1,0:T(8,128)(2,1)} %kb_ref.3, bf16[2,4096,128]{2,1,0:T(8,128)(2,1)} %pad_maximum_fusion.ext_ref), custom_call_target="tpu_custom_call" | custom-call | flops 1610612736 | bytes 9437184 | tf_op jit(solution)/shard_map/pallas_call | solution.py:80
  45.5 4.5 %fusion.2 = (bf16[2,2048,128]{2,1,0:T(8,128)(2,1)S(1)}, bf16[2,2048,128]{2,1,0:T(8,128)(2,1)}) fusion(bf16[2,2048,128]{2,1,0:T(8,128)(2,1)} %param.9, f32[2,2048,128]{2,1,0:T(8,128)S(1)} %convolution_bitcast_fusion.1, bf16[2,2048,128]{2,1,0:T(8,128)(2,1)} %shard_map.111, bf16[128,128]{1,0:T(8,128)(2,1)S(1)} %copy-done.6), kind=kOutput, calls=%fused_computation.10 | convolution fusion | flops 146800640 | bytes 6324224 | tf_op jit(solution)/shard_map/apc,cd->apd/dot_general | solution.py:203
  50.0 0.5 fusion.12
  50.5 0.3 fusion.16
  51.3 1.4 %convolution_convert_fusion.back_ref = bf16[2,2048,128]{2,1,0:T(8,128)(2,1)} fusion(bf16[2,2048,128]{2,1,0:T(8,128)(2,1)S(1)} %get-tuple-element.20, bf16[128,128]{1,0:T(8,128)(2,1)S(1)} %copy-done.6), kind=kOutput, calls=%fused_computation.7 | convolution fusion | flops 134742016 | bytes 2129920 | tf_op jit(solution)/shard_map/apc,dc->apd/dot_general | solution.py:211
  52.7 9.6 %shard_map.112 = (f32[2,2048,128]{2,1,0:T(8,128)}, bf16[2,1024,128]{2,1,0:T(8,128)(2,1)}, bf16[2,1024,128]{2,1,0:T(8,128)(2,1)}) custom-call(s32[192]{0:T(256)} %reshape.29.ids_ref, bf16[16,12,128,128]{3,2,1,0:T(8,128)(2,1)} %kb_ref.3, bf16[2,2048,128]{2,1,0:T(8,128)(2,1)} %convolution_convert_fusion.back_ref), custom_call_target="tpu_custom_call" | custom-call | flops 1610612736 | bytes 11534336 | tf_op jit(solution)/shard_map/pallas_call | solution.py:139
  62.4 0.9 collective-permute-start.8
  63.3 3.9 %collective-permute-start.6 = (bf16[2,1024,128]{2,1,0:T(8,128)(2,1)}, bf16[2,1024,128]{2,1,0:T(8,128)(2,1)S(1)}, u32[]{:S(2)}, u32[]{:S(2)}) collective-permute-start(bf16[2,1024,128]{2,1,0:T(8,128)(2,1)} %get-tuple-element.15), channel_id=1, source_target_pairs={{0,4},{4,8},{8,12},{12,16},{16,20},{20,24},{24,28},{1,5},{5,9},{9,... | collective-permute-start | bytes 1572872 | tf_op jit(solution)/shard_map/ppermute | solution.py:22
  67.2 1.3 %collective-permute-start.7 = (bf16[2,1024,128]{2,1,0:T(8,128)(2,1)}, bf16[2,1024,128]{2,1,0:T(8,128)(2,1)S(1)}, u32[]{:S(2)}, u32[]{:S(2)}) collective-permute-start(bf16[2,1024,128]{2,1,0:T(8,128)(2,1)} %get-tuple-element.16), channel_id=1, source_target_pairs={{4,0},{8,4},{12,8},{16,12},{20,16},{24,20},{28,24},{5,1},{9,5},{13... | collective-permute-start | bytes 1572872 | tf_op jit(solution)/shard_map/ppermute | solution.py:22
  68.5 0.3 fusion.35
  68.9 4.2 %collective-permute-start.9 = (f32[384,128]{1,0:T(8,128)S(1)}, f32[384,128]{1,0:T(8,128)S(1)}, u32[]{:S(2)}, u32[]{:S(2)}) collective-permute-start(f32[384,128]{1,0:T(8,128)S(1)} %pad_maximum_fusion.3), channel_id=1, source_target_pairs={{0,16},{4,20},{8,24},{12,28},{16,0},{20,4},{24,8},{28,12},{1,17},{... | collective-permute-start | bytes 589832 | tf_op jit(solution)/shard_map/ppermute | solution.py:16
  73.1 0.3 convolution_add_fusion.2
  73.3 19.2 %collective-permute-done.9 = f32[384,128]{1,0:T(8,128)S(1)} collective-permute-done((f32[384,128]{1,0:T(8,128)S(1)}, f32[384,128]{1,0:T(8,128)S(1)}, u32[]{:S(2)}, u32[]{:S(2)}) %collective-permute-start.9) | collective-permute-done | bytes 196640 | tf_op jit(solution)/shard_map/ppermute | solution.py:16
  92.6 0.3 fusion.17
  92.9 1.1 %collective-permute-done.10 = f32[256,128]{1,0:T(8,128)S(1)} collective-permute-done((f32[256,128]{1,0:T(8,128)S(1)}, f32[256,128]{1,0:T(8,128)S(1)}, u32[]{:S(2)}, u32[]{:S(2)}) %collective-permute-start.10) | collective-permute-done | bytes 131104 | tf_op jit(solution)/shard_map/ppermute | solution.py:16
  94.0 1.6 %collective-permute-start.11 = (f32[256,128]{1,0:T(8,128)S(1)}, f32[256,128]{1,0:T(8,128)S(1)}, u32[]{:S(2)}, u32[]{:S(2)}) collective-permute-start(f32[256,128]{1,0:T(8,128)S(1)} %add.82), channel_id=1, source_target_pairs={{0,2},{1,3},{2,0},{3,1},{4,6},{5,7},{6,4},{7,5},{8,10},{9,11},{10,... | collective-permute-start | bytes 393224 | tf_op jit(solution)/shard_map/ppermute | solution.py:16
  95.8 1.5 %fusion.10 = bf16[2,2048,128]{2,1,0:T(8,128)(2,1)} fusion(f32[2,1024,128]{2,1,0:T(8,128)S(1)} %get-tuple-element.19, f32[2,1024,128]{2,1,0:T(8,128)S(1)} %get-tuple-element.18, bf16[2,64,128]{2,1,0:T(8,128)(2,1)S(1)} %fusion.17, bf16[64,2048]{1,0:T(8,128)(2,1)S(1)} %copy-done), kind=kOutput, calls=%fused_computation.20 | convolution fusion | flops 68681728 | bytes 3440640 | tf_op jit(solution)/shard_map/rp,arc->apc/dot_general | solution.py:232
  97.2 2.4 %collective-permute-done.11 = f32[256,128]{1,0:T(8,128)S(1)} collective-permute-done((f32[256,128]{1,0:T(8,128)S(1)}, f32[256,128]{1,0:T(8,128)S(1)}, u32[]{:S(2)}, u32[]{:S(2)}) %collective-permute-start.11) | collective-permute-done | bytes 131104 | tf_op jit(solution)/shard_map/ppermute | solution.py:16
  99.6 0.7 fusion.47
  (46 shorter events, 1.5 us)
Async XLA Ops:
  0.6 1.0 copy-start
  0.6 5.5 %copy-start.1 = (bf16[2,2048,128]{2,1,0:T(8,128)(2,1)S(1)}, bf16[2,2048,128]{2,1,0:T(8,128)(2,1)}, u32[]{:S(2)}) copy-start(bf16[2,2048,128]{2,1,0:T(8,128)(2,1)} %param.8) | copy-start | bytes 3145732
  0.7 15.0 %copy-start.7 = (s32[16,12]{1,0:T(8,128)S(1)}, s32[16,12]{1,0:T(8,128)}, u32[]{:S(2)}) copy-start(s32[16,12]{1,0:T(8,128)} %param.11) | copy-start | bytes 2308
  0.7 30.9 %copy-start.4 = (f32[3,64,64]{2,1,0:T(8,128)S(1)}, f32[3,64,64]{2,1,0:T(8,128)}, u32[]{:S(2)}) copy-start(f32[3,64,64]{2,1,0:T(8,128)} %param.15) | copy-start | bytes 147460
  3.1 8.1 %collective-permute-start.2 = (f32[2,64,128]{2,1,0:T(8,128)S(1)}, f32[2,64,128]{2,1,0:T(8,128)S(1)}, u32[]{:S(2)}, u32[]{:S(2)}) collective-permute-start(f32[2,64,128]{2,1,0:T(8,128)S(1)} %convolution_bitcast_fusion.2), channel_id=1, source_target_pairs={{0,4},{4,0},{8,12},{12,8},{16,20},{20,16},{24,28},{28,24},{1,5},{5... | collective-permute-start | bytes 196616 | tf_op jit(solution)/shard_map/ppermute | solution.py:16
  7.2 28.4 %collective-permute-start = (bf16[2,1024,128]{2,1,0:T(8,128)(2,1)}, bf16[2,1024,128]{2,1,0:T(8,128)(2,1)}, u32[]{:S(2)}, u32[]{:S(2)}) collective-permute-start(bf16[2,1024,128]{2,1,0:T(8,128)(2,1)} %get-tuple-element.22), channel_id=1, source_target_pairs={{0,4},{4,8},{8,12},{12,16},{16,20},{20,24},{24,28},{1,5},{5,9},{9,... | collective-permute-start | bytes 1572872 | tf_op jit(solution)/shard_map/ppermute | solution.py:22
  9.9 25.7 %collective-permute-start.1 = (bf16[2,1024,128]{2,1,0:T(8,128)(2,1)}, bf16[2,1024,128]{2,1,0:T(8,128)(2,1)}, u32[]{:S(2)}, u32[]{:S(2)}) collective-permute-start(bf16[2,1024,128]{2,1,0:T(8,128)(2,1)} %get-tuple-element.23), channel_id=1, source_target_pairs={{4,0},{8,4},{12,8},{16,12},{20,16},{24,20},{28,24},{5,1},{9,5},{13... | collective-permute-start | bytes 1572872 | tf_op jit(solution)/shard_map/ppermute | solution.py:22
  11.2 17.0 %collective-permute-start.3 = (f32[2,64,128]{2,1,0:T(8,128)S(1)}, f32[2,64,128]{2,1,0:T(8,128)S(1)}, u32[]{:S(2)}, u32[]{:S(2)}) collective-permute-start(f32[2,64,128]{2,1,0:T(8,128)S(1)} %add.65), channel_id=1, source_target_pairs={{0,8},{4,12},{8,0},{12,4},{16,24},{20,28},{24,16},{28,20},{1,9},{5... | collective-permute-start | bytes 196616 | tf_op jit(solution)/shard_map/ppermute | solution.py:16
  28.2 5.6 %collective-permute-start.4 = (f32[2,64,128]{2,1,0:T(8,128)S(1)}, f32[2,64,128]{2,1,0:T(8,128)S(1)}, u32[]{:S(2)}, u32[]{:S(2)}) collective-permute-start(f32[2,64,128]{2,1,0:T(8,128)S(1)} %add.67), channel_id=1, source_target_pairs={{0,16},{4,20},{8,24},{12,28},{16,0},{20,4},{24,8},{28,12},{1,17},{... | collective-permute-start | bytes 196616 | tf_op jit(solution)/shard_map/ppermute | solution.py:16
  38.3 7.2 %copy-start.6 = (bf16[128,128]{1,0:T(8,128)(2,1)S(1)}, bf16[128,128]{1,0:T(8,128)(2,1)}, u32[]{:S(2)}) copy-start(bf16[128,128]{1,0:T(8,128)(2,1)} %param.13) | copy-start | bytes 98308
  45.5 4.5 %copy-start.2 = (bf16[2,2048,128]{2,1,0:T(8,128)(2,1)S(1)}, bf16[2,2048,128]{2,1,0:T(8,128)(2,1)}, u32[]{:S(2)}) copy-start(bf16[2,2048,128]{2,1,0:T(8,128)(2,1)} %shard_map.111) | copy-start | bytes 3145732
  50.0 1.0 copy-start.5
  51.2 11.1 %collective-permute-start.5 = (f32[384,128]{1,0:T(8,128)S(1)}, f32[384,128]{1,0:T(8,128)S(1)}, u32[]{:S(2)}, u32[]{:S(2)}) collective-permute-start(f32[384,128]{1,0:T(8,128)S(1)} %pad_maximum_fusion.1), channel_id=1, source_target_pairs={{0,4},{4,0},{8,12},{12,8},{16,20},{20,16},{24,28},{28,24},{1,5},{5... | collective-permute-start | bytes 589832 | tf_op jit(solution)/shard_map/ppermute | solution.py:16
  62.3 33.3 %copy-start.3 = (f32[2,2048,128]{2,1,0:T(8,128)S(1)}, f32[2,2048,128]{2,1,0:T(8,128)}, u32[]{:S(2)}) copy-start(f32[2,2048,128]{2,1,0:T(8,128)} %get-tuple-element.14) | copy-start | bytes 6291460
  62.4 6.4 %collective-permute-start.8 = (f32[384,128]{1,0:T(8,128)S(1)}, f32[384,128]{1,0:T(8,128)S(1)}, u32[]{:S(2)}, u32[]{:S(2)}) collective-permute-start(f32[384,128]{1,0:T(8,128)S(1)} %pad_maximum_fusion.2), channel_id=1, source_target_pairs={{0,8},{4,12},{8,0},{12,4},{16,24},{20,28},{24,16},{28,20},{1,9},{5... | collective-permute-start | bytes 589832 | tf_op jit(solution)/shard_map/ppermute | solution.py:16
  63.3 32.3 %collective-permute-start.6 = (bf16[2,1024,128]{2,1,0:T(8,128)(2,1)}, bf16[2,1024,128]{2,1,0:T(8,128)(2,1)S(1)}, u32[]{:S(2)}, u32[]{:S(2)}) collective-permute-start(bf16[2,1024,128]{2,1,0:T(8,128)(2,1)} %get-tuple-element.15), channel_id=1, source_target_pairs={{0,4},{4,8},{8,12},{12,16},{16,20},{20,24},{24,28},{1,5},{5,9},{9,... | collective-permute-start | bytes 1572872 | tf_op jit(solution)/shard_map/ppermute | solution.py:22
  67.2 28.3 %collective-permute-start.7 = (bf16[2,1024,128]{2,1,0:T(8,128)(2,1)}, bf16[2,1024,128]{2,1,0:T(8,128)(2,1)S(1)}, u32[]{:S(2)}, u32[]{:S(2)}) collective-permute-start(bf16[2,1024,128]{2,1,0:T(8,128)(2,1)} %get-tuple-element.16), channel_id=1, source_target_pairs={{4,0},{8,4},{12,8},{16,12},{20,16},{24,20},{28,24},{5,1},{9,5},{13... | collective-permute-start | bytes 1572872 | tf_op jit(solution)/shard_map/ppermute | solution.py:22
  68.9 23.7 %collective-permute-start.9 = (f32[384,128]{1,0:T(8,128)S(1)}, f32[384,128]{1,0:T(8,128)S(1)}, u32[]{:S(2)}, u32[]{:S(2)}) collective-permute-start(f32[384,128]{1,0:T(8,128)S(1)} %pad_maximum_fusion.3), channel_id=1, source_target_pairs={{0,16},{4,20},{8,24},{12,28},{16,0},{20,4},{24,8},{28,12},{1,17},{... | collective-permute-start | bytes 589832 | tf_op jit(solution)/shard_map/ppermute | solution.py:16
  92.6 1.4 %collective-permute-start.10 = (f32[256,128]{1,0:T(8,128)S(1)}, f32[256,128]{1,0:T(8,128)S(1)}, u32[]{:S(2)}, u32[]{:S(2)}) collective-permute-start(f32[256,128]{1,0:T(8,128)S(1)} %slice_add_fusion), channel_id=1, source_target_pairs={{0,1},{1,0},{2,3},{3,2},{4,5},{5,4},{6,7},{7,6},{8,9},{9,8},{10,11... | collective-permute-start | bytes 393224 | tf_op jit(solution)/shard_map/ppermute | solution.py:16
  94.0 5.6 %collective-permute-start.11 = (f32[256,128]{1,0:T(8,128)S(1)}, f32[256,128]{1,0:T(8,128)S(1)}, u32[]{:S(2)}, u32[]{:S(2)}) collective-permute-start(f32[256,128]{1,0:T(8,128)S(1)} %add.82), channel_id=1, source_target_pairs={{0,2},{1,3},{2,0},{3,1},{4,6},{5,7},{6,4},{7,5},{8,10},{9,11},{10,... | collective-permute-start | bytes 393224 | tf_op jit(solution)/shard_map/ppermute | solution.py:16

commit v7 on v4

--- a/solution.py
+++ b/solution.py
@@ -98,6 +98,105 @@
     )(ids, kernel_blocks, extended)
 
 
+def near_local_kernel(pairs, halo, own, ids_ref, kb_ref, feat_ref, out_ref, acc_ref):
+    g = pl.program_id(0)
+    tbs = kb_ref.shape[0]
+    for tb in range(tbs):
+        t = g * tbs + tb
+        acc_ref[...] = jnp.zeros(acc_ref.shape, acc_ref.dtype)
+        for k in range(pairs):
+            idx = ids_ref[t * pairs + k] - halo
+
+            @pl.when((idx >= 0) & (idx < own))
+            def _():
+                blk = feat_ref[jnp.clip(idx, 0, own - 1)]
+                acc_ref[...] += jnp.dot(kb_ref[tb, k], blk, preferred_element_type=jnp.float32)
+
+        out_ref[tb] = acc_ref[...]
+
+
+def near_halo_kernel(pairs, halo, own, cases, ids_ref, kb_ref, halo_ref, part_ref, out_ref, acc_ref):
+    g = pl.program_id(0)
+    tbs = kb_ref.shape[0]
+    rows = kb_ref.shape[2]
+    for tb in range(tbs):
+        t = g * tbs + tb
+        acc_ref[...] = part_ref[tb]
+        for k in range(pairs):
+            idx = ids_ref[t * pairs + k]
+            inside = (idx >= halo) & (idx < halo + own)
+            hidx = jnp.where(idx < halo, idx, idx - own)
+
+            @pl.when(jnp.logical_not(inside))
+            def _():
+                blk = halo_ref[jnp.clip(hidx, 0, 2 * halo - 1)]
+                acc_ref[...] += jnp.dot(kb_ref[tb, k], blk, preferred_element_type=jnp.float32)
+
+        width = acc_ref.shape[1] // cases
+        for c in range(cases):
+            out_ref[c, pl.ds(tb * rows, rows), :] = acc_ref[:, c * width : (c + 1) * width].astype(
+                out_ref.dtype
+            )
+
+
+def case_minor(x, rows):
+    cases, points, width = x.shape
+    return x.reshape(cases, points // rows, rows, width).transpose(1, 2, 0, 3).reshape(
+        points // rows, rows, cases * width
+    )
+
+
+def near_forward_split(ids, kernel_blocks, features, from_prev, from_next, halo):
+    cases, points_here, width = features.shape
+    blocks_here, pairs, rows, _ = kernel_blocks.shape
+    steps = blocks_here // TB
+    lanes = cases * width
+    feat = case_minor(features, rows)
+    flops = 2 * blocks_here * pairs * rows * rows * lanes
+    partial = pl.pallas_call(
+        functools.partial(near_local_kernel, pairs, halo, blocks_here),
+        out_shape=jax.ShapeDtypeStruct((blocks_here, rows, lanes), jnp.float32),
+        grid_spec=pltpu.PrefetchScalarGridSpec(
+            num_scalar_prefetch=1,
+            grid=(steps,),
+            in_specs=[
+                pl.BlockSpec((TB, pairs, rows, rows), lambda g, ids: (g, 0, 0, 0)),
+                pl.BlockSpec((blocks_here, rows, lanes), lambda g, ids: (0, 0, 0)),
+            ],
+            out_specs=pl.BlockSpec((TB, rows, lanes), lambda g, ids: (g, 0, 0)),
+            scratch_shapes=[pltpu.VMEM((rows, lanes), jnp.float32)],
+        ),
+        compiler_params=pltpu.CompilerParams(dimension_semantics=("arbitrary",)),
+        cost_estimate=pl.CostEstimate(
+            flops=flops // 2,
+            transcendentals=0,
+            bytes_accessed=kernel_blocks.size * 2 + features.size * 2 + blocks_here * rows * lanes * 4,
+        ),
+    )(ids, kernel_blocks, feat)
+    halo_blocks = case_minor(jnp.concatenate([from_prev, from_next], axis=1), rows)
+    return pl.pallas_call(
+        functools.partial(near_halo_kernel, pairs, halo, blocks_here, cases),
+        out_shape=jax.ShapeDtypeStruct((cases, points_here, width), jnp.bfloat16),
+        grid_spec=pltpu.PrefetchScalarGridSpec(
+            num_scalar_prefetch=1,
+            grid=(steps,),
+            in_specs=[
+                pl.BlockSpec((TB, pairs, rows, rows), lambda g, ids: (g, 0, 0, 0)),
+                pl.BlockSpec((2 * halo, rows, lanes), lambda g, ids: (0, 0, 0)),
+                pl.BlockSpec((TB, rows, lanes), lambda g, ids: (g, 0, 0)),
+            ],
+            out_specs=pl.BlockSpec((cases, TB * rows, width), lambda g, ids: (0, g, 0)),
+            scratch_shapes=[pltpu.VMEM((rows, lanes), jnp.float32)],
+        ),
+        compiler_params=pltpu.CompilerParams(dimension_semantics=("arbitrary",)),
+        cost_estimate=pl.CostEstimate(
+            flops=flops // 2,
+            transcendentals=0,
+            bytes_accessed=kernel_blocks.size * 2 + blocks_here * rows * lanes * 6,
+        ),
+    )(ids, kernel_blocks, halo_blocks, partial)
+
+
 def near_bwd_kernel(cases, pairs, rows, steps, ids_ref, kb_ref, back_ref, mid_ref, lo_ref, hi_ref, acc_ref):
     g = pl.program_id(0)
 
@@ -185,12 +284,12 @@
     tail = features[:, points_here - halo_points :]
     from_prev = shifted(tail, "leaf", 1)
     from_next = shifted(head, "leaf", -1)
-    extended = jnp.concatenate([from_prev, features, from_next], axis=1)
+
     local_ids = jnp.clip(
         near_pairs - (position * blocks_here - HALO), 0, span_blocks - 1
     ).reshape(-1).astype(jnp.int32)
 
-    near_bf = near_forward(local_ids, kernel_blocks, extended)
+    near_bf = near_forward_split(local_ids, kernel_blocks, features, from_prev, from_next, HALO)
 
     summary = jnp.einsum("rp,apc->arc", leaf_basis, features, preferred_element_type=jnp.float32)
     expansion, _ = expand(summary, translations, False)

time: 100 us -> 125 us (1.25)
  Pallas kernels: 16.8 us -> 48.5 us
  waiting for transfers between devices: 41 us -> 23 us
  starting transfers between devices: 20.4 us -> 26.1 us
  local copies, waits for them, and re-layouts: 3.33 us -> 8.94 us
  matrix products: 12.7 us -> 14.9 us
  other arithmetic: 3.04 us -> 1.49 us
    pallas_call x1 -> x2, Pallas kernels: 7.2 us -> 38.9 us  [the longest x1 19.8 us: near_forward_split(): pl.pallas_call(functools.partial(near_local_kernel, pairs, halo, blocks_h...]
    ppermute x8, waiting for transfers between devices: 27.7 us -> 12.6 us  [partner(): lax.ppermute(shard, axis, [(i, i ^ 1 << apart) for i in range(lax.axis_si...]
    ppermute x8, starting transfers between devices: 5.86 us -> 12.6 us  [partner(): lax.ppermute(shard, axis, [(i, i ^ 1 << apart) for i in range(lax.axis_si...]
    reshape x0 -> x4, local copies, waits for them, and re-layouts: none -> 5.14 us  [case_minor(): x.reshape(cases, points // rows, rows, width).transpose(1, 2, 0, 3)]
    dot_general x1, matrix products: 1.33 us -> 5.05 us  [on_device(): jnp.einsum('rp,ard->apd', leaf_basis, far_coeff, preferred_element_type=j...]
    ppermute x4, waiting for transfers between devices: 13.3 us -> 10.4 us  [shifted(): lax.ppermute(value, axis, [(source, source + steps) for source in range(l...]
    concatenate x1, other arithmetic: 2.67 us -> 1.12 us  [near_forward_split(): jnp.concatenate([from_prev, from_next], axis=1)]
    dot_general x1, matrix products: 4.54 us -> 3 us  [on_device(): jnp.einsum('apc,cd->apd', near_bf, w_near, preferred_element_type=jnp.flo...]
  transfers between devices with their start and end apart: 12 -> 12, of which waited for: 7 -> 6; matrix products, arithmetic and copies ran while one was open for 7% -> 6% of each run, Pallas kernels for 10% -> 24%
where the time goes in v7:
time: 125 us; the launch traced here: 124 us
  Pallas kernels  48.5 us (39%)
  starting transfers between devices  26.1 us (21%)
  waiting for transfers between devices  23 us (18%)
  matrix products  14.9 us (12%)
  local copies, waits for them, and re-layouts  8.94 us (7%)
  other arithmetic  1.49 us (1%)
    pallas_call x1, Pallas kernels, near_forward_split(): pl.pallas_call(functools.partial(near_local_kernel, pairs, halo, blocks_h...  19.8 us
    pallas_call x1, Pallas kernels, near_forward_split(): pl.pallas_call(functools.partial(near_halo_kernel, pairs, halo, blocks_he...  19.1 us
    ppermute x4, starting transfers between devices, shifted(): lax.ppermute(value, axis, [(source, source + steps) for source in range(l...  13.5 us
    ppermute x8, starting transfers between devices, partner(): lax.ppermute(shard, axis, [(i, i ^ 1 << apart) for i in range(lax.axis_si...  12.6 us
    ppermute x8, waiting for transfers between devices, partner(): lax.ppermute(shard, axis, [(i, i ^ 1 << apart) for i in range(lax.axis_si...  12.6 us
    ppermute x4, waiting for transfers between devices, shifted(): lax.ppermute(value, axis, [(source, source + steps) for source in range(l...  10.4 us
    pallas_call x1, Pallas kernels, near_backward(): pl.pallas_call(functools.partial(near_bwd_kernel, cases, pairs, rows, ste...  9.63 us
    reshape x4, local copies, waits for them, and re-layouts, case_minor(): x.reshape(cases, points // rows, rows, width).transpose(1, 2, 0, 3)  5.14 us
  transfers between devices with their start and end apart: 12, of which 6 were waited for; matrix products, arithmetic and copies ran while one was open for 6% of the time, Pallas kernels for 24%

profile of v7, /device:TPU:16, one launch (start us, length us, event | category | flops | bytes accessed | tf_op | source)
XLA Modules:
  0.0 123.9 jit_solution(1881951066398686778)
XLA Ops:
  0.7 0.9 copy-done
  1.6 1.5 %convolution_bitcast_fusion.2 = f32[2,64,128]{2,1,0:T(8,128)S(1)} fusion(bf16[2,2048,128]{2,1,0:T(8,128)(2,1)} %param.8, bf16[64,2048]{1,0:T(8,128)(2,1)S(1)} %copy-done), kind=kOutput, calls=%fused_computation.21 | convolution fusion | flops 67108864 | bytes 1376256 | tf_op jit(solution)/shard_map/rp,apc->arc/dot_general | solution.py:294
  3.1 1.6 %collective-permute-start.2 = (f32[2,64,128]{2,1,0:T(8,128)S(1)}, f32[2,64,128]{2,1,0:T(8,128)S(1)}, u32[]{:S(2)}, u32[]{:S(2)}) collective-permute-start(f32[2,64,128]{2,1,0:T(8,128)S(1)} %convolution_bitcast_fusion.2), channel_id=1, source_target_pairs={{0,4},{4,0},{8,12},{12,8},{16,20},{20,16},{24,28},{28,24},{1,5},{5... | collective-permute-start | bytes 196616 | tf_op jit(solution)/shard_map/ppermute | solution.py:16
  4.7 0.9 fusion.48
  5.6 2.4 %collective-permute-start = (bf16[2,1024,128]{2,1,0:T(8,128)(2,1)}, bf16[2,1024,128]{2,1,0:T(8,128)(2,1)S(1)}, u32[]{:S(2)}, u32[]{:S(2)}) collective-permute-start(bf16[2,1024,128]{2,1,0:T(8,128)(2,1)} %get-tuple-element.30), channel_id=1, source_target_pairs={{0,4},{4,8},{8,12},{12,16},{16,20},{20,24},{24,28},{1,5},{5,9},{9,... | collective-permute-start | bytes 1572872 | tf_op jit(solution)/shard_map/ppermute | solution.py:22
  8.0 4.3 %collective-permute-start.1 = (bf16[2,1024,128]{2,1,0:T(8,128)(2,1)S(1)}, bf16[2,1024,128]{2,1,0:T(8,128)(2,1)}, u32[]{:S(2)}, u32[]{:S(2)}) collective-permute-start(bf16[2,1024,128]{2,1,0:T(8,128)(2,1)S(1)} %get-tuple-element.31), channel_id=1, source_target_pairs={{4,0},{8,4},{12,8},{16,12},{20,16},{24,20},{28,24},{5,1},{9,5},{13... | collective-permute-start | bytes 1572872 | tf_op jit(solution)/shard_map/ppermute | solution.py:22
  12.3 0.7 reshape.41.ids_ref
  13.0 1.1 copy.22
  14.1 1.5 %reshape.45.feat_ref = bf16[16,128,256]{2,1,0:T(8,128)(2,1)} reshape(bf16[16,128,2,128]{3,2,1,0:T(2,128)(2,1)S(1)} %bitcast.102) | data formatting | bytes 2097152 | tf_op jit(solution)/shard_map/reshape | solution.py:144
  16.2 1.6 %collective-permute-start.3 = (f32[2,64,128]{2,1,0:T(8,128)S(1)}, f32[2,64,128]{2,1,0:T(8,128)S(1)}, u32[]{:S(2)}, u32[]{:S(2)}) collective-permute-start(f32[2,64,128]{2,1,0:T(8,128)S(1)} %add.65), channel_id=1, source_target_pairs={{0,8},{4,12},{8,0},{12,4},{16,24},{20,28},{24,16},{28,20},{1,9},{5... | collective-permute-start | bytes 196616 | tf_op jit(solution)/shard_map/ppermute | solution.py:16
  17.9 19.8 %shard_map.111.part_ref = f32[16,128,256]{2,1,0:T(8,128)} custom-call(s32[192]{0:T(256)} %reshape.41.ids_ref, bf16[16,12,128,128]{3,2,1,0:T(8,128)(2,1)} %kb_ref.5, bf16[16,128,256]{2,1,0:T(8,128)(2,1)} %reshape.45.feat_ref), custom_call_target="tpu_custom_call" | custom-call | flops 805306368 | bytes 9437184 | tf_op jit(solution)/shard_map/pallas_call | solution.py:156
  37.7 5.1 %collective-permute-start.4 = (f32[2,64,128]{2,1,0:T(8,128)S(1)}, f32[2,64,128]{2,1,0:T(8,128)S(1)}, u32[]{:S(2)}, u32[]{:S(2)}) collective-permute-start(f32[2,64,128]{2,1,0:T(8,128)S(1)} %add.67), channel_id=1, source_target_pairs={{0,16},{4,20},{8,24},{12,28},{16,0},{20,4},{24,8},{28,12},{1,17},{... | collective-permute-start | bytes 196616 | tf_op jit(solution)/shard_map/ppermute | solution.py:16
  43.1 2.0 %collective-permute-done.4 = f32[2,64,128]{2,1,0:T(8,128)S(1)} collective-permute-done((f32[2,64,128]{2,1,0:T(8,128)S(1)}, f32[2,64,128]{2,1,0:T(8,128)S(1)}, u32[]{:S(2)}, u32[]{:S(2)}) %collective-permute-start.4) | collective-permute-done | bytes 65568 | tf_op jit(solution)/shard_map/ppermute | solution.py:16
  45.5 1.1 pad_maximum_fusion
  46.7 1.1 copy.23
  47.8 1.5 %reshape.43.halo_ref = bf16[16,128,256]{2,1,0:T(8,128)(2,1)} reshape(bf16[16,128,2,128]{3,2,1,0:T(2,128)(2,1)S(1)} %bitcast.101) | data formatting | bytes 2097152 | tf_op jit(solution)/shard_map/reshape | solution.py:144
  49.2 19.1 %shard_map.112 = bf16[2,2048,128]{2,1,0:T(8,128)(2,1)} custom-call(s32[192]{0:T(256)} %reshape.41.ids_ref, bf16[16,12,128,128]{3,2,1,0:T(8,128)(2,1)} %kb_ref.5, bf16[16,128,256]{2,1,0:T(8,128)(2,1)} %reshape.43.halo_ref, f32[16,128,256]{2,1,0:T(8,128)} %shard_map.111.part_ref), custom_call_target="tpu_custom_call" | custom-call | flops 805306368 | bytes 9437184 | tf_op jit(solution)/shard_map/pallas_call | solution.py:177
  68.3 3.0 %fusion.40 = f32[2,2048,128]{2,1,0:T(8,128)} fusion(bf16[2,2048,128]{2,1,0:T(8,128)(2,1)} %shard_map.112, bf16[128,128]{1,0:T(8,128)(2,1)S(1)} %copy-done.7), kind=kOutput, calls=%fused_computation.65 | convolution fusion | flops 134217728 | bytes 3178496 | tf_op jit(solution)/shard_map/apc,cd->apd/dot_general | solution.py:302
  71.3 5.0 %fusion.3 = (bf16[2,2048,128]{2,1,0:T(8,128)(2,1)S(1)}, bf16[2,2048,128]{2,1,0:T(8,128)(2,1)}) fusion(bf16[2,2048,128]{2,1,0:T(8,128)(2,1)} %param.9, f32[2,2048,128]{2,1,0:T(8,128)} %fusion.40, bf16[64,2048]{1,0:T(8,128)(2,1)S(1)} %copy-done, bf16[2,64,128]{2,1,0:T(8,128)(2,1)S(1)} %fusion.19, bf16[128,128]{1,0:T(8,128)(2,1)S(1)} %copy-done.8), kind=kOutput, calls=%fused_computation.10 | convolution fusion | flops 83902464 | bytes 5570560 | tf_op jit(solution)/shard_map/rp,ard->apd/dot_general | solution.py:300
  77.6 1.4 %convolution_convert_fusion.back_ref = bf16[2,2048,128]{2,1,0:T(8,128)(2,1)} fusion(bf16[2,2048,128]{2,1,0:T(8,128)(2,1)S(1)} %get-tuple-element.28, bf16[128,128]{1,0:T(8,128)(2,1)S(1)} %copy-done.7), kind=kOutput, calls=%fused_computation.7 | convolution fusion | flops 134742016 | bytes 2129920 | tf_op jit(solution)/shard_map/apc,dc->apd/dot_general | solution.py:310
  79.0 9.6 %shard_map.113 = (f32[2,2048,128]{2,1,0:T(8,128)}, bf16[2,1024,128]{2,1,0:T(8,128)(2,1)}, bf16[2,1024,128]{2,1,0:T(8,128)(2,1)}) custom-call(s32[192]{0:T(256)} %reshape.41.ids_ref, bf16[16,12,128,128]{3,2,1,0:T(8,128)(2,1)} %kb_ref.5, bf16[2,2048,128]{2,1,0:T(8,128)(2,1)} %convolution_convert_fusion.back_ref), custom_call_target="tpu_custom_call" | custom-call | flops 1610612736 | bytes 11534336 | tf_op jit(solution)/shard_map/pallas_call | solution.py:238
  88.8 5.7 %collective-permute-done.6 = f32[384,128]{1,0:T(8,128)S(1)} collective-permute-done((f32[384,128]{1,0:T(8,128)S(1)}, f32[384,128]{1,0:T(8,128)S(1)}, u32[]{:S(2)}, u32[]{:S(2)}) %collective-permute-start.6) | collective-permute-done | bytes 196640 | tf_op jit(solution)/shard_map/ppermute | solution.py:16
  94.5 2.5 %collective-permute-start.9 = (f32[384,128]{1,0:T(8,128)S(1)}, f32[384,128]{1,0:T(8,128)S(1)}, u32[]{:S(2)}, u32[]{:S(2)}) collective-permute-start(f32[384,128]{1,0:T(8,128)S(1)} %pad_maximum_fusion.3), channel_id=1, source_target_pairs={{0,16},{4,20},{8,24},{12,28},{16,0},{20,4},{24,8},{28,12},{1,17},{... | collective-permute-start | bytes 589832 | tf_op jit(solution)/shard_map/ppermute | solution.py:16
  97.3 2.2 %collective-permute-start.7 = (bf16[2,1024,128]{2,1,0:T(8,128)(2,1)S(1)}, bf16[2,1024,128]{2,1,0:T(8,128)(2,1)S(1)}, u32[]{:S(2)}, u32[]{:S(2)}) collective-permute-start(bf16[2,1024,128]{2,1,0:T(8,128)(2,1)S(1)} %copy-done.11), channel_id=1, source_target_pairs={{0,4},{4,8},{8,12},{12,16},{16,20},{20,24},{24,28},{1,5},{5,9},{9,... | collective-permute-start | bytes 1572872 | tf_op jit(solution)/shard_map/ppermute | solution.py:22
  99.5 4.6 %collective-permute-start.8 = (bf16[2,1024,128]{2,1,0:T(8,128)(2,1)S(1)}, bf16[2,1024,128]{2,1,0:T(8,128)(2,1)S(1)}, u32[]{:S(2)}, u32[]{:S(2)}) collective-permute-start(bf16[2,1024,128]{2,1,0:T(8,128)(2,1)S(1)} %copy-done.10), channel_id=1, source_target_pairs={{4,0},{8,4},{12,8},{16,12},{20,16},{24,20},{28,24},{5,1},{9,5},{13... | collective-permute-start | bytes 1572872 | tf_op jit(solution)/shard_map/ppermute | solution.py:22
  104.4 1.1 collective-permute-done.10
  105.5 1.6 %collective-permute-start.11 = (f32[256,128]{1,0:T(8,128)S(1)}, f32[256,128]{1,0:T(8,128)S(1)}, u32[]{:S(2)}, u32[]{:S(2)}) collective-permute-start(f32[256,128]{1,0:T(8,128)S(1)} %add.82), channel_id=1, source_target_pairs={{0,2},{1,3},{2,0},{3,1},{4,6},{5,7},{6,4},{7,5},{8,10},{9,11},{10,... | collective-permute-start | bytes 393224 | tf_op jit(solution)/shard_map/ppermute | solution.py:16
  107.3 3.8 %collective-permute-done.11 = f32[256,128]{1,0:T(8,128)S(1)} collective-permute-done((f32[256,128]{1,0:T(8,128)S(1)}, f32[256,128]{1,0:T(8,128)S(1)}, u32[]{:S(2)}, u32[]{:S(2)}) %collective-permute-start.11) | collective-permute-done | bytes 131104 | tf_op jit(solution)/shard_map/ppermute | solution.py:16
  111.1 0.7 fusion.49
  111.8 6.1 %collective-permute-done.7 = bf16[2,1024,128]{2,1,0:T(8,128)(2,1)S(1)} collective-permute-done((bf16[2,1024,128]{2,1,0:T(8,128)(2,1)S(1)}, bf16[2,1024,128]{2,1,0:T(8,128)(2,1)S(1)}, u32[]{:S(2)}, u32[]{:S(2)}) %collective-permute-start.7) | collective-permute-done | bytes 524320 | tf_op jit(solution)/shard_map/ppermute | solution.py:22
  117.9 4.3 %collective-permute-done.8 = bf16[2,1024,128]{2,1,0:T(8,128)(2,1)S(1)} collective-permute-done((bf16[2,1024,128]{2,1,0:T(8,128)(2,1)S(1)}, bf16[2,1024,128]{2,1,0:T(8,128)(2,1)S(1)}, u32[]{:S(2)}, u32[]{:S(2)}) %collective-permute-start.8) | collective-permute-done | bytes 524320 | tf_op jit(solution)/shard_map/ppermute | solution.py:22
  122.4 1.5 %fusion.11 = bf16[2,2048,128]{2,1,0:T(8,128)(2,1)} fusion(f32[2,1024,128]{2,1,0:T(8,128)S(1)} %get-tuple-element.27, f32[2,1024,128]{2,1,0:T(8,128)S(1)} %get-tuple-element.26, bf16[2,64,128]{2,1,0:T(8,128)(2,1)S(1)} %fusion.18, bf16[64,2048]{1,0:T(8,128)(2,1)S(1)} %copy-done), kind=kOutput, calls=%fused_computation.19 | convolution fusion | flops 68681728 | bytes 3440640 | tf_op jit(solution)/shard_map/rp,arc->apc/dot_general | solution.py:331
  (59 shorter events, 3.7 us)
Async XLA Ops:
  0.6 1.0 copy-start
  0.6 4.0 %copy-start.1 = (bf16[2,2048,128]{2,1,0:T(8,128)(2,1)S(1)}, bf16[2,2048,128]{2,1,0:T(8,128)(2,1)}, u32[]{:S(2)}) copy-start(bf16[2,2048,128]{2,1,0:T(8,128)(2,1)} %param.8) | copy-start | bytes 3145732
  0.7 11.7 %copy-start.9 = (s32[16,12]{1,0:T(8,128)S(1)}, s32[16,12]{1,0:T(8,128)}, u32[]{:S(2)}) copy-start(s32[16,12]{1,0:T(8,128)} %param.11) | copy-start | bytes 2308
  3.1 12.5 %collective-permute-start.2 = (f32[2,64,128]{2,1,0:T(8,128)S(1)}, f32[2,64,128]{2,1,0:T(8,128)S(1)}, u32[]{:S(2)}, u32[]{:S(2)}) collective-permute-start(f32[2,64,128]{2,1,0:T(8,128)S(1)} %convolution_bitcast_fusion.2), channel_id=1, source_target_pairs={{0,4},{4,0},{8,12},{12,8},{16,20},{20,16},{24,28},{28,24},{1,5},{5... | collective-permute-start | bytes 196616 | tf_op jit(solution)/shard_map/ppermute | solution.py:16
  5.6 40.0 %collective-permute-start = (bf16[2,1024,128]{2,1,0:T(8,128)(2,1)}, bf16[2,1024,128]{2,1,0:T(8,128)(2,1)S(1)}, u32[]{:S(2)}, u32[]{:S(2)}) collective-permute-start(bf16[2,1024,128]{2,1,0:T(8,128)(2,1)} %get-tuple-element.30), channel_id=1, source_target_pairs={{0,4},{4,8},{8,12},{12,16},{16,20},{20,24},{24,28},{1,5},{5,9},{9,... | collective-permute-start | bytes 1572872 | tf_op jit(solution)/shard_map/ppermute | solution.py:22
  8.0 37.6 %collective-permute-start.1 = (bf16[2,1024,128]{2,1,0:T(8,128)(2,1)S(1)}, bf16[2,1024,128]{2,1,0:T(8,128)(2,1)}, u32[]{:S(2)}, u32[]{:S(2)}) collective-permute-start(bf16[2,1024,128]{2,1,0:T(8,128)(2,1)S(1)} %get-tuple-element.31), channel_id=1, source_target_pairs={{4,0},{8,4},{12,8},{16,12},{20,16},{24,20},{28,24},{5,1},{9,5},{13... | collective-permute-start | bytes 1572872 | tf_op jit(solution)/shard_map/ppermute | solution.py:22
  15.6 0.6 copy-start.5
  16.2 26.6 %copy-start.4 = (f32[3,64,64]{2,1,0:T(8,128)S(1)}, f32[3,64,64]{2,1,0:T(8,128)}, u32[]{:S(2)}) copy-start(f32[3,64,64]{2,1,0:T(8,128)} %param.15) | copy-start | bytes 147460
  16.2 29.1 %copy-start.6 = (f32[2,64,128]{2,1,0:T(8,128)S(1)}, f32[2,64,128]{2,1,0:T(8,128)}, u32[]{:S(2)}) copy-start(f32[2,64,128]{2,1,0:T(8,128)} %copy-done.5) | copy-start | bytes 196612
  16.2 21.5 %collective-permute-start.3 = (f32[2,64,128]{2,1,0:T(8,128)S(1)}, f32[2,64,128]{2,1,0:T(8,128)S(1)}, u32[]{:S(2)}, u32[]{:S(2)}) collective-permute-start(f32[2,64,128]{2,1,0:T(8,128)S(1)} %add.65), channel_id=1, source_target_pairs={{0,8},{4,12},{8,0},{12,4},{16,24},{20,28},{24,16},{28,20},{1,9},{5... | collective-permute-start | bytes 196616 | tf_op jit(solution)/shard_map/ppermute | solution.py:16
  37.7 7.4 %collective-permute-start.4 = (f32[2,64,128]{2,1,0:T(8,128)S(1)}, f32[2,64,128]{2,1,0:T(8,128)S(1)}, u32[]{:S(2)}, u32[]{:S(2)}) collective-permute-start(f32[2,64,128]{2,1,0:T(8,128)S(1)} %add.67), channel_id=1, source_target_pairs={{0,16},{4,20},{8,24},{12,28},{16,0},{20,4},{24,8},{28,12},{1,17},{... | collective-permute-start | bytes 196616 | tf_op jit(solution)/shard_map/ppermute | solution.py:16
  49.2 19.1 %copy-start.7 = (bf16[128,128]{1,0:T(8,128)(2,1)S(1)}, bf16[128,128]{1,0:T(8,128)(2,1)}, u32[]{:S(2)}) copy-start(bf16[128,128]{1,0:T(8,128)(2,1)} %param.13) | copy-start | bytes 98308
  68.3 3.0 %copy-start.8 = (bf16[128,128]{1,0:T(8,128)(2,1)S(1)}, bf16[128,128]{1,0:T(8,128)(2,1)}, u32[]{:S(2)}) copy-start(bf16[128,128]{1,0:T(8,128)(2,1)} %param.14) | copy-start | bytes 98308
  71.3 5.1 %copy-start.2 = (bf16[2,2048,128]{2,1,0:T(8,128)(2,1)S(1)}, bf16[2,2048,128]{2,1,0:T(8,128)(2,1)}, u32[]{:S(2)}) copy-start(bf16[2,2048,128]{2,1,0:T(8,128)(2,1)} %shard_map.112) | copy-start | bytes 3145732
  77.5 11.1 %collective-permute-start.5 = (f32[384,128]{1,0:T(8,128)S(1)}, f32[384,128]{1,0:T(8,128)S(1)}, u32[]{:S(2)}, u32[]{:S(2)}) collective-permute-start(f32[384,128]{1,0:T(8,128)S(1)} %pad_maximum_fusion.1), channel_id=1, source_target_pairs={{0,4},{4,0},{8,12},{12,8},{16,20},{20,16},{24,28},{28,24},{1,5},{5... | collective-permute-start | bytes 589832 | tf_op jit(solution)/shard_map/ppermute | solution.py:16
  88.6 8.6 %copy-start.11 = (bf16[2,1024,128]{2,1,0:T(8,128)(2,1)S(1)}, bf16[2,1024,128]{2,1,0:T(8,128)(2,1)}, u32[]{:S(2)}) copy-start(bf16[2,1024,128]{2,1,0:T(8,128)(2,1)} %get-tuple-element.23) | copy-start | bytes 1572868
  88.6 10.8 %copy-start.10 = (bf16[2,1024,128]{2,1,0:T(8,128)(2,1)S(1)}, bf16[2,1024,128]{2,1,0:T(8,128)(2,1)}, u32[]{:S(2)}) copy-start(bf16[2,1024,128]{2,1,0:T(8,128)(2,1)} %get-tuple-element.24) | copy-start | bytes 1572868
  88.7 33.6 %copy-start.3 = (f32[2,2048,128]{2,1,0:T(8,128)S(1)}, f32[2,2048,128]{2,1,0:T(8,128)}, u32[]{:S(2)}) copy-start(f32[2,2048,128]{2,1,0:T(8,128)} %get-tuple-element.22) | copy-start | bytes 6291460
  88.7 5.7 %collective-permute-start.6 = (f32[384,128]{1,0:T(8,128)S(1)}, f32[384,128]{1,0:T(8,128)S(1)}, u32[]{:S(2)}, u32[]{:S(2)}) collective-permute-start(f32[384,128]{1,0:T(8,128)S(1)} %pad_maximum_fusion.2), channel_id=1, source_target_pairs={{0,8},{4,12},{8,0},{12,4},{16,24},{20,28},{24,16},{28,20},{1,9},{5... | collective-permute-start | bytes 589832 | tf_op jit(solution)/shard_map/ppermute | solution.py:16
  94.5 9.5 %collective-permute-start.9 = (f32[384,128]{1,0:T(8,128)S(1)}, f32[384,128]{1,0:T(8,128)S(1)}, u32[]{:S(2)}, u32[]{:S(2)}) collective-permute-start(f32[384,128]{1,0:T(8,128)S(1)} %pad_maximum_fusion.3), channel_id=1, source_target_pairs={{0,16},{4,20},{8,24},{12,28},{16,0},{20,4},{24,8},{28,12},{1,17},{... | collective-permute-start | bytes 589832 | tf_op jit(solution)/shard_map/ppermute | solution.py:16
  97.3 20.7 %collective-permute-start.7 = (bf16[2,1024,128]{2,1,0:T(8,128)(2,1)S(1)}, bf16[2,1024,128]{2,1,0:T(8,128)(2,1)S(1)}, u32[]{:S(2)}, u32[]{:S(2)}) collective-permute-start(bf16[2,1024,128]{2,1,0:T(8,128)(2,1)S(1)} %copy-done.11), channel_id=1, source_target_pairs={{0,4},{4,8},{8,12},{12,16},{16,20},{20,24},{24,28},{1,5},{5,9},{9,... | collective-permute-start | bytes 1572872 | tf_op jit(solution)/shard_map/ppermute | solution.py:22
  99.5 22.7 %collective-permute-start.8 = (bf16[2,1024,128]{2,1,0:T(8,128)(2,1)S(1)}, bf16[2,1024,128]{2,1,0:T(8,128)(2,1)S(1)}, u32[]{:S(2)}, u32[]{:S(2)}) collective-permute-start(bf16[2,1024,128]{2,1,0:T(8,128)(2,1)S(1)} %copy-done.10), channel_id=1, source_target_pairs={{4,0},{8,4},{12,8},{16,12},{20,16},{24,20},{28,24},{5,1},{9,5},{13... | collective-permute-start | bytes 1572872 | tf_op jit(solution)/shard_map/ppermute | solution.py:22
  104.1 1.4 %collective-permute-start.10 = (f32[256,128]{1,0:T(8,128)S(1)}, f32[256,128]{1,0:T(8,128)S(1)}, u32[]{:S(2)}, u32[]{:S(2)}) collective-permute-start(f32[256,128]{1,0:T(8,128)S(1)} %slice_add_fusion), channel_id=1, source_target_pairs={{0,1},{1,0},{2,3},{3,2},{4,5},{5,4},{6,7},{7,6},{8,9},{9,8},{10,11... | collective-permute-start | bytes 393224 | tf_op jit(solution)/shard_map/ppermute | solution.py:16
  105.5 5.6 %collective-permute-start.11 = (f32[256,128]{1,0:T(8,128)S(1)}, f32[256,128]{1,0:T(8,128)S(1)}, u32[]{:S(2)}, u32[]{:S(2)}) collective-permute-start(f32[256,128]{1,0:T(8,128)S(1)} %add.82), channel_id=1, source_target_pairs={{0,2},{1,3},{2,0},{3,1},{4,6},{5,7},{6,4},{7,5},{8,10},{9,11},{10,... | collective-permute-start | bytes 393224 | tf_op jit(solution)/shard_map/ppermute | solution.py:16

commit v8 on v1

--- a/solution.py
+++ b/solution.py
@@ -9,7 +9,8 @@
 from jax.sharding import PartitionSpec as P
 
 HALO = 8
-TB = 4
+TB = 8
+BWD_TB = 4
 
 
 def partner(shard, axis, apart):
@@ -28,11 +29,12 @@
     return jnp.einsum("rs,asc->arc", matrix, sibling, precision=lax.Precision.HIGHEST)
 
 
-def expand(own_value, translations, flipped, rider=None):
+def expand(own_value, translations, flipped, rider=None, stages=()):
     depth_count = lax.axis_size("leaf").bit_length() - 1
     summed = jnp.zeros(own_value.shape, jnp.float32)
     node_value = own_value
     rows = own_value.shape[0] * own_value.shape[1]
+    staged = None
     for height in range(depth_count):
         if rider is None:
             sibling = partner(node_value, "leaf", height)
@@ -41,11 +43,14 @@
                 [node_value.reshape(rows, own_value.shape[2]), rider], axis=0
             )
             got = partner(packed, "leaf", height)
+            if height < len(stages):
+                staged = stages[height](staged)
+                got, staged = lax.optimization_barrier((got, staged))
             sibling = got[:rows].reshape(own_value.shape)
             rider = rider + got[rows:]
         summed = summed + apply_level(translations[height], sibling, flipped)
         node_value = node_value + sibling
-    return summed, rider
+    return summed, rider, staged
 
 
 def near_fwd_kernel(cases, pairs, rows, ids_ref, kb_ref, ext_ref, out_ref):
@@ -94,16 +99,21 @@
     )(ids, kernel_blocks, extended)
 
 
-def near_bwd_kernel(cases, pairs, rows, steps, ids_ref, kb_ref, back_ref, mid_ref, lo_ref, hi_ref, acc_ref):
+def near_bwd_kernel(cases, pairs, rows, steps, first, carry, ids_ref, kb_ref, back_ref, *refs):
+    if carry:
+        lo_in, hi_in, mid_ref, lo_ref, hi_ref, acc_ref = refs
+    else:
+        mid_ref, lo_ref, hi_ref, acc_ref = refs
     g = pl.program_id(0)
+    tbs = kb_ref.shape[0]
 
     @pl.when(g == 0)
     def _():
         acc_ref[...] = jnp.zeros(acc_ref.shape, acc_ref.dtype)
 
     width = back_ref.shape[2]
-    for tb in range(TB):
-        t = g * TB + tb
+    for tb in range(tbs):
+        t = first + g * tbs + tb
         lhs = jnp.concatenate([kb_ref[tb, k] for k in range(pairs)], axis=1)
         rhs = jnp.concatenate(
             [back_ref[c, pl.ds(tb * rows, rows), :] for c in range(cases)], axis=1
@@ -121,35 +131,49 @@
     def _():
         halo_points = lo_ref.shape[1]
         mid_points = mid_ref.shape[1]
-        lo_ref[...] = acc_ref[:, :halo_points, :].astype(lo_ref.dtype)
+        lo = acc_ref[:, :halo_points, :]
+        hi = acc_ref[:, halo_points + mid_points :, :]
+        if carry:
+            lo = lo + lo_in[...]
+            hi = hi + hi_in[...]
+        lo_ref[...] = lo.astype(lo_ref.dtype)
         mid_ref[...] = acc_ref[:, halo_points : halo_points + mid_points, :]
-        hi_ref[...] = acc_ref[:, halo_points + mid_points :, :].astype(hi_ref.dtype)
-
-
-def near_backward(ids, kernel_blocks, back_near, halo_points):
+        hi_ref[...] = hi.astype(hi_ref.dtype)
+
+
+def near_backward(ids, kernel_blocks, back_near, halo_points, first, count, carry=None):
     cases, points_here, width = back_near.shape
     blocks_here, pairs, rows, _ = kernel_blocks.shape
-    steps = blocks_here // TB
+    tbs = BWD_TB
+    steps = count // tbs
+    offset = first // tbs
     span_points = points_here + 2 * halo_points
-    flops = 2 * blocks_here * pairs * rows * rows * cases * width
+    flops = 2 * count * pairs * rows * rows * cases * width
+    halo_type = jnp.float32 if carry is None else jnp.bfloat16
+    halo_spec = pl.BlockSpec((cases, halo_points, width), lambda g, ids: (0, 0, 0))
+    in_specs = [
+        pl.BlockSpec((tbs, pairs, rows, rows), lambda g, ids: (g + offset, 0, 0, 0)),
+        pl.BlockSpec((cases, tbs * rows, width), lambda g, ids: (0, g + offset, 0)),
+    ]
+    operands = [ids, kernel_blocks, back_near]
+    if carry is not None:
+        in_specs += [halo_spec, halo_spec]
+        operands += list(carry)
     return pl.pallas_call(
-        functools.partial(near_bwd_kernel, cases, pairs, rows, steps),
+        functools.partial(near_bwd_kernel, cases, pairs, rows, steps, first, carry is not None),
         out_shape=(
             jax.ShapeDtypeStruct((cases, points_here, width), jnp.float32),
-            jax.ShapeDtypeStruct((cases, halo_points, width), jnp.bfloat16),
-            jax.ShapeDtypeStruct((cases, halo_points, width), jnp.bfloat16),
+            jax.ShapeDtypeStruct((cases, halo_points, width), halo_type),
+            jax.ShapeDtypeStruct((cases, halo_points, width), halo_type),
         ),
         grid_spec=pltpu.PrefetchScalarGridSpec(
             num_scalar_prefetch=1,
             grid=(steps,),
-            in_specs=[
-                pl.BlockSpec((TB, pairs, rows, rows), lambda g, ids: (g, 0, 0, 0)),
-                pl.BlockSpec((cases, TB * rows, width), lambda g, ids: (0, g, 0)),
-            ],
+            in_specs=in_specs,
             out_specs=[
                 pl.BlockSpec((cases, points_here, width), lambda g, ids: (0, 0, 0)),
-                pl.BlockSpec((cases, halo_points, width), lambda g, ids: (0, 0, 0)),
-                pl.BlockSpec((cases, halo_points, width), lambda g, ids: (0, 0, 0)),
+                halo_spec,
+                halo_spec,
             ],
             scratch_shapes=[pltpu.VMEM((cases, span_points, width), jnp.float32)],
         ),
@@ -159,9 +183,11 @@
         cost_estimate=pl.CostEstimate(
             flops=flops,
             transcendentals=0,
-            bytes_accessed=kernel_blocks.size * 2 + back_near.size * 2 + cases * span_points * width * 4,
-        ),
-    )(ids, kernel_blocks, back_near)
+            bytes_accessed=count * pairs * rows * rows * 2
+            + count * rows * cases * width * 2
+            + cases * span_points * width * 4,
+        ),
+    )(*operands)
 
 
 def on_device(
@@ -189,7 +215,7 @@
     near_bf = near_forward(local_ids, kernel_blocks, extended)
 
     summary = jnp.einsum("rp,apc->arc", leaf_basis, features, preferred_element_type=jnp.float32)
-    expansion, _ = expand(summary, translations, False)
+    expansion, _, _ = expand(summary, translations, False)
     exp_bf = expansion.astype(jnp.bfloat16)
     far_coeff = jnp.einsum("arc,cd->ard", exp_bf, w_far, preferred_element_type=jnp.float32).astype(
         jnp.bfloat16
@@ -208,7 +234,6 @@
         jnp.bfloat16
     )
 
-    mid, lo, hi = near_backward(local_ids, kernel_blocks, back_near, halo_points)
 
     scale = 1.0 / math.sqrt(
         cases_here * lax.axis_size("case") * points_here * lax.axis_size("leaf")
@@ -222,7 +247,22 @@
     grads = jnp.concatenate([near_term, far_term], axis=0)
 
     back_coeff = jnp.einsum("arc,dc->ard", projected, w_far, preferred_element_type=jnp.float32)
-    back_exp, grads = expand(back_coeff, translations, True, rider=grads)
+    half = blocks_here // 2
+
+    def first_half(_):
+        return near_backward(local_ids, kernel_blocks, back_near, halo_points, 0, half)
+
+    def second_half(prev):
+        mid_first, lo_first, hi_first = prev
+        mid_second, lo, hi = near_backward(
+            local_ids, kernel_blocks, back_near, halo_points, half, blocks_here - half,
+            carry=(lo_first, hi_first),
+        )
+        return mid_first + mid_second, lo, hi
+
+    back_exp, grads, (mid, lo, hi) = expand(
+        back_coeff, translations, True, rider=grads, stages=(first_half, second_half)
+    )
     back_far = jnp.einsum(
         "rp,arc->apc", leaf_basis, back_exp.astype(jnp.bfloat16), preferred_element_type=jnp.float32
     )

time: 107 us -> 101 us (0.944)
  waiting for transfers between devices: 46.9 us -> 36.6 us
  Pallas kernels: 16.8 us -> 21.4 us
    ppermute x4, waiting for transfers between devices: 19.8 us -> 14 us  [shifted(): lax.ppermute(value, axis, [(source, source + steps) for source in range(l...]
    pallas_call x1 -> x2, Pallas kernels: 9.62 us -> 14.9 us  [near_backward(): pl.pallas_call(functools.partial(near_bwd_kernel, cases, pairs, rows, ste...]
    ppermute x8, waiting for transfers between devices: 27.1 us -> 22.6 us  [partner(): lax.ppermute(shard, axis, [(i, i ^ 1 << apart) for i in range(lax.axis_si...]
    add x0 -> x1, other arithmetic: none -> 1.89 us  [second_half(): return (mid_first + mid_second, lo, hi)]
    add x1, other arithmetic: 1.79 us -> 0.18 us  [on_device(): mid[:, :halo_points] + got_prev]
    ppermute x4, starting transfers between devices: 13.5 us -> 14.6 us  [shifted(): lax.ppermute(value, axis, [(source, source + steps) for source in range(l...]
  transfers between devices with their start and end apart: 12 -> 12, of which waited for: 7 -> 7; matrix products, arithmetic and copies ran while one was open for 8% -> 8% of each run, Pallas kernels for 9% -> 15%
where the time goes in v8:
time: 101 us; the launch traced here: 100 us
  waiting for transfers between devices  36.6 us (36%)
  Pallas kernels  21.4 us (21%)
  starting transfers between devices  20.5 us (20%)
  matrix products  12.7 us (13%)
  other arithmetic  4.93 us (5%)
  local copies, waits for them, and re-layouts  3.33 us (3%)
  between operations  1.01 us (1%)
    ppermute x8, waiting for transfers between devices, partner(): lax.ppermute(shard, axis, [(i, i ^ 1 << apart) for i in range(lax.axis_si...  22.6 us
    pallas_call x2, Pallas kernels, near_backward(): pl.pallas_call(functools.partial(near_bwd_kernel, cases, pairs, rows, ste...  14.9 us
    ppermute x4, starting transfers between devices, shifted(): lax.ppermute(value, axis, [(source, source + steps) for source in range(l...  14.6 us
    ppermute x4, waiting for transfers between devices, shifted(): lax.ppermute(value, axis, [(source, source + steps) for source in range(l...  14 us
    pallas_call x1, Pallas kernels, near_forward(): pl.pallas_call(functools.partial(near_fwd_kernel, cases, pairs, rows), ou...  6.52 us
    ppermute x8, starting transfers between devices, partner(): lax.ppermute(shard, axis, [(i, i ^ 1 << apart) for i in range(lax.axis_si...  5.84 us
    dot_general x1, matrix products, on_device(): jnp.einsum('apc,cd->apd', near_bf, w_near, preferred_element_type=jnp.flo...  4.53 us
    concatenate x1, other arithmetic, on_device(): extended = jnp.concatenate([from_prev, features, from_next], axis=1)  2.67 us
  transfers between devices with their start and end apart: 12, of which 7 were waited for; matrix products, arithmetic and copies ran while one was open for 8% of the time, Pallas kernels for 15%

profile of v8, /device:TPU:16, one launch (start us, length us, event | category | flops | bytes accessed | tf_op | source)
XLA Modules:
  0.0 100.5 jit_solution(8753312627596631454)
XLA Ops:
  0.7 0.9 copy-done
  1.6 1.5 %convolution_bitcast_fusion.2 = f32[2,64,128]{2,1,0:T(8,128)S(1)} fusion(bf16[2,2048,128]{2,1,0:T(8,128)(2,1)} %param.8, bf16[64,2048]{1,0:T(8,128)(2,1)S(1)} %copy-done), kind=kOutput, calls=%fused_computation.22 | convolution fusion | flops 67108864 | bytes 1376256 | tf_op jit(solution)/shard_map/rp,apc->arc/dot_general | solution.py:217
  3.1 1.6 %collective-permute-start.2 = (f32[2,64,128]{2,1,0:T(8,128)S(1)}, f32[2,64,128]{2,1,0:T(8,128)S(1)}, u32[]{:S(2)}, u32[]{:S(2)}) collective-permute-start(f32[2,64,128]{2,1,0:T(8,128)S(1)} %convolution_bitcast_fusion.2), channel_id=1, source_target_pairs={{0,4},{4,0},{8,12},{12,8},{16,20},{20,16},{24,28},{28,24},{1,5},{5... | collective-permute-start | bytes 196616 | tf_op jit(solution)/shard_map/ppermute | solution.py:17
  4.7 1.0 %fusion.46 = (bf16[2,1024,128]{2,1,0:T(8,128)(2,1)}, bf16[2,1024,128]{2,1,0:T(8,128)(2,1)}) fusion(bf16[2,2048,128]{2,1,0:T(8,128)(2,1)S(1)} %copy-done.1), kind=kLoop, calls=%fused_computation.71 | loop fusion | bytes 2097152 | tf_op jit(solution)/shard_map/slice | solution.py:207
  5.7 2.4 %collective-permute-start = (bf16[2,1024,128]{2,1,0:T(8,128)(2,1)}, bf16[2,1024,128]{2,1,0:T(8,128)(2,1)}, u32[]{:S(2)}, u32[]{:S(2)}) collective-permute-start(bf16[2,1024,128]{2,1,0:T(8,128)(2,1)} %get-tuple-element.36), channel_id=1, source_target_pairs={{0,4},{4,8},{8,12},{12,16},{16,20},{20,24},{24,28},{1,5},{5,9},{9,... | collective-permute-start | bytes 1572872 | tf_op jit(solution)/shard_map/ppermute | solution.py:23
  8.2 4.3 %collective-permute-start.1 = (bf16[2,1024,128]{2,1,0:T(8,128)(2,1)}, bf16[2,1024,128]{2,1,0:T(8,128)(2,1)}, u32[]{:S(2)}, u32[]{:S(2)}) collective-permute-start(bf16[2,1024,128]{2,1,0:T(8,128)(2,1)} %get-tuple-element.37), channel_id=1, source_target_pairs={{4,0},{8,4},{12,8},{16,12},{20,16},{24,20},{28,24},{5,1},{9,5},{13... | collective-permute-start | bytes 1572872 | tf_op jit(solution)/shard_map/ppermute | solution.py:23
  12.5 1.6 %collective-permute-start.3 = (f32[2,64,128]{2,1,0:T(8,128)S(1)}, f32[2,64,128]{2,1,0:T(8,128)S(1)}, u32[]{:S(2)}, u32[]{:S(2)}) collective-permute-start(f32[2,64,128]{2,1,0:T(8,128)S(1)} %add.68), channel_id=1, source_target_pairs={{0,8},{4,12},{8,0},{12,4},{16,24},{20,28},{24,16},{28,20},{1,9},{5... | collective-permute-start | bytes 196616 | tf_op jit(solution)/shard_map/ppermute | solution.py:17
  14.2 0.7 reshape.29.ids_ref
  14.8 12.7 %collective-permute-done.3 = f32[2,64,128]{2,1,0:T(8,128)S(1)} collective-permute-done((f32[2,64,128]{2,1,0:T(8,128)S(1)}, f32[2,64,128]{2,1,0:T(8,128)S(1)}, u32[]{:S(2)}, u32[]{:S(2)}) %collective-permute-start.3) | collective-permute-done | bytes 65568 | tf_op jit(solution)/shard_map/ppermute | solution.py:17
  27.8 4.9 %collective-permute-done.4 = f32[2,64,128]{2,1,0:T(8,128)S(1)} collective-permute-done((f32[2,64,128]{2,1,0:T(8,128)S(1)}, f32[2,64,128]{2,1,0:T(8,128)S(1)}, u32[]{:S(2)}, u32[]{:S(2)}) %collective-permute-start.4) | collective-permute-done | bytes 65568 | tf_op jit(solution)/shard_map/ppermute | solution.py:17
  33.1 1.3 %convolution_bitcast_fusion.1 = f32[2,2048,128]{2,1,0:T(8,128)S(1)} fusion(bf16[2,64,128]{2,1,0:T(8,128)(2,1)S(1)} %fusion.18, bf16[64,2048]{1,0:T(8,128)(2,1)S(1)} %copy-done, bf16[128,128]{1,0:T(8,128)(2,1)} %param.14), kind=kOutput, calls=%fused_computation.3 | convolution fusion | flops 71319552 | bytes 2424832 | tf_op jit(solution)/shard_map/rp,ard->apd/dot_general | solution.py:223
  34.5 2.7 %pad_maximum_fusion.ext_ref = bf16[2,4096,128]{2,1,0:T(8,128)(2,1)} fusion(bf16[2,1024,128]{2,1,0:T(8,128)(2,1)} %collective-permute-done.1, bf16[2,2048,128]{2,1,0:T(8,128)(2,1)S(1)} %copy-done.1, bf16[2,1024,128]{2,1,0:T(8,128)(2,1)} %collective-permute-done), kind=kLoop, calls=%fused_computation.18 | loop fusion | flops 6291456 | bytes 4194304 | tf_op jit(solution)/shard_map/concatenate | solution.py:210
  37.2 6.5 %shard_map.111 = bf16[2,2048,128]{2,1,0:T(8,128)(2,1)} custom-call(s32[192]{0:T(256)} %reshape.29.ids_ref, bf16[16,12,128,128]{3,2,1,0:T(8,128)(2,1)} %kb_ref.5, bf16[2,4096,128]{2,1,0:T(8,128)(2,1)} %pad_maximum_fusion.ext_ref), custom_call_target="tpu_custom_call" | custom-call | flops 1610612736 | bytes 9437184 | tf_op jit(solution)/shard_map/pallas_call | solution.py:81
  43.7 4.5 %fusion.2 = (bf16[2,2048,128]{2,1,0:T(8,128)(2,1)S(1)}, bf16[2,2048,128]{2,1,0:T(8,128)(2,1)}) fusion(bf16[2,2048,128]{2,1,0:T(8,128)(2,1)} %param.9, f32[2,2048,128]{2,1,0:T(8,128)S(1)} %convolution_bitcast_fusion.1, bf16[2,2048,128]{2,1,0:T(8,128)(2,1)} %shard_map.111, bf16[128,128]{1,0:T(8,128)(2,1)S(1)} %copy-done.6), kind=kOutput, calls=%fused_computation.10 | convolution fusion | flops 146800640 | bytes 6324224 | tf_op jit(solution)/shard_map/apc,cd->apd/dot_general | solution.py:225
  48.2 0.3 fusion.16
  48.5 0.5 fusion.12
  49.5 1.4 %convolution_convert_fusion.back_ref = bf16[2,2048,128]{2,1,0:T(8,128)(2,1)} fusion(bf16[2,2048,128]{2,1,0:T(8,128)(2,1)S(1)} %get-tuple-element.34, bf16[128,128]{1,0:T(8,128)(2,1)S(1)} %copy-done.6), kind=kOutput, calls=%fused_computation.7 | convolution fusion | flops 134742016 | bytes 2129920 | tf_op jit(solution)/shard_map/apc,dc->apd/dot_general | solution.py:233
  50.9 7.2 %shard_map.112 = (f32[2,2048,128]{2,1,0:T(8,128)}, f32[2,1024,128]{2,1,0:T(8,128)}, f32[2,1024,128]{2,1,0:T(8,128)}) custom-call(s32[192]{0:T(256)} %reshape.29.ids_ref, bf16[16,12,128,128]{3,2,1,0:T(8,128)(2,1)} %kb_ref.5, bf16[2,2048,128]{2,1,0:T(8,128)(2,1)} %convolution_convert_fusion.back_ref), custom_call_target="tpu_custom_call" | custom-call | flops 805306368 | bytes 7864320 | tf_op jit(solution)/shard_map/pallas_call | solution.py:162
  58.1 0.6 collective-permute-start.6
  58.8 7.7 %shard_map.113 = (f32[2,2048,128]{2,1,0:T(8,128)}, bf16[2,1024,128]{2,1,0:T(8,128)(2,1)}, bf16[2,1024,128]{2,1,0:T(8,128)(2,1)}) custom-call(s32[192]{0:T(256)} %reshape.29.ids_ref, bf16[16,12,128,128]{3,2,1,0:T(8,128)(2,1)} %kb_ref.5, bf16[2,2048,128]{2,1,0:T(8,128)(2,1)} %convolution_convert_fusion.back_ref, f32[2,1024,128]{2,1,0:T(8,128)} %get-tuple-element.23.refs_0_, ...), custom_call_target="tpu_custom_call" | custom-call | flops 805306368 | bytes 7864320 | tf_op jit(solution)/shard_map/pallas_call | solution.py:162
  66.5 1.9 %add.77 = f32[2,2048,128]{2,1,0:T(8,128)S(1)} add(f32[2,2048,128]{2,1,0:T(8,128)S(1)} %copy-done.3, f32[2,2048,128]{2,1,0:T(8,128)} %get-tuple-element.25) | non-fusion elementwise | flops 524288 | bytes 6291456 | tf_op jit(solution)/shard_map/add | solution.py:261
  69.0 3.9 %collective-permute-start.7 = (bf16[2,1024,128]{2,1,0:T(8,128)(2,1)S(1)}, bf16[2,1024,128]{2,1,0:T(8,128)(2,1)S(1)}, u32[]{:S(2)}, u32[]{:S(2)}) collective-permute-start(bf16[2,1024,128]{2,1,0:T(8,128)(2,1)S(1)} %copy-done.9), channel_id=1, source_target_pairs={{0,4},{4,8},{8,12},{12,16},{16,20},{20,24},{24,28},{1,5},{5,9},{9,... | collective-permute-start | bytes 1572872 | tf_op jit(solution)/shard_map/ppermute | solution.py:23
  73.0 4.0 %collective-permute-start.8 = (bf16[2,1024,128]{2,1,0:T(8,128)(2,1)S(1)}, bf16[2,1024,128]{2,1,0:T(8,128)(2,1)S(1)}, u32[]{:S(2)}, u32[]{:S(2)}) collective-permute-start(bf16[2,1024,128]{2,1,0:T(8,128)(2,1)S(1)} %copy-done.8), channel_id=1, source_target_pairs={{4,0},{8,4},{12,8},{16,12},{20,16},{24,20},{28,24},{5,1},{9,5},{13... | collective-permute-start | bytes 1572872 | tf_op jit(solution)/shard_map/ppermute | solution.py:23
  77.2 0.3 convolution_add_fusion.2
  77.5 1.1 %collective-permute-done.10 = f32[256,128]{1,0:T(8,128)S(1)} collective-permute-done((f32[256,128]{1,0:T(8,128)S(1)}, f32[256,128]{1,0:T(8,128)S(1)}, u32[]{:S(2)}, u32[]{:S(2)}) %collective-permute-start.10) | collective-permute-done | bytes 131104 | tf_op jit(solution)/shard_map/ppermute | solution.py:17
  78.6 1.5 %collective-permute-start.11 = (f32[256,128]{1,0:T(8,128)S(1)}, f32[256,128]{1,0:T(8,128)S(1)}, u32[]{:S(2)}, u32[]{:S(2)}) collective-permute-start(f32[256,128]{1,0:T(8,128)S(1)} %add.86), channel_id=1, source_target_pairs={{0,2},{1,3},{2,0},{3,1},{4,6},{5,7},{6,4},{7,5},{8,10},{9,11},{10,... | collective-permute-start | bytes 393224 | tf_op jit(solution)/shard_map/ppermute | solution.py:17
  80.1 0.3 fusion.17
  80.4 3.8 %collective-permute-done.11 = f32[256,128]{1,0:T(8,128)S(1)} collective-permute-done((f32[256,128]{1,0:T(8,128)S(1)}, f32[256,128]{1,0:T(8,128)S(1)}, u32[]{:S(2)}, u32[]{:S(2)}) %collective-permute-start.11) | collective-permute-done | bytes 131104 | tf_op jit(solution)/shard_map/ppermute | solution.py:17
  84.2 0.7 fusion.47
  84.9 9.8 %collective-permute-done.7 = bf16[2,1024,128]{2,1,0:T(8,128)(2,1)S(1)} collective-permute-done((bf16[2,1024,128]{2,1,0:T(8,128)(2,1)S(1)}, bf16[2,1024,128]{2,1,0:T(8,128)(2,1)S(1)}, u32[]{:S(2)}, u32[]{:S(2)}) %collective-permute-start.7) | collective-permute-done | bytes 524320 | tf_op jit(solution)/shard_map/ppermute | solution.py:23
  94.7 4.1 %collective-permute-done.8 = bf16[2,1024,128]{2,1,0:T(8,128)(2,1)S(1)} collective-permute-done((bf16[2,1024,128]{2,1,0:T(8,128)(2,1)S(1)}, bf16[2,1024,128]{2,1,0:T(8,128)(2,1)S(1)}, u32[]{:S(2)}, u32[]{:S(2)}) %collective-permute-start.8) | collective-permute-done | bytes 524320 | tf_op jit(solution)/shard_map/ppermute | solution.py:23
  99.0 1.5 %fusion.10 = bf16[2,2048,128]{2,1,0:T(8,128)(2,1)} fusion(f32[2,1024,128]{2,1,0:T(8,128)S(1)} %get-tuple-element.33, f32[2,1024,128]{2,1,0:T(8,128)S(1)} %get-tuple-element.32, bf16[2,64,128]{2,1,0:T(8,128)(2,1)S(1)} %fusion.17, bf16[64,2048]{1,0:T(8,128)(2,1)S(1)} %copy-done), kind=kOutput, calls=%fused_computation.20 | convolution fusion | flops 68681728 | bytes 3440640 | tf_op jit(solution)/shard_map/rp,arc->apc/dot_general | solution.py:266
  (52 shorter events, 2.2 us)
Async XLA Ops:
  0.6 1.0 copy-start
  0.6 4.1 %copy-start.1 = (bf16[2,2048,128]{2,1,0:T(8,128)(2,1)S(1)}, bf16[2,2048,128]{2,1,0:T(8,128)(2,1)}, u32[]{:S(2)}) copy-start(bf16[2,2048,128]{2,1,0:T(8,128)(2,1)} %param.8) | copy-start | bytes 3145732
  0.7 13.5 %copy-start.7 = (s32[16,12]{1,0:T(8,128)S(1)}, s32[16,12]{1,0:T(8,128)}, u32[]{:S(2)}) copy-start(s32[16,12]{1,0:T(8,128)} %param.11) | copy-start | bytes 2308
  0.7 26.9 %copy-start.4 = (f32[3,64,64]{2,1,0:T(8,128)S(1)}, f32[3,64,64]{2,1,0:T(8,128)}, u32[]{:S(2)}) copy-start(f32[3,64,64]{2,1,0:T(8,128)} %param.15) | copy-start | bytes 147460
  3.1 9.4 %collective-permute-start.2 = (f32[2,64,128]{2,1,0:T(8,128)S(1)}, f32[2,64,128]{2,1,0:T(8,128)S(1)}, u32[]{:S(2)}, u32[]{:S(2)}) collective-permute-start(f32[2,64,128]{2,1,0:T(8,128)S(1)} %convolution_bitcast_fusion.2), channel_id=1, source_target_pairs={{0,4},{4,0},{8,12},{12,8},{16,20},{20,16},{24,28},{28,24},{1,5},{5... | collective-permute-start | bytes 196616 | tf_op jit(solution)/shard_map/ppermute | solution.py:17
  5.7 28.7 %collective-permute-start = (bf16[2,1024,128]{2,1,0:T(8,128)(2,1)}, bf16[2,1024,128]{2,1,0:T(8,128)(2,1)}, u32[]{:S(2)}, u32[]{:S(2)}) collective-permute-start(bf16[2,1024,128]{2,1,0:T(8,128)(2,1)} %get-tuple-element.36), channel_id=1, source_target_pairs={{0,4},{4,8},{8,12},{12,16},{16,20},{20,24},{24,28},{1,5},{5,9},{9,... | collective-permute-start | bytes 1572872 | tf_op jit(solution)/shard_map/ppermute | solution.py:23
  8.2 26.3 %collective-permute-start.1 = (bf16[2,1024,128]{2,1,0:T(8,128)(2,1)}, bf16[2,1024,128]{2,1,0:T(8,128)(2,1)}, u32[]{:S(2)}, u32[]{:S(2)}) collective-permute-start(bf16[2,1024,128]{2,1,0:T(8,128)(2,1)} %get-tuple-element.37), channel_id=1, source_target_pairs={{4,0},{8,4},{12,8},{16,12},{20,16},{24,20},{28,24},{5,1},{9,5},{13... | collective-permute-start | bytes 1572872 | tf_op jit(solution)/shard_map/ppermute | solution.py:23
  12.5 15.0 %collective-permute-start.3 = (f32[2,64,128]{2,1,0:T(8,128)S(1)}, f32[2,64,128]{2,1,0:T(8,128)S(1)}, u32[]{:S(2)}, u32[]{:S(2)}) collective-permute-start(f32[2,64,128]{2,1,0:T(8,128)S(1)} %add.68), channel_id=1, source_target_pairs={{0,8},{4,12},{8,0},{12,4},{16,24},{20,28},{24,16},{28,20},{1,9},{5... | collective-permute-start | bytes 196616 | tf_op jit(solution)/shard_map/ppermute | solution.py:17
  27.5 5.2 %collective-permute-start.4 = (f32[2,64,128]{2,1,0:T(8,128)S(1)}, f32[2,64,128]{2,1,0:T(8,128)S(1)}, u32[]{:S(2)}, u32[]{:S(2)}) collective-permute-start(f32[2,64,128]{2,1,0:T(8,128)S(1)} %add.70), channel_id=1, source_target_pairs={{0,16},{4,20},{8,24},{12,28},{16,0},{20,4},{24,8},{28,12},{1,17},{... | collective-permute-start | bytes 196616 | tf_op jit(solution)/shard_map/ppermute | solution.py:17
  37.2 6.5 %copy-start.6 = (bf16[128,128]{1,0:T(8,128)(2,1)S(1)}, bf16[128,128]{1,0:T(8,128)(2,1)}, u32[]{:S(2)}) copy-start(bf16[128,128]{1,0:T(8,128)(2,1)} %param.13) | copy-start | bytes 98308
  43.7 4.8 %copy-start.2 = (bf16[2,2048,128]{2,1,0:T(8,128)(2,1)S(1)}, bf16[2,2048,128]{2,1,0:T(8,128)(2,1)}, u32[]{:S(2)}) copy-start(bf16[2,2048,128]{2,1,0:T(8,128)(2,1)} %shard_map.111) | copy-start | bytes 3145732
  48.2 1.0 copy-start.5
  49.4 8.7 %collective-permute-start.5 = (f32[384,128]{1,0:T(8,128)S(1)}, f32[384,128]{1,0:T(8,128)S(1)}, u32[]{:S(2)}, u32[]{:S(2)}) collective-permute-start(f32[384,128]{1,0:T(8,128)S(1)} %pad_maximum_fusion.1), channel_id=1, source_target_pairs={{0,4},{4,0},{8,12},{12,8},{16,20},{20,16},{24,28},{28,24},{1,5},{5... | collective-permute-start | bytes 589832 | tf_op jit(solution)/shard_map/ppermute | solution.py:17
  58.1 8.4 %copy-start.3 = (f32[2,2048,128]{2,1,0:T(8,128)S(1)}, f32[2,2048,128]{2,1,0:T(8,128)}, u32[]{:S(2)}) copy-start(f32[2,2048,128]{2,1,0:T(8,128)} %get-tuple-element.22) | copy-start | bytes 6291460
  58.1 10.3 %collective-permute-start.6 = (f32[384,128]{1,0:T(8,128)S(1)}, f32[384,128]{1,0:T(8,128)S(1)}, u32[]{:S(2)}, u32[]{:S(2)}) collective-permute-start(f32[384,128]{1,0:T(8,128)S(1)} %pad_maximum_fusion.2), channel_id=1, source_target_pairs={{0,8},{4,12},{8,0},{12,4},{16,24},{20,28},{24,16},{28,20},{1,9},{5... | collective-permute-start | bytes 589832 | tf_op jit(solution)/shard_map/ppermute | solution.py:17
  66.5 2.5 %copy-start.9 = (bf16[2,1024,128]{2,1,0:T(8,128)(2,1)S(1)}, bf16[2,1024,128]{2,1,0:T(8,128)(2,1)}, u32[]{:S(2)}) copy-start(bf16[2,1024,128]{2,1,0:T(8,128)(2,1)} %get-tuple-element.29) | copy-start | bytes 1572868
  66.5 6.4 %copy-start.8 = (bf16[2,1024,128]{2,1,0:T(8,128)(2,1)S(1)}, bf16[2,1024,128]{2,1,0:T(8,128)(2,1)}, u32[]{:S(2)}) copy-start(bf16[2,1024,128]{2,1,0:T(8,128)(2,1)} %get-tuple-element.30) | copy-start | bytes 1572868
  68.5 8.6 %collective-permute-start.9 = (f32[384,128]{1,0:T(8,128)S(1)}, f32[384,128]{1,0:T(8,128)S(1)}, u32[]{:S(2)}, u32[]{:S(2)}) collective-permute-start(f32[384,128]{1,0:T(8,128)S(1)} %pad_maximum_fusion.3), channel_id=1, source_target_pairs={{0,16},{4,20},{8,24},{12,28},{16,0},{20,4},{24,8},{28,12},{1,17},{... | collective-permute-start | bytes 589832 | tf_op jit(solution)/shard_map/ppermute | solution.py:17
  69.0 25.7 %collective-permute-start.7 = (bf16[2,1024,128]{2,1,0:T(8,128)(2,1)S(1)}, bf16[2,1024,128]{2,1,0:T(8,128)(2,1)S(1)}, u32[]{:S(2)}, u32[]{:S(2)}) collective-permute-start(bf16[2,1024,128]{2,1,0:T(8,128)(2,1)S(1)} %copy-done.9), channel_id=1, source_target_pairs={{0,4},{4,8},{8,12},{12,16},{16,20},{20,24},{24,28},{1,5},{5,9},{9,... | collective-permute-start | bytes 1572872 | tf_op jit(solution)/shard_map/ppermute | solution.py:23
  73.0 25.9 %collective-permute-start.8 = (bf16[2,1024,128]{2,1,0:T(8,128)(2,1)S(1)}, bf16[2,1024,128]{2,1,0:T(8,128)(2,1)S(1)}, u32[]{:S(2)}, u32[]{:S(2)}) collective-permute-start(bf16[2,1024,128]{2,1,0:T(8,128)(2,1)S(1)} %copy-done.8), channel_id=1, source_target_pairs={{4,0},{8,4},{12,8},{16,12},{20,16},{24,20},{28,24},{5,1},{9,5},{13... | collective-permute-start | bytes 1572872 | tf_op jit(solution)/shard_map/ppermute | solution.py:23
  77.1 1.4 %collective-permute-start.10 = (f32[256,128]{1,0:T(8,128)S(1)}, f32[256,128]{1,0:T(8,128)S(1)}, u32[]{:S(2)}, u32[]{:S(2)}) collective-permute-start(f32[256,128]{1,0:T(8,128)S(1)} %slice_add_fusion), channel_id=1, source_target_pairs={{0,1},{1,0},{2,3},{3,2},{4,5},{5,4},{6,7},{7,6},{8,9},{9,8},{10,11... | collective-permute-start | bytes 393224 | tf_op jit(solution)/shard_map/ppermute | solution.py:17
  78.6 5.6 %collective-permute-start.11 = (f32[256,128]{1,0:T(8,128)S(1)}, f32[256,128]{1,0:T(8,128)S(1)}, u32[]{:S(2)}, u32[]{:S(2)}) collective-permute-start(f32[256,128]{1,0:T(8,128)S(1)} %add.86), channel_id=1, source_target_pairs={{0,2},{1,3},{2,0},{3,1},{4,6},{5,7},{6,4},{7,5},{8,10},{9,11},{10,... | collective-permute-start | bytes 393224 | tf_op jit(solution)/shard_map/ppermute | solution.py:17

commit v9 on v4

--- a/solution.py
+++ b/solution.py
@@ -9,7 +9,8 @@
 from jax.sharding import PartitionSpec as P
 
 HALO = 8
-TB = 4
+TB = 8
+BWD_TB = 4
 
 
 def partner(shard, axis, apart):
@@ -52,10 +53,28 @@
     return summed, rider, cover
 
 
-def near_fwd_kernel(cases, pairs, rows, ids_ref, kb_ref, ext_ref, out_ref):
+def near_fwd_kernel(cases, pairs, rows, ids_ref, kb_ref, prev_hbm, own_hbm, next_hbm, out_ref, ext_ref, sems):
     g = pl.program_id(0)
-    for tb in range(TB):
-        t = g * TB + tb
+    halo_points = prev_hbm.shape[1]
+    own_points = own_hbm.shape[1]
+
+    @pl.when(g == 0)
+    def _():
+        copies = [
+            pltpu.make_async_copy(prev_hbm, ext_ref.at[:, pl.ds(0, halo_points), :], sems.at[0]),
+            pltpu.make_async_copy(own_hbm, ext_ref.at[:, pl.ds(halo_points, own_points), :], sems.at[1]),
+            pltpu.make_async_copy(
+                next_hbm, ext_ref.at[:, pl.ds(halo_points + own_points, halo_points), :], sems.at[2]
+            ),
+        ]
+        for copy in copies:
+            copy.start()
+        for copy in copies:
+            copy.wait()
+
+    tbs = kb_ref.shape[0]
+    for tb in range(tbs):
+        t = g * tbs + tb
         lhs = jnp.concatenate([kb_ref[tb, k] for k in range(pairs)], axis=1)
         parts = []
         for k in range(pairs):
@@ -72,11 +91,13 @@
             )
 
 
-def near_forward(ids, kernel_blocks, extended):
-    cases, span_points, width = extended.shape
+def near_forward(ids, kernel_blocks, from_prev, features, from_next):
+    cases, points_here, width = features.shape
+    span_points = points_here + from_prev.shape[1] + from_next.shape[1]
     blocks_here, pairs, rows, _ = kernel_blocks.shape
     steps = blocks_here // TB
     flops = 2 * blocks_here * pairs * rows * rows * cases * width
+    hbm = pl.BlockSpec(memory_space=pl.ANY)
     return pl.pallas_call(
         functools.partial(near_fwd_kernel, cases, pairs, rows),
         out_shape=jax.ShapeDtypeStruct((cases, blocks_here * rows, width), jnp.bfloat16),
@@ -85,17 +106,23 @@
             grid=(steps,),
             in_specs=[
                 pl.BlockSpec((TB, pairs, rows, rows), lambda g, ids: (g, 0, 0, 0)),
-                pl.BlockSpec((cases, span_points, width), lambda g, ids: (0, 0, 0)),
+                hbm,
+                hbm,
+                hbm,
             ],
             out_specs=pl.BlockSpec((cases, TB * rows, width), lambda g, ids: (0, g, 0)),
+            scratch_shapes=[
+                pltpu.VMEM((cases, span_points, width), jnp.bfloat16),
+                pltpu.SemaphoreType.DMA((3,)),
+            ],
         ),
         compiler_params=pltpu.CompilerParams(dimension_semantics=("arbitrary",)),
         cost_estimate=pl.CostEstimate(
             flops=flops,
             transcendentals=0,
-            bytes_accessed=kernel_blocks.size * 2 + extended.size * 2 + cases * blocks_here * rows * width * 2,
-        ),
-    )(ids, kernel_blocks, extended)
+            bytes_accessed=kernel_blocks.size * 2 + cases * span_points * width * 2 + cases * blocks_here * rows * width * 2,
+        ),
+    )(ids, kernel_blocks, from_prev, features, from_next)
 
 
 def near_bwd_kernel(cases, pairs, rows, steps, ids_ref, kb_ref, back_ref, mid_ref, lo_ref, hi_ref, acc_ref):
@@ -106,18 +133,16 @@
         acc_ref[...] = jnp.zeros(acc_ref.shape, acc_ref.dtype)
 
     width = back_ref.shape[2]
-    for tb in range(TB):
-        t = g * TB + tb
-        lhs = jnp.concatenate([kb_ref[tb, k] for k in range(pairs)], axis=1)
+    for tb in range(BWD_TB):
+        t = g * BWD_TB + tb
         rhs = jnp.concatenate(
             [back_ref[c, pl.ds(tb * rows, rows), :] for c in range(cases)], axis=1
         )
-        res = lax.dot_general(
-            lhs, rhs, (((0,), (0,)), ((), ())), preferred_element_type=jnp.float32
-        )
         for k in range(pairs):
             start = pl.multiple_of(ids_ref[t * pairs + k] * rows, rows)
-            piece = res[k * rows : (k + 1) * rows]
+            piece = lax.dot_general(
+                kb_ref[tb, k], rhs, (((0,), (0,)), ((), ())), preferred_element_type=jnp.float32
+            )
             for c in range(cases):
                 acc_ref[c, pl.ds(start, rows), :] += piece[:, c * width : (c + 1) * width]
 
@@ -133,7 +158,7 @@
 def near_backward(ids, kernel_blocks, back_near, halo_points):
     cases, points_here, width = back_near.shape
     blocks_here, pairs, rows, _ = kernel_blocks.shape
-    steps = blocks_here // TB
+    steps = blocks_here // BWD_TB
     span_points = points_here + 2 * halo_points
     flops = 2 * blocks_here * pairs * rows * rows * cases * width
     return pl.pallas_call(
@@ -147,8 +172,8 @@
             num_scalar_prefetch=1,
             grid=(steps,),
             in_specs=[
-                pl.BlockSpec((TB, pairs, rows, rows), lambda g, ids: (g, 0, 0, 0)),
-                pl.BlockSpec((cases, TB * rows, width), lambda g, ids: (0, g, 0)),
+                pl.BlockSpec((BWD_TB, pairs, rows, rows), lambda g, ids: (g, 0, 0, 0)),
+                pl.BlockSpec((cases, BWD_TB * rows, width), lambda g, ids: (0, g, 0)),
             ],
             out_specs=[
                 pl.BlockSpec((cases, points_here, width), lambda g, ids: (0, 0, 0)),
@@ -185,12 +210,11 @@
     tail = features[:, points_here - halo_points :]
     from_prev = shifted(tail, "leaf", 1)
     from_next = shifted(head, "leaf", -1)
-    extended = jnp.concatenate([from_prev, features, from_next], axis=1)
     local_ids = jnp.clip(
         near_pairs - (position * blocks_here - HALO), 0, span_blocks - 1
     ).reshape(-1).astype(jnp.int32)
 
-    near_bf = near_forward(local_ids, kernel_blocks, extended)
+    near_bf = near_forward(local_ids, kernel_blocks, from_prev, features, from_next)
 
     summary = jnp.einsum("rp,apc->arc", leaf_basis, features, preferred_element_type=jnp.float32)
     expansion, _ = expand(summary, translations, False)

time: 100 us -> 96.3 us (0.963); the launches traced: 98.3 us -> 95.9 us
  other arithmetic: 3.04 us -> 0.37 us
  local copies, waits for them, and re-layouts: 3.33 us -> 4.93 us
    concatenate x1 -> x0, other arithmetic: 2.67 us -> none  [on_device(): extended = jnp.concatenate([from_prev, features, from_next], axis=1)]
    ppermute x4, starting transfers between devices: 14.6 us -> 12.6 us  [shifted(): lax.ppermute(value, axis, [(source, source + steps) for source in range(l...]
    ppermute x8, waiting for transfers between devices: 27.7 us -> 25.7 us  [partner(): lax.ppermute(shard, axis, [(i, i ^ 1 << apart) for i in range(lax.axis_si...]
    ppermute x8, starting transfers between devices: 5.86 us -> 7.48 us  [partner(): lax.ppermute(shard, axis, [(i, i ^ 1 << apart) for i in range(lax.axis_si...]
    unnamed x20 -> x24, local copies, waits for them, and re-layouts: 0.95 us -> 2.56 us
    ppermute x4, waiting for transfers between devices: 13.3 us -> 14.7 us  [shifted(): lax.ppermute(value, axis, [(source, source + steps) for source in range(l...]
  transfers between devices with their start and end apart: 12 -> 12, of which waited for: 7 -> 9; matrix products, arithmetic and copies ran while one was open for 7% -> 7% of each run, Pallas kernels for 10% -> 9%
where the time goes in v9:
time: 96.3 us; the launch traced here: 95.9 us
  waiting for transfers between devices  40.4 us (42%)
  starting transfers between devices  20 us (21%)
  Pallas kernels  16.4 us (17%)
  matrix products  12.7 us (13%)
  local copies, waits for them, and re-layouts  4.93 us (5%)
  between operations  0.97 us (1%)
    ppermute x8, waiting for transfers between devices, partner(): lax.ppermute(shard, axis, [(i, i ^ 1 << apart) for i in range(lax.axis_si...  25.7 us
    ppermute x4, waiting for transfers between devices, shifted(): lax.ppermute(value, axis, [(source, source + steps) for source in range(l...  14.7 us
    ppermute x4, starting transfers between devices, shifted(): lax.ppermute(value, axis, [(source, source + steps) for source in range(l...  12.6 us
    pallas_call x1, Pallas kernels, near_backward(): pl.pallas_call(functools.partial(near_bwd_kernel, cases, pairs, rows, ste...  8.93 us
    pallas_call x1, Pallas kernels, near_forward(): pl.pallas_call(functools.partial(near_fwd_kernel, cases, pairs, rows), ou...  7.49 us
    ppermute x8, starting transfers between devices, partner(): lax.ppermute(shard, axis, [(i, i ^ 1 << apart) for i in range(lax.axis_si...  7.48 us
    dot_general x1, matrix products, on_device(): jnp.einsum('apc,cd->apd', near_bf, w_near, preferred_element_type=jnp.flo...  4.55 us
    unnamed x24, local copies, waits for them, and re-layouts  2.56 us
  transfers between devices with their start and end apart: 12, of which 9 were waited for; matrix products, arithmetic and copies ran while one was open for 7% of the time, Pallas kernels for 9%

profile of v9, /device:TPU:16, one launch (start us, length us, event | category | flops | bytes accessed | tf_op | source)
XLA Modules:
  0.0 95.9 jit_solution(3308478504938800441)
XLA Ops:
  0.7 0.9 copy-done
  1.6 1.5 %convolution_bitcast_fusion.2 = f32[2,64,128]{2,1,0:T(8,128)S(1)} fusion(bf16[2,2048,128]{2,1,0:T(8,128)(2,1)} %own_hbm.1, bf16[64,2048]{1,0:T(8,128)(2,1)S(1)} %copy-done), kind=kOutput, calls=%fused_computation.21 | convolution fusion | flops 67108864 | bytes 1376256 | tf_op jit(solution)/shard_map/rp,apc->arc/dot_general | solution.py:219
  3.1 1.6 %collective-permute-start.2 = (f32[2,64,128]{2,1,0:T(8,128)S(1)}, f32[2,64,128]{2,1,0:T(8,128)S(1)}, u32[]{:S(2)}, u32[]{:S(2)}) collective-permute-start(f32[2,64,128]{2,1,0:T(8,128)S(1)} %convolution_bitcast_fusion.2), channel_id=1, source_target_pairs={{0,4},{4,0},{8,12},{12,8},{16,20},{20,16},{24,28},{28,24},{1,5},{5... | collective-permute-start | bytes 196616 | tf_op jit(solution)/shard_map/ppermute | solution.py:17
  4.7 1.0 %fusion.46 = (bf16[2,1024,128]{2,1,0:T(8,128)(2,1)}, bf16[2,1024,128]{2,1,0:T(8,128)(2,1)}) fusion(bf16[2,2048,128]{2,1,0:T(8,128)(2,1)S(1)} %copy-done.1), kind=kLoop, calls=%fused_computation.70 | loop fusion | bytes 2097152 | tf_op jit(solution)/shard_map/slice | solution.py:209
  5.7 2.3 %collective-permute-start.1 = (bf16[2,1024,128]{2,1,0:T(8,128)(2,1)}, bf16[2,1024,128]{2,1,0:T(8,128)(2,1)S(1)}, u32[]{:S(2)}, u32[]{:S(2)}) collective-permute-start(bf16[2,1024,128]{2,1,0:T(8,128)(2,1)} %get-tuple-element.30), channel_id=1, source_target_pairs={{4,0},{8,4},{12,8},{16,12},{20,16},{24,20},{28,24},{5,1},{9,5},{13... | collective-permute-start | bytes 1572872 | tf_op jit(solution)/shard_map/ppermute | solution.py:23
  8.0 3.5 %collective-permute-start = (bf16[2,1024,128]{2,1,0:T(8,128)(2,1)}, bf16[2,1024,128]{2,1,0:T(8,128)(2,1)S(1)}, u32[]{:S(2)}, u32[]{:S(2)}) collective-permute-start(bf16[2,1024,128]{2,1,0:T(8,128)(2,1)} %get-tuple-element.31), channel_id=1, source_target_pairs={{0,4},{4,8},{8,12},{12,16},{16,20},{20,24},{24,28},{1,5},{5,9},{9,... | collective-permute-start | bytes 1572872 | tf_op jit(solution)/shard_map/ppermute | solution.py:23
  11.6 1.7 %collective-permute-start.3 = (f32[2,64,128]{2,1,0:T(8,128)S(1)}, f32[2,64,128]{2,1,0:T(8,128)S(1)}, u32[]{:S(2)}, u32[]{:S(2)}) collective-permute-start(f32[2,64,128]{2,1,0:T(8,128)S(1)} %add.65), channel_id=1, source_target_pairs={{0,8},{4,12},{8,0},{12,4},{16,24},{20,28},{24,16},{28,20},{1,9},{5... | collective-permute-start | bytes 196616 | tf_op jit(solution)/shard_map/ppermute | solution.py:17
  13.3 0.7 reshape.29.ids_ref
  14.0 9.2 %collective-permute-done.3 = f32[2,64,128]{2,1,0:T(8,128)S(1)} collective-permute-done((f32[2,64,128]{2,1,0:T(8,128)S(1)}, f32[2,64,128]{2,1,0:T(8,128)S(1)}, u32[]{:S(2)}, u32[]{:S(2)}) %collective-permute-start.3) | collective-permute-done | bytes 65568 | tf_op jit(solution)/shard_map/ppermute | solution.py:17
  23.5 4.9 %collective-permute-done.4 = f32[2,64,128]{2,1,0:T(8,128)S(1)} collective-permute-done((f32[2,64,128]{2,1,0:T(8,128)S(1)}, f32[2,64,128]{2,1,0:T(8,128)S(1)}, u32[]{:S(2)}, u32[]{:S(2)}) %collective-permute-start.4) | collective-permute-done | bytes 65568 | tf_op jit(solution)/shard_map/ppermute | solution.py:17
  28.8 1.3 %convolution_bitcast_fusion.1 = f32[2,2048,128]{2,1,0:T(8,128)S(1)} fusion(bf16[2,64,128]{2,1,0:T(8,128)(2,1)S(1)} %fusion.18, bf16[64,2048]{1,0:T(8,128)(2,1)S(1)} %copy-done, bf16[128,128]{1,0:T(8,128)(2,1)} %param.14), kind=kOutput, calls=%fused_computation.3 | convolution fusion | flops 71319552 | bytes 2424832 | tf_op jit(solution)/shard_map/rp,ard->apd/dot_general | solution.py:225
  30.1 2.3 %collective-permute-done.1.next_hbm = bf16[2,1024,128]{2,1,0:T(8,128)(2,1)S(1)} collective-permute-done((bf16[2,1024,128]{2,1,0:T(8,128)(2,1)}, bf16[2,1024,128]{2,1,0:T(8,128)(2,1)S(1)}, u32[]{:S(2)}, u32[]{:S(2)}) %collective-permute-start.1) | collective-permute-done | bytes 524320 | tf_op jit(solution)/shard_map/ppermute | solution.py:23
  32.5 0.8 copy-done.4
  33.3 0.8 copy-done.5
  34.1 7.5 %shard_map.111 = bf16[2,2048,128]{2,1,0:T(8,128)(2,1)} custom-call(s32[192]{0:T(256)} %reshape.29.ids_ref, bf16[16,12,128,128]{3,2,1,0:T(8,128)(2,1)} %kb_ref.3, bf16[2,1024,128]{2,1,0:T(8,128)(2,1)} %copy-done.5, bf16[2,2048,128]{2,1,0:T(8,128)(2,1)} %own_hbm.1, bf16[2,1024,128]{2,1,0:T(8,128)(2,1)} %copy-done.4), custom_call_target="tpu_custom_call" | custom-call | flops 1610612736 | bytes 9437184 | tf_op jit(solution)/shard_map/pallas_call | solution.py:101
  41.6 4.6 %fusion.2 = (bf16[2,2048,128]{2,1,0:T(8,128)(2,1)S(1)}, bf16[2,2048,128]{2,1,0:T(8,128)(2,1)}) fusion(bf16[2,2048,128]{2,1,0:T(8,128)(2,1)} %param.9, f32[2,2048,128]{2,1,0:T(8,128)S(1)} %convolution_bitcast_fusion.1, bf16[2,2048,128]{2,1,0:T(8,128)(2,1)} %shard_map.111, bf16[128,128]{1,0:T(8,128)(2,1)} %param.13), kind=kOutput, calls=%fused_computation.10 | convolution fusion | flops 146800640 | bytes 6324224 | tf_op jit(solution)/shard_map/apc,cd->apd/dot_general | solution.py:227
  46.1 0.5 fusion.12
  47.3 0.6 collective-permute-start.5
  47.9 1.4 %convolution_convert_fusion.back_ref = bf16[2,2048,128]{2,1,0:T(8,128)(2,1)} fusion(bf16[2,2048,128]{2,1,0:T(8,128)(2,1)S(1)} %get-tuple-element.28, bf16[128,128]{1,0:T(8,128)(2,1)S(1)} %copy-done.8), kind=kOutput, calls=%fused_computation.7 | convolution fusion | flops 134742016 | bytes 2129920 | tf_op jit(solution)/shard_map/apc,dc->apd/dot_general | solution.py:235
  49.4 8.9 %shard_map.112 = (f32[2,2048,128]{2,1,0:T(8,128)}, bf16[2,1024,128]{2,1,0:T(8,128)(2,1)}, bf16[2,1024,128]{2,1,0:T(8,128)(2,1)}) custom-call(s32[192]{0:T(256)} %reshape.29.ids_ref, bf16[16,12,128,128]{3,2,1,0:T(8,128)(2,1)} %kb_ref.3, bf16[2,2048,128]{2,1,0:T(8,128)(2,1)} %convolution_convert_fusion.back_ref), custom_call_target="tpu_custom_call" | custom-call | flops 1610612736 | bytes 11534336 | tf_op jit(solution)/shard_map/pallas_call | solution.py:164
  58.4 1.7 %collective-permute-start.6 = (f32[384,128]{1,0:T(8,128)S(1)}, f32[384,128]{1,0:T(8,128)S(1)}, u32[]{:S(2)}, u32[]{:S(2)}) collective-permute-start(f32[384,128]{1,0:T(8,128)S(1)} %pad_maximum_fusion.1), channel_id=1, source_target_pairs={{0,8},{4,12},{8,0},{12,4},{16,24},{20,28},{24,16},{28,20},{1,9},{5... | collective-permute-start | bytes 589832 | tf_op jit(solution)/shard_map/ppermute | solution.py:17
  60.1 4.9 %collective-permute-done.6 = f32[384,128]{1,0:T(8,128)S(1)} collective-permute-done((f32[384,128]{1,0:T(8,128)S(1)}, f32[384,128]{1,0:T(8,128)S(1)}, u32[]{:S(2)}, u32[]{:S(2)}) %collective-permute-start.6) | collective-permute-done | bytes 196640 | tf_op jit(solution)/shard_map/ppermute | solution.py:17
  65.6 2.3 %collective-permute-start.7 = (bf16[2,1024,128]{2,1,0:T(8,128)(2,1)S(1)}, bf16[2,1024,128]{2,1,0:T(8,128)(2,1)S(1)}, u32[]{:S(2)}, u32[]{:S(2)}) collective-permute-start(bf16[2,1024,128]{2,1,0:T(8,128)(2,1)S(1)} %copy-done.11), channel_id=1, source_target_pairs={{0,4},{4,8},{8,12},{12,16},{16,20},{20,24},{24,28},{1,5},{5,9},{9,... | collective-permute-start | bytes 1572872 | tf_op jit(solution)/shard_map/ppermute | solution.py:23
  67.9 4.5 %collective-permute-start.8 = (bf16[2,1024,128]{2,1,0:T(8,128)(2,1)S(1)}, bf16[2,1024,128]{2,1,0:T(8,128)(2,1)S(1)}, u32[]{:S(2)}, u32[]{:S(2)}) collective-permute-start(bf16[2,1024,128]{2,1,0:T(8,128)(2,1)S(1)} %copy-done.10), channel_id=1, source_target_pairs={{4,0},{8,4},{12,8},{16,12},{20,16},{24,20},{28,24},{5,1},{9,5},{13... | collective-permute-start | bytes 1572872 | tf_op jit(solution)/shard_map/ppermute | solution.py:23
  72.4 1.7 %collective-permute-done.9 = f32[384,128]{1,0:T(8,128)S(1)} collective-permute-done((f32[384,128]{1,0:T(8,128)S(1)}, f32[384,128]{1,0:T(8,128)S(1)}, u32[]{:S(2)}, u32[]{:S(2)}) %collective-permute-start.9) | collective-permute-done | bytes 196640 | tf_op jit(solution)/shard_map/ppermute | solution.py:17
  74.4 1.1 %collective-permute-done.10 = f32[256,128]{1,0:T(8,128)S(1)} collective-permute-done((f32[256,128]{1,0:T(8,128)S(1)}, f32[256,128]{1,0:T(8,128)S(1)}, u32[]{:S(2)}, u32[]{:S(2)}) %collective-permute-start.10) | collective-permute-done | bytes 131104 | tf_op jit(solution)/shard_map/ppermute | solution.py:17
  75.5 1.4 %collective-permute-start.11 = (f32[256,128]{1,0:T(8,128)S(1)}, f32[256,128]{1,0:T(8,128)S(1)}, u32[]{:S(2)}, u32[]{:S(2)}) collective-permute-start(f32[256,128]{1,0:T(8,128)S(1)} %add.82), channel_id=1, source_target_pairs={{0,2},{1,3},{2,0},{3,1},{4,6},{5,7},{6,4},{7,5},{8,10},{9,11},{10,... | collective-permute-start | bytes 393224 | tf_op jit(solution)/shard_map/ppermute | solution.py:17
  77.2 3.9 %collective-permute-done.11 = f32[256,128]{1,0:T(8,128)S(1)} collective-permute-done((f32[256,128]{1,0:T(8,128)S(1)}, f32[256,128]{1,0:T(8,128)S(1)}, u32[]{:S(2)}, u32[]{:S(2)}) %collective-permute-start.11) | collective-permute-done | bytes 131104 | tf_op jit(solution)/shard_map/ppermute | solution.py:17
  81.1 0.7 fusion.47
  81.8 7.3 %collective-permute-done.7 = bf16[2,1024,128]{2,1,0:T(8,128)(2,1)S(1)} collective-permute-done((bf16[2,1024,128]{2,1,0:T(8,128)(2,1)S(1)}, bf16[2,1024,128]{2,1,0:T(8,128)(2,1)S(1)}, u32[]{:S(2)}, u32[]{:S(2)}) %collective-permute-start.7) | collective-permute-done | bytes 524320 | tf_op jit(solution)/shard_map/ppermute | solution.py:23
  89.1 5.2 %collective-permute-done.8 = bf16[2,1024,128]{2,1,0:T(8,128)(2,1)S(1)} collective-permute-done((bf16[2,1024,128]{2,1,0:T(8,128)(2,1)S(1)}, bf16[2,1024,128]{2,1,0:T(8,128)(2,1)S(1)}, u32[]{:S(2)}, u32[]{:S(2)}) %collective-permute-start.8) | collective-permute-done | bytes 524320 | tf_op jit(solution)/shard_map/ppermute | solution.py:23
  94.4 1.5 %fusion.10 = bf16[2,2048,128]{2,1,0:T(8,128)(2,1)} fusion(f32[2,1024,128]{2,1,0:T(8,128)S(1)} %get-tuple-element.27, f32[2,1024,128]{2,1,0:T(8,128)S(1)} %get-tuple-element.26, bf16[2,64,128]{2,1,0:T(8,128)(2,1)S(1)} %fusion.17, bf16[64,2048]{1,0:T(8,128)(2,1)S(1)} %copy-done), kind=kOutput, calls=%fused_computation.19 | convolution fusion | flops 68681728 | bytes 3440640 | tf_op jit(solution)/shard_map/rp,arc->apc/dot_general | solution.py:256
  (53 shorter events, 2.9 us)
Async XLA Ops:
  0.6 1.0 copy-start
  0.6 4.1 %copy-start.1 = (bf16[2,2048,128]{2,1,0:T(8,128)(2,1)S(1)}, bf16[2,2048,128]{2,1,0:T(8,128)(2,1)}, u32[]{:S(2)}) copy-start(bf16[2,2048,128]{2,1,0:T(8,128)(2,1)} %own_hbm.1) | copy-start | bytes 3145732
  0.7 12.6 %copy-start.9 = (s32[16,12]{1,0:T(8,128)S(1)}, s32[16,12]{1,0:T(8,128)}, u32[]{:S(2)}) copy-start(s32[16,12]{1,0:T(8,128)} %param.11) | copy-start | bytes 2308
  0.7 22.6 %copy-start.6 = (f32[3,64,64]{2,1,0:T(8,128)S(1)}, f32[3,64,64]{2,1,0:T(8,128)}, u32[]{:S(2)}) copy-start(f32[3,64,64]{2,1,0:T(8,128)} %param.15) | copy-start | bytes 147460
  3.1 8.5 %collective-permute-start.2 = (f32[2,64,128]{2,1,0:T(8,128)S(1)}, f32[2,64,128]{2,1,0:T(8,128)S(1)}, u32[]{:S(2)}, u32[]{:S(2)}) collective-permute-start(f32[2,64,128]{2,1,0:T(8,128)S(1)} %convolution_bitcast_fusion.2), channel_id=1, source_target_pairs={{0,4},{4,0},{8,12},{12,8},{16,20},{20,16},{24,28},{28,24},{1,5},{5... | collective-permute-start | bytes 196616 | tf_op jit(solution)/shard_map/ppermute | solution.py:17
  5.7 26.7 %collective-permute-start.1 = (bf16[2,1024,128]{2,1,0:T(8,128)(2,1)}, bf16[2,1024,128]{2,1,0:T(8,128)(2,1)S(1)}, u32[]{:S(2)}, u32[]{:S(2)}) collective-permute-start(bf16[2,1024,128]{2,1,0:T(8,128)(2,1)} %get-tuple-element.30), channel_id=1, source_target_pairs={{4,0},{8,4},{12,8},{16,12},{20,16},{24,20},{28,24},{5,1},{9,5},{13... | collective-permute-start | bytes 1572872 | tf_op jit(solution)/shard_map/ppermute | solution.py:23
  8.0 24.4 %collective-permute-start = (bf16[2,1024,128]{2,1,0:T(8,128)(2,1)}, bf16[2,1024,128]{2,1,0:T(8,128)(2,1)S(1)}, u32[]{:S(2)}, u32[]{:S(2)}) collective-permute-start(bf16[2,1024,128]{2,1,0:T(8,128)(2,1)} %get-tuple-element.31), channel_id=1, source_target_pairs={{0,4},{4,8},{8,12},{12,16},{16,20},{20,24},{24,28},{1,5},{5,9},{9,... | collective-permute-start | bytes 1572872 | tf_op jit(solution)/shard_map/ppermute | solution.py:23
  11.6 11.5 %collective-permute-start.3 = (f32[2,64,128]{2,1,0:T(8,128)S(1)}, f32[2,64,128]{2,1,0:T(8,128)S(1)}, u32[]{:S(2)}, u32[]{:S(2)}) collective-permute-start(f32[2,64,128]{2,1,0:T(8,128)S(1)} %add.65), channel_id=1, source_target_pairs={{0,8},{4,12},{8,0},{12,4},{16,24},{20,28},{24,16},{28,20},{1,9},{5... | collective-permute-start | bytes 196616 | tf_op jit(solution)/shard_map/ppermute | solution.py:17
  23.2 5.2 %collective-permute-start.4 = (f32[2,64,128]{2,1,0:T(8,128)S(1)}, f32[2,64,128]{2,1,0:T(8,128)S(1)}, u32[]{:S(2)}, u32[]{:S(2)}) collective-permute-start(f32[2,64,128]{2,1,0:T(8,128)S(1)} %add.67), channel_id=1, source_target_pairs={{0,16},{4,20},{8,24},{12,28},{16,0},{20,4},{24,8},{28,12},{1,17},{... | collective-permute-start | bytes 196616 | tf_op jit(solution)/shard_map/ppermute | solution.py:17
  32.5 0.8 copy-start.4
  33.3 0.8 copy-start.5
  41.5 4.6 %copy-start.2 = (bf16[2,2048,128]{2,1,0:T(8,128)(2,1)S(1)}, bf16[2,2048,128]{2,1,0:T(8,128)(2,1)}, u32[]{:S(2)}) copy-start(bf16[2,2048,128]{2,1,0:T(8,128)(2,1)} %shard_map.111) | copy-start | bytes 3145732
  46.1 1.0 %copy-start.7 = (bf16[128,128]{1,0:T(8,128)(2,1)S(1)}, bf16[128,128]{1,0:T(8,128)(2,1)}, u32[]{:S(2)}) copy-start(bf16[128,128]{1,0:T(8,128)(2,1)} %param.14) | copy-start | bytes 98308
  46.1 1.8 %copy-start.8 = (bf16[128,128]{1,0:T(8,128)(2,1)S(1)}, bf16[128,128]{1,0:T(8,128)(2,1)}, u32[]{:S(2)}) copy-start(bf16[128,128]{1,0:T(8,128)(2,1)} %param.13) | copy-start | bytes 98308
  47.3 11.0 %collective-permute-start.5 = (f32[384,128]{1,0:T(8,128)S(1)}, f32[384,128]{1,0:T(8,128)S(1)}, u32[]{:S(2)}, u32[]{:S(2)}) collective-permute-start(f32[384,128]{1,0:T(8,128)S(1)} %pad_maximum_fusion), channel_id=1, source_target_pairs={{0,4},{4,0},{8,12},{12,8},{16,20},{20,16},{24,28},{28,24},{1,5},{5... | collective-permute-start | bytes 589832 | tf_op jit(solution)/shard_map/ppermute | solution.py:17
  58.3 7.3 %copy-start.11 = (bf16[2,1024,128]{2,1,0:T(8,128)(2,1)S(1)}, bf16[2,1024,128]{2,1,0:T(8,128)(2,1)}, u32[]{:S(2)}) copy-start(bf16[2,1024,128]{2,1,0:T(8,128)(2,1)} %get-tuple-element.23) | copy-start | bytes 1572868
  58.3 9.6 %copy-start.10 = (bf16[2,1024,128]{2,1,0:T(8,128)(2,1)S(1)}, bf16[2,1024,128]{2,1,0:T(8,128)(2,1)}, u32[]{:S(2)}) copy-start(bf16[2,1024,128]{2,1,0:T(8,128)(2,1)} %get-tuple-element.24) | copy-start | bytes 1572868
  58.3 35.9 %copy-start.3 = (f32[2,2048,128]{2,1,0:T(8,128)S(1)}, f32[2,2048,128]{2,1,0:T(8,128)}, u32[]{:S(2)}) copy-start(f32[2,2048,128]{2,1,0:T(8,128)} %get-tuple-element.22) | copy-start | bytes 6291460
  58.4 6.6 %collective-permute-start.6 = (f32[384,128]{1,0:T(8,128)S(1)}, f32[384,128]{1,0:T(8,128)S(1)}, u32[]{:S(2)}, u32[]{:S(2)}) collective-permute-start(f32[384,128]{1,0:T(8,128)S(1)} %pad_maximum_fusion.1), channel_id=1, source_target_pairs={{0,8},{4,12},{8,0},{12,4},{16,24},{20,28},{24,16},{28,20},{1,9},{5... | collective-permute-start | bytes 589832 | tf_op jit(solution)/shard_map/ppermute | solution.py:17
  65.1 9.0 %collective-permute-start.9 = (f32[384,128]{1,0:T(8,128)S(1)}, f32[384,128]{1,0:T(8,128)S(1)}, u32[]{:S(2)}, u32[]{:S(2)}) collective-permute-start(f32[384,128]{1,0:T(8,128)S(1)} %pad_maximum_fusion.2), channel_id=1, source_target_pairs={{0,16},{4,20},{8,24},{12,28},{16,0},{20,4},{24,8},{28,12},{1,17},{... | collective-permute-start | bytes 589832 | tf_op jit(solution)/shard_map/ppermute | solution.py:17
  65.6 23.4 %collective-permute-start.7 = (bf16[2,1024,128]{2,1,0:T(8,128)(2,1)S(1)}, bf16[2,1024,128]{2,1,0:T(8,128)(2,1)S(1)}, u32[]{:S(2)}, u32[]{:S(2)}) collective-permute-start(bf16[2,1024,128]{2,1,0:T(8,128)(2,1)S(1)} %copy-done.11), channel_id=1, source_target_pairs={{0,4},{4,8},{8,12},{12,16},{16,20},{20,24},{24,28},{1,5},{5,9},{9,... | collective-permute-start | bytes 1572872 | tf_op jit(solution)/shard_map/ppermute | solution.py:23
  67.9 26.3 %collective-permute-start.8 = (bf16[2,1024,128]{2,1,0:T(8,128)(2,1)S(1)}, bf16[2,1024,128]{2,1,0:T(8,128)(2,1)S(1)}, u32[]{:S(2)}, u32[]{:S(2)}) collective-permute-start(bf16[2,1024,128]{2,1,0:T(8,128)(2,1)S(1)} %copy-done.10), channel_id=1, source_target_pairs={{4,0},{8,4},{12,8},{16,12},{20,16},{24,20},{28,24},{5,1},{9,5},{13... | collective-permute-start | bytes 1572872 | tf_op jit(solution)/shard_map/ppermute | solution.py:23
  74.1 1.4 %collective-permute-start.10 = (f32[256,128]{1,0:T(8,128)S(1)}, f32[256,128]{1,0:T(8,128)S(1)}, u32[]{:S(2)}, u32[]{:S(2)}) collective-permute-start(f32[256,128]{1,0:T(8,128)S(1)} %slice_add_fusion), channel_id=1, source_target_pairs={{0,1},{1,0},{2,3},{3,2},{4,5},{5,4},{6,7},{7,6},{8,9},{9,8},{10,11... | collective-permute-start | bytes 393224 | tf_op jit(solution)/shard_map/ppermute | solution.py:17
  75.5 5.6 %collective-permute-start.11 = (f32[256,128]{1,0:T(8,128)S(1)}, f32[256,128]{1,0:T(8,128)S(1)}, u32[]{:S(2)}, u32[]{:S(2)}) collective-permute-start(f32[256,128]{1,0:T(8,128)S(1)} %add.82), channel_id=1, source_target_pairs={{0,2},{1,3},{2,0},{3,1},{4,6},{5,7},{6,4},{7,5},{8,10},{9,11},{10,... | collective-permute-start | bytes 393224 | tf_op jit(solution)/shard_map/ppermute | solution.py:17

commit v10 on v9

--- a/solution.py
+++ b/solution.py
@@ -53,7 +53,10 @@
     return summed, rider, cover
 
 
-def near_fwd_kernel(cases, pairs, rows, ids_ref, kb_ref, prev_hbm, own_hbm, next_hbm, out_ref, ext_ref, sems):
+def near_fwd_kernel(
+    cases, pairs, rows, ids_ref, kb_ref, prev_hbm, own_hbm, next_hbm, basis_ref, coeff_ref,
+    w_ref, cot_ref, near_ref, out_ref, slope_ref, back_ref, ext_ref, sems,
+):
     g = pl.program_id(0)
     halo_points = prev_hbm.shape[1]
     own_points = own_hbm.shape[1]
@@ -73,6 +76,7 @@
             copy.wait()
 
     tbs = kb_ref.shape[0]
+    w = w_ref[...]
     for tb in range(tbs):
         t = g * tbs + tb
         lhs = jnp.concatenate([kb_ref[tb, k] for k in range(pairs)], axis=1)
@@ -85,22 +89,37 @@
         rhs = jnp.concatenate(parts, axis=0)
         acc = jnp.dot(lhs, rhs, preferred_element_type=jnp.float32)
         width = acc.shape[1] // cases
+        basis = basis_ref[:, pl.ds(tb * rows, rows)]
+        here = pl.ds(tb * rows, rows)
         for c in range(cases):
-            out_ref[c, pl.ds(tb * rows, rows), :] = acc[:, c * width : (c + 1) * width].astype(
-                out_ref.dtype
+            near = acc[:, c * width : (c + 1) * width].astype(jnp.bfloat16)
+            near_ref[c, here, :] = near
+            far = lax.dot_general(
+                basis, coeff_ref[c], (((0,), (0,)), ((), ())), preferred_element_type=jnp.float32
             )
-
-
-def near_forward(ids, kernel_blocks, from_prev, features, from_next):
+            mixed = jnp.dot(near, w, preferred_element_type=jnp.float32) + far
+            gelu_value, pullback = jax.vjp(jax.nn.gelu, mixed)
+            out_ref[c, here, :] = gelu_value.astype(out_ref.dtype)
+            slope = pullback(cot_ref[c, here, :].astype(jnp.float32))[0].astype(jnp.bfloat16)
+            slope_ref[c, here, :] = slope
+            back_ref[c, here, :] = lax.dot_general(
+                slope, w, (((1,), (1,)), ((), ())), preferred_element_type=jnp.float32
+            ).astype(back_ref.dtype)
+
+
+def near_forward(ids, kernel_blocks, from_prev, features, from_next, leaf_basis, far_coeff, w_near, cotangent):
     cases, points_here, width = features.shape
     span_points = points_here + from_prev.shape[1] + from_next.shape[1]
     blocks_here, pairs, rows, _ = kernel_blocks.shape
+    rank = leaf_basis.shape[0]
     steps = blocks_here // TB
     flops = 2 * blocks_here * pairs * rows * rows * cases * width
     hbm = pl.BlockSpec(memory_space=pl.ANY)
+    block = pl.BlockSpec((cases, TB * rows, width), lambda g, ids: (0, g, 0))
+    result = jax.ShapeDtypeStruct((cases, blocks_here * rows, width), jnp.bfloat16)
     return pl.pallas_call(
         functools.partial(near_fwd_kernel, cases, pairs, rows),
-        out_shape=jax.ShapeDtypeStruct((cases, blocks_here * rows, width), jnp.bfloat16),
+        out_shape=(result, result, result, result),
         grid_spec=pltpu.PrefetchScalarGridSpec(
             num_scalar_prefetch=1,
             grid=(steps,),
@@ -109,8 +128,12 @@
                 hbm,
                 hbm,
                 hbm,
+                pl.BlockSpec((rank, TB * rows), lambda g, ids: (0, g)),
+                pl.BlockSpec((cases, rank, width), lambda g, ids: (0, 0, 0)),
+                pl.BlockSpec((width, width), lambda g, ids: (0, 0)),
+                block,
             ],
-            out_specs=pl.BlockSpec((cases, TB * rows, width), lambda g, ids: (0, g, 0)),
+            out_specs=[block, block, block, block],
             scratch_shapes=[
                 pltpu.VMEM((cases, span_points, width), jnp.bfloat16),
                 pltpu.SemaphoreType.DMA((3,)),
@@ -118,11 +141,11 @@
         ),
         compiler_params=pltpu.CompilerParams(dimension_semantics=("arbitrary",)),
         cost_estimate=pl.CostEstimate(
-            flops=flops,
-            transcendentals=0,
-            bytes_accessed=kernel_blocks.size * 2 + cases * span_points * width * 2 + cases * blocks_here * rows * width * 2,
-        ),
-    )(ids, kernel_blocks, from_prev, features, from_next)
+            flops=flops + 6 * cases * points_here * width * width,
+            transcendentals=cases * points_here * width,
+            bytes_accessed=kernel_blocks.size * 2 + cases * span_points * width * 2 + 5 * cases * points_here * width * 2,
+        ),
+    )(ids, kernel_blocks, from_prev, features, from_next, leaf_basis, far_coeff, w_near, cotangent)
 
 
 def near_bwd_kernel(cases, pairs, rows, steps, ids_ref, kb_ref, back_ref, mid_ref, lo_ref, hi_ref, acc_ref):
@@ -214,28 +237,19 @@
         near_pairs - (position * blocks_here - HALO), 0, span_blocks - 1
     ).reshape(-1).astype(jnp.int32)
 
-    near_bf = near_forward(local_ids, kernel_blocks, from_prev, features, from_next)
-
     summary = jnp.einsum("rp,apc->arc", leaf_basis, features, preferred_element_type=jnp.float32)
     expansion, _ = expand(summary, translations, False)
     exp_bf = expansion.astype(jnp.bfloat16)
     far_coeff = jnp.einsum("arc,cd->ard", exp_bf, w_far, preferred_element_type=jnp.float32).astype(
         jnp.bfloat16
     )
-    far_field = jnp.einsum("rp,ard->apd", leaf_basis, far_coeff, preferred_element_type=jnp.float32)
-    mixed = (
-        jnp.einsum("apc,cd->apd", near_bf, w_near, preferred_element_type=jnp.float32) + far_field
-    )
-    output = jax.nn.gelu(mixed).astype(jnp.bfloat16)
-    _, pullback = jax.vjp(jax.nn.gelu, mixed)
-    slope = pullback(cotangent.astype(jnp.float32))[0].astype(jnp.bfloat16)
+    near_bf, output, slope, back_near = near_forward(
+        local_ids, kernel_blocks, from_prev, features, from_next, leaf_basis, far_coeff, w_near,
+        cotangent,
+    )
     projected = jnp.einsum(
         "rp,apc->arc", leaf_basis, slope, preferred_element_type=jnp.float32
     ).astype(jnp.bfloat16)
-    back_near = jnp.einsum("apc,dc->apd", slope, w_near, preferred_element_type=jnp.float32).astype(
-        jnp.bfloat16
-    )
-
     mid, lo, hi = near_backward(local_ids, kernel_blocks, back_near, halo_points)
 
     scale = 1.0 / math.sqrt(

time: 96.3 us -> 100 us (1.038)
  Pallas kernels: 16.4 us -> 25.4 us
  matrix products: 12.7 us -> 9.12 us
  local copies, waits for them, and re-layouts: 4.93 us -> 3.05 us
    pallas_call x1, Pallas kernels: 7.49 us -> 16.5 us  [near_forward(): pl.pallas_call(functools.partial(near_fwd_kernel, cases, pairs, rows), ou...]
    dot_general x3 -> x1, matrix products: 7.28 us -> 0.75 us  [on_device(): jnp.einsum('arc,cd->ard', exp_bf, w_far, preferred_element_type=jnp.float32)]
    dot_general x1, matrix products: 0.47 us -> 2.04 us  [on_device(): jnp.einsum('apc,apd->cd', near_bf, slope, preferred_element_type=jnp.floa...]
    dot_general x1, matrix products: 0.31 us -> 1.52 us  [on_device(): jnp.einsum('rp,apc->arc', leaf_basis, slope, preferred_element_type=jnp.f...]
    unnamed x24 -> x20, local copies, waits for them, and re-layouts: 2.56 us -> 1.65 us
  transfers between devices with their start and end apart: 12 -> 12, of which waited for: 9 -> 9; matrix products, arithmetic and copies ran while one was open for 7% -> 4% of each run, Pallas kernels for 9% -> 9%
where the time goes in v10:
time: 100 us; the launch traced here: 99.8 us
  waiting for transfers between devices  41.1 us (41%)
  Pallas kernels  25.4 us (25%)
  starting transfers between devices  19.7 us (20%)
  matrix products  9.12 us (9%)
  local copies, waits for them, and re-layouts  3.05 us (3%)
    ppermute x8, waiting for transfers between devices, partner(): lax.ppermute(shard, axis, [(i, i ^ 1 << apart) for i in range(lax.axis_si...  25.8 us
    pallas_call x1, Pallas kernels, near_forward(): pl.pallas_call(functools.partial(near_fwd_kernel, cases, pairs, rows), ou...  16.5 us
    ppermute x4, waiting for transfers between devices, shifted(): lax.ppermute(value, axis, [(source, source + steps) for source in range(l...  15.3 us
    ppermute x4, starting transfers between devices, shifted(): lax.ppermute(value, axis, [(source, source + steps) for source in range(l...  12.6 us
    pallas_call x1, Pallas kernels, near_backward(): pl.pallas_call(functools.partial(near_bwd_kernel, cases, pairs, rows, ste...  8.95 us
    ppermute x8, starting transfers between devices, partner(): lax.ppermute(shard, axis, [(i, i ^ 1 << apart) for i in range(lax.axis_si...  7.12 us
    dot_general x1, matrix products, on_device(): jnp.einsum('apc,apd->cd', near_bf, slope, preferred_element_type=jnp.floa...  2.04 us
  transfers between devices with their start and end apart: 12, of which 9 were waited for; matrix products, arithmetic and copies ran while one was open for 4% of the time, Pallas kernels for 9%

profile of v10, /device:TPU:16, one launch (start us, length us, event | category | flops | bytes accessed | tf_op | source)
XLA Modules:
  0.0 99.8 jit_solution(594197400591634605)
XLA Ops:
  0.7 1.7 %convolution_bitcast_fusion.1 = f32[2,64,128]{2,1,0:T(8,128)S(1)} fusion(bf16[2,2048,128]{2,1,0:T(8,128)(2,1)} %own_hbm.1, bf16[64,2048]{1,0:T(8,128)(2,1)} %basis_ref.1), kind=kOutput, calls=%fused_computation.3 | convolution fusion | flops 67108864 | bytes 1376256 | tf_op jit(solution)/shard_map/rp,apc->arc/dot_general | solution.py:240
  2.4 1.6 %collective-permute-start.2 = (f32[2,64,128]{2,1,0:T(8,128)S(1)}, f32[2,64,128]{2,1,0:T(8,128)S(1)}, u32[]{:S(2)}, u32[]{:S(2)}) collective-permute-start(f32[2,64,128]{2,1,0:T(8,128)S(1)} %convolution_bitcast_fusion.1), channel_id=1, source_target_pairs={{0,4},{4,0},{8,12},{12,8},{16,20},{20,16},{24,28},{28,24},{1,5},{5... | collective-permute-start | bytes 196616 | tf_op jit(solution)/shard_map/ppermute | solution.py:17
  4.0 2.3 %collective-permute-start.1 = (bf16[2,1024,128]{2,1,0:T(8,128)(2,1)S(1)}, bf16[2,1024,128]{2,1,0:T(8,128)(2,1)S(1)}, u32[]{:S(2)}, u32[]{:S(2)}) collective-permute-start(bf16[2,1024,128]{2,1,0:T(8,128)(2,1)S(1)} %get-tuple-element.36), channel_id=1, source_target_pairs={{4,0},{8,4},{12,8},{16,12},{20,16},{24,20},{28,24},{5,1},{9,5},{13... | collective-permute-start | bytes 1572872 | tf_op jit(solution)/shard_map/ppermute | solution.py:23
  6.3 3.5 %collective-permute-start = (bf16[2,1024,128]{2,1,0:T(8,128)(2,1)S(1)}, bf16[2,1024,128]{2,1,0:T(8,128)(2,1)S(1)}, u32[]{:S(2)}, u32[]{:S(2)}) collective-permute-start(bf16[2,1024,128]{2,1,0:T(8,128)(2,1)S(1)} %get-tuple-element.37), channel_id=1, source_target_pairs={{0,4},{4,8},{8,12},{12,16},{16,20},{20,24},{24,28},{1,5},{5,9},{9,... | collective-permute-start | bytes 1572872 | tf_op jit(solution)/shard_map/ppermute | solution.py:23
  9.9 1.7 %collective-permute-start.3 = (f32[2,64,128]{2,1,0:T(8,128)S(1)}, f32[2,64,128]{2,1,0:T(8,128)S(1)}, u32[]{:S(2)}, u32[]{:S(2)}) collective-permute-start(f32[2,64,128]{2,1,0:T(8,128)S(1)} %add.53), channel_id=1, source_target_pairs={{0,8},{4,12},{8,0},{12,4},{16,24},{20,28},{24,16},{28,20},{1,9},{5... | collective-permute-start | bytes 196616 | tf_op jit(solution)/shard_map/ppermute | solution.py:17
  11.6 0.7 reshape.29.ids_ref
  12.3 9.0 %collective-permute-done.3 = f32[2,64,128]{2,1,0:T(8,128)S(1)} collective-permute-done((f32[2,64,128]{2,1,0:T(8,128)S(1)}, f32[2,64,128]{2,1,0:T(8,128)S(1)}, u32[]{:S(2)}, u32[]{:S(2)}) %collective-permute-start.3) | collective-permute-done | bytes 65568 | tf_op jit(solution)/shard_map/ppermute | solution.py:17
  21.5 4.9 %collective-permute-done.4 = f32[2,64,128]{2,1,0:T(8,128)S(1)} collective-permute-done((f32[2,64,128]{2,1,0:T(8,128)S(1)}, f32[2,64,128]{2,1,0:T(8,128)S(1)}, u32[]{:S(2)}, u32[]{:S(2)}) %collective-permute-start.4) | collective-permute-done | bytes 65568 | tf_op jit(solution)/shard_map/ppermute | solution.py:17
  26.9 0.8 convolution_convert_fusion.1.coeff_ref
  27.7 2.9 %collective-permute-done.1.next_hbm = bf16[2,1024,128]{2,1,0:T(8,128)(2,1)S(1)} collective-permute-done((bf16[2,1024,128]{2,1,0:T(8,128)(2,1)S(1)}, bf16[2,1024,128]{2,1,0:T(8,128)(2,1)S(1)}, u32[]{:S(2)}, u32[]{:S(2)}) %collective-permute-start.1) | collective-permute-done | bytes 524320 | tf_op jit(solution)/shard_map/ppermute | solution.py:23
  30.6 0.8 copy-done.4
  31.3 0.8 copy-done.5
  32.2 16.5 %shard_map.111 = (bf16[2,2048,128]{2,1,0:T(8,128)(2,1)}, bf16[2,2048,128]{2,1,0:T(8,128)(2,1)}, bf16[2,2048,128]{2,1,0:T(8,128)(2,1)}, bf16[2,2048,128]{2,1,0:T(8,128)(2,1)}) custom-call(s32[192]{0:T(256)} %reshape.29.ids_ref, bf16[16,12,128,128]{3,2,1,0:T(8,128)(2,1)} %kb_ref.3, bf16[2,1024,128]{2,1,0:T(8,128)(2,1)} %copy-done.5, ...), custom_call_target="tpu_custom_call" | custom-call | flops 2013265920 | bytes 13631488 | tf_op jit(solution)/shard_map/pallas_call | solution.py:120
  48.7 1.5 %fusion.6 = bf16[2,64,128]{2,1,0:T(8,128)(2,1)S(1)} fusion(bf16[2,2048,128]{2,1,0:T(8,128)(2,1)} %get-tuple-element.20, bf16[64,2048]{1,0:T(8,128)(2,1)S(1)} %copy-done.2), kind=kOutput, calls=%fused_computation.16 | convolution fusion | flops 67125248 | bytes 1343488 | tf_op jit(solution)/shard_map/rp,apc->arc/dot_general | solution.py:250
  50.5 2.0 %fusion.2 = f32[128,128]{1,0:T(8,128)S(1)} fusion(bf16[2,2048,128]{2,1,0:T(8,128)(2,1)} %get-tuple-element.21, bf16[2,2048,128]{2,1,0:T(8,128)(2,1)} %get-tuple-element.20), kind=kOutput, calls=%fused_computation.9 | convolution fusion | flops 134234112 | bytes 2162688 | tf_op jit(solution)/shard_map/apc,apd->cd/dot_general | solution.py:259
  52.6 0.7 collective-permute-start.5
  53.2 8.9 %shard_map.112 = (f32[2,2048,128]{2,1,0:T(8,128)}, bf16[2,1024,128]{2,1,0:T(8,128)(2,1)}, bf16[2,1024,128]{2,1,0:T(8,128)(2,1)}) custom-call(s32[192]{0:T(256)} %reshape.29.ids_ref, bf16[16,12,128,128]{3,2,1,0:T(8,128)(2,1)} %kb_ref.3, bf16[2,2048,128]{2,1,0:T(8,128)(2,1)} %get-tuple-element.22.back_ref), custom_call_target="tpu_custom_call" | custom-call | flops 1610612736 | bytes 11534336 | tf_op jit(solution)/shard_map/pallas_call | solution.py:187
  62.3 1.2 %collective-permute-start.6 = (f32[384,128]{1,0:T(8,128)S(1)}, f32[384,128]{1,0:T(8,128)S(1)}, u32[]{:S(2)}, u32[]{:S(2)}) collective-permute-start(f32[384,128]{1,0:T(8,128)S(1)} %pad_maximum_fusion.1), channel_id=1, source_target_pairs={{0,8},{4,12},{8,0},{12,4},{16,24},{20,28},{24,16},{28,20},{1,9},{5... | collective-permute-start | bytes 589832 | tf_op jit(solution)/shard_map/ppermute | solution.py:17
  63.4 5.4 %collective-permute-done.6 = f32[384,128]{1,0:T(8,128)S(1)} collective-permute-done((f32[384,128]{1,0:T(8,128)S(1)}, f32[384,128]{1,0:T(8,128)S(1)}, u32[]{:S(2)}, u32[]{:S(2)}) %collective-permute-start.6) | collective-permute-done | bytes 196640 | tf_op jit(solution)/shard_map/ppermute | solution.py:17
  69.0 0.3 collective-permute-start.9
  69.5 2.2 %collective-permute-start.7 = (bf16[2,1024,128]{2,1,0:T(8,128)(2,1)S(1)}, bf16[2,1024,128]{2,1,0:T(8,128)(2,1)S(1)}, u32[]{:S(2)}, u32[]{:S(2)}) collective-permute-start(bf16[2,1024,128]{2,1,0:T(8,128)(2,1)S(1)} %copy-done.9), channel_id=1, source_target_pairs={{0,4},{4,8},{8,12},{12,16},{16,20},{20,24},{24,28},{1,5},{5,9},{9,... | collective-permute-start | bytes 1572872 | tf_op jit(solution)/shard_map/ppermute | solution.py:23
  71.8 4.5 %collective-permute-start.8 = (bf16[2,1024,128]{2,1,0:T(8,128)(2,1)S(1)}, bf16[2,1024,128]{2,1,0:T(8,128)(2,1)S(1)}, u32[]{:S(2)}, u32[]{:S(2)}) collective-permute-start(bf16[2,1024,128]{2,1,0:T(8,128)(2,1)S(1)} %copy-done.8), channel_id=1, source_target_pairs={{4,0},{8,4},{12,8},{16,12},{20,16},{24,20},{28,24},{5,1},{9,5},{13... | collective-permute-start | bytes 1572872 | tf_op jit(solution)/shard_map/ppermute | solution.py:23
  76.3 1.6 %collective-permute-done.9 = f32[384,128]{1,0:T(8,128)S(1)} collective-permute-done((f32[384,128]{1,0:T(8,128)S(1)}, f32[384,128]{1,0:T(8,128)S(1)}, u32[]{:S(2)}, u32[]{:S(2)}) %collective-permute-start.9) | collective-permute-done | bytes 196640 | tf_op jit(solution)/shard_map/ppermute | solution.py:17
  78.0 0.3 convolution_add_fusion.1
  78.3 1.1 %collective-permute-done.10 = f32[256,128]{1,0:T(8,128)S(1)} collective-permute-done((f32[256,128]{1,0:T(8,128)S(1)}, f32[256,128]{1,0:T(8,128)S(1)}, u32[]{:S(2)}, u32[]{:S(2)}) %collective-permute-start.10) | collective-permute-done | bytes 131104 | tf_op jit(solution)/shard_map/ppermute | solution.py:17
  79.4 1.6 %collective-permute-start.11 = (f32[256,128]{1,0:T(8,128)S(1)}, f32[256,128]{1,0:T(8,128)S(1)}, u32[]{:S(2)}, u32[]{:S(2)}) collective-permute-start(f32[256,128]{1,0:T(8,128)S(1)} %add.67), channel_id=1, source_target_pairs={{0,2},{1,3},{2,0},{3,1},{4,6},{5,7},{6,4},{7,5},{8,10},{9,11},{10,... | collective-permute-start | bytes 393224 | tf_op jit(solution)/shard_map/ppermute | solution.py:17
  81.0 0.3 fusion.7
  81.2 3.8 %collective-permute-done.11 = f32[256,128]{1,0:T(8,128)S(1)} collective-permute-done((f32[256,128]{1,0:T(8,128)S(1)}, f32[256,128]{1,0:T(8,128)S(1)}, u32[]{:S(2)}, u32[]{:S(2)}) %collective-permute-start.11) | collective-permute-done | bytes 131104 | tf_op jit(solution)/shard_map/ppermute | solution.py:17
  85.0 0.7 fusion.33
  85.7 7.3 %collective-permute-done.7 = bf16[2,1024,128]{2,1,0:T(8,128)(2,1)S(1)} collective-permute-done((bf16[2,1024,128]{2,1,0:T(8,128)(2,1)S(1)}, bf16[2,1024,128]{2,1,0:T(8,128)(2,1)S(1)}, u32[]{:S(2)}, u32[]{:S(2)}) %collective-permute-start.7) | collective-permute-done | bytes 524320 | tf_op jit(solution)/shard_map/ppermute | solution.py:23
  92.9 5.2 %collective-permute-done.8 = bf16[2,1024,128]{2,1,0:T(8,128)(2,1)S(1)} collective-permute-done((bf16[2,1024,128]{2,1,0:T(8,128)(2,1)S(1)}, bf16[2,1024,128]{2,1,0:T(8,128)(2,1)S(1)}, u32[]{:S(2)}, u32[]{:S(2)}) %collective-permute-start.8) | collective-permute-done | bytes 524320 | tf_op jit(solution)/shard_map/ppermute | solution.py:23
  98.3 1.5 %fusion = bf16[2,2048,128]{2,1,0:T(8,128)(2,1)} fusion(f32[2,1024,128]{2,1,0:T(8,128)S(1)} %get-tuple-element.35, f32[2,1024,128]{2,1,0:T(8,128)S(1)} %get-tuple-element.34, bf16[2,64,128]{2,1,0:T(8,128)(2,1)S(1)} %fusion.7, bf16[64,2048]{1,0:T(8,128)(2,1)S(1)} %copy-done.2), kind=kOutput, calls=%fused_computation.2 | convolution fusion | flops 68681728 | bytes 3440640 | tf_op jit(solution)/shard_map/rp,arc->apc/dot_general | solution.py:270
  (47 shorter events, 1.8 us)
Async XLA Ops:
  0.6 26.3 %copy-start = (bf16[128,128]{1,0:T(8,128)(2,1)S(1)}, bf16[128,128]{1,0:T(8,128)(2,1)}, u32[]{:S(2)}) copy-start(bf16[128,128]{1,0:T(8,128)(2,1)} %param.14) | copy-start | bytes 98308
  0.6 3.3 %copy-start.1 = (bf16[2,2048,128]{2,1,0:T(8,128)(2,1)S(1)}, bf16[2,2048,128]{2,1,0:T(8,128)(2,1)}, u32[]{:S(2)}) copy-start(bf16[2,2048,128]{2,1,0:T(8,128)(2,1)} %own_hbm.1) | copy-start | bytes 3145732
  0.7 10.9 %copy-start.7 = (s32[16,12]{1,0:T(8,128)S(1)}, s32[16,12]{1,0:T(8,128)}, u32[]{:S(2)}) copy-start(s32[16,12]{1,0:T(8,128)} %param.11) | copy-start | bytes 2308
  0.7 20.7 %copy-start.6 = (f32[3,64,64]{2,1,0:T(8,128)S(1)}, f32[3,64,64]{2,1,0:T(8,128)}, u32[]{:S(2)}) copy-start(f32[3,64,64]{2,1,0:T(8,128)} %param.15) | copy-start | bytes 147460
  2.4 7.5 %collective-permute-start.2 = (f32[2,64,128]{2,1,0:T(8,128)S(1)}, f32[2,64,128]{2,1,0:T(8,128)S(1)}, u32[]{:S(2)}, u32[]{:S(2)}) collective-permute-start(f32[2,64,128]{2,1,0:T(8,128)S(1)} %convolution_bitcast_fusion.1), channel_id=1, source_target_pairs={{0,4},{4,0},{8,12},{12,8},{16,20},{20,16},{24,28},{28,24},{1,5},{5... | collective-permute-start | bytes 196616 | tf_op jit(solution)/shard_map/ppermute | solution.py:17
  4.0 26.5 %collective-permute-start.1 = (bf16[2,1024,128]{2,1,0:T(8,128)(2,1)S(1)}, bf16[2,1024,128]{2,1,0:T(8,128)(2,1)S(1)}, u32[]{:S(2)}, u32[]{:S(2)}) collective-permute-start(bf16[2,1024,128]{2,1,0:T(8,128)(2,1)S(1)} %get-tuple-element.36), channel_id=1, source_target_pairs={{4,0},{8,4},{12,8},{16,12},{20,16},{24,20},{28,24},{5,1},{9,5},{13... | collective-permute-start | bytes 1572872 | tf_op jit(solution)/shard_map/ppermute | solution.py:23
  6.3 24.2 %collective-permute-start = (bf16[2,1024,128]{2,1,0:T(8,128)(2,1)S(1)}, bf16[2,1024,128]{2,1,0:T(8,128)(2,1)S(1)}, u32[]{:S(2)}, u32[]{:S(2)}) collective-permute-start(bf16[2,1024,128]{2,1,0:T(8,128)(2,1)S(1)} %get-tuple-element.37), channel_id=1, source_target_pairs={{0,4},{4,8},{8,12},{12,16},{16,20},{20,24},{24,28},{1,5},{5,9},{9,... | collective-permute-start | bytes 1572872 | tf_op jit(solution)/shard_map/ppermute | solution.py:23
  9.9 11.3 %collective-permute-start.3 = (f32[2,64,128]{2,1,0:T(8,128)S(1)}, f32[2,64,128]{2,1,0:T(8,128)S(1)}, u32[]{:S(2)}, u32[]{:S(2)}) collective-permute-start(f32[2,64,128]{2,1,0:T(8,128)S(1)} %add.53), channel_id=1, source_target_pairs={{0,8},{4,12},{8,0},{12,4},{16,24},{20,28},{24,16},{28,20},{1,9},{5... | collective-permute-start | bytes 196616 | tf_op jit(solution)/shard_map/ppermute | solution.py:17
  21.2 5.2 %collective-permute-start.4 = (f32[2,64,128]{2,1,0:T(8,128)S(1)}, f32[2,64,128]{2,1,0:T(8,128)S(1)}, u32[]{:S(2)}, u32[]{:S(2)}) collective-permute-start(f32[2,64,128]{2,1,0:T(8,128)S(1)} %add.55), channel_id=1, source_target_pairs={{0,16},{4,20},{8,24},{12,28},{16,0},{20,4},{24,8},{28,12},{1,17},{... | collective-permute-start | bytes 196616 | tf_op jit(solution)/shard_map/ppermute | solution.py:17
  27.7 21.0 %copy-start.2 = (bf16[64,2048]{1,0:T(8,128)(2,1)S(1)}, bf16[64,2048]{1,0:T(8,128)(2,1)}, u32[]{:S(2)}) copy-start(bf16[64,2048]{1,0:T(8,128)(2,1)} %basis_ref.1) | copy-start | bytes 786436
  30.5 0.8 copy-start.4
  31.3 0.8 copy-start.5
  52.6 9.6 %collective-permute-start.5 = (f32[384,128]{1,0:T(8,128)S(1)}, f32[384,128]{1,0:T(8,128)S(1)}, u32[]{:S(2)}, u32[]{:S(2)}) collective-permute-start(f32[384,128]{1,0:T(8,128)S(1)} %pad_maximum_fusion), channel_id=1, source_target_pairs={{0,4},{4,0},{8,12},{12,8},{16,20},{20,16},{24,28},{28,24},{1,5},{5... | collective-permute-start | bytes 589832 | tf_op jit(solution)/shard_map/ppermute | solution.py:17
  62.2 7.3 %copy-start.9 = (bf16[2,1024,128]{2,1,0:T(8,128)(2,1)S(1)}, bf16[2,1024,128]{2,1,0:T(8,128)(2,1)}, u32[]{:S(2)}) copy-start(bf16[2,1024,128]{2,1,0:T(8,128)(2,1)} %get-tuple-element.31) | copy-start | bytes 1572868
  62.2 9.6 %copy-start.8 = (bf16[2,1024,128]{2,1,0:T(8,128)(2,1)S(1)}, bf16[2,1024,128]{2,1,0:T(8,128)(2,1)}, u32[]{:S(2)}) copy-start(bf16[2,1024,128]{2,1,0:T(8,128)(2,1)} %get-tuple-element.32) | copy-start | bytes 1572868
  62.2 35.9 %copy-start.3 = (f32[2,2048,128]{2,1,0:T(8,128)S(1)}, f32[2,2048,128]{2,1,0:T(8,128)}, u32[]{:S(2)}) copy-start(f32[2,2048,128]{2,1,0:T(8,128)} %get-tuple-element.30) | copy-start | bytes 6291460
  62.3 6.6 %collective-permute-start.6 = (f32[384,128]{1,0:T(8,128)S(1)}, f32[384,128]{1,0:T(8,128)S(1)}, u32[]{:S(2)}, u32[]{:S(2)}) collective-permute-start(f32[384,128]{1,0:T(8,128)S(1)} %pad_maximum_fusion.1), channel_id=1, source_target_pairs={{0,8},{4,12},{8,0},{12,4},{16,24},{20,28},{24,16},{28,20},{1,9},{5... | collective-permute-start | bytes 589832 | tf_op jit(solution)/shard_map/ppermute | solution.py:17
  69.0 9.0 %collective-permute-start.9 = (f32[384,128]{1,0:T(8,128)S(1)}, f32[384,128]{1,0:T(8,128)S(1)}, u32[]{:S(2)}, u32[]{:S(2)}) collective-permute-start(f32[384,128]{1,0:T(8,128)S(1)} %pad_maximum_fusion.2), channel_id=1, source_target_pairs={{0,16},{4,20},{8,24},{12,28},{16,0},{20,4},{24,8},{28,12},{1,17},{... | collective-permute-start | bytes 589832 | tf_op jit(solution)/shard_map/ppermute | solution.py:17
  69.5 23.4 %collective-permute-start.7 = (bf16[2,1024,128]{2,1,0:T(8,128)(2,1)S(1)}, bf16[2,1024,128]{2,1,0:T(8,128)(2,1)S(1)}, u32[]{:S(2)}, u32[]{:S(2)}) collective-permute-start(bf16[2,1024,128]{2,1,0:T(8,128)(2,1)S(1)} %copy-done.9), channel_id=1, source_target_pairs={{0,4},{4,8},{8,12},{12,16},{16,20},{20,24},{24,28},{1,5},{5,9},{9,... | collective-permute-start | bytes 1572872 | tf_op jit(solution)/shard_map/ppermute | solution.py:23
  71.8 26.3 %collective-permute-start.8 = (bf16[2,1024,128]{2,1,0:T(8,128)(2,1)S(1)}, bf16[2,1024,128]{2,1,0:T(8,128)(2,1)S(1)}, u32[]{:S(2)}, u32[]{:S(2)}) collective-permute-start(bf16[2,1024,128]{2,1,0:T(8,128)(2,1)S(1)} %copy-done.8), channel_id=1, source_target_pairs={{4,0},{8,4},{12,8},{16,12},{20,16},{24,20},{28,24},{5,1},{9,5},{13... | collective-permute-start | bytes 1572872 | tf_op jit(solution)/shard_map/ppermute | solution.py:23
  77.9 1.4 %collective-permute-start.10 = (f32[256,128]{1,0:T(8,128)S(1)}, f32[256,128]{1,0:T(8,128)S(1)}, u32[]{:S(2)}, u32[]{:S(2)}) collective-permute-start(f32[256,128]{1,0:T(8,128)S(1)} %slice_add_fusion), channel_id=1, source_target_pairs={{0,1},{1,0},{2,3},{3,2},{4,5},{5,4},{6,7},{7,6},{8,9},{9,8},{10,11... | collective-permute-start | bytes 393224 | tf_op jit(solution)/shard_map/ppermute | solution.py:17
  79.4 5.6 %collective-permute-start.11 = (f32[256,128]{1,0:T(8,128)S(1)}, f32[256,128]{1,0:T(8,128)S(1)}, u32[]{:S(2)}, u32[]{:S(2)}) collective-permute-start(f32[256,128]{1,0:T(8,128)S(1)} %add.67), channel_id=1, source_target_pairs={{0,2},{1,3},{2,0},{3,1},{4,6},{5,7},{6,4},{7,5},{8,10},{9,11},{10,... | collective-permute-start | bytes 393224 | tf_op jit(solution)/shard_map/ppermute | solution.py:17

commit v11 on v9

--- a/solution.py
+++ b/solution.py
@@ -206,15 +206,21 @@
     span_blocks = blocks_here + 2 * HALO
     position = lax.axis_index("leaf")
 
-    head = features[:, :halo_points]
-    tail = features[:, points_here - halo_points :]
-    from_prev = shifted(tail, "leaf", 1)
-    from_next = shifted(head, "leaf", -1)
     local_ids = jnp.clip(
         near_pairs - (position * blocks_here - HALO), 0, span_blocks - 1
     ).reshape(-1).astype(jnp.int32)
 
-    near_bf = near_forward(local_ids, kernel_blocks, from_prev, features, from_next)
+    halos = []
+    waited = ()
+    for c in range(cases_here):
+        head = features[c : c + 1, :halo_points]
+        tail = features[c : c + 1, points_here - halo_points :]
+        if waited:
+            head, tail, _ = lax.optimization_barrier((head, tail, waited))
+        from_prev = shifted(tail, "leaf", 1)
+        from_next = shifted(head, "leaf", -1)
+        halos.append((from_prev, from_next))
+        waited = (from_prev, from_next)
 
     summary = jnp.einsum("rp,apc->arc", leaf_basis, features, preferred_element_type=jnp.float32)
     expansion, _ = expand(summary, translations, False)
@@ -223,21 +229,43 @@
         jnp.bfloat16
     )
     far_field = jnp.einsum("rp,ard->apd", leaf_basis, far_coeff, preferred_element_type=jnp.float32)
-    mixed = (
-        jnp.einsum("apc,cd->apd", near_bf, w_near, preferred_element_type=jnp.float32) + far_field
-    )
-    output = jax.nn.gelu(mixed).astype(jnp.bfloat16)
-    _, pullback = jax.vjp(jax.nn.gelu, mixed)
-    slope = pullback(cotangent.astype(jnp.float32))[0].astype(jnp.bfloat16)
+
+    near_parts, output_parts, slope_parts, scattered = [], [], [], []
+    for c in range(cases_here):
+        from_prev, from_next = halos[c]
+        near_c = near_forward(local_ids, kernel_blocks, from_prev, features[c : c + 1], from_next)
+        mixed = (
+            jnp.einsum("apc,cd->apd", near_c, w_near, preferred_element_type=jnp.float32)
+            + far_field[c : c + 1]
+        )
+        output_parts.append(jax.nn.gelu(mixed).astype(jnp.bfloat16))
+        _, pullback = jax.vjp(jax.nn.gelu, mixed)
+        slope_c = pullback(cotangent[c : c + 1].astype(jnp.float32))[0].astype(jnp.bfloat16)
+        back_c = jnp.einsum(
+            "apc,dc->apd", slope_c, w_near, preferred_element_type=jnp.float32
+        ).astype(jnp.bfloat16)
+        mid_c, lo_c, hi_c = near_backward(local_ids, kernel_blocks, back_c, halo_points)
+        got_prev = shifted(hi_c, "leaf", 1).astype(jnp.float32)
+        got_next = shifted(lo_c, "leaf", -1).astype(jnp.float32)
+        scattered.append(
+            jnp.concatenate(
+                [
+                    mid_c[:, :halo_points] + got_prev,
+                    mid_c[:, halo_points : points_here - halo_points],
+                    mid_c[:, points_here - halo_points :] + got_next,
+                ],
+                axis=1,
+            )
+        )
+        near_parts.append(near_c)
+        slope_parts.append(slope_c)
+    near_bf = jnp.concatenate(near_parts, axis=0)
+    slope = jnp.concatenate(slope_parts, axis=0)
+    output = jnp.concatenate(output_parts, axis=0)
+
     projected = jnp.einsum(
         "rp,apc->arc", leaf_basis, slope, preferred_element_type=jnp.float32
     ).astype(jnp.bfloat16)
-    back_near = jnp.einsum("apc,dc->apd", slope, w_near, preferred_element_type=jnp.float32).astype(
-        jnp.bfloat16
-    )
-
-    mid, lo, hi = near_backward(local_ids, kernel_blocks, back_near, halo_points)
-
     scale = 1.0 / math.sqrt(
         cases_here * lax.axis_size("case") * points_here * lax.axis_size("leaf")
     )
@@ -250,9 +278,7 @@
     grads = jnp.concatenate([near_term, far_term], axis=0)
 
     back_coeff = jnp.einsum("arc,dc->ard", projected, w_far, preferred_element_type=jnp.float32)
-    back_exp, grads, (mid, lo, hi) = expand(
-        back_coeff, translations, True, rider=grads, cover=(mid, lo, hi)
-    )
+    back_exp, grads = expand(back_coeff, translations, True, rider=grads)
     back_far = jnp.einsum(
         "rp,arc->apc", leaf_basis, back_exp.astype(jnp.bfloat16), preferred_element_type=jnp.float32
     )
@@ -261,16 +287,7 @@
     for height in range(case_depth):
         grads = grads + partner(grads, "case", height)
 
-    got_prev = shifted(hi, "leaf", 1).astype(jnp.float32)
-    got_next = shifted(lo, "leaf", -1).astype(jnp.float32)
-    near_back = jnp.concatenate(
-        [
-            mid[:, :halo_points] + got_prev,
-            mid[:, halo_points : points_here - halo_points],
-            mid[:, points_here - halo_points :] + got_next,
-        ],
-        axis=1,
-    )
+    near_back = jnp.concatenate(scattered, axis=0)
     grad_features = (near_back + back_far).astype(jnp.bfloat16)
     grad_near = grads[:width]
     grad_far = grads[width:]

time: 96.3 us -> 110 us (1.14)
  the two profiles are of different devices: /device:TPU:16 before, /device:TPU:0 now
where the time goes in v11:
time: 110 us; the launch traced here: 109 us
  starting transfers between devices  42.7 us (39%)
  Pallas kernels  27.5 us (25%)
  waiting for transfers between devices  18.7 us (17%)
  matrix products  12.4 us (11%)
  local copies, waits for them, and re-layouts  5.11 us (5%)
  other arithmetic  1.44 us (1%)
    ppermute x8, starting transfers between devices, shifted(): lax.ppermute(value, axis, [(source, source + steps) for source in range(l...  22.3 us
    ppermute x8, starting transfers between devices, partner(): lax.ppermute(shard, axis, [(i, i ^ 1 << apart) for i in range(lax.axis_si...  20.4 us
    ppermute x8, waiting for transfers between devices, partner(): lax.ppermute(shard, axis, [(i, i ^ 1 << apart) for i in range(lax.axis_si...  16.4 us
    pallas_call x2, Pallas kernels, near_backward(): pl.pallas_call(functools.partial(near_bwd_kernel, cases, pairs, rows, ste...  14 us
    pallas_call x2, Pallas kernels, near_forward(): pl.pallas_call(functools.partial(near_fwd_kernel, cases, pairs, rows), ou...  13.5 us
    dot_general x2, matrix products, on_device(): jnp.einsum('apc,cd->apd', near_c, w_near, preferred_element_type=jnp.floa...  3.48 us
    ppermute x8, waiting for transfers between devices, shifted(): lax.ppermute(value, axis, [(source, source + steps) for source in range(l...  2.23 us
  transfers between devices with their start and end apart: 16, of which 8 were waited for; matrix products, arithmetic and copies ran while one was open for 7% of the time, Pallas kernels for 19%

profile of v11, /device:TPU:0, one launch (start us, length us, event | category | flops | bytes accessed | tf_op | source)
XLA Modules:
  0.0 108.9 jit_solution(12700100140820678055)
XLA Ops:
  1.6 1.5 %convolution_bitcast_fusion.4 = f32[2,64,128]{2,1,0:T(8,128)S(1)} fusion(bf16[2,2048,128]{2,1,0:T(8,128)(2,1)} %param.8, bf16[64,2048]{1,0:T(8,128)(2,1)S(1)} %copy-done), kind=kOutput, calls=%fused_computation.20 | convolution fusion | flops 67108864 | bytes 1376256 | tf_op jit(solution)/shard_map/rp,apc->arc/dot_general | solution.py:225
  3.1 3.0 %collective-permute-start.2 = (f32[2,64,128]{2,1,0:T(8,128)S(1)}, f32[2,64,128]{2,1,0:T(8,128)S(1)}, u32[]{:S(2)}, u32[]{:S(2)}) collective-permute-start(f32[2,64,128]{2,1,0:T(8,128)S(1)} %convolution_bitcast_fusion.4), channel_id=1, source_target_pairs={{0,4},{4,0},{8,12},{12,8},{16,20},{20,16},{24,28},{28,24},{1,5},{5... | collective-permute-start | bytes 196616 | tf_op jit(solution)/shard_map/ppermute | solution.py:17
  7.0 1.3 %collective-permute-start.1 = (bf16[1,1024,128]{2,1,0:T(8,128)(2,1)S(1)}, bf16[1,1024,128]{2,1,0:T(8,128)(2,1)S(1)}, u32[]{:S(2)}, u32[]{:S(2)}) collective-permute-start(bf16[1,1024,128]{2,1,0:T(8,128)(2,1)S(1)} %get-tuple-element.30), channel_id=1, source_target_pairs={{4,0},{8,4},{12,8},{16,12},{20,16},{24,20},{28,24},{5,1},{9,5},{13... | collective-permute-start | bytes 786440 | tf_op jit(solution)/shard_map/ppermute | solution.py:23
  8.3 4.6 %collective-permute-start = (bf16[1,1024,128]{2,1,0:T(8,128)(2,1)S(1)}, bf16[1,1024,128]{2,1,0:T(8,128)(2,1)S(1)}, u32[]{:S(2)}, u32[]{:S(2)}) collective-permute-start(bf16[1,1024,128]{2,1,0:T(8,128)(2,1)S(1)} %get-tuple-element.32), channel_id=1, source_target_pairs={{0,4},{4,8},{8,12},{12,16},{16,20},{20,24},{24,28},{1,5},{5,9},{9,... | collective-permute-start | bytes 786440 | tf_op jit(solution)/shard_map/ppermute | solution.py:23
  14.0 1.6 %collective-permute-start.3 = (f32[2,64,128]{2,1,0:T(8,128)S(1)}, f32[2,64,128]{2,1,0:T(8,128)S(1)}, u32[]{:S(2)}, u32[]{:S(2)}) collective-permute-start(f32[2,64,128]{2,1,0:T(8,128)S(1)} %add.83), channel_id=1, source_target_pairs={{0,8},{4,12},{8,0},{12,4},{16,24},{20,28},{24,16},{28,20},{1,9},{5... | collective-permute-start | bytes 196616 | tf_op jit(solution)/shard_map/ppermute | solution.py:17
  16.3 2.0 %collective-permute-done.3 = f32[2,64,128]{2,1,0:T(8,128)S(1)} collective-permute-done((f32[2,64,128]{2,1,0:T(8,128)S(1)}, f32[2,64,128]{2,1,0:T(8,128)S(1)}, u32[]{:S(2)}, u32[]{:S(2)}) %collective-permute-start.3) | collective-permute-done | bytes 65568 | tf_op jit(solution)/shard_map/ppermute | solution.py:17
  18.3 2.6 %collective-permute-start.4 = (f32[2,64,128]{2,1,0:T(8,128)S(1)}, f32[2,64,128]{2,1,0:T(8,128)S(1)}, u32[]{:S(2)}, u32[]{:S(2)}) collective-permute-start(f32[2,64,128]{2,1,0:T(8,128)S(1)} %add.85), channel_id=1, source_target_pairs={{0,16},{4,20},{8,24},{12,28},{16,0},{20,4},{24,8},{28,12},{1,17},{... | collective-permute-start | bytes 196616 | tf_op jit(solution)/shard_map/ppermute | solution.py:17
  21.2 2.4 %collective-permute-done.4 = f32[2,64,128]{2,1,0:T(8,128)S(1)} collective-permute-done((f32[2,64,128]{2,1,0:T(8,128)S(1)}, f32[2,64,128]{2,1,0:T(8,128)S(1)}, u32[]{:S(2)}, u32[]{:S(2)}) %collective-permute-start.4) | collective-permute-done | bytes 65568 | tf_op jit(solution)/shard_map/ppermute | solution.py:17
  24.0 4.6 %collective-permute-start.5 = (bf16[1,1024,128]{2,1,0:T(8,128)(2,1)}, bf16[1,1024,128]{2,1,0:T(8,128)(2,1)S(1)}, u32[]{:S(2)}, u32[]{:S(2)}) collective-permute-start(bf16[1,1024,128]{2,1,0:T(8,128)(2,1)} %get-tuple-element.12), channel_id=1, source_target_pairs={{0,4},{4,8},{8,12},{12,16},{16,20},{20,24},{24,28},{1,5},{5,9},{9,... | collective-permute-start | bytes 786440 | tf_op jit(solution)/shard_map/ppermute | solution.py:23
  28.6 1.3 %collective-permute-start.6 = (bf16[1,1024,128]{2,1,0:T(8,128)(2,1)}, bf16[1,1024,128]{2,1,0:T(8,128)(2,1)S(1)}, u32[]{:S(2)}, u32[]{:S(2)}) collective-permute-start(bf16[1,1024,128]{2,1,0:T(8,128)(2,1)} %get-tuple-element.13), channel_id=1, source_target_pairs={{4,0},{8,4},{12,8},{16,12},{20,16},{24,20},{28,24},{5,1},{9,5},{13... | collective-permute-start | bytes 786440 | tf_op jit(solution)/shard_map/ppermute | solution.py:23
  29.9 1.3 %convolution_bitcast_fusion.1 = f32[2,2048,128]{2,1,0:T(8,128)S(1)} fusion(bf16[2,64,128]{2,1,0:T(8,128)(2,1)S(1)} %fusion.13, bf16[64,2048]{1,0:T(8,128)(2,1)S(1)} %copy-done, bf16[128,128]{1,0:T(8,128)(2,1)} %param.14), kind=kOutput, calls=%fused_computation.1 | convolution fusion | flops 71319552 | bytes 2424832 | tf_op jit(solution)/shard_map/rp,ard->apd/dot_general | solution.py:231
  31.2 6.7 %shard_map.111 = bf16[1,2048,128]{2,1,0:T(8,128)(2,1)} custom-call(s32[192]{0:T(256)} %reshape.47.ids_ref, bf16[16,12,128,128]{3,2,1,0:T(8,128)(2,1)} %kb_ref.7, bf16[1,1024,128]{2,1,0:T(8,128)(2,1)} %copy-done.10, bf16[1,2048,128]{2,1,0:T(8,128)(2,1)} %get-tuple-element.28.own_hbm, bf16[1,1024,128]{2,1,0:T(8,128)(2,1)} %copy-done.9), custom_call_target="tpu_custom_call" | custom-call | flops 805306368 | bytes 7864320 | tf_op jit(solution)/shard_map/pallas_call | solution.py:101
  39.2 6.8 %shard_map.112 = bf16[1,2048,128]{2,1,0:T(8,128)(2,1)} custom-call(s32[192]{0:T(256)} %reshape.47.ids_ref, bf16[16,12,128,128]{3,2,1,0:T(8,128)(2,1)} %kb_ref.7, bf16[1,1024,128]{2,1,0:T(8,128)(2,1)} %copy-done.11, bf16[1,2048,128]{2,1,0:T(8,128)(2,1)} %get-tuple-element.29.own_hbm, bf16[1,1024,128]{2,1,0:T(8,128)(2,1)} %copy-done.12), custom_call_target="tpu_custom_call" | custom-call | flops 805306368 | bytes 7864320 | tf_op jit(solution)/shard_map/pallas_call | solution.py:101
  46.1 1.4 %fusion.1 = f32[1,2048,128]{2,1,0:T(8,128)S(1)} fusion(bf16[128,128]{1,0:T(8,128)(2,1)S(1)} %copy-done.7, f32[2,2048,128]{2,1,0:T(8,128)S(1)} %convolution_bitcast_fusion.1, bf16[1,2048,128]{2,1,0:T(8,128)(2,1)} %shard_map.112), kind=kOutput, calls=%fused_computation.5 | convolution fusion | flops 67371008 | bytes 2654208 | tf_op jit(solution)/shard_map/apc,cd->apd/dot_general | solution.py:238
  47.6 2.0 %fusion.16 = (bf16[1,2048,128]{2,1,0:T(8,128)(2,1)S(1)}, bf16[1,2048,128]{2,1,0:T(8,128)(2,1)S(1)}, bf16[1,2048,128]{2,1,0:T(8,128)(2,1)S(1)}, bf16[1,2048,128]{2,1,0:T(8,128)(2,1)S(1)}) fusion(bf16[2,2048,128]{2,1,0:T(8,128)(2,1)S(1)} %copy-done.15, f32[1,2048,128]{2,1,0:T(8,128)S(1)} %fusion.1, f32[2,2048,128]{2,1,0:T(8,128)S(1)} %convolution_bitcast_fusion.1, ...), kind=kOutput, calls=%fused_computation.38 | convolution fusion | flops 79429632 | bytes 5799936 | tf_op jit(solution)/shard_map/apc,cd->apd/dot_general | solution.py:238
  50.5 1.1 %fusion.2.back_ref = bf16[1,2048,128]{2,1,0:T(8,128)(2,1)} fusion(bf16[128,128]{1,0:T(8,128)(2,1)S(1)} %copy-done.8, bf16[1,2048,128]{2,1,0:T(8,128)(2,1)S(1)} %get-tuple-element.22), kind=kOutput, calls=%fused_computation.8 | convolution fusion | flops 67371008 | bytes 1081344 | tf_op jit(solution)/shard_map/apc,dc->apd/dot_general | solution.py:244
  51.6 1.1 %fusion.3.back_ref = bf16[1,2048,128]{2,1,0:T(8,128)(2,1)} fusion(bf16[128,128]{1,0:T(8,128)(2,1)S(1)} %copy-done.8, bf16[1,2048,128]{2,1,0:T(8,128)(2,1)S(1)} %get-tuple-element.23), kind=kOutput, calls=%fused_computation.9 | convolution fusion | flops 67371008 | bytes 1081344 | tf_op jit(solution)/shard_map/apc,dc->apd/dot_general | solution.py:244
  53.1 2.4 %collective-permute-start.11 = (f32[384,128]{1,0:T(8,128)S(1)}, f32[384,128]{1,0:T(8,128)S(1)}, u32[]{:S(2)}, u32[]{:S(2)}) collective-permute-start(f32[384,128]{1,0:T(8,128)S(1)} %pad_maximum_fusion.4), channel_id=1, source_target_pairs={{0,4},{4,0},{8,12},{12,8},{16,20},{20,16},{24,28},{28,24},{1,5},{5... | collective-permute-start | bytes 589832 | tf_op jit(solution)/shard_map/ppermute | solution.py:17
  55.5 7.0 %shard_map.114 = (f32[1,2048,128]{2,1,0:T(8,128)}, bf16[1,1024,128]{2,1,0:T(8,128)(2,1)}, bf16[1,1024,128]{2,1,0:T(8,128)(2,1)}) custom-call(s32[192]{0:T(256)} %reshape.47.ids_ref, bf16[16,12,128,128]{3,2,1,0:T(8,128)(2,1)} %kb_ref.7, bf16[1,2048,128]{2,1,0:T(8,128)(2,1)} %fusion.3.back_ref), custom_call_target="tpu_custom_call" | custom-call | flops 805306368 | bytes 8912896 | tf_op jit(solution)/shard_map/pallas_call | solution.py:164
  62.5 1.9 %collective-permute-start.9 = (bf16[1,1024,128]{2,1,0:T(8,128)(2,1)}, bf16[1,1024,128]{2,1,0:T(8,128)(2,1)S(1)}, u32[]{:S(2)}, u32[]{:S(2)}) collective-permute-start(bf16[1,1024,128]{2,1,0:T(8,128)(2,1)} %get-tuple-element.18), channel_id=1, source_target_pairs={{0,4},{4,8},{8,12},{12,16},{16,20},{20,24},{24,28},{1,5},{5,9},{9,... | collective-permute-start | bytes 786440 | tf_op jit(solution)/shard_map/ppermute | solution.py:23
  64.4 1.3 %collective-permute-start.10 = (bf16[1,1024,128]{2,1,0:T(8,128)(2,1)}, bf16[1,1024,128]{2,1,0:T(8,128)(2,1)S(1)}, u32[]{:S(2)}, u32[]{:S(2)}) collective-permute-start(bf16[1,1024,128]{2,1,0:T(8,128)(2,1)} %get-tuple-element.19), channel_id=1, source_target_pairs={{4,0},{8,4},{12,8},{16,12},{20,16},{24,20},{28,24},{5,1},{9,5},{13... | collective-permute-start | bytes 786440 | tf_op jit(solution)/shard_map/ppermute | solution.py:23
  65.7 7.0 %shard_map.113 = (f32[1,2048,128]{2,1,0:T(8,128)}, bf16[1,1024,128]{2,1,0:T(8,128)(2,1)}, bf16[1,1024,128]{2,1,0:T(8,128)(2,1)}) custom-call(s32[192]{0:T(256)} %reshape.47.ids_ref, bf16[16,12,128,128]{3,2,1,0:T(8,128)(2,1)} %kb_ref.7, bf16[1,2048,128]{2,1,0:T(8,128)(2,1)} %fusion.2.back_ref), custom_call_target="tpu_custom_call" | custom-call | flops 805306368 | bytes 8912896 | tf_op jit(solution)/shard_map/pallas_call | solution.py:164
  72.7 6.0 %collective-permute-start.7 = (bf16[1,1024,128]{2,1,0:T(8,128)(2,1)}, bf16[1,1024,128]{2,1,0:T(8,128)(2,1)S(1)}, u32[]{:S(2)}, u32[]{:S(2)}) collective-permute-start(bf16[1,1024,128]{2,1,0:T(8,128)(2,1)} %get-tuple-element.15), channel_id=1, source_target_pairs={{0,4},{4,8},{8,12},{12,16},{16,20},{20,24},{24,28},{1,5},{5,9},{9,... | collective-permute-start | bytes 786440 | tf_op jit(solution)/shard_map/ppermute | solution.py:23
  78.8 1.3 %collective-permute-start.8 = (bf16[1,1024,128]{2,1,0:T(8,128)(2,1)}, bf16[1,1024,128]{2,1,0:T(8,128)(2,1)S(1)}, u32[]{:S(2)}, u32[]{:S(2)}) collective-permute-start(bf16[1,1024,128]{2,1,0:T(8,128)(2,1)} %get-tuple-element.16), channel_id=1, source_target_pairs={{4,0},{8,4},{12,8},{16,12},{20,16},{24,20},{28,24},{5,1},{9,5},{13... | collective-permute-start | bytes 786440 | tf_op jit(solution)/shard_map/ppermute | solution.py:23
  81.2 5.0 %collective-permute-start.12 = (f32[384,128]{1,0:T(8,128)S(1)}, f32[384,128]{1,0:T(8,128)S(1)}, u32[]{:S(2)}, u32[]{:S(2)}) collective-permute-start(f32[384,128]{1,0:T(8,128)S(1)} %pad_maximum_fusion.5), channel_id=1, source_target_pairs={{0,8},{4,12},{8,0},{12,4},{16,24},{20,28},{24,16},{28,20},{1,9},{5... | collective-permute-start | bytes 589832 | tf_op jit(solution)/shard_map/ppermute | solution.py:17
  86.4 1.8 %collective-permute-done.8 = bf16[1,1024,128]{2,1,0:T(8,128)(2,1)S(1)} collective-permute-done((bf16[1,1024,128]{2,1,0:T(8,128)(2,1)}, bf16[1,1024,128]{2,1,0:T(8,128)(2,1)S(1)}, u32[]{:S(2)}, u32[]{:S(2)}) %collective-permute-start.8) | collective-permute-done | bytes 262176 | tf_op jit(solution)/shard_map/ppermute | solution.py:23
  88.2 3.5 %collective-permute-done.12 = f32[384,128]{1,0:T(8,128)S(1)} collective-permute-done((f32[384,128]{1,0:T(8,128)S(1)}, f32[384,128]{1,0:T(8,128)S(1)}, u32[]{:S(2)}, u32[]{:S(2)}) %collective-permute-start.12) | collective-permute-done | bytes 196640 | tf_op jit(solution)/shard_map/ppermute | solution.py:17
  91.7 4.2 %collective-permute-start.13 = (f32[384,128]{1,0:T(8,128)S(1)}, f32[384,128]{1,0:T(8,128)S(1)}, u32[]{:S(2)}, u32[]{:S(2)}) collective-permute-start(f32[384,128]{1,0:T(8,128)S(1)} %pad_maximum_fusion.6), channel_id=1, source_target_pairs={{0,16},{4,20},{8,24},{12,28},{16,0},{20,4},{24,8},{28,12},{1,17},{... | collective-permute-start | bytes 589832 | tf_op jit(solution)/shard_map/ppermute | solution.py:17
  96.2 4.7 %collective-permute-done.13 = f32[384,128]{1,0:T(8,128)S(1)} collective-permute-done((f32[384,128]{1,0:T(8,128)S(1)}, f32[384,128]{1,0:T(8,128)S(1)}, u32[]{:S(2)}, u32[]{:S(2)}) %collective-permute-start.13) | collective-permute-done | bytes 196640 | tf_op jit(solution)/shard_map/ppermute | solution.py:17
  102.6 1.3 %collective-permute-start.15 = (f32[256,128]{1,0:T(8,128)S(1)}, f32[256,128]{1,0:T(8,128)S(1)}, u32[]{:S(2)}, u32[]{:S(2)}) collective-permute-start(f32[256,128]{1,0:T(8,128)S(1)} %add.105), channel_id=1, source_target_pairs={{0,2},{1,3},{2,0},{3,1},{4,6},{5,7},{6,4},{7,5},{8,10},{9,11},{10,... | collective-permute-start | bytes 393224 | tf_op jit(solution)/shard_map/ppermute | solution.py:17
  104.0 1.5 %fusion.4 = bf16[2,2048,128]{2,1,0:T(8,128)(2,1)} fusion(f32[1,1024,128]{2,1,0:T(8,128)S(1)} %get-tuple-element.27, f32[1,1024,128]{2,1,0:T(8,128)S(1)} %get-tuple-element.26, f32[1,1024,128]{2,1,0:T(8,128)S(1)} %get-tuple-element.21, f32[1,1024,128]{2,1,0:T(8,128)S(1)} %get-tuple-element.20, bf16[2,64,128]{2,1,0:T(8,128)(2,1)S(1)} %fusion.12, ...), kind=kOutput, calls=%fused_computation.11 | convolution fusion | flops 69730304 | bytes 3440640 | tf_op jit(solution)/shard_map/rp,arc->apc/dot_general | solution.py:282
  105.4 2.8 %collective-permute-done.15 = f32[256,128]{1,0:T(8,128)S(1)} collective-permute-done((f32[256,128]{1,0:T(8,128)S(1)}, f32[256,128]{1,0:T(8,128)S(1)}, u32[]{:S(2)}, u32[]{:S(2)}) %collective-permute-start.15) | collective-permute-done | bytes 131104 | tf_op jit(solution)/shard_map/ppermute | solution.py:17
  (76 shorter events, 10.7 us)
Async XLA Ops:
  0.6 1.0 copy-start
  0.6 5.5 %copy-start.1 = (bf16[2,2048,128]{2,1,0:T(8,128)(2,1)S(1)}, bf16[2,2048,128]{2,1,0:T(8,128)(2,1)}, u32[]{:S(2)}) copy-start(bf16[2,2048,128]{2,1,0:T(8,128)(2,1)} %param.8) | copy-start | bytes 3145732
  3.1 12.5 %copy-start.14 = (s32[16,12]{1,0:T(8,128)S(1)}, s32[16,12]{1,0:T(8,128)}, u32[]{:S(2)}) copy-start(s32[16,12]{1,0:T(8,128)} %param.11) | copy-start | bytes 2308
  3.1 17.8 %copy-start.6 = (f32[3,64,64]{2,1,0:T(8,128)S(1)}, f32[3,64,64]{2,1,0:T(8,128)}, u32[]{:S(2)}) copy-start(f32[3,64,64]{2,1,0:T(8,128)} %param.15) | copy-start | bytes 147460
  3.1 10.8 %collective-permute-start.2 = (f32[2,64,128]{2,1,0:T(8,128)S(1)}, f32[2,64,128]{2,1,0:T(8,128)S(1)}, u32[]{:S(2)}, u32[]{:S(2)}) collective-permute-start(f32[2,64,128]{2,1,0:T(8,128)S(1)} %convolution_bitcast_fusion.4), channel_id=1, source_target_pairs={{0,4},{4,0},{8,12},{12,8},{16,20},{20,16},{24,28},{28,24},{1,5},{5... | collective-permute-start | bytes 196616 | tf_op jit(solution)/shard_map/ppermute | solution.py:17
  7.0 16.9 %collective-permute-start.1 = (bf16[1,1024,128]{2,1,0:T(8,128)(2,1)S(1)}, bf16[1,1024,128]{2,1,0:T(8,128)(2,1)S(1)}, u32[]{:S(2)}, u32[]{:S(2)}) collective-permute-start(bf16[1,1024,128]{2,1,0:T(8,128)(2,1)S(1)} %get-tuple-element.30), channel_id=1, source_target_pairs={{4,0},{8,4},{12,8},{16,12},{20,16},{24,20},{28,24},{5,1},{9,5},{13... | collective-permute-start | bytes 786440 | tf_op jit(solution)/shard_map/ppermute | solution.py:23
  8.3 15.6 %collective-permute-start = (bf16[1,1024,128]{2,1,0:T(8,128)(2,1)S(1)}, bf16[1,1024,128]{2,1,0:T(8,128)(2,1)S(1)}, u32[]{:S(2)}, u32[]{:S(2)}) collective-permute-start(bf16[1,1024,128]{2,1,0:T(8,128)(2,1)S(1)} %get-tuple-element.32), channel_id=1, source_target_pairs={{0,4},{4,8},{8,12},{12,16},{16,20},{20,24},{24,28},{1,5},{5,9},{9,... | collective-permute-start | bytes 786440 | tf_op jit(solution)/shard_map/ppermute | solution.py:23
  14.0 4.3 %collective-permute-start.3 = (f32[2,64,128]{2,1,0:T(8,128)S(1)}, f32[2,64,128]{2,1,0:T(8,128)S(1)}, u32[]{:S(2)}, u32[]{:S(2)}) collective-permute-start(f32[2,64,128]{2,1,0:T(8,128)S(1)} %add.83), channel_id=1, source_target_pairs={{0,8},{4,12},{8,0},{12,4},{16,24},{20,28},{24,16},{28,20},{1,9},{5... | collective-permute-start | bytes 196616 | tf_op jit(solution)/shard_map/ppermute | solution.py:17
  18.3 5.2 %collective-permute-start.4 = (f32[2,64,128]{2,1,0:T(8,128)S(1)}, f32[2,64,128]{2,1,0:T(8,128)S(1)}, u32[]{:S(2)}, u32[]{:S(2)}) collective-permute-start(f32[2,64,128]{2,1,0:T(8,128)S(1)} %add.85), channel_id=1, source_target_pairs={{0,16},{4,20},{8,24},{12,28},{16,0},{20,4},{24,8},{28,12},{1,17},{... | collective-permute-start | bytes 196616 | tf_op jit(solution)/shard_map/ppermute | solution.py:17
  24.0 7.3 %copy-start.9 = (bf16[1,1024,128]{2,1,0:T(8,128)(2,1)}, bf16[1,1024,128]{2,1,0:T(8,128)(2,1)S(1)}, u32[]{:S(2)}) copy-start(bf16[1,1024,128]{2,1,0:T(8,128)(2,1)S(1)} %collective-permute-done.1.next_hbm) | copy-start | bytes 786436
  24.0 7.3 %copy-start.10 = (bf16[1,1024,128]{2,1,0:T(8,128)(2,1)}, bf16[1,1024,128]{2,1,0:T(8,128)(2,1)S(1)}, u32[]{:S(2)}) copy-start(bf16[1,1024,128]{2,1,0:T(8,128)(2,1)S(1)} %collective-permute-done.prev_hbm) | copy-start | bytes 786436
  24.0 14.4 %collective-permute-start.5 = (bf16[1,1024,128]{2,1,0:T(8,128)(2,1)}, bf16[1,1024,128]{2,1,0:T(8,128)(2,1)S(1)}, u32[]{:S(2)}, u32[]{:S(2)}) collective-permute-start(bf16[1,1024,128]{2,1,0:T(8,128)(2,1)} %get-tuple-element.12), channel_id=1, source_target_pairs={{0,4},{4,8},{8,12},{12,16},{16,20},{20,24},{24,28},{1,5},{5,9},{9,... | collective-permute-start | bytes 786440 | tf_op jit(solution)/shard_map/ppermute | solution.py:23
  28.6 9.8 %collective-permute-start.6 = (bf16[1,1024,128]{2,1,0:T(8,128)(2,1)}, bf16[1,1024,128]{2,1,0:T(8,128)(2,1)S(1)}, u32[]{:S(2)}, u32[]{:S(2)}) collective-permute-start(bf16[1,1024,128]{2,1,0:T(8,128)(2,1)} %get-tuple-element.13), channel_id=1, source_target_pairs={{4,0},{8,4},{12,8},{16,12},{20,16},{24,20},{28,24},{5,1},{9,5},{13... | collective-permute-start | bytes 786440 | tf_op jit(solution)/shard_map/ppermute | solution.py:23
  38.4 0.7 copy-start.11
  38.4 0.8 copy-start.12
  39.2 6.8 %copy-start.7 = (bf16[128,128]{1,0:T(8,128)(2,1)S(1)}, bf16[128,128]{1,0:T(8,128)(2,1)}, u32[]{:S(2)}) copy-start(bf16[128,128]{1,0:T(8,128)(2,1)} %param.13) | copy-start | bytes 98308
  46.0 1.5 %copy-start.5 = (bf16[1,2048,128]{2,1,0:T(8,128)(2,1)S(1)}, bf16[1,2048,128]{2,1,0:T(8,128)(2,1)}, u32[]{:S(2)}) copy-start(bf16[1,2048,128]{2,1,0:T(8,128)(2,1)} %shard_map.111) | copy-start | bytes 1572868
  46.0 1.5 %copy-start.8 = (bf16[128,128]{1,0:T(8,128)(2,1)S(1)}, bf16[128,128]{1,0:T(8,128)(2,1)}, u32[]{:S(2)}) copy-start(bf16[128,128]{1,0:T(8,128)(2,1)} %param.13) | copy-start | bytes 98308
  46.0 1.5 %copy-start.15 = (bf16[2,2048,128]{2,1,0:T(8,128)(2,1)S(1)}, bf16[2,2048,128]{2,1,0:T(8,128)(2,1)}, u32[]{:S(2)}) copy-start(bf16[2,2048,128]{2,1,0:T(8,128)(2,1)} %param.9) | copy-start | bytes 3145732
  47.6 2.1 %copy-start.2 = (bf16[1,2048,128]{2,1,0:T(8,128)(2,1)S(1)}, bf16[1,2048,128]{2,1,0:T(8,128)(2,1)}, u32[]{:S(2)}) copy-start(bf16[1,2048,128]{2,1,0:T(8,128)(2,1)} %shard_map.112) | copy-start | bytes 1572868
  50.2 2.7 %copy-start.13 = (bf16[128,128]{1,0:T(8,128)(2,1)S(1)}, bf16[128,128]{1,0:T(8,128)(2,1)}, u32[]{:S(2)}) copy-start(bf16[128,128]{1,0:T(8,128)(2,1)} %param.14) | copy-start | bytes 98308
  53.1 28.1 %collective-permute-start.11 = (f32[384,128]{1,0:T(8,128)S(1)}, f32[384,128]{1,0:T(8,128)S(1)}, u32[]{:S(2)}, u32[]{:S(2)}) collective-permute-start(f32[384,128]{1,0:T(8,128)S(1)} %pad_maximum_fusion.4), channel_id=1, source_target_pairs={{0,4},{4,0},{8,12},{12,8},{16,20},{20,16},{24,28},{28,24},{1,5},{5... | collective-permute-start | bytes 589832 | tf_op jit(solution)/shard_map/ppermute | solution.py:17
  62.5 23.8 %collective-permute-start.9 = (bf16[1,1024,128]{2,1,0:T(8,128)(2,1)}, bf16[1,1024,128]{2,1,0:T(8,128)(2,1)S(1)}, u32[]{:S(2)}, u32[]{:S(2)}) collective-permute-start(bf16[1,1024,128]{2,1,0:T(8,128)(2,1)} %get-tuple-element.18), channel_id=1, source_target_pairs={{0,4},{4,8},{8,12},{12,16},{16,20},{20,24},{24,28},{1,5},{5,9},{9,... | collective-permute-start | bytes 786440 | tf_op jit(solution)/shard_map/ppermute | solution.py:23
  64.4 21.8 %collective-permute-start.10 = (bf16[1,1024,128]{2,1,0:T(8,128)(2,1)}, bf16[1,1024,128]{2,1,0:T(8,128)(2,1)S(1)}, u32[]{:S(2)}, u32[]{:S(2)}) collective-permute-start(bf16[1,1024,128]{2,1,0:T(8,128)(2,1)} %get-tuple-element.19), channel_id=1, source_target_pairs={{4,0},{8,4},{12,8},{16,12},{20,16},{24,20},{28,24},{5,1},{9,5},{13... | collective-permute-start | bytes 786440 | tf_op jit(solution)/shard_map/ppermute | solution.py:23
  72.7 13.5 %copy-start.4 = (f32[1,2048,128]{2,1,0:T(8,128)S(1)}, f32[1,2048,128]{2,1,0:T(8,128)}, u32[]{:S(2)}) copy-start(f32[1,2048,128]{2,1,0:T(8,128)} %get-tuple-element.17) | copy-start | bytes 3145732
  72.7 13.6 %collective-permute-start.7 = (bf16[1,1024,128]{2,1,0:T(8,128)(2,1)}, bf16[1,1024,128]{2,1,0:T(8,128)(2,1)S(1)}, u32[]{:S(2)}, u32[]{:S(2)}) collective-permute-start(bf16[1,1024,128]{2,1,0:T(8,128)(2,1)} %get-tuple-element.15), channel_id=1, source_target_pairs={{0,4},{4,8},{8,12},{12,16},{16,20},{20,24},{24,28},{1,5},{5,9},{9,... | collective-permute-start | bytes 786440 | tf_op jit(solution)/shard_map/ppermute | solution.py:23
  78.8 9.4 %collective-permute-start.8 = (bf16[1,1024,128]{2,1,0:T(8,128)(2,1)}, bf16[1,1024,128]{2,1,0:T(8,128)(2,1)S(1)}, u32[]{:S(2)}, u32[]{:S(2)}) collective-permute-start(bf16[1,1024,128]{2,1,0:T(8,128)(2,1)} %get-tuple-element.16), channel_id=1, source_target_pairs={{4,0},{8,4},{12,8},{16,12},{20,16},{24,20},{28,24},{5,1},{9,5},{13... | collective-permute-start | bytes 786440 | tf_op jit(solution)/shard_map/ppermute | solution.py:23
  81.1 7.0 %copy-start.3 = (f32[1,2048,128]{2,1,0:T(8,128)S(1)}, f32[1,2048,128]{2,1,0:T(8,128)}, u32[]{:S(2)}) copy-start(f32[1,2048,128]{2,1,0:T(8,128)} %get-tuple-element.14) | copy-start | bytes 3145732
  81.2 10.5 %collective-permute-start.12 = (f32[384,128]{1,0:T(8,128)S(1)}, f32[384,128]{1,0:T(8,128)S(1)}, u32[]{:S(2)}, u32[]{:S(2)}) collective-permute-start(f32[384,128]{1,0:T(8,128)S(1)} %pad_maximum_fusion.5), channel_id=1, source_target_pairs={{0,8},{4,12},{8,0},{12,4},{16,24},{20,28},{24,16},{28,20},{1,9},{5... | collective-permute-start | bytes 589832 | tf_op jit(solution)/shard_map/ppermute | solution.py:17
  91.7 9.1 %collective-permute-start.13 = (f32[384,128]{1,0:T(8,128)S(1)}, f32[384,128]{1,0:T(8,128)S(1)}, u32[]{:S(2)}, u32[]{:S(2)}) collective-permute-start(f32[384,128]{1,0:T(8,128)S(1)} %pad_maximum_fusion.6), channel_id=1, source_target_pairs={{0,16},{4,20},{8,24},{12,28},{16,0},{20,4},{24,8},{28,12},{1,17},{... | collective-permute-start | bytes 589832 | tf_op jit(solution)/shard_map/ppermute | solution.py:17
  101.2 1.4 %collective-permute-start.14 = (f32[256,128]{1,0:T(8,128)S(1)}, f32[256,128]{1,0:T(8,128)S(1)}, u32[]{:S(2)}, u32[]{:S(2)}) collective-permute-start(f32[256,128]{1,0:T(8,128)S(1)} %slice_add_fusion), channel_id=1, source_target_pairs={{0,1},{1,0},{2,3},{3,2},{4,5},{5,4},{6,7},{7,6},{8,9},{9,8},{10,11... | collective-permute-start | bytes 393224 | tf_op jit(solution)/shard_map/ppermute | solution.py:17
  102.6 5.6 %collective-permute-start.15 = (f32[256,128]{1,0:T(8,128)S(1)}, f32[256,128]{1,0:T(8,128)S(1)}, u32[]{:S(2)}, u32[]{:S(2)}) collective-permute-start(f32[256,128]{1,0:T(8,128)S(1)} %add.105), channel_id=1, source_target_pairs={{0,2},{1,3},{2,0},{3,1},{4,6},{5,7},{6,4},{7,5},{8,10},{9,11},{10,... | collective-permute-start | bytes 393224 | tf_op jit(solution)/shard_map/ppermute | solution.py:17

commit v12 on v9

--- a/solution.py
+++ b/solution.py
@@ -29,11 +29,12 @@
     return jnp.einsum("rs,asc->arc", matrix, sibling, precision=lax.Precision.HIGHEST)
 
 
-def expand(own_value, translations, flipped, rider=None, cover=None):
+def expand(own_value, translations, flipped, rider=None, stages=()):
     depth_count = lax.axis_size("leaf").bit_length() - 1
     summed = jnp.zeros(own_value.shape, jnp.float32)
     node_value = own_value
     rows = own_value.shape[0] * own_value.shape[1]
+    staged = None
     for height in range(depth_count):
         if rider is None:
             sibling = partner(node_value, "leaf", height)
@@ -42,15 +43,16 @@
                 [node_value.reshape(rows, own_value.shape[2]), rider], axis=0
             )
             got = partner(packed, "leaf", height)
-            if cover is not None and height < 2:
-                got, cover = lax.optimization_barrier((got, cover))
+            if height < len(stages):
+                staged = stages[height](staged)
+                got, staged = lax.optimization_barrier((got, staged))
             sibling = got[:rows].reshape(own_value.shape)
             rider = rider + got[rows:]
         summed = summed + apply_level(translations[height], sibling, flipped)
         node_value = node_value + sibling
-    if cover is None:
+    if not stages:
         return summed, rider
-    return summed, rider, cover
+    return summed, rider, staged
 
 
 def near_fwd_kernel(cases, pairs, rows, ids_ref, kb_ref, prev_hbm, own_hbm, next_hbm, out_ref, ext_ref, sems):
@@ -236,7 +238,6 @@
         jnp.bfloat16
     )
 
-    mid, lo, hi = near_backward(local_ids, kernel_blocks, back_near, halo_points)
 
     scale = 1.0 / math.sqrt(
         cases_here * lax.axis_size("case") * points_here * lax.axis_size("leaf")
@@ -251,7 +252,14 @@
 
     back_coeff = jnp.einsum("arc,dc->ard", projected, w_far, preferred_element_type=jnp.float32)
     back_exp, grads, (mid, lo, hi) = expand(
-        back_coeff, translations, True, rider=grads, cover=(mid, lo, hi)
+        back_coeff,
+        translations,
+        True,
+        rider=grads,
+        stages=(
+            lambda _: back_near,
+            lambda ready: near_backward(local_ids, kernel_blocks, ready, halo_points),
+        ),
     )
     back_far = jnp.einsum(
         "rp,arc->apc", leaf_basis, back_exp.astype(jnp.bfloat16), preferred_element_type=jnp.float32

time: 96.3 us -> 95.6 us (level)
    ppermute x8, waiting for transfers between devices: 25.7 us -> 23.5 us  [partner(): lax.ppermute(shard, axis, [(i, i ^ 1 << apart) for i in range(lax.axis_si...]
    ppermute x4, waiting for transfers between devices: 14.7 us -> 16.5 us  [shifted(): lax.ppermute(value, axis, [(source, source + steps) for source in range(l...]
    unnamed x24 -> x20, local copies, waits for them, and re-layouts: 2.56 us -> 2.54 us
where the time goes in v12:
time: 95.6 us; the launch traced here: 95.2 us
  waiting for transfers between devices  40 us (42%)
  starting transfers between devices  19.9 us (21%)
  Pallas kernels  16.4 us (17%)
  matrix products  12.7 us (13%)
  local copies, waits for them, and re-layouts  4.91 us (5%)
    ppermute x8, waiting for transfers between devices, partner(): lax.ppermute(shard, axis, [(i, i ^ 1 << apart) for i in range(lax.axis_si...  23.5 us
    ppermute x4, waiting for transfers between devices, shifted(): lax.ppermute(value, axis, [(source, source + steps) for source in range(l...  16.5 us
    ppermute x4, starting transfers between devices, shifted(): lax.ppermute(value, axis, [(source, source + steps) for source in range(l...  12.6 us
    pallas_call x1, Pallas kernels, near_backward(): pl.pallas_call(functools.partial(near_bwd_kernel, cases, pairs, rows, ste...  8.91 us
    pallas_call x1, Pallas kernels, near_forward(): pl.pallas_call(functools.partial(near_fwd_kernel, cases, pairs, rows), ou...  7.47 us
    ppermute x8, starting transfers between devices, partner(): lax.ppermute(shard, axis, [(i, i ^ 1 << apart) for i in range(lax.axis_si...  7.38 us
    dot_general x1, matrix products, on_device(): jnp.einsum('apc,cd->apd', near_bf, w_near, preferred_element_type=jnp.flo...  4.55 us
    unnamed x20, local copies, waits for them, and re-layouts  2.54 us
  transfers between devices with their start and end apart: 12, of which 9 were waited for; matrix products, arithmetic and copies ran while one was open for 7% of the time, Pallas kernels for 9%

profile of v12, /device:TPU:16, one launch (start us, length us, event | category | flops | bytes accessed | tf_op | source)
XLA Modules:
  0.0 95.2 jit_solution(13176172653171986177)
XLA Ops:
  0.7 0.9 copy-done
  1.6 1.5 %convolution_bitcast_fusion.2 = f32[2,64,128]{2,1,0:T(8,128)S(1)} fusion(bf16[2,2048,128]{2,1,0:T(8,128)(2,1)} %own_hbm.1, bf16[64,2048]{1,0:T(8,128)(2,1)S(1)} %copy-done), kind=kOutput, calls=%fused_computation.21 | convolution fusion | flops 67108864 | bytes 1376256 | tf_op jit(solution)/shard_map/rp,apc->arc/dot_general | solution.py:221
  3.1 1.6 %collective-permute-start.2 = (f32[2,64,128]{2,1,0:T(8,128)S(1)}, f32[2,64,128]{2,1,0:T(8,128)S(1)}, u32[]{:S(2)}, u32[]{:S(2)}) collective-permute-start(f32[2,64,128]{2,1,0:T(8,128)S(1)} %convolution_bitcast_fusion.2), channel_id=1, source_target_pairs={{0,4},{4,0},{8,12},{12,8},{16,20},{20,16},{24,28},{28,24},{1,5},{5... | collective-permute-start | bytes 196616 | tf_op jit(solution)/shard_map/ppermute | solution.py:17
  4.7 1.0 %fusion.46 = (bf16[2,1024,128]{2,1,0:T(8,128)(2,1)}, bf16[2,1024,128]{2,1,0:T(8,128)(2,1)}) fusion(bf16[2,2048,128]{2,1,0:T(8,128)(2,1)S(1)} %copy-done.1), kind=kLoop, calls=%fused_computation.70 | loop fusion | bytes 2097152 | tf_op jit(solution)/shard_map/slice | solution.py:211
  5.7 2.3 %collective-permute-start.1 = (bf16[2,1024,128]{2,1,0:T(8,128)(2,1)}, bf16[2,1024,128]{2,1,0:T(8,128)(2,1)S(1)}, u32[]{:S(2)}, u32[]{:S(2)}) collective-permute-start(bf16[2,1024,128]{2,1,0:T(8,128)(2,1)} %get-tuple-element.26), channel_id=1, source_target_pairs={{4,0},{8,4},{12,8},{16,12},{20,16},{24,20},{28,24},{5,1},{9,5},{13... | collective-permute-start | bytes 1572872 | tf_op jit(solution)/shard_map/ppermute | solution.py:23
  8.0 3.5 %collective-permute-start = (bf16[2,1024,128]{2,1,0:T(8,128)(2,1)}, bf16[2,1024,128]{2,1,0:T(8,128)(2,1)S(1)}, u32[]{:S(2)}, u32[]{:S(2)}) collective-permute-start(bf16[2,1024,128]{2,1,0:T(8,128)(2,1)} %get-tuple-element.27), channel_id=1, source_target_pairs={{0,4},{4,8},{8,12},{12,16},{16,20},{20,24},{24,28},{1,5},{5,9},{9,... | collective-permute-start | bytes 1572872 | tf_op jit(solution)/shard_map/ppermute | solution.py:23
  11.6 1.7 %collective-permute-start.3 = (f32[2,64,128]{2,1,0:T(8,128)S(1)}, f32[2,64,128]{2,1,0:T(8,128)S(1)}, u32[]{:S(2)}, u32[]{:S(2)}) collective-permute-start(f32[2,64,128]{2,1,0:T(8,128)S(1)} %add.65), channel_id=1, source_target_pairs={{0,8},{4,12},{8,0},{12,4},{16,24},{20,28},{24,16},{28,20},{1,9},{5... | collective-permute-start | bytes 196616 | tf_op jit(solution)/shard_map/ppermute | solution.py:17
  13.3 0.7 reshape.29.ids_ref
  14.0 9.2 %collective-permute-done.3 = f32[2,64,128]{2,1,0:T(8,128)S(1)} collective-permute-done((f32[2,64,128]{2,1,0:T(8,128)S(1)}, f32[2,64,128]{2,1,0:T(8,128)S(1)}, u32[]{:S(2)}, u32[]{:S(2)}) %collective-permute-start.3) | collective-permute-done | bytes 65568 | tf_op jit(solution)/shard_map/ppermute | solution.py:17
  23.5 4.9 %collective-permute-done.4 = f32[2,64,128]{2,1,0:T(8,128)S(1)} collective-permute-done((f32[2,64,128]{2,1,0:T(8,128)S(1)}, f32[2,64,128]{2,1,0:T(8,128)S(1)}, u32[]{:S(2)}, u32[]{:S(2)}) %collective-permute-start.4) | collective-permute-done | bytes 65568 | tf_op jit(solution)/shard_map/ppermute | solution.py:17
  28.8 1.3 %convolution_bitcast_fusion.1 = f32[2,2048,128]{2,1,0:T(8,128)S(1)} fusion(bf16[2,64,128]{2,1,0:T(8,128)(2,1)S(1)} %fusion.18, bf16[64,2048]{1,0:T(8,128)(2,1)S(1)} %copy-done, bf16[128,128]{1,0:T(8,128)(2,1)} %param.14), kind=kOutput, calls=%fused_computation.3 | convolution fusion | flops 71319552 | bytes 2424832 | tf_op jit(solution)/shard_map/rp,ard->apd/dot_general | solution.py:227
  30.1 2.3 %collective-permute-done.1.next_hbm = bf16[2,1024,128]{2,1,0:T(8,128)(2,1)S(1)} collective-permute-done((bf16[2,1024,128]{2,1,0:T(8,128)(2,1)}, bf16[2,1024,128]{2,1,0:T(8,128)(2,1)S(1)}, u32[]{:S(2)}, u32[]{:S(2)}) %collective-permute-start.1) | collective-permute-done | bytes 524320 | tf_op jit(solution)/shard_map/ppermute | solution.py:23
  32.5 0.8 copy-done.4
  33.3 0.8 copy-done.5
  34.0 7.5 %shard_map.111 = bf16[2,2048,128]{2,1,0:T(8,128)(2,1)} custom-call(s32[192]{0:T(256)} %reshape.29.ids_ref, bf16[16,12,128,128]{3,2,1,0:T(8,128)(2,1)} %kb_ref.3, bf16[2,1024,128]{2,1,0:T(8,128)(2,1)} %copy-done.5, bf16[2,2048,128]{2,1,0:T(8,128)(2,1)} %own_hbm.1, bf16[2,1024,128]{2,1,0:T(8,128)(2,1)} %copy-done.4), custom_call_target="tpu_custom_call" | custom-call | flops 1610612736 | bytes 9437184 | tf_op jit(solution)/shard_map/pallas_call | solution.py:103
  41.5 4.6 %fusion.2 = (bf16[2,2048,128]{2,1,0:T(8,128)(2,1)S(1)}, bf16[2,2048,128]{2,1,0:T(8,128)(2,1)}) fusion(bf16[2,2048,128]{2,1,0:T(8,128)(2,1)} %param.9, f32[2,2048,128]{2,1,0:T(8,128)S(1)} %convolution_bitcast_fusion.1, bf16[2,2048,128]{2,1,0:T(8,128)(2,1)} %shard_map.111, bf16[128,128]{1,0:T(8,128)(2,1)} %param.13), kind=kOutput, calls=%fused_computation.10 | convolution fusion | flops 146800640 | bytes 6324224 | tf_op jit(solution)/shard_map/apc,cd->apd/dot_general | solution.py:229
  46.1 0.5 fusion.12
  47.3 0.7 collective-permute-start.5
  47.9 1.4 %convolution_convert_fusion.back_ref = bf16[2,2048,128]{2,1,0:T(8,128)(2,1)} fusion(bf16[2,2048,128]{2,1,0:T(8,128)(2,1)S(1)} %get-tuple-element.24, bf16[128,128]{1,0:T(8,128)(2,1)S(1)} %copy-done.8), kind=kOutput, calls=%fused_computation.7 | convolution fusion | flops 134742016 | bytes 2129920 | tf_op jit(solution)/shard_map/apc,dc->apd/dot_general | solution.py:237
  49.4 3.7 %collective-permute-done.5 = f32[384,128]{1,0:T(8,128)S(1)} collective-permute-done((f32[384,128]{1,0:T(8,128)S(1)}, f32[384,128]{1,0:T(8,128)S(1)}, u32[]{:S(2)}, u32[]{:S(2)}) %collective-permute-start.5) | collective-permute-done | bytes 196640 | tf_op jit(solution)/shard_map/ppermute | solution.py:17
  53.1 1.6 %collective-permute-start.6 = (f32[384,128]{1,0:T(8,128)S(1)}, f32[384,128]{1,0:T(8,128)S(1)}, u32[]{:S(2)}, u32[]{:S(2)}) collective-permute-start(f32[384,128]{1,0:T(8,128)S(1)} %pad_maximum_fusion.1), channel_id=1, source_target_pairs={{0,8},{4,12},{8,0},{12,4},{16,24},{20,28},{24,16},{28,20},{1,9},{5... | collective-permute-start | bytes 589832 | tf_op jit(solution)/shard_map/ppermute | solution.py:17
  54.7 8.9 %shard_map.112 = (f32[2,2048,128]{2,1,0:T(8,128)}, bf16[2,1024,128]{2,1,0:T(8,128)(2,1)}, bf16[2,1024,128]{2,1,0:T(8,128)(2,1)}) custom-call(s32[192]{0:T(256)} %reshape.29.ids_ref, bf16[16,12,128,128]{3,2,1,0:T(8,128)(2,1)} %kb_ref.3, bf16[2,2048,128]{2,1,0:T(8,128)(2,1)} %convolution_convert_fusion.back_ref), custom_call_target="tpu_custom_call" | custom-call | flops 1610612736 | bytes 11534336 | tf_op jit(solution)/shard_map/pallas_call | solution.py:166
  64.4 3.7 %collective-permute-start.7 = (bf16[2,1024,128]{2,1,0:T(8,128)(2,1)}, bf16[2,1024,128]{2,1,0:T(8,128)(2,1)S(1)}, u32[]{:S(2)}, u32[]{:S(2)}) collective-permute-start(bf16[2,1024,128]{2,1,0:T(8,128)(2,1)} %get-tuple-element.19), channel_id=1, source_target_pairs={{0,4},{4,8},{8,12},{12,16},{16,20},{20,24},{24,28},{1,5},{5,9},{9,... | collective-permute-start | bytes 1572872 | tf_op jit(solution)/shard_map/ppermute | solution.py:23
  68.1 3.1 %collective-permute-start.8 = (bf16[2,1024,128]{2,1,0:T(8,128)(2,1)}, bf16[2,1024,128]{2,1,0:T(8,128)(2,1)S(1)}, u32[]{:S(2)}, u32[]{:S(2)}) collective-permute-start(bf16[2,1024,128]{2,1,0:T(8,128)(2,1)} %get-tuple-element.20), channel_id=1, source_target_pairs={{4,0},{8,4},{12,8},{16,12},{20,16},{24,20},{28,24},{5,1},{9,5},{13... | collective-permute-start | bytes 1572872 | tf_op jit(solution)/shard_map/ppermute | solution.py:23
  71.2 0.5 collective-permute-done.9
  72.0 1.1 %collective-permute-done.10 = f32[256,128]{1,0:T(8,128)S(1)} collective-permute-done((f32[256,128]{1,0:T(8,128)S(1)}, f32[256,128]{1,0:T(8,128)S(1)}, u32[]{:S(2)}, u32[]{:S(2)}) %collective-permute-start.10) | collective-permute-done | bytes 131104 | tf_op jit(solution)/shard_map/ppermute | solution.py:17
  73.1 1.3 %collective-permute-start.11 = (f32[256,128]{1,0:T(8,128)S(1)}, f32[256,128]{1,0:T(8,128)S(1)}, u32[]{:S(2)}, u32[]{:S(2)}) collective-permute-start(f32[256,128]{1,0:T(8,128)S(1)} %add.82), channel_id=1, source_target_pairs={{0,2},{1,3},{2,0},{3,1},{4,6},{5,7},{6,4},{7,5},{8,10},{9,11},{10,... | collective-permute-start | bytes 393224 | tf_op jit(solution)/shard_map/ppermute | solution.py:17
  74.7 4.1 %collective-permute-done.11 = f32[256,128]{1,0:T(8,128)S(1)} collective-permute-done((f32[256,128]{1,0:T(8,128)S(1)}, f32[256,128]{1,0:T(8,128)S(1)}, u32[]{:S(2)}, u32[]{:S(2)}) %collective-permute-start.11) | collective-permute-done | bytes 131104 | tf_op jit(solution)/shard_map/ppermute | solution.py:17
  78.8 0.7 fusion.47
  79.4 10.1 %collective-permute-done.7 = bf16[2,1024,128]{2,1,0:T(8,128)(2,1)S(1)} collective-permute-done((bf16[2,1024,128]{2,1,0:T(8,128)(2,1)}, bf16[2,1024,128]{2,1,0:T(8,128)(2,1)S(1)}, u32[]{:S(2)}, u32[]{:S(2)}) %collective-permute-start.7) | collective-permute-done | bytes 524320 | tf_op jit(solution)/shard_map/ppermute | solution.py:23
  89.5 4.0 %collective-permute-done.8 = bf16[2,1024,128]{2,1,0:T(8,128)(2,1)S(1)} collective-permute-done((bf16[2,1024,128]{2,1,0:T(8,128)(2,1)}, bf16[2,1024,128]{2,1,0:T(8,128)(2,1)S(1)}, u32[]{:S(2)}, u32[]{:S(2)}) %collective-permute-start.8) | collective-permute-done | bytes 524320 | tf_op jit(solution)/shard_map/ppermute | solution.py:23
  93.7 1.5 %fusion.10 = bf16[2,2048,128]{2,1,0:T(8,128)(2,1)} fusion(f32[2,1024,128]{2,1,0:T(8,128)S(1)} %get-tuple-element.23, f32[2,1024,128]{2,1,0:T(8,128)S(1)} %get-tuple-element.22, bf16[2,64,128]{2,1,0:T(8,128)(2,1)S(1)} %fusion.17, bf16[64,2048]{1,0:T(8,128)(2,1)S(1)} %copy-done), kind=kOutput, calls=%fused_computation.19 | convolution fusion | flops 68681728 | bytes 3440640 | tf_op jit(solution)/shard_map/rp,arc->apc/dot_general | solution.py:264
  (49 shorter events, 3.0 us)
Async XLA Ops:
  0.6 1.0 %copy-start = (bf16[64,2048]{1,0:T(8,128)(2,1)S(1)}, bf16[64,2048]{1,0:T(8,128)(2,1)}, u32[]{:S(2)}) copy-start(bf16[64,2048]{1,0:T(8,128)(2,1)} %param.12) | copy-start | bytes 786436
  0.6 4.1 %copy-start.1 = (bf16[2,2048,128]{2,1,0:T(8,128)(2,1)S(1)}, bf16[2,2048,128]{2,1,0:T(8,128)(2,1)}, u32[]{:S(2)}) copy-start(bf16[2,2048,128]{2,1,0:T(8,128)(2,1)} %own_hbm.1) | copy-start | bytes 3145732
  0.7 12.6 %copy-start.9 = (s32[16,12]{1,0:T(8,128)S(1)}, s32[16,12]{1,0:T(8,128)}, u32[]{:S(2)}) copy-start(s32[16,12]{1,0:T(8,128)} %param.11) | copy-start | bytes 2308
  0.7 22.6 %copy-start.6 = (f32[3,64,64]{2,1,0:T(8,128)S(1)}, f32[3,64,64]{2,1,0:T(8,128)}, u32[]{:S(2)}) copy-start(f32[3,64,64]{2,1,0:T(8,128)} %param.15) | copy-start | bytes 147460
  3.1 8.5 %collective-permute-start.2 = (f32[2,64,128]{2,1,0:T(8,128)S(1)}, f32[2,64,128]{2,1,0:T(8,128)S(1)}, u32[]{:S(2)}, u32[]{:S(2)}) collective-permute-start(f32[2,64,128]{2,1,0:T(8,128)S(1)} %convolution_bitcast_fusion.2), channel_id=1, source_target_pairs={{0,4},{4,0},{8,12},{12,8},{16,20},{20,16},{24,28},{28,24},{1,5},{5... | collective-permute-start | bytes 196616 | tf_op jit(solution)/shard_map/ppermute | solution.py:17
  5.7 26.7 %collective-permute-start.1 = (bf16[2,1024,128]{2,1,0:T(8,128)(2,1)}, bf16[2,1024,128]{2,1,0:T(8,128)(2,1)S(1)}, u32[]{:S(2)}, u32[]{:S(2)}) collective-permute-start(bf16[2,1024,128]{2,1,0:T(8,128)(2,1)} %get-tuple-element.26), channel_id=1, source_target_pairs={{4,0},{8,4},{12,8},{16,12},{20,16},{24,20},{28,24},{5,1},{9,5},{13... | collective-permute-start | bytes 1572872 | tf_op jit(solution)/shard_map/ppermute | solution.py:23
  8.0 24.4 %collective-permute-start = (bf16[2,1024,128]{2,1,0:T(8,128)(2,1)}, bf16[2,1024,128]{2,1,0:T(8,128)(2,1)S(1)}, u32[]{:S(2)}, u32[]{:S(2)}) collective-permute-start(bf16[2,1024,128]{2,1,0:T(8,128)(2,1)} %get-tuple-element.27), channel_id=1, source_target_pairs={{0,4},{4,8},{8,12},{12,16},{16,20},{20,24},{24,28},{1,5},{5,9},{9,... | collective-permute-start | bytes 1572872 | tf_op jit(solution)/shard_map/ppermute | solution.py:23
  11.6 11.5 %collective-permute-start.3 = (f32[2,64,128]{2,1,0:T(8,128)S(1)}, f32[2,64,128]{2,1,0:T(8,128)S(1)}, u32[]{:S(2)}, u32[]{:S(2)}) collective-permute-start(f32[2,64,128]{2,1,0:T(8,128)S(1)} %add.65), channel_id=1, source_target_pairs={{0,8},{4,12},{8,0},{12,4},{16,24},{20,28},{24,16},{28,20},{1,9},{5... | collective-permute-start | bytes 196616 | tf_op jit(solution)/shard_map/ppermute | solution.py:17
  23.2 5.2 %collective-permute-start.4 = (f32[2,64,128]{2,1,0:T(8,128)S(1)}, f32[2,64,128]{2,1,0:T(8,128)S(1)}, u32[]{:S(2)}, u32[]{:S(2)}) collective-permute-start(f32[2,64,128]{2,1,0:T(8,128)S(1)} %add.67), channel_id=1, source_target_pairs={{0,16},{4,20},{8,24},{12,28},{16,0},{20,4},{24,8},{28,12},{1,17},{... | collective-permute-start | bytes 196616 | tf_op jit(solution)/shard_map/ppermute | solution.py:17
  32.5 0.8 copy-start.4
  33.3 0.8 copy-start.5
  41.5 4.6 %copy-start.2 = (bf16[2,2048,128]{2,1,0:T(8,128)(2,1)S(1)}, bf16[2,2048,128]{2,1,0:T(8,128)(2,1)}, u32[]{:S(2)}) copy-start(bf16[2,2048,128]{2,1,0:T(8,128)(2,1)} %shard_map.111) | copy-start | bytes 3145732
  46.1 1.0 %copy-start.7 = (bf16[128,128]{1,0:T(8,128)(2,1)S(1)}, bf16[128,128]{1,0:T(8,128)(2,1)}, u32[]{:S(2)}) copy-start(bf16[128,128]{1,0:T(8,128)(2,1)} %param.14) | copy-start | bytes 98308
  46.1 1.9 %copy-start.8 = (bf16[128,128]{1,0:T(8,128)(2,1)S(1)}, bf16[128,128]{1,0:T(8,128)(2,1)}, u32[]{:S(2)}) copy-start(bf16[128,128]{1,0:T(8,128)(2,1)} %param.13) | copy-start | bytes 98308
  47.3 5.8 %collective-permute-start.5 = (f32[384,128]{1,0:T(8,128)S(1)}, f32[384,128]{1,0:T(8,128)S(1)}, u32[]{:S(2)}, u32[]{:S(2)}) collective-permute-start(f32[384,128]{1,0:T(8,128)S(1)} %pad_maximum_fusion), channel_id=1, source_target_pairs={{0,4},{4,0},{8,12},{12,8},{16,20},{20,16},{24,28},{28,24},{1,5},{5... | collective-permute-start | bytes 589832 | tf_op jit(solution)/shard_map/ppermute | solution.py:17
  53.1 10.5 %collective-permute-start.6 = (f32[384,128]{1,0:T(8,128)S(1)}, f32[384,128]{1,0:T(8,128)S(1)}, u32[]{:S(2)}, u32[]{:S(2)}) collective-permute-start(f32[384,128]{1,0:T(8,128)S(1)} %pad_maximum_fusion.1), channel_id=1, source_target_pairs={{0,8},{4,12},{8,0},{12,4},{16,24},{20,28},{24,16},{28,20},{1,9},{5... | collective-permute-start | bytes 589832 | tf_op jit(solution)/shard_map/ppermute | solution.py:17
  63.6 29.9 %copy-start.3 = (f32[2,2048,128]{2,1,0:T(8,128)S(1)}, f32[2,2048,128]{2,1,0:T(8,128)}, u32[]{:S(2)}) copy-start(f32[2,2048,128]{2,1,0:T(8,128)} %get-tuple-element.18) | copy-start | bytes 6291460
  63.7 8.0 %collective-permute-start.9 = (f32[384,128]{1,0:T(8,128)S(1)}, f32[384,128]{1,0:T(8,128)S(1)}, u32[]{:S(2)}, u32[]{:S(2)}) collective-permute-start(f32[384,128]{1,0:T(8,128)S(1)} %pad_maximum_fusion.2), channel_id=1, source_target_pairs={{0,16},{4,20},{8,24},{12,28},{16,0},{20,4},{24,8},{28,12},{1,17},{... | collective-permute-start | bytes 589832 | tf_op jit(solution)/shard_map/ppermute | solution.py:17
  64.4 25.1 %collective-permute-start.7 = (bf16[2,1024,128]{2,1,0:T(8,128)(2,1)}, bf16[2,1024,128]{2,1,0:T(8,128)(2,1)S(1)}, u32[]{:S(2)}, u32[]{:S(2)}) collective-permute-start(bf16[2,1024,128]{2,1,0:T(8,128)(2,1)} %get-tuple-element.19), channel_id=1, source_target_pairs={{0,4},{4,8},{8,12},{12,16},{16,20},{20,24},{24,28},{1,5},{5,9},{9,... | collective-permute-start | bytes 1572872 | tf_op jit(solution)/shard_map/ppermute | solution.py:23
  68.1 25.5 %collective-permute-start.8 = (bf16[2,1024,128]{2,1,0:T(8,128)(2,1)}, bf16[2,1024,128]{2,1,0:T(8,128)(2,1)S(1)}, u32[]{:S(2)}, u32[]{:S(2)}) collective-permute-start(bf16[2,1024,128]{2,1,0:T(8,128)(2,1)} %get-tuple-element.20), channel_id=1, source_target_pairs={{4,0},{8,4},{12,8},{16,12},{20,16},{24,20},{28,24},{5,1},{9,5},{13... | collective-permute-start | bytes 1572872 | tf_op jit(solution)/shard_map/ppermute | solution.py:23
  71.7 1.4 %collective-permute-start.10 = (f32[256,128]{1,0:T(8,128)S(1)}, f32[256,128]{1,0:T(8,128)S(1)}, u32[]{:S(2)}, u32[]{:S(2)}) collective-permute-start(f32[256,128]{1,0:T(8,128)S(1)} %slice_add_fusion), channel_id=1, source_target_pairs={{0,1},{1,0},{2,3},{3,2},{4,5},{5,4},{6,7},{7,6},{8,9},{9,8},{10,11... | collective-permute-start | bytes 393224 | tf_op jit(solution)/shard_map/ppermute | solution.py:17
  73.1 5.6 %collective-permute-start.11 = (f32[256,128]{1,0:T(8,128)S(1)}, f32[256,128]{1,0:T(8,128)S(1)}, u32[]{:S(2)}, u32[]{:S(2)}) collective-permute-start(f32[256,128]{1,0:T(8,128)S(1)} %add.82), channel_id=1, source_target_pairs={{0,2},{1,3},{2,0},{3,1},{4,6},{5,7},{6,4},{7,5},{8,10},{9,11},{10,... | collective-permute-start | bytes 393224 | tf_op jit(solution)/shard_map/ppermute | solution.py:17

commit v13 on v12

--- a/solution.py
+++ b/solution.py
@@ -211,6 +211,7 @@
     head = features[:, :halo_points]
     tail = features[:, points_here - halo_points :]
     from_prev = shifted(tail, "leaf", 1)
+    head, from_prev = lax.optimization_barrier((head, from_prev))
     from_next = shifted(head, "leaf", -1)
     local_ids = jnp.clip(
         near_pairs - (position * blocks_here - HALO), 0, span_blocks - 1
@@ -269,8 +270,10 @@
     for height in range(case_depth):
         grads = grads + partner(grads, "case", height)
 
-    got_prev = shifted(hi, "leaf", 1).astype(jnp.float32)
+    got_prev = shifted(hi, "leaf", 1)
+    lo, got_prev = lax.optimization_barrier((lo, got_prev))
     got_next = shifted(lo, "leaf", -1).astype(jnp.float32)
+    got_prev = got_prev.astype(jnp.float32)
     near_back = jnp.concatenate(
         [
             mid[:, :halo_points] + got_prev,

time: 95.6 us -> 110 us (1.15)
  the two profiles are of different devices: /device:TPU:16 before, /device:TPU:14 now
where the time goes in v13:
time: 110 us
  waiting for transfers between devices  57.7 us (52%)
  starting transfers between devices  18.2 us (17%)
  Pallas kernels  16.4 us (15%)
  matrix products  11.5 us (10%)
  local copies, waits for them, and re-layouts  4.36 us (4%)
    ppermute x8, waiting for transfers between devices, partner(): lax.ppermute(shard, axis, [(i, i ^ 1 << apart) for i in range(lax.axis_si...  39.7 us
    ppermute x4, waiting for transfers between devices, shifted(): lax.ppermute(value, axis, [(source, source + steps) for source in range(l...  18 us
    ppermute x4, starting transfers between devices, shifted(): lax.ppermute(value, axis, [(source, source + steps) for source in range(l...  11.3 us
    pallas_call x1, Pallas kernels, near_backward(): pl.pallas_call(functools.partial(near_bwd_kernel, cases, pairs, rows, ste...  8.91 us
    pallas_call x1, Pallas kernels, near_forward(): pl.pallas_call(functools.partial(near_fwd_kernel, cases, pairs, rows), ou...  7.48 us
    ppermute x8, starting transfers between devices, partner(): lax.ppermute(shard, axis, [(i, i ^ 1 << apart) for i in range(lax.axis_si...  6.9 us
    dot_general x1, matrix products, on_device(): jnp.einsum('apc,cd->apd', near_bf, w_near, preferred_element_type=jnp.flo...  4.55 us
  transfers between devices with their start and end apart: 12, of which 7 were waited for; matrix products, arithmetic and copies ran while one was open for 5% of the time, Pallas kernels for 8%

profile of v13, /device:TPU:14, one launch (start us, length us, event | category | flops | bytes accessed | tf_op | source)
XLA Modules:
  0.0 109.5 jit_solution(17031048389679209749)
XLA Ops:
  0.7 2.2 %fusion.46 = (bf16[2,1024,128]{2,1,0:T(8,128)(2,1)S(1)}, bf16[2,1024,128]{2,1,0:T(8,128)(2,1)}) fusion(bf16[2,2048,128]{2,1,0:T(8,128)(2,1)} %own_hbm.1), kind=kLoop, calls=%fused_computation.70 | loop fusion | bytes 2097152 | tf_op jit(solution)/shard_map/slice | solution.py:212
  2.9 3.4 %collective-permute-start = (bf16[2,1024,128]{2,1,0:T(8,128)(2,1)S(1)}, bf16[2,1024,128]{2,1,0:T(8,128)(2,1)S(1)}, u32[]{:S(2)}, u32[]{:S(2)}) collective-permute-start(bf16[2,1024,128]{2,1,0:T(8,128)(2,1)S(1)} %get-tuple-element.34), channel_id=1, source_target_pairs={{0,4},{4,8},{8,12},{12,16},{16,20},{20,24},{24,28},{1,5},{5,9},{9,... | collective-permute-start | bytes 1572872 | tf_op jit(solution)/shard_map/ppermute | solution.py:23
  6.3 0.3 convolution_bitcast_fusion.2
  6.6 0.6 collective-permute-start.2
  7.2 12.6 %collective-permute-done.2 = f32[2,64,128]{2,1,0:T(8,128)S(1)} collective-permute-done((f32[2,64,128]{2,1,0:T(8,128)S(1)}, f32[2,64,128]{2,1,0:T(8,128)S(1)}, u32[]{:S(2)}, u32[]{:S(2)}) %collective-permute-start.2) | collective-permute-done | bytes 65568 | tf_op jit(solution)/shard_map/ppermute | solution.py:17
  19.8 0.5 collective-permute-start.3
  20.3 0.7 reshape.29.ids_ref
  21.0 3.2 %collective-permute-done.3 = f32[2,64,128]{2,1,0:T(8,128)S(1)} collective-permute-done((f32[2,64,128]{2,1,0:T(8,128)S(1)}, f32[2,64,128]{2,1,0:T(8,128)S(1)}, u32[]{:S(2)}, u32[]{:S(2)}) %collective-permute-start.3) | collective-permute-done | bytes 65568 | tf_op jit(solution)/shard_map/ppermute | solution.py:17
  24.2 2.7 %collective-permute-start.4 = (f32[2,64,128]{2,1,0:T(8,128)S(1)}, f32[2,64,128]{2,1,0:T(8,128)S(1)}, u32[]{:S(2)}, u32[]{:S(2)}) collective-permute-start(f32[2,64,128]{2,1,0:T(8,128)S(1)} %add.67), channel_id=1, source_target_pairs={{0,16},{4,20},{8,24},{12,28},{16,0},{20,4},{24,8},{28,12},{1,17},{... | collective-permute-start | bytes 196616 | tf_op jit(solution)/shard_map/ppermute | solution.py:17
  27.0 3.3 %collective-permute-start.1 = (bf16[2,1024,128]{2,1,0:T(8,128)(2,1)}, bf16[2,1024,128]{2,1,0:T(8,128)(2,1)S(1)}, u32[]{:S(2)}, u32[]{:S(2)}) collective-permute-start(bf16[2,1024,128]{2,1,0:T(8,128)(2,1)} %get-tuple-element.18), channel_id=1, source_target_pairs={{4,0},{8,4},{12,8},{16,12},{20,16},{24,20},{28,24},{5,1},{9,5},{13... | collective-permute-start | bytes 1572872 | tf_op jit(solution)/shard_map/ppermute | solution.py:23
  30.8 1.3 %convolution_bitcast_fusion.1 = f32[2,2048,128]{2,1,0:T(8,128)S(1)} fusion(bf16[2,64,128]{2,1,0:T(8,128)(2,1)S(1)} %fusion.18, bf16[64,2048]{1,0:T(8,128)(2,1)S(1)} %copy-done, bf16[128,128]{1,0:T(8,128)(2,1)} %param.14), kind=kOutput, calls=%fused_computation.3 | convolution fusion | flops 71319552 | bytes 2424832 | tf_op jit(solution)/shard_map/rp,ard->apd/dot_general | solution.py:228
  32.1 9.6 %collective-permute-done.1.next_hbm = bf16[2,1024,128]{2,1,0:T(8,128)(2,1)S(1)} collective-permute-done((bf16[2,1024,128]{2,1,0:T(8,128)(2,1)}, bf16[2,1024,128]{2,1,0:T(8,128)(2,1)S(1)}, u32[]{:S(2)}, u32[]{:S(2)}) %collective-permute-start.1) | collective-permute-done | bytes 524320 | tf_op jit(solution)/shard_map/ppermute | solution.py:23
  41.7 0.8 copy-done.5
  42.5 7.5 %shard_map.111 = bf16[2,2048,128]{2,1,0:T(8,128)(2,1)} custom-call(s32[192]{0:T(256)} %reshape.29.ids_ref, bf16[16,12,128,128]{3,2,1,0:T(8,128)(2,1)} %kb_ref.3, bf16[2,1024,128]{2,1,0:T(8,128)(2,1)} %copy-done.4, bf16[2,2048,128]{2,1,0:T(8,128)(2,1)} %own_hbm.1, bf16[2,1024,128]{2,1,0:T(8,128)(2,1)} %copy-done.5), custom_call_target="tpu_custom_call" | custom-call | flops 1610612736 | bytes 9437184 | tf_op jit(solution)/shard_map/pallas_call | solution.py:103
  50.0 4.6 %fusion.2 = (bf16[2,2048,128]{2,1,0:T(8,128)(2,1)S(1)}, bf16[2,2048,128]{2,1,0:T(8,128)(2,1)}) fusion(bf16[2,2048,128]{2,1,0:T(8,128)(2,1)} %param.9, f32[2,2048,128]{2,1,0:T(8,128)S(1)} %convolution_bitcast_fusion.1, bf16[2,2048,128]{2,1,0:T(8,128)(2,1)} %shard_map.111, bf16[128,128]{1,0:T(8,128)(2,1)} %param.13), kind=kOutput, calls=%fused_computation.10 | convolution fusion | flops 146800640 | bytes 6324224 | tf_op jit(solution)/shard_map/apc,cd->apd/dot_general | solution.py:230
  54.5 0.5 fusion.12
  55.0 0.3 fusion.16
  55.7 1.4 %collective-permute-start.5 = (f32[384,128]{1,0:T(8,128)S(1)}, f32[384,128]{1,0:T(8,128)S(1)}, u32[]{:S(2)}, u32[]{:S(2)}) collective-permute-start(f32[384,128]{1,0:T(8,128)S(1)} %pad_maximum_fusion), channel_id=1, source_target_pairs={{0,4},{4,0},{8,12},{12,8},{16,20},{20,16},{24,28},{28,24},{1,5},{5... | collective-permute-start | bytes 589832 | tf_op jit(solution)/shard_map/ppermute | solution.py:17
  57.1 1.4 %convolution_convert_fusion.back_ref = bf16[2,2048,128]{2,1,0:T(8,128)(2,1)} fusion(bf16[2,2048,128]{2,1,0:T(8,128)(2,1)S(1)} %get-tuple-element.32, bf16[128,128]{1,0:T(8,128)(2,1)S(1)} %copy-done.8), kind=kOutput, calls=%fused_computation.7 | convolution fusion | flops 134742016 | bytes 2129920 | tf_op jit(solution)/shard_map/apc,dc->apd/dot_general | solution.py:238
  58.5 3.0 %collective-permute-done.5 = f32[384,128]{1,0:T(8,128)S(1)} collective-permute-done((f32[384,128]{1,0:T(8,128)S(1)}, f32[384,128]{1,0:T(8,128)S(1)}, u32[]{:S(2)}, u32[]{:S(2)}) %collective-permute-start.5) | collective-permute-done | bytes 196640 | tf_op jit(solution)/shard_map/ppermute | solution.py:17
  61.5 1.1 collective-permute-start.6
  62.6 8.9 %shard_map.112 = (f32[2,2048,128]{2,1,0:T(8,128)}, bf16[2,1024,128]{2,1,0:T(8,128)(2,1)}, bf16[2,1024,128]{2,1,0:T(8,128)(2,1)}) custom-call(s32[192]{0:T(256)} %reshape.29.ids_ref, bf16[16,12,128,128]{3,2,1,0:T(8,128)(2,1)} %kb_ref.3, bf16[2,2048,128]{2,1,0:T(8,128)(2,1)} %convolution_convert_fusion.back_ref), custom_call_target="tpu_custom_call" | custom-call | flops 1610612736 | bytes 11534336 | tf_op jit(solution)/shard_map/pallas_call | solution.py:166
  71.6 2.7 %collective-permute-start.7 = (bf16[2,1024,128]{2,1,0:T(8,128)(2,1)}, bf16[2,1024,128]{2,1,0:T(8,128)(2,1)S(1)}, u32[]{:S(2)}, u32[]{:S(2)}) collective-permute-start(bf16[2,1024,128]{2,1,0:T(8,128)(2,1)} %get-tuple-element.26), channel_id=1, source_target_pairs={{0,4},{4,8},{8,12},{12,16},{16,20},{20,24},{24,28},{1,5},{5,9},{9,... | collective-permute-start | bytes 1572872 | tf_op jit(solution)/shard_map/ppermute | solution.py:23
  74.6 15.8 %collective-permute-done.9 = f32[384,128]{1,0:T(8,128)S(1)} collective-permute-done((f32[384,128]{1,0:T(8,128)S(1)}, f32[384,128]{1,0:T(8,128)S(1)}, u32[]{:S(2)}, u32[]{:S(2)}) %collective-permute-start.9) | collective-permute-done | bytes 196640 | tf_op jit(solution)/shard_map/ppermute | solution.py:17
  90.5 1.9 %collective-permute-start.8 = (bf16[2,1024,128]{2,1,0:T(8,128)(2,1)}, bf16[2,1024,128]{2,1,0:T(8,128)(2,1)S(1)}, u32[]{:S(2)}, u32[]{:S(2)}) collective-permute-start(bf16[2,1024,128]{2,1,0:T(8,128)(2,1)} %get-tuple-element.28), channel_id=1, source_target_pairs={{4,0},{8,4},{12,8},{16,12},{20,16},{24,20},{28,24},{5,1},{9,5},{13... | collective-permute-start | bytes 1572872 | tf_op jit(solution)/shard_map/ppermute | solution.py:23
  92.5 0.3 convolution_add_fusion.2
  92.8 0.6 collective-permute-start.11
  93.4 0.3 fusion.17
  93.6 5.1 %collective-permute-done.11 = f32[256,128]{1,0:T(8,128)S(1)} collective-permute-done((f32[256,128]{1,0:T(8,128)S(1)}, f32[256,128]{1,0:T(8,128)S(1)}, u32[]{:S(2)}, u32[]{:S(2)}) %collective-permute-start.11) | collective-permute-done | bytes 131104 | tf_op jit(solution)/shard_map/ppermute | solution.py:17
  98.8 0.7 fusion.47
  99.4 8.4 %collective-permute-done.8 = bf16[2,1024,128]{2,1,0:T(8,128)(2,1)S(1)} collective-permute-done((bf16[2,1024,128]{2,1,0:T(8,128)(2,1)}, bf16[2,1024,128]{2,1,0:T(8,128)(2,1)S(1)}, u32[]{:S(2)}, u32[]{:S(2)}) %collective-permute-start.8) | collective-permute-done | bytes 524320 | tf_op jit(solution)/shard_map/ppermute | solution.py:23
  108.0 1.5 %fusion.10 = bf16[2,2048,128]{2,1,0:T(8,128)(2,1)} fusion(f32[2,1024,128]{2,1,0:T(8,128)S(1)} %get-tuple-element.31, f32[2,1024,128]{2,1,0:T(8,128)S(1)} %get-tuple-element.30, bf16[2,64,128]{2,1,0:T(8,128)(2,1)S(1)} %fusion.17, bf16[64,2048]{1,0:T(8,128)(2,1)S(1)} %copy-done), kind=kOutput, calls=%fused_computation.19 | convolution fusion | flops 68681728 | bytes 3440640 | tf_op jit(solution)/shard_map/rp,arc->apc/dot_general | solution.py:265
  (49 shorter events, 1.8 us)
Async XLA Ops:
  0.6 5.7 %copy-start = (bf16[64,2048]{1,0:T(8,128)(2,1)S(1)}, bf16[64,2048]{1,0:T(8,128)(2,1)}, u32[]{:S(2)}) copy-start(bf16[64,2048]{1,0:T(8,128)(2,1)} %param.12) | copy-start | bytes 786436
  0.6 5.6 %copy-start.1 = (bf16[2,2048,128]{2,1,0:T(8,128)(2,1)S(1)}, bf16[2,2048,128]{2,1,0:T(8,128)(2,1)}, u32[]{:S(2)}) copy-start(bf16[2,2048,128]{2,1,0:T(8,128)(2,1)} %own_hbm.1) | copy-start | bytes 3145732
  0.7 19.7 %copy-start.9 = (s32[16,12]{1,0:T(8,128)S(1)}, s32[16,12]{1,0:T(8,128)}, u32[]{:S(2)}) copy-start(s32[16,12]{1,0:T(8,128)} %param.11) | copy-start | bytes 2308
  0.7 26.2 %copy-start.6 = (f32[3,64,64]{2,1,0:T(8,128)S(1)}, f32[3,64,64]{2,1,0:T(8,128)}, u32[]{:S(2)}) copy-start(f32[3,64,64]{2,1,0:T(8,128)} %param.15) | copy-start | bytes 147460
  2.9 24.2 %collective-permute-start = (bf16[2,1024,128]{2,1,0:T(8,128)(2,1)S(1)}, bf16[2,1024,128]{2,1,0:T(8,128)(2,1)S(1)}, u32[]{:S(2)}, u32[]{:S(2)}) collective-permute-start(bf16[2,1024,128]{2,1,0:T(8,128)(2,1)S(1)} %get-tuple-element.34), channel_id=1, source_target_pairs={{0,4},{4,8},{8,12},{12,16},{16,20},{20,24},{24,28},{1,5},{5,9},{9,... | collective-permute-start | bytes 1572872 | tf_op jit(solution)/shard_map/ppermute | solution.py:23
  6.6 13.2 %collective-permute-start.2 = (f32[2,64,128]{2,1,0:T(8,128)S(1)}, f32[2,64,128]{2,1,0:T(8,128)S(1)}, u32[]{:S(2)}, u32[]{:S(2)}) collective-permute-start(f32[2,64,128]{2,1,0:T(8,128)S(1)} %convolution_bitcast_fusion.2), channel_id=1, source_target_pairs={{0,4},{4,0},{8,12},{12,8},{16,20},{20,16},{24,28},{28,24},{1,5},{5... | collective-permute-start | bytes 196616 | tf_op jit(solution)/shard_map/ppermute | solution.py:17
  19.8 4.3 %collective-permute-start.3 = (f32[2,64,128]{2,1,0:T(8,128)S(1)}, f32[2,64,128]{2,1,0:T(8,128)S(1)}, u32[]{:S(2)}, u32[]{:S(2)}) collective-permute-start(f32[2,64,128]{2,1,0:T(8,128)S(1)} %add.65), channel_id=1, source_target_pairs={{0,8},{4,12},{8,0},{12,4},{16,24},{20,28},{24,16},{28,20},{1,9},{5... | collective-permute-start | bytes 196616 | tf_op jit(solution)/shard_map/ppermute | solution.py:17
  24.2 6.2 %collective-permute-start.4 = (f32[2,64,128]{2,1,0:T(8,128)S(1)}, f32[2,64,128]{2,1,0:T(8,128)S(1)}, u32[]{:S(2)}, u32[]{:S(2)}) collective-permute-start(f32[2,64,128]{2,1,0:T(8,128)S(1)} %add.67), channel_id=1, source_target_pairs={{0,16},{4,20},{8,24},{12,28},{16,0},{20,4},{24,8},{28,12},{1,17},{... | collective-permute-start | bytes 196616 | tf_op jit(solution)/shard_map/ppermute | solution.py:17
  27.0 14.6 %copy-start.4 = (bf16[2,1024,128]{2,1,0:T(8,128)(2,1)}, bf16[2,1024,128]{2,1,0:T(8,128)(2,1)S(1)}, u32[]{:S(2)}) copy-start(bf16[2,1024,128]{2,1,0:T(8,128)(2,1)S(1)} %collective-permute-done.prev_hbm) | copy-start | bytes 1572868
  27.0 14.6 %collective-permute-start.1 = (bf16[2,1024,128]{2,1,0:T(8,128)(2,1)}, bf16[2,1024,128]{2,1,0:T(8,128)(2,1)S(1)}, u32[]{:S(2)}, u32[]{:S(2)}) collective-permute-start(bf16[2,1024,128]{2,1,0:T(8,128)(2,1)} %get-tuple-element.18), channel_id=1, source_target_pairs={{4,0},{8,4},{12,8},{16,12},{20,16},{24,20},{28,24},{5,1},{9,5},{13... | collective-permute-start | bytes 1572872 | tf_op jit(solution)/shard_map/ppermute | solution.py:23
  41.7 0.8 copy-start.5
  50.0 4.6 %copy-start.2 = (bf16[2,2048,128]{2,1,0:T(8,128)(2,1)S(1)}, bf16[2,2048,128]{2,1,0:T(8,128)(2,1)}, u32[]{:S(2)}) copy-start(bf16[2,2048,128]{2,1,0:T(8,128)(2,1)} %shard_map.111) | copy-start | bytes 3145732
  54.5 1.0 copy-start.7
  54.5 2.5 %copy-start.8 = (bf16[128,128]{1,0:T(8,128)(2,1)S(1)}, bf16[128,128]{1,0:T(8,128)(2,1)}, u32[]{:S(2)}) copy-start(bf16[128,128]{1,0:T(8,128)(2,1)} %param.13) | copy-start | bytes 98308
  55.7 5.7 %collective-permute-start.5 = (f32[384,128]{1,0:T(8,128)S(1)}, f32[384,128]{1,0:T(8,128)S(1)}, u32[]{:S(2)}, u32[]{:S(2)}) collective-permute-start(f32[384,128]{1,0:T(8,128)S(1)} %pad_maximum_fusion), channel_id=1, source_target_pairs={{0,4},{4,0},{8,12},{12,8},{16,20},{20,16},{24,28},{28,24},{1,5},{5... | collective-permute-start | bytes 589832 | tf_op jit(solution)/shard_map/ppermute | solution.py:17
  61.5 10.0 %collective-permute-start.6 = (f32[384,128]{1,0:T(8,128)S(1)}, f32[384,128]{1,0:T(8,128)S(1)}, u32[]{:S(2)}, u32[]{:S(2)}) collective-permute-start(f32[384,128]{1,0:T(8,128)S(1)} %pad_maximum_fusion.1), channel_id=1, source_target_pairs={{0,8},{4,12},{8,0},{12,4},{16,24},{20,28},{24,16},{28,20},{1,9},{5... | collective-permute-start | bytes 589832 | tf_op jit(solution)/shard_map/ppermute | solution.py:17
  71.5 36.4 %copy-start.3 = (f32[2,2048,128]{2,1,0:T(8,128)S(1)}, f32[2,2048,128]{2,1,0:T(8,128)}, u32[]{:S(2)}) copy-start(f32[2,2048,128]{2,1,0:T(8,128)} %get-tuple-element.24) | copy-start | bytes 6291460
  71.6 19.0 %collective-permute-start.7 = (bf16[2,1024,128]{2,1,0:T(8,128)(2,1)}, bf16[2,1024,128]{2,1,0:T(8,128)(2,1)S(1)}, u32[]{:S(2)}, u32[]{:S(2)}) collective-permute-start(bf16[2,1024,128]{2,1,0:T(8,128)(2,1)} %get-tuple-element.26), channel_id=1, source_target_pairs={{0,4},{4,8},{8,12},{12,16},{16,20},{20,24},{24,28},{1,5},{5,9},{9,... | collective-permute-start | bytes 1572872 | tf_op jit(solution)/shard_map/ppermute | solution.py:23
  74.3 16.2 %collective-permute-start.9 = (f32[384,128]{1,0:T(8,128)S(1)}, f32[384,128]{1,0:T(8,128)S(1)}, u32[]{:S(2)}, u32[]{:S(2)}) collective-permute-start(f32[384,128]{1,0:T(8,128)S(1)} %pad_maximum_fusion.2), channel_id=1, source_target_pairs={{0,16},{4,20},{8,24},{12,28},{16,0},{20,4},{24,8},{28,12},{1,17},{... | collective-permute-start | bytes 589832 | tf_op jit(solution)/shard_map/ppermute | solution.py:17
  90.5 2.3 %collective-permute-start.10 = (f32[256,128]{1,0:T(8,128)S(1)}, f32[256,128]{1,0:T(8,128)S(1)}, u32[]{:S(2)}, u32[]{:S(2)}) collective-permute-start(f32[256,128]{1,0:T(8,128)S(1)} %slice_add_fusion), channel_id=1, source_target_pairs={{0,1},{1,0},{2,3},{3,2},{4,5},{5,4},{6,7},{7,6},{8,9},{9,8},{10,11... | collective-permute-start | bytes 393224 | tf_op jit(solution)/shard_map/ppermute | solution.py:17
  90.5 17.3 %collective-permute-start.8 = (bf16[2,1024,128]{2,1,0:T(8,128)(2,1)}, bf16[2,1024,128]{2,1,0:T(8,128)(2,1)S(1)}, u32[]{:S(2)}, u32[]{:S(2)}) collective-permute-start(bf16[2,1024,128]{2,1,0:T(8,128)(2,1)} %get-tuple-element.28), channel_id=1, source_target_pairs={{4,0},{8,4},{12,8},{16,12},{20,16},{24,20},{28,24},{5,1},{9,5},{13... | collective-permute-start | bytes 1572872 | tf_op jit(solution)/shard_map/ppermute | solution.py:23
  92.8 5.9 %collective-permute-start.11 = (f32[256,128]{1,0:T(8,128)S(1)}, f32[256,128]{1,0:T(8,128)S(1)}, u32[]{:S(2)}, u32[]{:S(2)}) collective-permute-start(f32[256,128]{1,0:T(8,128)S(1)} %add.82), channel_id=1, source_target_pairs={{0,2},{1,3},{2,0},{3,1},{4,6},{5,7},{6,4},{7,5},{8,10},{9,11},{10,... | collective-permute-start | bytes 393224 | tf_op jit(solution)/shard_map/ppermute | solution.py:17

commit v14 on v12

--- a/solution.py
+++ b/solution.py
@@ -23,13 +23,19 @@
     return lax.ppermute(value, axis, [(source, source + steps) for source in range(leading, last)])
 
 
+def case_sum(value):
+    for height in range(lax.axis_size("case").bit_length() - 1):
+        value = value + partner(value, "case", height)
+    return value
+
+
 def apply_level(matrix, sibling, flipped):
     if flipped:
         return jnp.einsum("sr,asc->arc", matrix, sibling, precision=lax.Precision.HIGHEST)
     return jnp.einsum("rs,asc->arc", matrix, sibling, precision=lax.Precision.HIGHEST)
 
 
-def expand(own_value, translations, flipped, rider=None, stages=()):
+def expand(own_value, translations, flipped, rider=None, stages=(), last_hook=None):
     depth_count = lax.axis_size("leaf").bit_length() - 1
     summed = jnp.zeros(own_value.shape, jnp.float32)
     node_value = own_value
@@ -39,6 +45,8 @@
         if rider is None:
             sibling = partner(node_value, "leaf", height)
         else:
+            if last_hook is not None and height == depth_count - 1:
+                rider = last_hook(rider)
             packed = jnp.concatenate(
                 [node_value.reshape(rows, own_value.shape[2]), rider], axis=0
             )
@@ -260,14 +268,12 @@
             lambda _: back_near,
             lambda ready: near_backward(local_ids, kernel_blocks, ready, halo_points),
         ),
+        last_hook=case_sum,
     )
     back_far = jnp.einsum(
         "rp,arc->apc", leaf_basis, back_exp.astype(jnp.bfloat16), preferred_element_type=jnp.float32
     )
 
-    case_depth = lax.axis_size("case").bit_length() - 1
-    for height in range(case_depth):
-        grads = grads + partner(grads, "case", height)
 
     got_prev = shifted(hi, "leaf", 1).astype(jnp.float32)
     got_next = shifted(lo, "leaf", -1).astype(jnp.float32)

time: 95.6 us -> 101 us (1.056)
  the two profiles are of different devices: /device:TPU:16 before, /device:TPU:0 now
where the time goes in v14:
time: 101 us; the launch traced here: 100 us
  waiting for transfers between devices  36.9 us (37%)
  starting transfers between devices  29 us (29%)
  Pallas kernels  16.4 us (16%)
  matrix products  12.7 us (13%)
  local copies, waits for them, and re-layouts  4.12 us (4%)
    ppermute x8, waiting for transfers between devices, partner(): lax.ppermute(shard, axis, [(i, i ^ 1 << apart) for i in range(lax.axis_si...  35.3 us
    ppermute x8, starting transfers between devices, partner(): lax.ppermute(shard, axis, [(i, i ^ 1 << apart) for i in range(lax.axis_si...  18.2 us
    ppermute x4, starting transfers between devices, shifted(): lax.ppermute(value, axis, [(source, source + steps) for source in range(l...  10.8 us
    pallas_call x1, Pallas kernels, near_backward(): pl.pallas_call(functools.partial(near_bwd_kernel, cases, pairs, rows, ste...  8.91 us
    pallas_call x1, Pallas kernels, near_forward(): pl.pallas_call(functools.partial(near_fwd_kernel, cases, pairs, rows), ou...  7.48 us
    dot_general x1, matrix products, on_device(): jnp.einsum('apc,cd->apd', near_bf, w_near, preferred_element_type=jnp.flo...  4.55 us
  transfers between devices with their start and end apart: 12, of which 6 were waited for; matrix products, arithmetic and copies ran while one was open for 7% of the time, Pallas kernels for 9%

profile of v14, /device:TPU:0, one launch (start us, length us, event | category | flops | bytes accessed | tf_op | source)
XLA Modules:
  0.0 100.4 jit_solution(5468544730695151618)
XLA Ops:
  0.7 0.9 copy-done
  1.6 1.5 %convolution_bitcast_fusion.2 = f32[2,64,128]{2,1,0:T(8,128)S(1)} fusion(bf16[2,2048,128]{2,1,0:T(8,128)(2,1)} %own_hbm.1, bf16[64,2048]{1,0:T(8,128)(2,1)S(1)} %copy-done), kind=kOutput, calls=%fused_computation.21 | convolution fusion | flops 67108864 | bytes 1376256 | tf_op jit(solution)/shard_map/rp,apc->arc/dot_general | solution.py:229
  3.1 3.0 %collective-permute-start.2 = (f32[2,64,128]{2,1,0:T(8,128)S(1)}, f32[2,64,128]{2,1,0:T(8,128)S(1)}, u32[]{:S(2)}, u32[]{:S(2)}) collective-permute-start(f32[2,64,128]{2,1,0:T(8,128)S(1)} %convolution_bitcast_fusion.2), channel_id=1, source_target_pairs={{0,4},{4,0},{8,12},{12,8},{16,20},{20,16},{24,28},{28,24},{1,5},{5... | collective-permute-start | bytes 196616 | tf_op jit(solution)/shard_map/ppermute | solution.py:17
  6.1 1.0 %fusion.46 = (bf16[2,1024,128]{2,1,0:T(8,128)(2,1)}, bf16[2,1024,128]{2,1,0:T(8,128)(2,1)}) fusion(bf16[2,2048,128]{2,1,0:T(8,128)(2,1)S(1)} %copy-done.1), kind=kLoop, calls=%fused_computation.70 | loop fusion | bytes 2097152 | tf_op jit(solution)/shard_map/slice | solution.py:219
  7.2 1.3 %collective-permute-start.1 = (bf16[2,1024,128]{2,1,0:T(8,128)(2,1)}, bf16[2,1024,128]{2,1,0:T(8,128)(2,1)S(1)}, u32[]{:S(2)}, u32[]{:S(2)}) collective-permute-start(bf16[2,1024,128]{2,1,0:T(8,128)(2,1)} %get-tuple-element.26), channel_id=1, source_target_pairs={{4,0},{8,4},{12,8},{16,12},{20,16},{24,20},{28,24},{5,1},{9,5},{13... | collective-permute-start | bytes 1572872 | tf_op jit(solution)/shard_map/ppermute | solution.py:23
  8.5 4.6 %collective-permute-start = (bf16[2,1024,128]{2,1,0:T(8,128)(2,1)}, bf16[2,1024,128]{2,1,0:T(8,128)(2,1)S(1)}, u32[]{:S(2)}, u32[]{:S(2)}) collective-permute-start(bf16[2,1024,128]{2,1,0:T(8,128)(2,1)} %get-tuple-element.27), channel_id=1, source_target_pairs={{0,4},{4,8},{8,12},{12,16},{16,20},{20,24},{24,28},{1,5},{5,9},{9,... | collective-permute-start | bytes 1572872 | tf_op jit(solution)/shard_map/ppermute | solution.py:23
  13.1 1.6 %collective-permute-start.3 = (f32[2,64,128]{2,1,0:T(8,128)S(1)}, f32[2,64,128]{2,1,0:T(8,128)S(1)}, u32[]{:S(2)}, u32[]{:S(2)}) collective-permute-start(f32[2,64,128]{2,1,0:T(8,128)S(1)} %add.65), channel_id=1, source_target_pairs={{0,8},{4,12},{8,0},{12,4},{16,24},{20,28},{24,16},{28,20},{1,9},{5... | collective-permute-start | bytes 196616 | tf_op jit(solution)/shard_map/ppermute | solution.py:17
  14.7 0.7 reshape.29.ids_ref
  15.4 8.6 %collective-permute-done.3 = f32[2,64,128]{2,1,0:T(8,128)S(1)} collective-permute-done((f32[2,64,128]{2,1,0:T(8,128)S(1)}, f32[2,64,128]{2,1,0:T(8,128)S(1)}, u32[]{:S(2)}, u32[]{:S(2)}) %collective-permute-start.3) | collective-permute-done | bytes 65568 | tf_op jit(solution)/shard_map/ppermute | solution.py:17
  24.0 3.3 %collective-permute-start.4 = (f32[2,64,128]{2,1,0:T(8,128)S(1)}, f32[2,64,128]{2,1,0:T(8,128)S(1)}, u32[]{:S(2)}, u32[]{:S(2)}) collective-permute-start(f32[2,64,128]{2,1,0:T(8,128)S(1)} %add.67), channel_id=1, source_target_pairs={{0,16},{4,20},{8,24},{12,28},{16,0},{20,4},{24,8},{28,12},{1,17},{... | collective-permute-start | bytes 196616 | tf_op jit(solution)/shard_map/ppermute | solution.py:17
  27.5 2.0 %collective-permute-done.4 = f32[2,64,128]{2,1,0:T(8,128)S(1)} collective-permute-done((f32[2,64,128]{2,1,0:T(8,128)S(1)}, f32[2,64,128]{2,1,0:T(8,128)S(1)}, u32[]{:S(2)}, u32[]{:S(2)}) %collective-permute-start.4) | collective-permute-done | bytes 65568 | tf_op jit(solution)/shard_map/ppermute | solution.py:17
  29.9 1.3 %convolution_bitcast_fusion.1 = f32[2,2048,128]{2,1,0:T(8,128)S(1)} fusion(bf16[2,64,128]{2,1,0:T(8,128)(2,1)S(1)} %fusion.18, bf16[64,2048]{1,0:T(8,128)(2,1)S(1)} %copy-done, bf16[128,128]{1,0:T(8,128)(2,1)} %param.14), kind=kOutput, calls=%fused_computation.3 | convolution fusion | flops 71319552 | bytes 2424832 | tf_op jit(solution)/shard_map/rp,ard->apd/dot_general | solution.py:235
  31.3 1.6 %collective-permute-done.prev_hbm = bf16[2,1024,128]{2,1,0:T(8,128)(2,1)S(1)} collective-permute-done((bf16[2,1024,128]{2,1,0:T(8,128)(2,1)}, bf16[2,1024,128]{2,1,0:T(8,128)(2,1)S(1)}, u32[]{:S(2)}, u32[]{:S(2)}) %collective-permute-start) | collective-permute-done | bytes 524320 | tf_op jit(solution)/shard_map/ppermute | solution.py:23
  32.8 0.8 copy-done.5
  33.6 7.5 %shard_map.111 = bf16[2,2048,128]{2,1,0:T(8,128)(2,1)} custom-call(s32[192]{0:T(256)} %reshape.29.ids_ref, bf16[16,12,128,128]{3,2,1,0:T(8,128)(2,1)} %kb_ref.3, bf16[2,1024,128]{2,1,0:T(8,128)(2,1)} %copy-done.5, bf16[2,2048,128]{2,1,0:T(8,128)(2,1)} %own_hbm.1, bf16[2,1024,128]{2,1,0:T(8,128)(2,1)} %copy-done.4), custom_call_target="tpu_custom_call" | custom-call | flops 1610612736 | bytes 9437184 | tf_op jit(solution)/shard_map/pallas_call | solution.py:111
  41.1 4.6 %fusion.2 = (bf16[2,2048,128]{2,1,0:T(8,128)(2,1)S(1)}, bf16[2,2048,128]{2,1,0:T(8,128)(2,1)}) fusion(bf16[2,2048,128]{2,1,0:T(8,128)(2,1)} %param.9, f32[2,2048,128]{2,1,0:T(8,128)S(1)} %convolution_bitcast_fusion.1, bf16[2,2048,128]{2,1,0:T(8,128)(2,1)} %shard_map.111, bf16[128,128]{1,0:T(8,128)(2,1)} %param.13), kind=kOutput, calls=%fused_computation.10 | convolution fusion | flops 146800640 | bytes 6324224 | tf_op jit(solution)/shard_map/apc,cd->apd/dot_general | solution.py:237
  45.7 0.5 fusion.12
  46.2 0.3 fusion.16
  46.9 2.4 %collective-permute-start.5 = (f32[384,128]{1,0:T(8,128)S(1)}, f32[384,128]{1,0:T(8,128)S(1)}, u32[]{:S(2)}, u32[]{:S(2)}) collective-permute-start(f32[384,128]{1,0:T(8,128)S(1)} %pad_maximum_fusion), channel_id=1, source_target_pairs={{0,4},{4,0},{8,12},{12,8},{16,20},{20,16},{24,28},{28,24},{1,5},{5... | collective-permute-start | bytes 589832 | tf_op jit(solution)/shard_map/ppermute | solution.py:17
  49.3 1.4 %convolution_convert_fusion.back_ref = bf16[2,2048,128]{2,1,0:T(8,128)(2,1)} fusion(bf16[2,2048,128]{2,1,0:T(8,128)(2,1)S(1)} %get-tuple-element.24, bf16[128,128]{1,0:T(8,128)(2,1)S(1)} %copy-done.8), kind=kOutput, calls=%fused_computation.7 | convolution fusion | flops 134742016 | bytes 2129920 | tf_op jit(solution)/shard_map/apc,dc->apd/dot_general | solution.py:245
  50.7 3.7 %collective-permute-done.5 = f32[384,128]{1,0:T(8,128)S(1)} collective-permute-done((f32[384,128]{1,0:T(8,128)S(1)}, f32[384,128]{1,0:T(8,128)S(1)}, u32[]{:S(2)}, u32[]{:S(2)}) %collective-permute-start.5) | collective-permute-done | bytes 196640 | tf_op jit(solution)/shard_map/ppermute | solution.py:17
  54.4 1.8 %collective-permute-start.6 = (f32[384,128]{1,0:T(8,128)S(1)}, f32[384,128]{1,0:T(8,128)S(1)}, u32[]{:S(2)}, u32[]{:S(2)}) collective-permute-start(f32[384,128]{1,0:T(8,128)S(1)} %pad_maximum_fusion.1), channel_id=1, source_target_pairs={{0,8},{4,12},{8,0},{12,4},{16,24},{20,28},{24,16},{28,20},{1,9},{5... | collective-permute-start | bytes 589832 | tf_op jit(solution)/shard_map/ppermute | solution.py:17
  56.2 8.9 %shard_map.112 = (f32[2,2048,128]{2,1,0:T(8,128)}, bf16[2,1024,128]{2,1,0:T(8,128)(2,1)}, bf16[2,1024,128]{2,1,0:T(8,128)(2,1)}) custom-call(s32[192]{0:T(256)} %reshape.29.ids_ref, bf16[16,12,128,128]{3,2,1,0:T(8,128)(2,1)} %kb_ref.3, bf16[2,2048,128]{2,1,0:T(8,128)(2,1)} %convolution_convert_fusion.back_ref), custom_call_target="tpu_custom_call" | custom-call | flops 1610612736 | bytes 11534336 | tf_op jit(solution)/shard_map/pallas_call | solution.py:174
  65.2 1.3 %collective-permute-done.9 = f32[256,128]{1,0:T(8,128)S(1)} collective-permute-done((f32[256,128]{1,0:T(8,128)S(1)}, f32[256,128]{1,0:T(8,128)S(1)}, u32[]{:S(2)}, u32[]{:S(2)}) %collective-permute-start.9) | collective-permute-done | bytes 131104 | tf_op jit(solution)/shard_map/ppermute | solution.py:17
  66.6 1.5 %collective-permute-start.10 = (f32[256,128]{1,0:T(8,128)S(1)}, f32[256,128]{1,0:T(8,128)S(1)}, u32[]{:S(2)}, u32[]{:S(2)}) collective-permute-start(f32[256,128]{1,0:T(8,128)S(1)} %add.79), channel_id=1, source_target_pairs={{0,2},{1,3},{2,0},{3,1},{4,6},{5,7},{6,4},{7,5},{8,10},{9,11},{10,... | collective-permute-start | bytes 393224 | tf_op jit(solution)/shard_map/ppermute | solution.py:17
  68.4 3.7 %collective-permute-start.7 = (bf16[2,1024,128]{2,1,0:T(8,128)(2,1)}, bf16[2,1024,128]{2,1,0:T(8,128)(2,1)S(1)}, u32[]{:S(2)}, u32[]{:S(2)}) collective-permute-start(bf16[2,1024,128]{2,1,0:T(8,128)(2,1)} %get-tuple-element.19), channel_id=1, source_target_pairs={{0,4},{4,8},{8,12},{12,16},{16,20},{20,24},{24,28},{1,5},{5,9},{9,... | collective-permute-start | bytes 1572872 | tf_op jit(solution)/shard_map/ppermute | solution.py:23
  72.1 1.3 %collective-permute-start.8 = (bf16[2,1024,128]{2,1,0:T(8,128)(2,1)}, bf16[2,1024,128]{2,1,0:T(8,128)(2,1)S(1)}, u32[]{:S(2)}, u32[]{:S(2)}) collective-permute-start(bf16[2,1024,128]{2,1,0:T(8,128)(2,1)} %get-tuple-element.20), channel_id=1, source_target_pairs={{4,0},{8,4},{12,8},{16,12},{20,16},{24,20},{28,24},{5,1},{9,5},{13... | collective-permute-start | bytes 1572872 | tf_op jit(solution)/shard_map/ppermute | solution.py:23
  73.4 4.4 %collective-permute-start.11 = (f32[384,128]{1,0:T(8,128)S(1)}, f32[384,128]{1,0:T(8,128)S(1)}, u32[]{:S(2)}, u32[]{:S(2)}) collective-permute-start(f32[384,128]{1,0:T(8,128)S(1)} %pad_maximum_fusion.2), channel_id=1, source_target_pairs={{0,16},{4,20},{8,24},{12,28},{16,0},{20,4},{24,8},{28,12},{1,17},{... | collective-permute-start | bytes 589832 | tf_op jit(solution)/shard_map/ppermute | solution.py:17
  78.1 19.7 %collective-permute-done.11 = f32[384,128]{1,0:T(8,128)S(1)} collective-permute-done((f32[384,128]{1,0:T(8,128)S(1)}, f32[384,128]{1,0:T(8,128)S(1)}, u32[]{:S(2)}, u32[]{:S(2)}) %collective-permute-start.11) | collective-permute-done | bytes 196640 | tf_op jit(solution)/shard_map/ppermute | solution.py:17
  97.8 0.7 fusion.47
  98.5 0.3 fusion.17
  99.0 1.5 %fusion.10 = bf16[2,2048,128]{2,1,0:T(8,128)(2,1)} fusion(f32[2,1024,128]{2,1,0:T(8,128)S(1)} %get-tuple-element.23, f32[2,1024,128]{2,1,0:T(8,128)S(1)} %get-tuple-element.22, bf16[2,64,128]{2,1,0:T(8,128)(2,1)S(1)} %fusion.17, bf16[64,2048]{1,0:T(8,128)(2,1)S(1)} %copy-done), kind=kOutput, calls=%fused_computation.19 | convolution fusion | flops 68681728 | bytes 3440640 | tf_op jit(solution)/shard_map/rp,arc->apc/dot_general | solution.py:273
  (49 shorter events, 1.9 us)
Async XLA Ops:
  0.6 1.0 copy-start
  0.6 5.5 %copy-start.1 = (bf16[2,2048,128]{2,1,0:T(8,128)(2,1)S(1)}, bf16[2,2048,128]{2,1,0:T(8,128)(2,1)}, u32[]{:S(2)}) copy-start(bf16[2,2048,128]{2,1,0:T(8,128)(2,1)} %own_hbm.1) | copy-start | bytes 3145732
  0.7 14.1 %copy-start.9 = (s32[16,12]{1,0:T(8,128)S(1)}, s32[16,12]{1,0:T(8,128)}, u32[]{:S(2)}) copy-start(s32[16,12]{1,0:T(8,128)} %param.11) | copy-start | bytes 2308
  0.7 26.6 %copy-start.6 = (f32[3,64,64]{2,1,0:T(8,128)S(1)}, f32[3,64,64]{2,1,0:T(8,128)}, u32[]{:S(2)}) copy-start(f32[3,64,64]{2,1,0:T(8,128)} %param.15) | copy-start | bytes 147460
  3.1 10.0 %collective-permute-start.2 = (f32[2,64,128]{2,1,0:T(8,128)S(1)}, f32[2,64,128]{2,1,0:T(8,128)S(1)}, u32[]{:S(2)}, u32[]{:S(2)}) collective-permute-start(f32[2,64,128]{2,1,0:T(8,128)S(1)} %convolution_bitcast_fusion.2), channel_id=1, source_target_pairs={{0,4},{4,0},{8,12},{12,8},{16,20},{20,16},{24,28},{28,24},{1,5},{5... | collective-permute-start | bytes 196616 | tf_op jit(solution)/shard_map/ppermute | solution.py:17
  7.2 24.1 %collective-permute-start.1 = (bf16[2,1024,128]{2,1,0:T(8,128)(2,1)}, bf16[2,1024,128]{2,1,0:T(8,128)(2,1)S(1)}, u32[]{:S(2)}, u32[]{:S(2)}) collective-permute-start(bf16[2,1024,128]{2,1,0:T(8,128)(2,1)} %get-tuple-element.26), channel_id=1, source_target_pairs={{4,0},{8,4},{12,8},{16,12},{20,16},{24,20},{28,24},{5,1},{9,5},{13... | collective-permute-start | bytes 1572872 | tf_op jit(solution)/shard_map/ppermute | solution.py:23
  8.5 24.3 %collective-permute-start = (bf16[2,1024,128]{2,1,0:T(8,128)(2,1)}, bf16[2,1024,128]{2,1,0:T(8,128)(2,1)S(1)}, u32[]{:S(2)}, u32[]{:S(2)}) collective-permute-start(bf16[2,1024,128]{2,1,0:T(8,128)(2,1)} %get-tuple-element.27), channel_id=1, source_target_pairs={{0,4},{4,8},{8,12},{12,16},{16,20},{20,24},{24,28},{1,5},{5,9},{9,... | collective-permute-start | bytes 1572872 | tf_op jit(solution)/shard_map/ppermute | solution.py:23
  13.1 10.9 %collective-permute-start.3 = (f32[2,64,128]{2,1,0:T(8,128)S(1)}, f32[2,64,128]{2,1,0:T(8,128)S(1)}, u32[]{:S(2)}, u32[]{:S(2)}) collective-permute-start(f32[2,64,128]{2,1,0:T(8,128)S(1)} %add.65), channel_id=1, source_target_pairs={{0,8},{4,12},{8,0},{12,4},{16,24},{20,28},{24,16},{28,20},{1,9},{5... | collective-permute-start | bytes 196616 | tf_op jit(solution)/shard_map/ppermute | solution.py:17
  24.0 5.5 %collective-permute-start.4 = (f32[2,64,128]{2,1,0:T(8,128)S(1)}, f32[2,64,128]{2,1,0:T(8,128)S(1)}, u32[]{:S(2)}, u32[]{:S(2)}) collective-permute-start(f32[2,64,128]{2,1,0:T(8,128)S(1)} %add.67), channel_id=1, source_target_pairs={{0,16},{4,20},{8,24},{12,28},{16,0},{20,4},{24,8},{28,12},{1,17},{... | collective-permute-start | bytes 196616 | tf_op jit(solution)/shard_map/ppermute | solution.py:17
  31.3 1.6 %copy-start.4 = (bf16[2,1024,128]{2,1,0:T(8,128)(2,1)}, bf16[2,1024,128]{2,1,0:T(8,128)(2,1)S(1)}, u32[]{:S(2)}) copy-start(bf16[2,1024,128]{2,1,0:T(8,128)(2,1)S(1)} %collective-permute-done.1.next_hbm) | copy-start | bytes 1572868
  32.8 0.8 copy-start.5
  41.1 4.6 %copy-start.2 = (bf16[2,2048,128]{2,1,0:T(8,128)(2,1)S(1)}, bf16[2,2048,128]{2,1,0:T(8,128)(2,1)}, u32[]{:S(2)}) copy-start(bf16[2,2048,128]{2,1,0:T(8,128)(2,1)} %shard_map.111) | copy-start | bytes 3145732
  45.7 1.0 copy-start.7
  45.7 3.6 %copy-start.8 = (bf16[128,128]{1,0:T(8,128)(2,1)S(1)}, bf16[128,128]{1,0:T(8,128)(2,1)}, u32[]{:S(2)}) copy-start(bf16[128,128]{1,0:T(8,128)(2,1)} %param.13) | copy-start | bytes 98308
  46.9 7.5 %collective-permute-start.5 = (f32[384,128]{1,0:T(8,128)S(1)}, f32[384,128]{1,0:T(8,128)S(1)}, u32[]{:S(2)}, u32[]{:S(2)}) collective-permute-start(f32[384,128]{1,0:T(8,128)S(1)} %pad_maximum_fusion), channel_id=1, source_target_pairs={{0,4},{4,0},{8,12},{12,8},{16,20},{20,16},{24,28},{28,24},{1,5},{5... | collective-permute-start | bytes 589832 | tf_op jit(solution)/shard_map/ppermute | solution.py:17
  54.4 10.7 %collective-permute-start.6 = (f32[384,128]{1,0:T(8,128)S(1)}, f32[384,128]{1,0:T(8,128)S(1)}, u32[]{:S(2)}, u32[]{:S(2)}) collective-permute-start(f32[384,128]{1,0:T(8,128)S(1)} %pad_maximum_fusion.1), channel_id=1, source_target_pairs={{0,8},{4,12},{8,0},{12,4},{16,24},{20,28},{24,16},{28,20},{1,9},{5... | collective-permute-start | bytes 589832 | tf_op jit(solution)/shard_map/ppermute | solution.py:17
  65.1 33.7 %copy-start.3 = (f32[2,2048,128]{2,1,0:T(8,128)S(1)}, f32[2,2048,128]{2,1,0:T(8,128)}, u32[]{:S(2)}) copy-start(f32[2,2048,128]{2,1,0:T(8,128)} %get-tuple-element.18) | copy-start | bytes 6291460
  65.1 1.4 %collective-permute-start.9 = (f32[256,128]{1,0:T(8,128)S(1)}, f32[256,128]{1,0:T(8,128)S(1)}, u32[]{:S(2)}, u32[]{:S(2)}) collective-permute-start(f32[256,128]{1,0:T(8,128)S(1)} %slice_add_fusion.1), channel_id=1, source_target_pairs={{0,1},{1,0},{2,3},{3,2},{4,5},{5,4},{6,7},{7,6},{8,9},{9,8},{10,11... | collective-permute-start | bytes 393224 | tf_op jit(solution)/shard_map/ppermute | solution.py:17
  66.6 6.8 %collective-permute-start.10 = (f32[256,128]{1,0:T(8,128)S(1)}, f32[256,128]{1,0:T(8,128)S(1)}, u32[]{:S(2)}, u32[]{:S(2)}) collective-permute-start(f32[256,128]{1,0:T(8,128)S(1)} %add.79), channel_id=1, source_target_pairs={{0,2},{1,3},{2,0},{3,1},{4,6},{5,7},{6,4},{7,5},{8,10},{9,11},{10,... | collective-permute-start | bytes 393224 | tf_op jit(solution)/shard_map/ppermute | solution.py:17
  68.4 30.3 %collective-permute-start.7 = (bf16[2,1024,128]{2,1,0:T(8,128)(2,1)}, bf16[2,1024,128]{2,1,0:T(8,128)(2,1)S(1)}, u32[]{:S(2)}, u32[]{:S(2)}) collective-permute-start(bf16[2,1024,128]{2,1,0:T(8,128)(2,1)} %get-tuple-element.19), channel_id=1, source_target_pairs={{0,4},{4,8},{8,12},{12,16},{16,20},{20,24},{24,28},{1,5},{5,9},{9,... | collective-permute-start | bytes 1572872 | tf_op jit(solution)/shard_map/ppermute | solution.py:23
  72.1 26.7 %collective-permute-start.8 = (bf16[2,1024,128]{2,1,0:T(8,128)(2,1)}, bf16[2,1024,128]{2,1,0:T(8,128)(2,1)S(1)}, u32[]{:S(2)}, u32[]{:S(2)}) collective-permute-start(bf16[2,1024,128]{2,1,0:T(8,128)(2,1)} %get-tuple-element.20), channel_id=1, source_target_pairs={{4,0},{8,4},{12,8},{16,12},{20,16},{24,20},{28,24},{5,1},{9,5},{13... | collective-permute-start | bytes 1572872 | tf_op jit(solution)/shard_map/ppermute | solution.py:23
  73.4 24.3 %collective-permute-start.11 = (f32[384,128]{1,0:T(8,128)S(1)}, f32[384,128]{1,0:T(8,128)S(1)}, u32[]{:S(2)}, u32[]{:S(2)}) collective-permute-start(f32[384,128]{1,0:T(8,128)S(1)} %pad_maximum_fusion.2), channel_id=1, source_target_pairs={{0,16},{4,20},{8,24},{12,28},{16,0},{20,4},{24,8},{28,12},{1,17},{... | collective-permute-start | bytes 589832 | tf_op jit(solution)/shard_map/ppermute | solution.py:17

commit v15 on v12

--- a/solution.py
+++ b/solution.py
@@ -271,15 +271,16 @@
 
     got_prev = shifted(hi, "leaf", 1).astype(jnp.float32)
     got_next = shifted(lo, "leaf", -1).astype(jnp.float32)
+    base = lax.optimization_barrier(mid + back_far)
     near_back = jnp.concatenate(
         [
-            mid[:, :halo_points] + got_prev,
-            mid[:, halo_points : points_here - halo_points],
-            mid[:, points_here - halo_points :] + got_next,
+            base[:, :halo_points] + got_prev,
+            base[:, halo_points : points_here - halo_points],
+            base[:, points_here - halo_points :] + got_next,
         ],
         axis=1,
     )
-    grad_features = (near_back + back_far).astype(jnp.bfloat16)
+    grad_features = near_back.astype(jnp.bfloat16)
     grad_near = grads[:width]
     grad_far = grads[width:]
     return (output, grad_features, grad_near, grad_far)

time: 95.6 us -> 95.2 us (level)
  other arithmetic: 0.37 us -> 1.65 us
  matrix products: 12.7 us -> 11.7 us
  waiting for transfers between devices: 40 us -> 39 us
    concatenate x0 -> x1, other arithmetic: none -> 1.04 us  [on_device(): jnp.concatenate([base[:, :halo_points] + got_prev, base[:, halo_points:po...]
    dot_general x1, matrix products: 1.47 us -> 0.49 us  [on_device(): jnp.einsum('rp,arc->apc', leaf_basis, back_exp.astype(jnp.bfloat16), pref...]
  transfers between devices with their start and end apart: 12 -> 12, of which waited for: 9 -> 9; matrix products, arithmetic and copies ran while one was open for 7% -> 8% of each run, Pallas kernels for 9% -> 9%
where the time goes in v15:
time: 95.2 us; the launch traced here: 94.8 us
  waiting for transfers between devices  39 us (41%)
  starting transfers between devices  20.2 us (21%)
  Pallas kernels  16.4 us (17%)
  matrix products  11.7 us (12%)
  local copies, waits for them, and re-layouts  4.91 us (5%)
  other arithmetic  1.65 us (2%)
  between operations  0.98 us (1%)
    ppermute x8, waiting for transfers between devices, partner(): lax.ppermute(shard, axis, [(i, i ^ 1 << apart) for i in range(lax.axis_si...  22.9 us
    ppermute x4, waiting for transfers between devices, shifted(): lax.ppermute(value, axis, [(source, source + steps) for source in range(l...  16.1 us
    ppermute x4, starting transfers between devices, shifted(): lax.ppermute(value, axis, [(source, source + steps) for source in range(l...  12.7 us
    pallas_call x1, Pallas kernels, near_backward(): pl.pallas_call(functools.partial(near_bwd_kernel, cases, pairs, rows, ste...  8.91 us
    ppermute x8, starting transfers between devices, partner(): lax.ppermute(shard, axis, [(i, i ^ 1 << apart) for i in range(lax.axis_si...  7.51 us
    pallas_call x1, Pallas kernels, near_forward(): pl.pallas_call(functools.partial(near_fwd_kernel, cases, pairs, rows), ou...  7.47 us
    dot_general x1, matrix products, on_device(): jnp.einsum('apc,cd->apd', near_bf, w_near, preferred_element_type=jnp.flo...  4.55 us
    unnamed x20, local copies, waits for them, and re-layouts  2.54 us
  transfers between devices with their start and end apart: 12, of which 9 were waited for; matrix products, arithmetic and copies ran while one was open for 8% of the time, Pallas kernels for 9%

profile of v15, /device:TPU:16, one launch (start us, length us, event | category | flops | bytes accessed | tf_op | source)
XLA Modules:
  0.0 94.8 jit_solution(10092792651405105880)
XLA Ops:
  0.7 0.9 copy-done
  1.6 1.5 %convolution_bitcast_fusion.2 = f32[2,64,128]{2,1,0:T(8,128)S(1)} fusion(bf16[2,2048,128]{2,1,0:T(8,128)(2,1)} %own_hbm.1, bf16[64,2048]{1,0:T(8,128)(2,1)S(1)} %copy-done), kind=kOutput, calls=%fused_computation.19 | convolution fusion | flops 67108864 | bytes 1376256 | tf_op jit(solution)/shard_map/rp,apc->arc/dot_general | solution.py:221
  3.1 1.6 %collective-permute-start.2 = (f32[2,64,128]{2,1,0:T(8,128)S(1)}, f32[2,64,128]{2,1,0:T(8,128)S(1)}, u32[]{:S(2)}, u32[]{:S(2)}) collective-permute-start(f32[2,64,128]{2,1,0:T(8,128)S(1)} %convolution_bitcast_fusion.2), channel_id=1, source_target_pairs={{0,4},{4,0},{8,12},{12,8},{16,20},{20,16},{24,28},{28,24},{1,5},{5... | collective-permute-start | bytes 196616 | tf_op jit(solution)/shard_map/ppermute | solution.py:17
  4.7 1.0 %fusion.45 = (bf16[2,1024,128]{2,1,0:T(8,128)(2,1)}, bf16[2,1024,128]{2,1,0:T(8,128)(2,1)}) fusion(bf16[2,2048,128]{2,1,0:T(8,128)(2,1)S(1)} %copy-done.1), kind=kLoop, calls=%fused_computation.71 | loop fusion | bytes 2097152 | tf_op jit(solution)/shard_map/slice | solution.py:211
  5.7 2.3 %collective-permute-start.1 = (bf16[2,1024,128]{2,1,0:T(8,128)(2,1)}, bf16[2,1024,128]{2,1,0:T(8,128)(2,1)S(1)}, u32[]{:S(2)}, u32[]{:S(2)}) collective-permute-start(bf16[2,1024,128]{2,1,0:T(8,128)(2,1)} %get-tuple-element.26), channel_id=1, source_target_pairs={{4,0},{8,4},{12,8},{16,12},{20,16},{24,20},{28,24},{5,1},{9,5},{13... | collective-permute-start | bytes 1572872 | tf_op jit(solution)/shard_map/ppermute | solution.py:23
  8.0 3.5 %collective-permute-start = (bf16[2,1024,128]{2,1,0:T(8,128)(2,1)}, bf16[2,1024,128]{2,1,0:T(8,128)(2,1)S(1)}, u32[]{:S(2)}, u32[]{:S(2)}) collective-permute-start(bf16[2,1024,128]{2,1,0:T(8,128)(2,1)} %get-tuple-element.27), channel_id=1, source_target_pairs={{0,4},{4,8},{8,12},{12,16},{16,20},{20,24},{24,28},{1,5},{5,9},{9,... | collective-permute-start | bytes 1572872 | tf_op jit(solution)/shard_map/ppermute | solution.py:23
  11.6 1.7 %collective-permute-start.3 = (f32[2,64,128]{2,1,0:T(8,128)S(1)}, f32[2,64,128]{2,1,0:T(8,128)S(1)}, u32[]{:S(2)}, u32[]{:S(2)}) collective-permute-start(f32[2,64,128]{2,1,0:T(8,128)S(1)} %add.65), channel_id=1, source_target_pairs={{0,8},{4,12},{8,0},{12,4},{16,24},{20,28},{24,16},{28,20},{1,9},{5... | collective-permute-start | bytes 196616 | tf_op jit(solution)/shard_map/ppermute | solution.py:17
  13.3 0.7 reshape.29.ids_ref
  14.0 9.2 %collective-permute-done.3 = f32[2,64,128]{2,1,0:T(8,128)S(1)} collective-permute-done((f32[2,64,128]{2,1,0:T(8,128)S(1)}, f32[2,64,128]{2,1,0:T(8,128)S(1)}, u32[]{:S(2)}, u32[]{:S(2)}) %collective-permute-start.3) | collective-permute-done | bytes 65568 | tf_op jit(solution)/shard_map/ppermute | solution.py:17
  23.5 4.9 %collective-permute-done.4 = f32[2,64,128]{2,1,0:T(8,128)S(1)} collective-permute-done((f32[2,64,128]{2,1,0:T(8,128)S(1)}, f32[2,64,128]{2,1,0:T(8,128)S(1)}, u32[]{:S(2)}, u32[]{:S(2)}) %collective-permute-start.4) | collective-permute-done | bytes 65568 | tf_op jit(solution)/shard_map/ppermute | solution.py:17
  28.8 1.3 %convolution_bitcast_fusion.1 = f32[2,2048,128]{2,1,0:T(8,128)S(1)} fusion(bf16[2,64,128]{2,1,0:T(8,128)(2,1)S(1)} %fusion.17, bf16[64,2048]{1,0:T(8,128)(2,1)S(1)} %copy-done, bf16[128,128]{1,0:T(8,128)(2,1)} %param.14), kind=kOutput, calls=%fused_computation.3 | convolution fusion | flops 71319552 | bytes 2424832 | tf_op jit(solution)/shard_map/rp,ard->apd/dot_general | solution.py:227
  30.1 2.3 %collective-permute-done.1.next_hbm = bf16[2,1024,128]{2,1,0:T(8,128)(2,1)S(1)} collective-permute-done((bf16[2,1024,128]{2,1,0:T(8,128)(2,1)}, bf16[2,1024,128]{2,1,0:T(8,128)(2,1)S(1)}, u32[]{:S(2)}, u32[]{:S(2)}) %collective-permute-start.1) | collective-permute-done | bytes 524320 | tf_op jit(solution)/shard_map/ppermute | solution.py:23
  32.5 0.8 copy-done.4
  33.3 0.8 copy-done.5
  34.0 7.5 %shard_map.111 = bf16[2,2048,128]{2,1,0:T(8,128)(2,1)} custom-call(s32[192]{0:T(256)} %reshape.29.ids_ref, bf16[16,12,128,128]{3,2,1,0:T(8,128)(2,1)} %kb_ref.3, bf16[2,1024,128]{2,1,0:T(8,128)(2,1)} %copy-done.5, bf16[2,2048,128]{2,1,0:T(8,128)(2,1)} %own_hbm.1, bf16[2,1024,128]{2,1,0:T(8,128)(2,1)} %copy-done.4), custom_call_target="tpu_custom_call" | custom-call | flops 1610612736 | bytes 9437184 | tf_op jit(solution)/shard_map/pallas_call | solution.py:103
  41.5 4.6 %fusion.2 = (bf16[2,2048,128]{2,1,0:T(8,128)(2,1)S(1)}, bf16[2,2048,128]{2,1,0:T(8,128)(2,1)}) fusion(bf16[2,2048,128]{2,1,0:T(8,128)(2,1)} %param.9, f32[2,2048,128]{2,1,0:T(8,128)S(1)} %convolution_bitcast_fusion.1, bf16[2,2048,128]{2,1,0:T(8,128)(2,1)} %shard_map.111, bf16[128,128]{1,0:T(8,128)(2,1)} %param.13), kind=kOutput, calls=%fused_computation.10 | convolution fusion | flops 146800640 | bytes 6324224 | tf_op jit(solution)/shard_map/apc,cd->apd/dot_general | solution.py:229
  47.3 0.7 collective-permute-start.5
  47.9 1.4 %convolution_convert_fusion.back_ref = bf16[2,2048,128]{2,1,0:T(8,128)(2,1)} fusion(bf16[2,2048,128]{2,1,0:T(8,128)(2,1)S(1)} %get-tuple-element.24, bf16[128,128]{1,0:T(8,128)(2,1)S(1)} %copy-done.8), kind=kOutput, calls=%fused_computation.7 | convolution fusion | flops 134742016 | bytes 2129920 | tf_op jit(solution)/shard_map/apc,dc->apd/dot_general | solution.py:237
  49.4 3.7 %collective-permute-done.5 = f32[384,128]{1,0:T(8,128)S(1)} collective-permute-done((f32[384,128]{1,0:T(8,128)S(1)}, f32[384,128]{1,0:T(8,128)S(1)}, u32[]{:S(2)}, u32[]{:S(2)}) %collective-permute-start.5) | collective-permute-done | bytes 196640 | tf_op jit(solution)/shard_map/ppermute | solution.py:17
  53.1 1.6 %collective-permute-start.6 = (f32[384,128]{1,0:T(8,128)S(1)}, f32[384,128]{1,0:T(8,128)S(1)}, u32[]{:S(2)}, u32[]{:S(2)}) collective-permute-start(f32[384,128]{1,0:T(8,128)S(1)} %pad_maximum_fusion.2), channel_id=1, source_target_pairs={{0,8},{4,12},{8,0},{12,4},{16,24},{20,28},{24,16},{28,20},{1,9},{5... | collective-permute-start | bytes 589832 | tf_op jit(solution)/shard_map/ppermute | solution.py:17
  54.7 8.9 %shard_map.112 = (f32[2,2048,128]{2,1,0:T(8,128)}, bf16[2,1024,128]{2,1,0:T(8,128)(2,1)}, bf16[2,1024,128]{2,1,0:T(8,128)(2,1)}) custom-call(s32[192]{0:T(256)} %reshape.29.ids_ref, bf16[16,12,128,128]{3,2,1,0:T(8,128)(2,1)} %kb_ref.3, bf16[2,2048,128]{2,1,0:T(8,128)(2,1)} %convolution_convert_fusion.back_ref), custom_call_target="tpu_custom_call" | custom-call | flops 1610612736 | bytes 11534336 | tf_op jit(solution)/shard_map/pallas_call | solution.py:166
  64.4 3.6 %collective-permute-start.8 = (bf16[2,1024,128]{2,1,0:T(8,128)(2,1)}, bf16[2,1024,128]{2,1,0:T(8,128)(2,1)S(1)}, u32[]{:S(2)}, u32[]{:S(2)}) collective-permute-start(bf16[2,1024,128]{2,1,0:T(8,128)(2,1)} %get-tuple-element.20), channel_id=1, source_target_pairs={{0,4},{4,8},{8,12},{12,16},{16,20},{20,24},{24,28},{1,5},{5,9},{9,... | collective-permute-start | bytes 1572872 | tf_op jit(solution)/shard_map/ppermute | solution.py:23
  68.1 3.2 %collective-permute-start.9 = (bf16[2,1024,128]{2,1,0:T(8,128)(2,1)}, bf16[2,1024,128]{2,1,0:T(8,128)(2,1)S(1)}, u32[]{:S(2)}, u32[]{:S(2)}) collective-permute-start(bf16[2,1024,128]{2,1,0:T(8,128)(2,1)} %get-tuple-element.21), channel_id=1, source_target_pairs={{4,0},{8,4},{12,8},{16,12},{20,16},{24,20},{28,24},{5,1},{9,5},{13... | collective-permute-start | bytes 1572872 | tf_op jit(solution)/shard_map/ppermute | solution.py:23
  71.6 0.5 collective-permute-done.7
  72.5 1.1 %collective-permute-done.10 = f32[256,128]{1,0:T(8,128)S(1)} collective-permute-done((f32[256,128]{1,0:T(8,128)S(1)}, f32[256,128]{1,0:T(8,128)S(1)}, u32[]{:S(2)}, u32[]{:S(2)}) %collective-permute-start.10) | collective-permute-done | bytes 131104 | tf_op jit(solution)/shard_map/ppermute | solution.py:17
  73.5 1.4 %collective-permute-start.11 = (f32[256,128]{1,0:T(8,128)S(1)}, f32[256,128]{1,0:T(8,128)S(1)}, u32[]{:S(2)}, u32[]{:S(2)}) collective-permute-start(f32[256,128]{1,0:T(8,128)S(1)} %add.82), channel_id=1, source_target_pairs={{0,2},{1,3},{2,0},{3,1},{4,6},{5,7},{6,4},{7,5},{8,10},{9,11},{10,... | collective-permute-start | bytes 393224 | tf_op jit(solution)/shard_map/ppermute | solution.py:17
  74.9 0.5 convolution_bitcast_fusion
  75.7 3.5 %collective-permute-done.11 = f32[256,128]{1,0:T(8,128)S(1)} collective-permute-done((f32[256,128]{1,0:T(8,128)S(1)}, f32[256,128]{1,0:T(8,128)S(1)}, u32[]{:S(2)}, u32[]{:S(2)}) %collective-permute-start.11) | collective-permute-done | bytes 131104 | tf_op jit(solution)/shard_map/ppermute | solution.py:17
  79.2 0.7 fusion.46
  79.8 9.7 %collective-permute-done.8 = bf16[2,1024,128]{2,1,0:T(8,128)(2,1)S(1)} collective-permute-done((bf16[2,1024,128]{2,1,0:T(8,128)(2,1)}, bf16[2,1024,128]{2,1,0:T(8,128)(2,1)S(1)}, u32[]{:S(2)}, u32[]{:S(2)}) %collective-permute-start.8) | collective-permute-done | bytes 524320 | tf_op jit(solution)/shard_map/ppermute | solution.py:23
  89.6 4.0 %collective-permute-done.9 = bf16[2,1024,128]{2,1,0:T(8,128)(2,1)S(1)} collective-permute-done((bf16[2,1024,128]{2,1,0:T(8,128)(2,1)}, bf16[2,1024,128]{2,1,0:T(8,128)(2,1)S(1)}, u32[]{:S(2)}, u32[]{:S(2)}) %collective-permute-start.9) | collective-permute-done | bytes 524320 | tf_op jit(solution)/shard_map/ppermute | solution.py:23
  93.8 1.0 %pad_maximum_fusion = bf16[2,2048,128]{2,1,0:T(8,128)(2,1)} fusion(bf16[2,1024,128]{2,1,0:T(8,128)(2,1)S(1)} %get-tuple-element.23, bf16[2,1024,128]{2,1,0:T(8,128)(2,1)S(1)} %get-tuple-element.22), kind=kLoop, calls=%fused_computation.39 | loop fusion | flops 2097152 | bytes 2097152 | tf_op jit(solution)/shard_map/concatenate | solution.py:275
  (51 shorter events, 3.7 us)
Async XLA Ops:
  0.6 1.0 %copy-start = (bf16[64,2048]{1,0:T(8,128)(2,1)S(1)}, bf16[64,2048]{1,0:T(8,128)(2,1)}, u32[]{:S(2)}) copy-start(bf16[64,2048]{1,0:T(8,128)(2,1)} %param.12) | copy-start | bytes 786436
  0.6 4.1 %copy-start.1 = (bf16[2,2048,128]{2,1,0:T(8,128)(2,1)S(1)}, bf16[2,2048,128]{2,1,0:T(8,128)(2,1)}, u32[]{:S(2)}) copy-start(bf16[2,2048,128]{2,1,0:T(8,128)(2,1)} %own_hbm.1) | copy-start | bytes 3145732
  0.7 12.6 %copy-start.9 = (s32[16,12]{1,0:T(8,128)S(1)}, s32[16,12]{1,0:T(8,128)}, u32[]{:S(2)}) copy-start(s32[16,12]{1,0:T(8,128)} %param.11) | copy-start | bytes 2308
  0.7 22.6 %copy-start.6 = (f32[3,64,64]{2,1,0:T(8,128)S(1)}, f32[3,64,64]{2,1,0:T(8,128)}, u32[]{:S(2)}) copy-start(f32[3,64,64]{2,1,0:T(8,128)} %param.15) | copy-start | bytes 147460
  3.1 8.5 %collective-permute-start.2 = (f32[2,64,128]{2,1,0:T(8,128)S(1)}, f32[2,64,128]{2,1,0:T(8,128)S(1)}, u32[]{:S(2)}, u32[]{:S(2)}) collective-permute-start(f32[2,64,128]{2,1,0:T(8,128)S(1)} %convolution_bitcast_fusion.2), channel_id=1, source_target_pairs={{0,4},{4,0},{8,12},{12,8},{16,20},{20,16},{24,28},{28,24},{1,5},{5... | collective-permute-start | bytes 196616 | tf_op jit(solution)/shard_map/ppermute | solution.py:17
  5.7 26.7 %collective-permute-start.1 = (bf16[2,1024,128]{2,1,0:T(8,128)(2,1)}, bf16[2,1024,128]{2,1,0:T(8,128)(2,1)S(1)}, u32[]{:S(2)}, u32[]{:S(2)}) collective-permute-start(bf16[2,1024,128]{2,1,0:T(8,128)(2,1)} %get-tuple-element.26), channel_id=1, source_target_pairs={{4,0},{8,4},{12,8},{16,12},{20,16},{24,20},{28,24},{5,1},{9,5},{13... | collective-permute-start | bytes 1572872 | tf_op jit(solution)/shard_map/ppermute | solution.py:23
  8.0 24.4 %collective-permute-start = (bf16[2,1024,128]{2,1,0:T(8,128)(2,1)}, bf16[2,1024,128]{2,1,0:T(8,128)(2,1)S(1)}, u32[]{:S(2)}, u32[]{:S(2)}) collective-permute-start(bf16[2,1024,128]{2,1,0:T(8,128)(2,1)} %get-tuple-element.27), channel_id=1, source_target_pairs={{0,4},{4,8},{8,12},{12,16},{16,20},{20,24},{24,28},{1,5},{5,9},{9,... | collective-permute-start | bytes 1572872 | tf_op jit(solution)/shard_map/ppermute | solution.py:23
  11.6 11.5 %collective-permute-start.3 = (f32[2,64,128]{2,1,0:T(8,128)S(1)}, f32[2,64,128]{2,1,0:T(8,128)S(1)}, u32[]{:S(2)}, u32[]{:S(2)}) collective-permute-start(f32[2,64,128]{2,1,0:T(8,128)S(1)} %add.65), channel_id=1, source_target_pairs={{0,8},{4,12},{8,0},{12,4},{16,24},{20,28},{24,16},{28,20},{1,9},{5... | collective-permute-start | bytes 196616 | tf_op jit(solution)/shard_map/ppermute | solution.py:17
  23.2 5.2 %collective-permute-start.4 = (f32[2,64,128]{2,1,0:T(8,128)S(1)}, f32[2,64,128]{2,1,0:T(8,128)S(1)}, u32[]{:S(2)}, u32[]{:S(2)}) collective-permute-start(f32[2,64,128]{2,1,0:T(8,128)S(1)} %add.67), channel_id=1, source_target_pairs={{0,16},{4,20},{8,24},{12,28},{16,0},{20,4},{24,8},{28,12},{1,17},{... | collective-permute-start | bytes 196616 | tf_op jit(solution)/shard_map/ppermute | solution.py:17
  32.5 0.8 copy-start.4
  33.3 0.8 copy-start.5
  41.5 4.6 %copy-start.2 = (bf16[2,2048,128]{2,1,0:T(8,128)(2,1)S(1)}, bf16[2,2048,128]{2,1,0:T(8,128)(2,1)}, u32[]{:S(2)}) copy-start(bf16[2,2048,128]{2,1,0:T(8,128)(2,1)} %shard_map.111) | copy-start | bytes 3145732
  46.1 1.0 %copy-start.7 = (bf16[128,128]{1,0:T(8,128)(2,1)S(1)}, bf16[128,128]{1,0:T(8,128)(2,1)}, u32[]{:S(2)}) copy-start(bf16[128,128]{1,0:T(8,128)(2,1)} %param.14) | copy-start | bytes 98308
  46.1 1.9 %copy-start.8 = (bf16[128,128]{1,0:T(8,128)(2,1)S(1)}, bf16[128,128]{1,0:T(8,128)(2,1)}, u32[]{:S(2)}) copy-start(bf16[128,128]{1,0:T(8,128)(2,1)} %param.13) | copy-start | bytes 98308
  47.3 5.8 %collective-permute-start.5 = (f32[384,128]{1,0:T(8,128)S(1)}, f32[384,128]{1,0:T(8,128)S(1)}, u32[]{:S(2)}, u32[]{:S(2)}) collective-permute-start(f32[384,128]{1,0:T(8,128)S(1)} %pad_maximum_fusion.1), channel_id=1, source_target_pairs={{0,4},{4,0},{8,12},{12,8},{16,20},{20,16},{24,28},{28,24},{1,5},{5... | collective-permute-start | bytes 589832 | tf_op jit(solution)/shard_map/ppermute | solution.py:17
  53.1 10.8 %collective-permute-start.6 = (f32[384,128]{1,0:T(8,128)S(1)}, f32[384,128]{1,0:T(8,128)S(1)}, u32[]{:S(2)}, u32[]{:S(2)}) collective-permute-start(f32[384,128]{1,0:T(8,128)S(1)} %pad_maximum_fusion.2), channel_id=1, source_target_pairs={{0,8},{4,12},{8,0},{12,4},{16,24},{20,28},{24,16},{28,20},{1,9},{5... | collective-permute-start | bytes 589832 | tf_op jit(solution)/shard_map/ppermute | solution.py:17
  64.0 11.5 %copy-start.3 = (f32[2,2048,128]{2,1,0:T(8,128)S(1)}, f32[2,2048,128]{2,1,0:T(8,128)}, u32[]{:S(2)}) copy-start(f32[2,2048,128]{2,1,0:T(8,128)} %get-tuple-element.18) | copy-start | bytes 6291460
  64.0 8.1 %collective-permute-start.7 = (f32[384,128]{1,0:T(8,128)S(1)}, f32[384,128]{1,0:T(8,128)S(1)}, u32[]{:S(2)}, u32[]{:S(2)}) collective-permute-start(f32[384,128]{1,0:T(8,128)S(1)} %pad_maximum_fusion.3), channel_id=1, source_target_pairs={{0,16},{4,20},{8,24},{12,28},{16,0},{20,4},{24,8},{28,12},{1,17},{... | collective-permute-start | bytes 589832 | tf_op jit(solution)/shard_map/ppermute | solution.py:17
  64.4 25.1 %collective-permute-start.8 = (bf16[2,1024,128]{2,1,0:T(8,128)(2,1)}, bf16[2,1024,128]{2,1,0:T(8,128)(2,1)S(1)}, u32[]{:S(2)}, u32[]{:S(2)}) collective-permute-start(bf16[2,1024,128]{2,1,0:T(8,128)(2,1)} %get-tuple-element.20), channel_id=1, source_target_pairs={{0,4},{4,8},{8,12},{12,16},{16,20},{20,24},{24,28},{1,5},{5,9},{9,... | collective-permute-start | bytes 1572872 | tf_op jit(solution)/shard_map/ppermute | solution.py:23
  68.1 25.5 %collective-permute-start.9 = (bf16[2,1024,128]{2,1,0:T(8,128)(2,1)}, bf16[2,1024,128]{2,1,0:T(8,128)(2,1)S(1)}, u32[]{:S(2)}, u32[]{:S(2)}) collective-permute-start(bf16[2,1024,128]{2,1,0:T(8,128)(2,1)} %get-tuple-element.21), channel_id=1, source_target_pairs={{4,0},{8,4},{12,8},{16,12},{20,16},{24,20},{28,24},{5,1},{9,5},{13... | collective-permute-start | bytes 1572872 | tf_op jit(solution)/shard_map/ppermute | solution.py:23
  72.1 1.4 %collective-permute-start.10 = (f32[256,128]{1,0:T(8,128)S(1)}, f32[256,128]{1,0:T(8,128)S(1)}, u32[]{:S(2)}, u32[]{:S(2)}) collective-permute-start(f32[256,128]{1,0:T(8,128)S(1)} %slice_add_fusion.2), channel_id=1, source_target_pairs={{0,1},{1,0},{2,3},{3,2},{4,5},{5,4},{6,7},{7,6},{8,9},{9,8},{10,11... | collective-permute-start | bytes 393224 | tf_op jit(solution)/shard_map/ppermute | solution.py:17
  73.5 5.6 %collective-permute-start.11 = (f32[256,128]{1,0:T(8,128)S(1)}, f32[256,128]{1,0:T(8,128)S(1)}, u32[]{:S(2)}, u32[]{:S(2)}) collective-permute-start(f32[256,128]{1,0:T(8,128)S(1)} %add.82), channel_id=1, source_target_pairs={{0,2},{1,3},{2,0},{3,1},{4,6},{5,7},{6,4},{7,5},{8,10},{9,11},{10,... | collective-permute-start | bytes 393224 | tf_op jit(solution)/shard_map/ppermute | solution.py:17

commit v16 on v15

--- a/solution.py
+++ b/solution.py
@@ -109,7 +109,7 @@
             in_specs=[
                 pl.BlockSpec((TB, pairs, rows, rows), lambda g, ids: (g, 0, 0, 0)),
                 hbm,
-                hbm,
+                pl.BlockSpec((cases, points_here, width), lambda g, ids: (0, 0, 0)),
                 hbm,
             ],
             out_specs=pl.BlockSpec((cases, TB * rows, width), lambda g, ids: (0, g, 0)),

time: 95.2 us -> 95.2 us (level)
  no operation moved by 1% of the time
where the time goes in v16:
time: 95.2 us; the launch traced here: 94.8 us
  waiting for transfers between devices  38.9 us (41%)
  starting transfers between devices  20.3 us (21%)
  Pallas kernels  16.4 us (17%)
  matrix products  11.7 us (12%)
  local copies, waits for them, and re-layouts  4.91 us (5%)
  other arithmetic  1.65 us (2%)
  between operations  0.98 us (1%)
    ppermute x8, waiting for transfers between devices, partner(): lax.ppermute(shard, axis, [(i, i ^ 1 << apart) for i in range(lax.axis_si...  22.9 us
    ppermute x4, waiting for transfers between devices, shifted(): lax.ppermute(value, axis, [(source, source + steps) for source in range(l...  16 us
    ppermute x4, starting transfers between devices, shifted(): lax.ppermute(value, axis, [(source, source + steps) for source in range(l...  12.7 us
    pallas_call x1, Pallas kernels, near_backward(): pl.pallas_call(functools.partial(near_bwd_kernel, cases, pairs, rows, ste...  8.9 us
    ppermute x8, starting transfers between devices, partner(): lax.ppermute(shard, axis, [(i, i ^ 1 << apart) for i in range(lax.axis_si...  7.56 us
    pallas_call x1, Pallas kernels, near_forward(): pl.pallas_call(functools.partial(near_fwd_kernel, cases, pairs, rows), ou...  7.45 us
    dot_general x1, matrix products, on_device(): jnp.einsum('apc,cd->apd', near_bf, w_near, preferred_element_type=jnp.flo...  4.56 us
    unnamed x20, local copies, waits for them, and re-layouts  2.54 us
  transfers between devices with their start and end apart: 12, of which 9 were waited for; matrix products, arithmetic and copies ran while one was open for 8% of the time, Pallas kernels for 9%

profile of v16, /device:TPU:16, one launch (start us, length us, event | category | flops | bytes accessed | tf_op | source)
XLA Modules:
  0.0 94.8 jit_solution(8900988135641952265)
XLA Ops:
  0.7 0.9 copy-done
  1.6 1.5 %convolution_bitcast_fusion.2 = f32[2,64,128]{2,1,0:T(8,128)S(1)} fusion(bf16[2,2048,128]{2,1,0:T(8,128)(2,1)} %own_hbm.1, bf16[64,2048]{1,0:T(8,128)(2,1)S(1)} %copy-done), kind=kOutput, calls=%fused_computation.19 | convolution fusion | flops 67108864 | bytes 1376256 | tf_op jit(solution)/shard_map/rp,apc->arc/dot_general | solution.py:221
  3.1 1.6 %collective-permute-start.2 = (f32[2,64,128]{2,1,0:T(8,128)S(1)}, f32[2,64,128]{2,1,0:T(8,128)S(1)}, u32[]{:S(2)}, u32[]{:S(2)}) collective-permute-start(f32[2,64,128]{2,1,0:T(8,128)S(1)} %convolution_bitcast_fusion.2), channel_id=1, source_target_pairs={{0,4},{4,0},{8,12},{12,8},{16,20},{20,16},{24,28},{28,24},{1,5},{5... | collective-permute-start | bytes 196616 | tf_op jit(solution)/shard_map/ppermute | solution.py:17
  4.7 1.0 %fusion.45 = (bf16[2,1024,128]{2,1,0:T(8,128)(2,1)}, bf16[2,1024,128]{2,1,0:T(8,128)(2,1)}) fusion(bf16[2,2048,128]{2,1,0:T(8,128)(2,1)S(1)} %copy-done.1), kind=kLoop, calls=%fused_computation.71 | loop fusion | bytes 2097152 | tf_op jit(solution)/shard_map/slice | solution.py:211
  5.7 2.3 %collective-permute-start.1 = (bf16[2,1024,128]{2,1,0:T(8,128)(2,1)}, bf16[2,1024,128]{2,1,0:T(8,128)(2,1)S(1)}, u32[]{:S(2)}, u32[]{:S(2)}) collective-permute-start(bf16[2,1024,128]{2,1,0:T(8,128)(2,1)} %get-tuple-element.26), channel_id=1, source_target_pairs={{4,0},{8,4},{12,8},{16,12},{20,16},{24,20},{28,24},{5,1},{9,5},{13... | collective-permute-start | bytes 1572872 | tf_op jit(solution)/shard_map/ppermute | solution.py:23
  8.0 3.5 %collective-permute-start = (bf16[2,1024,128]{2,1,0:T(8,128)(2,1)}, bf16[2,1024,128]{2,1,0:T(8,128)(2,1)S(1)}, u32[]{:S(2)}, u32[]{:S(2)}) collective-permute-start(bf16[2,1024,128]{2,1,0:T(8,128)(2,1)} %get-tuple-element.27), channel_id=1, source_target_pairs={{0,4},{4,8},{8,12},{12,16},{16,20},{20,24},{24,28},{1,5},{5,9},{9,... | collective-permute-start | bytes 1572872 | tf_op jit(solution)/shard_map/ppermute | solution.py:23
  11.6 1.7 %collective-permute-start.3 = (f32[2,64,128]{2,1,0:T(8,128)S(1)}, f32[2,64,128]{2,1,0:T(8,128)S(1)}, u32[]{:S(2)}, u32[]{:S(2)}) collective-permute-start(f32[2,64,128]{2,1,0:T(8,128)S(1)} %add.65), channel_id=1, source_target_pairs={{0,8},{4,12},{8,0},{12,4},{16,24},{20,28},{24,16},{28,20},{1,9},{5... | collective-permute-start | bytes 196616 | tf_op jit(solution)/shard_map/ppermute | solution.py:17
  13.3 0.7 reshape.29.ids_ref
  14.0 9.2 %collective-permute-done.3 = f32[2,64,128]{2,1,0:T(8,128)S(1)} collective-permute-done((f32[2,64,128]{2,1,0:T(8,128)S(1)}, f32[2,64,128]{2,1,0:T(8,128)S(1)}, u32[]{:S(2)}, u32[]{:S(2)}) %collective-permute-start.3) | collective-permute-done | bytes 65568 | tf_op jit(solution)/shard_map/ppermute | solution.py:17
  23.5 4.9 %collective-permute-done.4 = f32[2,64,128]{2,1,0:T(8,128)S(1)} collective-permute-done((f32[2,64,128]{2,1,0:T(8,128)S(1)}, f32[2,64,128]{2,1,0:T(8,128)S(1)}, u32[]{:S(2)}, u32[]{:S(2)}) %collective-permute-start.4) | collective-permute-done | bytes 65568 | tf_op jit(solution)/shard_map/ppermute | solution.py:17
  28.8 1.3 %convolution_bitcast_fusion.1 = f32[2,2048,128]{2,1,0:T(8,128)S(1)} fusion(bf16[2,64,128]{2,1,0:T(8,128)(2,1)S(1)} %fusion.17, bf16[64,2048]{1,0:T(8,128)(2,1)S(1)} %copy-done, bf16[128,128]{1,0:T(8,128)(2,1)} %param.14), kind=kOutput, calls=%fused_computation.3 | convolution fusion | flops 71319552 | bytes 2424832 | tf_op jit(solution)/shard_map/rp,ard->apd/dot_general | solution.py:227
  30.1 2.3 %collective-permute-done.1.next_hbm = bf16[2,1024,128]{2,1,0:T(8,128)(2,1)S(1)} collective-permute-done((bf16[2,1024,128]{2,1,0:T(8,128)(2,1)}, bf16[2,1024,128]{2,1,0:T(8,128)(2,1)S(1)}, u32[]{:S(2)}, u32[]{:S(2)}) %collective-permute-start.1) | collective-permute-done | bytes 524320 | tf_op jit(solution)/shard_map/ppermute | solution.py:23
  32.5 0.8 copy-done.4
  33.3 0.8 copy-done.5
  34.0 7.5 %shard_map.111 = bf16[2,2048,128]{2,1,0:T(8,128)(2,1)} custom-call(s32[192]{0:T(256)} %reshape.29.ids_ref, bf16[16,12,128,128]{3,2,1,0:T(8,128)(2,1)} %kb_ref.3, bf16[2,1024,128]{2,1,0:T(8,128)(2,1)} %copy-done.5, bf16[2,2048,128]{2,1,0:T(8,128)(2,1)} %own_hbm.1, bf16[2,1024,128]{2,1,0:T(8,128)(2,1)} %copy-done.4), custom_call_target="tpu_custom_call" | custom-call | flops 1610612736 | bytes 9437184 | tf_op jit(solution)/shard_map/pallas_call | solution.py:103
  41.5 4.6 %fusion.2 = (bf16[2,2048,128]{2,1,0:T(8,128)(2,1)S(1)}, bf16[2,2048,128]{2,1,0:T(8,128)(2,1)}) fusion(bf16[2,2048,128]{2,1,0:T(8,128)(2,1)} %param.9, f32[2,2048,128]{2,1,0:T(8,128)S(1)} %convolution_bitcast_fusion.1, bf16[2,2048,128]{2,1,0:T(8,128)(2,1)} %shard_map.111, bf16[128,128]{1,0:T(8,128)(2,1)} %param.13), kind=kOutput, calls=%fused_computation.10 | convolution fusion | flops 146800640 | bytes 6324224 | tf_op jit(solution)/shard_map/apc,cd->apd/dot_general | solution.py:229
  47.2 0.7 collective-permute-start.5
  47.9 1.4 %convolution_convert_fusion.back_ref = bf16[2,2048,128]{2,1,0:T(8,128)(2,1)} fusion(bf16[2,2048,128]{2,1,0:T(8,128)(2,1)S(1)} %get-tuple-element.24, bf16[128,128]{1,0:T(8,128)(2,1)S(1)} %copy-done.8), kind=kOutput, calls=%fused_computation.7 | convolution fusion | flops 134742016 | bytes 2129920 | tf_op jit(solution)/shard_map/apc,dc->apd/dot_general | solution.py:237
  49.3 3.7 %collective-permute-done.5 = f32[384,128]{1,0:T(8,128)S(1)} collective-permute-done((f32[384,128]{1,0:T(8,128)S(1)}, f32[384,128]{1,0:T(8,128)S(1)}, u32[]{:S(2)}, u32[]{:S(2)}) %collective-permute-start.5) | collective-permute-done | bytes 196640 | tf_op jit(solution)/shard_map/ppermute | solution.py:17
  53.1 1.6 %collective-permute-start.6 = (f32[384,128]{1,0:T(8,128)S(1)}, f32[384,128]{1,0:T(8,128)S(1)}, u32[]{:S(2)}, u32[]{:S(2)}) collective-permute-start(f32[384,128]{1,0:T(8,128)S(1)} %pad_maximum_fusion.2), channel_id=1, source_target_pairs={{0,8},{4,12},{8,0},{12,4},{16,24},{20,28},{24,16},{28,20},{1,9},{5... | collective-permute-start | bytes 589832 | tf_op jit(solution)/shard_map/ppermute | solution.py:17
  54.7 8.9 %shard_map.112 = (f32[2,2048,128]{2,1,0:T(8,128)}, bf16[2,1024,128]{2,1,0:T(8,128)(2,1)}, bf16[2,1024,128]{2,1,0:T(8,128)(2,1)}) custom-call(s32[192]{0:T(256)} %reshape.29.ids_ref, bf16[16,12,128,128]{3,2,1,0:T(8,128)(2,1)} %kb_ref.3, bf16[2,2048,128]{2,1,0:T(8,128)(2,1)} %convolution_convert_fusion.back_ref), custom_call_target="tpu_custom_call" | custom-call | flops 1610612736 | bytes 11534336 | tf_op jit(solution)/shard_map/pallas_call | solution.py:166
  64.4 3.6 %collective-permute-start.8 = (bf16[2,1024,128]{2,1,0:T(8,128)(2,1)}, bf16[2,1024,128]{2,1,0:T(8,128)(2,1)S(1)}, u32[]{:S(2)}, u32[]{:S(2)}) collective-permute-start(bf16[2,1024,128]{2,1,0:T(8,128)(2,1)} %get-tuple-element.20), channel_id=1, source_target_pairs={{0,4},{4,8},{8,12},{12,16},{16,20},{20,24},{24,28},{1,5},{5,9},{9,... | collective-permute-start | bytes 1572872 | tf_op jit(solution)/shard_map/ppermute | solution.py:23
  68.0 3.2 %collective-permute-start.9 = (bf16[2,1024,128]{2,1,0:T(8,128)(2,1)}, bf16[2,1024,128]{2,1,0:T(8,128)(2,1)S(1)}, u32[]{:S(2)}, u32[]{:S(2)}) collective-permute-start(bf16[2,1024,128]{2,1,0:T(8,128)(2,1)} %get-tuple-element.21), channel_id=1, source_target_pairs={{4,0},{8,4},{12,8},{16,12},{20,16},{24,20},{28,24},{5,1},{9,5},{13... | collective-permute-start | bytes 1572872 | tf_op jit(solution)/shard_map/ppermute | solution.py:23
  71.5 0.6 collective-permute-done.7
  72.5 1.1 %collective-permute-done.10 = f32[256,128]{1,0:T(8,128)S(1)} collective-permute-done((f32[256,128]{1,0:T(8,128)S(1)}, f32[256,128]{1,0:T(8,128)S(1)}, u32[]{:S(2)}, u32[]{:S(2)}) %collective-permute-start.10) | collective-permute-done | bytes 131104 | tf_op jit(solution)/shard_map/ppermute | solution.py:17
  73.5 1.4 %collective-permute-start.11 = (f32[256,128]{1,0:T(8,128)S(1)}, f32[256,128]{1,0:T(8,128)S(1)}, u32[]{:S(2)}, u32[]{:S(2)}) collective-permute-start(f32[256,128]{1,0:T(8,128)S(1)} %add.82), channel_id=1, source_target_pairs={{0,2},{1,3},{2,0},{3,1},{4,6},{5,7},{6,4},{7,5},{8,10},{9,11},{10,... | collective-permute-start | bytes 393224 | tf_op jit(solution)/shard_map/ppermute | solution.py:17
  75.0 0.5 convolution_bitcast_fusion
  75.7 3.4 %collective-permute-done.11 = f32[256,128]{1,0:T(8,128)S(1)} collective-permute-done((f32[256,128]{1,0:T(8,128)S(1)}, f32[256,128]{1,0:T(8,128)S(1)}, u32[]{:S(2)}, u32[]{:S(2)}) %collective-permute-start.11) | collective-permute-done | bytes 131104 | tf_op jit(solution)/shard_map/ppermute | solution.py:17
  79.2 0.7 fusion.46
  79.8 9.7 %collective-permute-done.8 = bf16[2,1024,128]{2,1,0:T(8,128)(2,1)S(1)} collective-permute-done((bf16[2,1024,128]{2,1,0:T(8,128)(2,1)}, bf16[2,1024,128]{2,1,0:T(8,128)(2,1)S(1)}, u32[]{:S(2)}, u32[]{:S(2)}) %collective-permute-start.8) | collective-permute-done | bytes 524320 | tf_op jit(solution)/shard_map/ppermute | solution.py:23
  89.5 4.0 %collective-permute-done.9 = bf16[2,1024,128]{2,1,0:T(8,128)(2,1)S(1)} collective-permute-done((bf16[2,1024,128]{2,1,0:T(8,128)(2,1)}, bf16[2,1024,128]{2,1,0:T(8,128)(2,1)S(1)}, u32[]{:S(2)}, u32[]{:S(2)}) %collective-permute-start.9) | collective-permute-done | bytes 524320 | tf_op jit(solution)/shard_map/ppermute | solution.py:23
  93.7 1.0 %pad_maximum_fusion = bf16[2,2048,128]{2,1,0:T(8,128)(2,1)} fusion(bf16[2,1024,128]{2,1,0:T(8,128)(2,1)S(1)} %get-tuple-element.23, bf16[2,1024,128]{2,1,0:T(8,128)(2,1)S(1)} %get-tuple-element.22), kind=kLoop, calls=%fused_computation.39 | loop fusion | flops 2097152 | bytes 2097152 | tf_op jit(solution)/shard_map/concatenate | solution.py:275
  (51 shorter events, 3.7 us)
Async XLA Ops:
  0.6 1.0 %copy-start = (bf16[64,2048]{1,0:T(8,128)(2,1)S(1)}, bf16[64,2048]{1,0:T(8,128)(2,1)}, u32[]{:S(2)}) copy-start(bf16[64,2048]{1,0:T(8,128)(2,1)} %param.12) | copy-start | bytes 786436
  0.6 4.1 %copy-start.1 = (bf16[2,2048,128]{2,1,0:T(8,128)(2,1)S(1)}, bf16[2,2048,128]{2,1,0:T(8,128)(2,1)}, u32[]{:S(2)}) copy-start(bf16[2,2048,128]{2,1,0:T(8,128)(2,1)} %own_hbm.1) | copy-start | bytes 3145732
  0.7 12.6 %copy-start.9 = (s32[16,12]{1,0:T(8,128)S(1)}, s32[16,12]{1,0:T(8,128)}, u32[]{:S(2)}) copy-start(s32[16,12]{1,0:T(8,128)} %param.11) | copy-start | bytes 2308
  0.7 22.6 %copy-start.6 = (f32[3,64,64]{2,1,0:T(8,128)S(1)}, f32[3,64,64]{2,1,0:T(8,128)}, u32[]{:S(2)}) copy-start(f32[3,64,64]{2,1,0:T(8,128)} %param.15) | copy-start | bytes 147460
  3.1 8.5 %collective-permute-start.2 = (f32[2,64,128]{2,1,0:T(8,128)S(1)}, f32[2,64,128]{2,1,0:T(8,128)S(1)}, u32[]{:S(2)}, u32[]{:S(2)}) collective-permute-start(f32[2,64,128]{2,1,0:T(8,128)S(1)} %convolution_bitcast_fusion.2), channel_id=1, source_target_pairs={{0,4},{4,0},{8,12},{12,8},{16,20},{20,16},{24,28},{28,24},{1,5},{5... | collective-permute-start | bytes 196616 | tf_op jit(solution)/shard_map/ppermute | solution.py:17
  5.7 26.7 %collective-permute-start.1 = (bf16[2,1024,128]{2,1,0:T(8,128)(2,1)}, bf16[2,1024,128]{2,1,0:T(8,128)(2,1)S(1)}, u32[]{:S(2)}, u32[]{:S(2)}) collective-permute-start(bf16[2,1024,128]{2,1,0:T(8,128)(2,1)} %get-tuple-element.26), channel_id=1, source_target_pairs={{4,0},{8,4},{12,8},{16,12},{20,16},{24,20},{28,24},{5,1},{9,5},{13... | collective-permute-start | bytes 1572872 | tf_op jit(solution)/shard_map/ppermute | solution.py:23
  8.0 24.4 %collective-permute-start = (bf16[2,1024,128]{2,1,0:T(8,128)(2,1)}, bf16[2,1024,128]{2,1,0:T(8,128)(2,1)S(1)}, u32[]{:S(2)}, u32[]{:S(2)}) collective-permute-start(bf16[2,1024,128]{2,1,0:T(8,128)(2,1)} %get-tuple-element.27), channel_id=1, source_target_pairs={{0,4},{4,8},{8,12},{12,16},{16,20},{20,24},{24,28},{1,5},{5,9},{9,... | collective-permute-start | bytes 1572872 | tf_op jit(solution)/shard_map/ppermute | solution.py:23
  11.6 11.5 %collective-permute-start.3 = (f32[2,64,128]{2,1,0:T(8,128)S(1)}, f32[2,64,128]{2,1,0:T(8,128)S(1)}, u32[]{:S(2)}, u32[]{:S(2)}) collective-permute-start(f32[2,64,128]{2,1,0:T(8,128)S(1)} %add.65), channel_id=1, source_target_pairs={{0,8},{4,12},{8,0},{12,4},{16,24},{20,28},{24,16},{28,20},{1,9},{5... | collective-permute-start | bytes 196616 | tf_op jit(solution)/shard_map/ppermute | solution.py:17
  23.2 5.2 %collective-permute-start.4 = (f32[2,64,128]{2,1,0:T(8,128)S(1)}, f32[2,64,128]{2,1,0:T(8,128)S(1)}, u32[]{:S(2)}, u32[]{:S(2)}) collective-permute-start(f32[2,64,128]{2,1,0:T(8,128)S(1)} %add.67), channel_id=1, source_target_pairs={{0,16},{4,20},{8,24},{12,28},{16,0},{20,4},{24,8},{28,12},{1,17},{... | collective-permute-start | bytes 196616 | tf_op jit(solution)/shard_map/ppermute | solution.py:17
  32.5 0.8 copy-start.4
  33.3 0.8 copy-start.5
  41.5 4.6 %copy-start.2 = (bf16[2,2048,128]{2,1,0:T(8,128)(2,1)S(1)}, bf16[2,2048,128]{2,1,0:T(8,128)(2,1)}, u32[]{:S(2)}) copy-start(bf16[2,2048,128]{2,1,0:T(8,128)(2,1)} %shard_map.111) | copy-start | bytes 3145732
  46.1 1.0 %copy-start.7 = (bf16[128,128]{1,0:T(8,128)(2,1)S(1)}, bf16[128,128]{1,0:T(8,128)(2,1)}, u32[]{:S(2)}) copy-start(bf16[128,128]{1,0:T(8,128)(2,1)} %param.14) | copy-start | bytes 98308
  46.1 1.8 %copy-start.8 = (bf16[128,128]{1,0:T(8,128)(2,1)S(1)}, bf16[128,128]{1,0:T(8,128)(2,1)}, u32[]{:S(2)}) copy-start(bf16[128,128]{1,0:T(8,128)(2,1)} %param.13) | copy-start | bytes 98308
  47.2 5.8 %collective-permute-start.5 = (f32[384,128]{1,0:T(8,128)S(1)}, f32[384,128]{1,0:T(8,128)S(1)}, u32[]{:S(2)}, u32[]{:S(2)}) collective-permute-start(f32[384,128]{1,0:T(8,128)S(1)} %pad_maximum_fusion.1), channel_id=1, source_target_pairs={{0,4},{4,0},{8,12},{12,8},{16,20},{20,16},{24,28},{28,24},{1,5},{5... | collective-permute-start | bytes 589832 | tf_op jit(solution)/shard_map/ppermute | solution.py:17
  53.1 10.8 %collective-permute-start.6 = (f32[384,128]{1,0:T(8,128)S(1)}, f32[384,128]{1,0:T(8,128)S(1)}, u32[]{:S(2)}, u32[]{:S(2)}) collective-permute-start(f32[384,128]{1,0:T(8,128)S(1)} %pad_maximum_fusion.2), channel_id=1, source_target_pairs={{0,8},{4,12},{8,0},{12,4},{16,24},{20,28},{24,16},{28,20},{1,9},{5... | collective-permute-start | bytes 589832 | tf_op jit(solution)/shard_map/ppermute | solution.py:17
  63.9 11.6 %copy-start.3 = (f32[2,2048,128]{2,1,0:T(8,128)S(1)}, f32[2,2048,128]{2,1,0:T(8,128)}, u32[]{:S(2)}) copy-start(f32[2,2048,128]{2,1,0:T(8,128)} %get-tuple-element.18) | copy-start | bytes 6291460
  64.0 8.1 %collective-permute-start.7 = (f32[384,128]{1,0:T(8,128)S(1)}, f32[384,128]{1,0:T(8,128)S(1)}, u32[]{:S(2)}, u32[]{:S(2)}) collective-permute-start(f32[384,128]{1,0:T(8,128)S(1)} %pad_maximum_fusion.3), channel_id=1, source_target_pairs={{0,16},{4,20},{8,24},{12,28},{16,0},{20,4},{24,8},{28,12},{1,17},{... | collective-permute-start | bytes 589832 | tf_op jit(solution)/shard_map/ppermute | solution.py:17
  64.4 25.1 %collective-permute-start.8 = (bf16[2,1024,128]{2,1,0:T(8,128)(2,1)}, bf16[2,1024,128]{2,1,0:T(8,128)(2,1)S(1)}, u32[]{:S(2)}, u32[]{:S(2)}) collective-permute-start(bf16[2,1024,128]{2,1,0:T(8,128)(2,1)} %get-tuple-element.20), channel_id=1, source_target_pairs={{0,4},{4,8},{8,12},{12,16},{16,20},{20,24},{24,28},{1,5},{5,9},{9,... | collective-permute-start | bytes 1572872 | tf_op jit(solution)/shard_map/ppermute | solution.py:23
  68.0 25.5 %collective-permute-start.9 = (bf16[2,1024,128]{2,1,0:T(8,128)(2,1)}, bf16[2,1024,128]{2,1,0:T(8,128)(2,1)S(1)}, u32[]{:S(2)}, u32[]{:S(2)}) collective-permute-start(bf16[2,1024,128]{2,1,0:T(8,128)(2,1)} %get-tuple-element.21), channel_id=1, source_target_pairs={{4,0},{8,4},{12,8},{16,12},{20,16},{24,20},{28,24},{5,1},{9,5},{13... | collective-permute-start | bytes 1572872 | tf_op jit(solution)/shard_map/ppermute | solution.py:23
  72.1 1.4 %collective-permute-start.10 = (f32[256,128]{1,0:T(8,128)S(1)}, f32[256,128]{1,0:T(8,128)S(1)}, u32[]{:S(2)}, u32[]{:S(2)}) collective-permute-start(f32[256,128]{1,0:T(8,128)S(1)} %slice_add_fusion.2), channel_id=1, source_target_pairs={{0,1},{1,0},{2,3},{3,2},{4,5},{5,4},{6,7},{7,6},{8,9},{9,8},{10,11... | collective-permute-start | bytes 393224 | tf_op jit(solution)/shard_map/ppermute | solution.py:17
  73.5 5.6 %collective-permute-start.11 = (f32[256,128]{1,0:T(8,128)S(1)}, f32[256,128]{1,0:T(8,128)S(1)}, u32[]{:S(2)}, u32[]{:S(2)}) collective-permute-start(f32[256,128]{1,0:T(8,128)S(1)} %add.82), channel_id=1, source_target_pairs={{0,2},{1,3},{2,0},{3,1},{4,6},{5,7},{6,4},{7,5},{8,10},{9,11},{10,... | collective-permute-start | bytes 393224 | tf_op jit(solution)/shard_map/ppermute | solution.py:17

commit v17 on v15

--- a/solution.py
+++ b/solution.py
@@ -10,7 +10,7 @@
 
 HALO = 8
 TB = 8
-BWD_TB = 4
+BWD_TB = 8
 
 
 def partner(shard, axis, apart):

time: 95.2 us -> 94.8 us (level)
  no operation moved by 1% of the time
where the time goes in v17:
time: 94.8 us; the launch traced here: 94.5 us
  waiting for transfers between devices  39 us (41%)
  starting transfers between devices  20.2 us (21%)
  Pallas kernels  16 us (17%)
  matrix products  11.7 us (12%)
  local copies, waits for them, and re-layouts  4.91 us (5%)
  other arithmetic  1.65 us (2%)
  between operations  0.98 us (1%)
    ppermute x8, waiting for transfers between devices, partner(): lax.ppermute(shard, axis, [(i, i ^ 1 << apart) for i in range(lax.axis_si...  22.9 us
    ppermute x4, waiting for transfers between devices, shifted(): lax.ppermute(value, axis, [(source, source + steps) for source in range(l...  16.1 us
    ppermute x4, starting transfers between devices, shifted(): lax.ppermute(value, axis, [(source, source + steps) for source in range(l...  12.7 us
    pallas_call x1, Pallas kernels, near_backward(): pl.pallas_call(functools.partial(near_bwd_kernel, cases, pairs, rows, ste...  8.54 us
    ppermute x8, starting transfers between devices, partner(): lax.ppermute(shard, axis, [(i, i ^ 1 << apart) for i in range(lax.axis_si...  7.52 us
    pallas_call x1, Pallas kernels, near_forward(): pl.pallas_call(functools.partial(near_fwd_kernel, cases, pairs, rows), ou...  7.47 us
    dot_general x1, matrix products, on_device(): jnp.einsum('apc,cd->apd', near_bf, w_near, preferred_element_type=jnp.flo...  4.55 us
    unnamed x20, local copies, waits for them, and re-layouts  2.54 us
  transfers between devices with their start and end apart: 12, of which 9 were waited for; matrix products, arithmetic and copies ran while one was open for 8% of the time, Pallas kernels for 9%

profile of v17, /device:TPU:16, one launch (start us, length us, event | category | flops | bytes accessed | tf_op | source)
XLA Modules:
  0.0 94.5 jit_solution(17641049580082875131)
XLA Ops:
  0.7 0.9 copy-done
  1.6 1.5 %convolution_bitcast_fusion.2 = f32[2,64,128]{2,1,0:T(8,128)S(1)} fusion(bf16[2,2048,128]{2,1,0:T(8,128)(2,1)} %own_hbm.1, bf16[64,2048]{1,0:T(8,128)(2,1)S(1)} %copy-done), kind=kOutput, calls=%fused_computation.19 | convolution fusion | flops 67108864 | bytes 1376256 | tf_op jit(solution)/shard_map/rp,apc->arc/dot_general | solution.py:221
  3.1 1.6 %collective-permute-start.2 = (f32[2,64,128]{2,1,0:T(8,128)S(1)}, f32[2,64,128]{2,1,0:T(8,128)S(1)}, u32[]{:S(2)}, u32[]{:S(2)}) collective-permute-start(f32[2,64,128]{2,1,0:T(8,128)S(1)} %convolution_bitcast_fusion.2), channel_id=1, source_target_pairs={{0,4},{4,0},{8,12},{12,8},{16,20},{20,16},{24,28},{28,24},{1,5},{5... | collective-permute-start | bytes 196616 | tf_op jit(solution)/shard_map/ppermute | solution.py:17
  4.7 1.0 %fusion.45 = (bf16[2,1024,128]{2,1,0:T(8,128)(2,1)}, bf16[2,1024,128]{2,1,0:T(8,128)(2,1)}) fusion(bf16[2,2048,128]{2,1,0:T(8,128)(2,1)S(1)} %copy-done.1), kind=kLoop, calls=%fused_computation.71 | loop fusion | bytes 2097152 | tf_op jit(solution)/shard_map/slice | solution.py:211
  5.7 2.3 %collective-permute-start.1 = (bf16[2,1024,128]{2,1,0:T(8,128)(2,1)}, bf16[2,1024,128]{2,1,0:T(8,128)(2,1)S(1)}, u32[]{:S(2)}, u32[]{:S(2)}) collective-permute-start(bf16[2,1024,128]{2,1,0:T(8,128)(2,1)} %get-tuple-element.26), channel_id=1, source_target_pairs={{4,0},{8,4},{12,8},{16,12},{20,16},{24,20},{28,24},{5,1},{9,5},{13... | collective-permute-start | bytes 1572872 | tf_op jit(solution)/shard_map/ppermute | solution.py:23
  8.0 3.5 %collective-permute-start = (bf16[2,1024,128]{2,1,0:T(8,128)(2,1)}, bf16[2,1024,128]{2,1,0:T(8,128)(2,1)S(1)}, u32[]{:S(2)}, u32[]{:S(2)}) collective-permute-start(bf16[2,1024,128]{2,1,0:T(8,128)(2,1)} %get-tuple-element.27), channel_id=1, source_target_pairs={{0,4},{4,8},{8,12},{12,16},{16,20},{20,24},{24,28},{1,5},{5,9},{9,... | collective-permute-start | bytes 1572872 | tf_op jit(solution)/shard_map/ppermute | solution.py:23
  11.6 1.7 %collective-permute-start.3 = (f32[2,64,128]{2,1,0:T(8,128)S(1)}, f32[2,64,128]{2,1,0:T(8,128)S(1)}, u32[]{:S(2)}, u32[]{:S(2)}) collective-permute-start(f32[2,64,128]{2,1,0:T(8,128)S(1)} %add.65), channel_id=1, source_target_pairs={{0,8},{4,12},{8,0},{12,4},{16,24},{20,28},{24,16},{28,20},{1,9},{5... | collective-permute-start | bytes 196616 | tf_op jit(solution)/shard_map/ppermute | solution.py:17
  13.3 0.7 reshape.29.ids_ref
  14.0 9.2 %collective-permute-done.3 = f32[2,64,128]{2,1,0:T(8,128)S(1)} collective-permute-done((f32[2,64,128]{2,1,0:T(8,128)S(1)}, f32[2,64,128]{2,1,0:T(8,128)S(1)}, u32[]{:S(2)}, u32[]{:S(2)}) %collective-permute-start.3) | collective-permute-done | bytes 65568 | tf_op jit(solution)/shard_map/ppermute | solution.py:17
  23.5 4.9 %collective-permute-done.4 = f32[2,64,128]{2,1,0:T(8,128)S(1)} collective-permute-done((f32[2,64,128]{2,1,0:T(8,128)S(1)}, f32[2,64,128]{2,1,0:T(8,128)S(1)}, u32[]{:S(2)}, u32[]{:S(2)}) %collective-permute-start.4) | collective-permute-done | bytes 65568 | tf_op jit(solution)/shard_map/ppermute | solution.py:17
  28.8 1.3 %convolution_bitcast_fusion.1 = f32[2,2048,128]{2,1,0:T(8,128)S(1)} fusion(bf16[2,64,128]{2,1,0:T(8,128)(2,1)S(1)} %fusion.17, bf16[64,2048]{1,0:T(8,128)(2,1)S(1)} %copy-done, bf16[128,128]{1,0:T(8,128)(2,1)} %param.14), kind=kOutput, calls=%fused_computation.3 | convolution fusion | flops 71319552 | bytes 2424832 | tf_op jit(solution)/shard_map/rp,ard->apd/dot_general | solution.py:227
  30.1 2.3 %collective-permute-done.1.next_hbm = bf16[2,1024,128]{2,1,0:T(8,128)(2,1)S(1)} collective-permute-done((bf16[2,1024,128]{2,1,0:T(8,128)(2,1)}, bf16[2,1024,128]{2,1,0:T(8,128)(2,1)S(1)}, u32[]{:S(2)}, u32[]{:S(2)}) %collective-permute-start.1) | collective-permute-done | bytes 524320 | tf_op jit(solution)/shard_map/ppermute | solution.py:23
  32.5 0.8 copy-done.4
  33.3 0.8 copy-done.5
  34.0 7.5 %shard_map.111 = bf16[2,2048,128]{2,1,0:T(8,128)(2,1)} custom-call(s32[192]{0:T(256)} %reshape.29.ids_ref, bf16[16,12,128,128]{3,2,1,0:T(8,128)(2,1)} %kb_ref.3, bf16[2,1024,128]{2,1,0:T(8,128)(2,1)} %copy-done.5, bf16[2,2048,128]{2,1,0:T(8,128)(2,1)} %own_hbm.1, bf16[2,1024,128]{2,1,0:T(8,128)(2,1)} %copy-done.4), custom_call_target="tpu_custom_call" | custom-call | flops 1610612736 | bytes 9437184 | tf_op jit(solution)/shard_map/pallas_call | solution.py:103
  41.5 4.6 %fusion.2 = (bf16[2,2048,128]{2,1,0:T(8,128)(2,1)S(1)}, bf16[2,2048,128]{2,1,0:T(8,128)(2,1)}) fusion(bf16[2,2048,128]{2,1,0:T(8,128)(2,1)} %param.9, f32[2,2048,128]{2,1,0:T(8,128)S(1)} %convolution_bitcast_fusion.1, bf16[2,2048,128]{2,1,0:T(8,128)(2,1)} %shard_map.111, bf16[128,128]{1,0:T(8,128)(2,1)} %param.13), kind=kOutput, calls=%fused_computation.10 | convolution fusion | flops 146800640 | bytes 6324224 | tf_op jit(solution)/shard_map/apc,cd->apd/dot_general | solution.py:229
  47.3 0.7 collective-permute-start.5
  47.9 1.4 %convolution_convert_fusion.back_ref = bf16[2,2048,128]{2,1,0:T(8,128)(2,1)} fusion(bf16[2,2048,128]{2,1,0:T(8,128)(2,1)S(1)} %get-tuple-element.24, bf16[128,128]{1,0:T(8,128)(2,1)S(1)} %copy-done.8), kind=kOutput, calls=%fused_computation.7 | convolution fusion | flops 134742016 | bytes 2129920 | tf_op jit(solution)/shard_map/apc,dc->apd/dot_general | solution.py:237
  49.4 3.7 %collective-permute-done.5 = f32[384,128]{1,0:T(8,128)S(1)} collective-permute-done((f32[384,128]{1,0:T(8,128)S(1)}, f32[384,128]{1,0:T(8,128)S(1)}, u32[]{:S(2)}, u32[]{:S(2)}) %collective-permute-start.5) | collective-permute-done | bytes 196640 | tf_op jit(solution)/shard_map/ppermute | solution.py:17
  53.1 1.6 %collective-permute-start.6 = (f32[384,128]{1,0:T(8,128)S(1)}, f32[384,128]{1,0:T(8,128)S(1)}, u32[]{:S(2)}, u32[]{:S(2)}) collective-permute-start(f32[384,128]{1,0:T(8,128)S(1)} %pad_maximum_fusion.2), channel_id=1, source_target_pairs={{0,8},{4,12},{8,0},{12,4},{16,24},{20,28},{24,16},{28,20},{1,9},{5... | collective-permute-start | bytes 589832 | tf_op jit(solution)/shard_map/ppermute | solution.py:17
  54.7 8.5 %shard_map.112 = (f32[2,2048,128]{2,1,0:T(8,128)}, bf16[2,1024,128]{2,1,0:T(8,128)(2,1)}, bf16[2,1024,128]{2,1,0:T(8,128)(2,1)}) custom-call(s32[192]{0:T(256)} %reshape.29.ids_ref, bf16[16,12,128,128]{3,2,1,0:T(8,128)(2,1)} %kb_ref.3, bf16[2,2048,128]{2,1,0:T(8,128)(2,1)} %convolution_convert_fusion.back_ref), custom_call_target="tpu_custom_call" | custom-call | flops 1610612736 | bytes 11534336 | tf_op jit(solution)/shard_map/pallas_call | solution.py:166
  64.1 3.6 %collective-permute-start.8 = (bf16[2,1024,128]{2,1,0:T(8,128)(2,1)}, bf16[2,1024,128]{2,1,0:T(8,128)(2,1)S(1)}, u32[]{:S(2)}, u32[]{:S(2)}) collective-permute-start(bf16[2,1024,128]{2,1,0:T(8,128)(2,1)} %get-tuple-element.20), channel_id=1, source_target_pairs={{0,4},{4,8},{8,12},{12,16},{16,20},{20,24},{24,28},{1,5},{5,9},{9,... | collective-permute-start | bytes 1572872 | tf_op jit(solution)/shard_map/ppermute | solution.py:23
  67.7 3.2 %collective-permute-start.9 = (bf16[2,1024,128]{2,1,0:T(8,128)(2,1)}, bf16[2,1024,128]{2,1,0:T(8,128)(2,1)S(1)}, u32[]{:S(2)}, u32[]{:S(2)}) collective-permute-start(bf16[2,1024,128]{2,1,0:T(8,128)(2,1)} %get-tuple-element.21), channel_id=1, source_target_pairs={{4,0},{8,4},{12,8},{16,12},{20,16},{24,20},{28,24},{5,1},{9,5},{13... | collective-permute-start | bytes 1572872 | tf_op jit(solution)/shard_map/ppermute | solution.py:23
  71.2 0.5 collective-permute-done.7
  72.1 1.1 %collective-permute-done.10 = f32[256,128]{1,0:T(8,128)S(1)} collective-permute-done((f32[256,128]{1,0:T(8,128)S(1)}, f32[256,128]{1,0:T(8,128)S(1)}, u32[]{:S(2)}, u32[]{:S(2)}) %collective-permute-start.10) | collective-permute-done | bytes 131104 | tf_op jit(solution)/shard_map/ppermute | solution.py:17
  73.2 1.4 %collective-permute-start.11 = (f32[256,128]{1,0:T(8,128)S(1)}, f32[256,128]{1,0:T(8,128)S(1)}, u32[]{:S(2)}, u32[]{:S(2)}) collective-permute-start(f32[256,128]{1,0:T(8,128)S(1)} %add.82), channel_id=1, source_target_pairs={{0,2},{1,3},{2,0},{3,1},{4,6},{5,7},{6,4},{7,5},{8,10},{9,11},{10,... | collective-permute-start | bytes 393224 | tf_op jit(solution)/shard_map/ppermute | solution.py:17
  74.6 0.5 convolution_bitcast_fusion
  75.3 3.5 %collective-permute-done.11 = f32[256,128]{1,0:T(8,128)S(1)} collective-permute-done((f32[256,128]{1,0:T(8,128)S(1)}, f32[256,128]{1,0:T(8,128)S(1)}, u32[]{:S(2)}, u32[]{:S(2)}) %collective-permute-start.11) | collective-permute-done | bytes 131104 | tf_op jit(solution)/shard_map/ppermute | solution.py:17
  78.8 0.7 fusion.46
  79.5 9.7 %collective-permute-done.8 = bf16[2,1024,128]{2,1,0:T(8,128)(2,1)S(1)} collective-permute-done((bf16[2,1024,128]{2,1,0:T(8,128)(2,1)}, bf16[2,1024,128]{2,1,0:T(8,128)(2,1)S(1)}, u32[]{:S(2)}, u32[]{:S(2)}) %collective-permute-start.8) | collective-permute-done | bytes 524320 | tf_op jit(solution)/shard_map/ppermute | solution.py:23
  89.2 4.0 %collective-permute-done.9 = bf16[2,1024,128]{2,1,0:T(8,128)(2,1)S(1)} collective-permute-done((bf16[2,1024,128]{2,1,0:T(8,128)(2,1)}, bf16[2,1024,128]{2,1,0:T(8,128)(2,1)S(1)}, u32[]{:S(2)}, u32[]{:S(2)}) %collective-permute-start.9) | collective-permute-done | bytes 524320 | tf_op jit(solution)/shard_map/ppermute | solution.py:23
  93.4 1.0 %pad_maximum_fusion = bf16[2,2048,128]{2,1,0:T(8,128)(2,1)} fusion(bf16[2,1024,128]{2,1,0:T(8,128)(2,1)S(1)} %get-tuple-element.23, bf16[2,1024,128]{2,1,0:T(8,128)(2,1)S(1)} %get-tuple-element.22), kind=kLoop, calls=%fused_computation.39 | loop fusion | flops 2097152 | bytes 2097152 | tf_op jit(solution)/shard_map/concatenate | solution.py:275
  (51 shorter events, 3.7 us)
Async XLA Ops:
  0.6 1.0 %copy-start = (bf16[64,2048]{1,0:T(8,128)(2,1)S(1)}, bf16[64,2048]{1,0:T(8,128)(2,1)}, u32[]{:S(2)}) copy-start(bf16[64,2048]{1,0:T(8,128)(2,1)} %param.12) | copy-start | bytes 786436
  0.6 4.1 %copy-start.1 = (bf16[2,2048,128]{2,1,0:T(8,128)(2,1)S(1)}, bf16[2,2048,128]{2,1,0:T(8,128)(2,1)}, u32[]{:S(2)}) copy-start(bf16[2,2048,128]{2,1,0:T(8,128)(2,1)} %own_hbm.1) | copy-start | bytes 3145732
  0.7 12.6 %copy-start.9 = (s32[16,12]{1,0:T(8,128)S(1)}, s32[16,12]{1,0:T(8,128)}, u32[]{:S(2)}) copy-start(s32[16,12]{1,0:T(8,128)} %param.11) | copy-start | bytes 2308
  0.7 22.6 %copy-start.6 = (f32[3,64,64]{2,1,0:T(8,128)S(1)}, f32[3,64,64]{2,1,0:T(8,128)}, u32[]{:S(2)}) copy-start(f32[3,64,64]{2,1,0:T(8,128)} %param.15) | copy-start | bytes 147460
  3.1 8.5 %collective-permute-start.2 = (f32[2,64,128]{2,1,0:T(8,128)S(1)}, f32[2,64,128]{2,1,0:T(8,128)S(1)}, u32[]{:S(2)}, u32[]{:S(2)}) collective-permute-start(f32[2,64,128]{2,1,0:T(8,128)S(1)} %convolution_bitcast_fusion.2), channel_id=1, source_target_pairs={{0,4},{4,0},{8,12},{12,8},{16,20},{20,16},{24,28},{28,24},{1,5},{5... | collective-permute-start | bytes 196616 | tf_op jit(solution)/shard_map/ppermute | solution.py:17
  5.7 26.7 %collective-permute-start.1 = (bf16[2,1024,128]{2,1,0:T(8,128)(2,1)}, bf16[2,1024,128]{2,1,0:T(8,128)(2,1)S(1)}, u32[]{:S(2)}, u32[]{:S(2)}) collective-permute-start(bf16[2,1024,128]{2,1,0:T(8,128)(2,1)} %get-tuple-element.26), channel_id=1, source_target_pairs={{4,0},{8,4},{12,8},{16,12},{20,16},{24,20},{28,24},{5,1},{9,5},{13... | collective-permute-start | bytes 1572872 | tf_op jit(solution)/shard_map/ppermute | solution.py:23
  8.0 24.4 %collective-permute-start = (bf16[2,1024,128]{2,1,0:T(8,128)(2,1)}, bf16[2,1024,128]{2,1,0:T(8,128)(2,1)S(1)}, u32[]{:S(2)}, u32[]{:S(2)}) collective-permute-start(bf16[2,1024,128]{2,1,0:T(8,128)(2,1)} %get-tuple-element.27), channel_id=1, source_target_pairs={{0,4},{4,8},{8,12},{12,16},{16,20},{20,24},{24,28},{1,5},{5,9},{9,... | collective-permute-start | bytes 1572872 | tf_op jit(solution)/shard_map/ppermute | solution.py:23
  11.6 11.5 %collective-permute-start.3 = (f32[2,64,128]{2,1,0:T(8,128)S(1)}, f32[2,64,128]{2,1,0:T(8,128)S(1)}, u32[]{:S(2)}, u32[]{:S(2)}) collective-permute-start(f32[2,64,128]{2,1,0:T(8,128)S(1)} %add.65), channel_id=1, source_target_pairs={{0,8},{4,12},{8,0},{12,4},{16,24},{20,28},{24,16},{28,20},{1,9},{5... | collective-permute-start | bytes 196616 | tf_op jit(solution)/shard_map/ppermute | solution.py:17
  23.2 5.2 %collective-permute-start.4 = (f32[2,64,128]{2,1,0:T(8,128)S(1)}, f32[2,64,128]{2,1,0:T(8,128)S(1)}, u32[]{:S(2)}, u32[]{:S(2)}) collective-permute-start(f32[2,64,128]{2,1,0:T(8,128)S(1)} %add.67), channel_id=1, source_target_pairs={{0,16},{4,20},{8,24},{12,28},{16,0},{20,4},{24,8},{28,12},{1,17},{... | collective-permute-start | bytes 196616 | tf_op jit(solution)/shard_map/ppermute | solution.py:17
  32.5 0.8 copy-start.4
  33.3 0.8 copy-start.5
  41.5 4.6 %copy-start.2 = (bf16[2,2048,128]{2,1,0:T(8,128)(2,1)S(1)}, bf16[2,2048,128]{2,1,0:T(8,128)(2,1)}, u32[]{:S(2)}) copy-start(bf16[2,2048,128]{2,1,0:T(8,128)(2,1)} %shard_map.111) | copy-start | bytes 3145732
  46.1 1.0 %copy-start.7 = (bf16[128,128]{1,0:T(8,128)(2,1)S(1)}, bf16[128,128]{1,0:T(8,128)(2,1)}, u32[]{:S(2)}) copy-start(bf16[128,128]{1,0:T(8,128)(2,1)} %param.14) | copy-start | bytes 98308
  46.1 1.9 %copy-start.8 = (bf16[128,128]{1,0:T(8,128)(2,1)S(1)}, bf16[128,128]{1,0:T(8,128)(2,1)}, u32[]{:S(2)}) copy-start(bf16[128,128]{1,0:T(8,128)(2,1)} %param.13) | copy-start | bytes 98308
  47.3 5.8 %collective-permute-start.5 = (f32[384,128]{1,0:T(8,128)S(1)}, f32[384,128]{1,0:T(8,128)S(1)}, u32[]{:S(2)}, u32[]{:S(2)}) collective-permute-start(f32[384,128]{1,0:T(8,128)S(1)} %pad_maximum_fusion.1), channel_id=1, source_target_pairs={{0,4},{4,0},{8,12},{12,8},{16,20},{20,16},{24,28},{28,24},{1,5},{5... | collective-permute-start | bytes 589832 | tf_op jit(solution)/shard_map/ppermute | solution.py:17
  53.1 10.4 %collective-permute-start.6 = (f32[384,128]{1,0:T(8,128)S(1)}, f32[384,128]{1,0:T(8,128)S(1)}, u32[]{:S(2)}, u32[]{:S(2)}) collective-permute-start(f32[384,128]{1,0:T(8,128)S(1)} %pad_maximum_fusion.2), channel_id=1, source_target_pairs={{0,8},{4,12},{8,0},{12,4},{16,24},{20,28},{24,16},{28,20},{1,9},{5... | collective-permute-start | bytes 589832 | tf_op jit(solution)/shard_map/ppermute | solution.py:17
  63.6 11.5 %copy-start.3 = (f32[2,2048,128]{2,1,0:T(8,128)S(1)}, f32[2,2048,128]{2,1,0:T(8,128)}, u32[]{:S(2)}) copy-start(f32[2,2048,128]{2,1,0:T(8,128)} %get-tuple-element.18) | copy-start | bytes 6291460
  63.6 8.1 %collective-permute-start.7 = (f32[384,128]{1,0:T(8,128)S(1)}, f32[384,128]{1,0:T(8,128)S(1)}, u32[]{:S(2)}, u32[]{:S(2)}) collective-permute-start(f32[384,128]{1,0:T(8,128)S(1)} %pad_maximum_fusion.3), channel_id=1, source_target_pairs={{0,16},{4,20},{8,24},{12,28},{16,0},{20,4},{24,8},{28,12},{1,17},{... | collective-permute-start | bytes 589832 | tf_op jit(solution)/shard_map/ppermute | solution.py:17
  64.1 25.1 %collective-permute-start.8 = (bf16[2,1024,128]{2,1,0:T(8,128)(2,1)}, bf16[2,1024,128]{2,1,0:T(8,128)(2,1)S(1)}, u32[]{:S(2)}, u32[]{:S(2)}) collective-permute-start(bf16[2,1024,128]{2,1,0:T(8,128)(2,1)} %get-tuple-element.20), channel_id=1, source_target_pairs={{0,4},{4,8},{8,12},{12,16},{16,20},{20,24},{24,28},{1,5},{5,9},{9,... | collective-permute-start | bytes 1572872 | tf_op jit(solution)/shard_map/ppermute | solution.py:23
  67.7 25.5 %collective-permute-start.9 = (bf16[2,1024,128]{2,1,0:T(8,128)(2,1)}, bf16[2,1024,128]{2,1,0:T(8,128)(2,1)S(1)}, u32[]{:S(2)}, u32[]{:S(2)}) collective-permute-start(bf16[2,1024,128]{2,1,0:T(8,128)(2,1)} %get-tuple-element.21), channel_id=1, source_target_pairs={{4,0},{8,4},{12,8},{16,12},{20,16},{24,20},{28,24},{5,1},{9,5},{13... | collective-permute-start | bytes 1572872 | tf_op jit(solution)/shard_map/ppermute | solution.py:23
  71.7 1.4 %collective-permute-start.10 = (f32[256,128]{1,0:T(8,128)S(1)}, f32[256,128]{1,0:T(8,128)S(1)}, u32[]{:S(2)}, u32[]{:S(2)}) collective-permute-start(f32[256,128]{1,0:T(8,128)S(1)} %slice_add_fusion.2), channel_id=1, source_target_pairs={{0,1},{1,0},{2,3},{3,2},{4,5},{5,4},{6,7},{7,6},{8,9},{9,8},{10,11... | collective-permute-start | bytes 393224 | tf_op jit(solution)/shard_map/ppermute | solution.py:17
  73.2 5.6 %collective-permute-start.11 = (f32[256,128]{1,0:T(8,128)S(1)}, f32[256,128]{1,0:T(8,128)S(1)}, u32[]{:S(2)}, u32[]{:S(2)}) collective-permute-start(f32[256,128]{1,0:T(8,128)S(1)} %add.82), channel_id=1, source_target_pairs={{0,2},{1,3},{2,0},{3,1},{4,6},{5,7},{6,4},{7,5},{8,10},{9,11},{10,... | collective-permute-start | bytes 393224 | tf_op jit(solution)/shard_map/ppermute | solution.py:17
